TPU v7x, 32 devices: a whole 2x2x4 slice. The times are simulated.
32 devices in a mesh: seq: 8 (over z, y), fsdp: 4 (over x, core).
Axes of the slice: x: 2, y: 2, z: 4, core: 2. Of those that a mesh axis runs over, the one named last changes fastest.
Arguments:
- tokens: bfloat16 [2048, 2048], P('seq', 'fsdp'), may hold values from -6 to 6
- deal_order: int32 [8, 8], replicated, may hold values from 0 to 7, each once within a row
- lengths: int32 [4], replicated, may hold values from 1 to 1024, 2048 in all
- x_weight: bfloat16 [2048, 1536], P(None, 'fsdp'), may hold values from -0.0390625 to 0.0390625
- z_weight: bfloat16 [2048, 1536], P(None, 'fsdp'), may hold values from -0.125 to 0.125
- shared_weight: bfloat16 [2048, 512], P('fsdp'), may hold values from -0.0390625 to 0.0390625
- step_weight: bfloat16 [2048, 24], P(None, 'fsdp'), may hold values from -0.125 to 0.125
- conv_heads: float32 [4, 1536], P(None, 'fsdp'), may hold values from -3 to 3
- conv_shared: float32 [4, 512], replicated, may hold values from -3 to 3
- step_bias: float32 [24], P('fsdp'), as said below
- decay_log: float32 [24], P('fsdp'), may hold values from -7.1 to -2.8, as said below
- skip_gain: float32 [24], P('fsdp'), may hold values from 0.5 to 1.5
Outputs:
- mixed: bfloat16 [2048, 1536], P('seq', 'fsdp')
Inputs may be any that keep to these rules, and one draw needn't show every extreme that they name: `deal_order`: each row is a permutation of 0 to 7. The lengths sum to 2048. `decay_log`: one value a head. `step_bias`: one value a head.
All inputs are finite; a program needn't handle non-finite values.
Results may differ from a plain program's by a relative error of at most 0.0095.
Values may be sent and summed in bfloat16 or wider, within the bound.
No kernel may reach another device: no remote copies, remote signals or barrier semaphores. Data moves between devices by JAX's collectives and lax.ppermute only.
A program may use at most 128 MiB of HBM per device.

v0:
```python
import jax
import jax.numpy as jnp
from jax import lax
from jax.sharding import PartitionSpec as P

precise = lax.Precision.HIGHEST


def shifted(array, axis, by):
    count = lax.axis_size(axis)
    pairs = [(i, i + by) for i in range(count) if 0 <= i + by < count]
    return lax.ppermute(array, axis, pairs)


def prefix(part, axis, combine, identity):
    place = lax.axis_index(axis)
    gathered = jax.tree.map(lambda a: lax.all_gather(a, axis), part)
    state = jax.tree.map(lambda a, e: jnp.zeros_like(a) + jnp.asarray(e, a.dtype), part, identity)

    def one(turn, state):
        return combine(
            state, jax.tree.map(lambda a: lax.dynamic_index_in_dim(a, turn, 0, False), gathered)
        )

    return lax.fori_loop(0, place, one, state)


def segment_of(positions, lengths):
    prompt_ends = jnp.cumsum(lengths)
    counted = (positions[:, None] >= prompt_ends[None, :]).astype(jnp.int32)
    return jnp.sum(counted, axis=1)


def causal_conv(extended, segment_ids, weights, conv_width):
    out_rows = extended.shape[0] - conv_width + 1
    target = segment_ids[conv_width - 1 :]
    running = jnp.zeros((out_rows, extended.shape[1]), jnp.float32)
    for tap_index in range(conv_width):
        matched = (segment_ids[tap_index : tap_index + out_rows] == target).astype(jnp.float32)
        running = (
            running
            + weights[tap_index][None, :]
            * extended[tap_index : tap_index + out_rows]
            * matched[:, None]
        )
    return running


def local_terms(x_heads, b_rows, c_rows, step_size, decay_log, segment_ids, seg_before):
    log_decay = -jnp.exp(decay_log)[None, :] * step_size
    cum_decay = jnp.cumsum(log_decay, axis=0)
    positions_in = jnp.arange(x_heads.shape[0], dtype=jnp.int32)
    same_prompt = (segment_ids[:, None] == segment_ids[None, :]) & (
        positions_in[:, None] >= positions_in[None, :]
    )
    decay_gap = cum_decay.T[:, :, None] - cum_decay.T[:, None, :]
    decay_matrix = jnp.exp(jnp.where(same_prompt[None], decay_gap, -jnp.inf))
    scores = jnp.dot(c_rows, b_rows.T, precision=precise)
    x_step = x_heads * step_size[:, :, None]
    intra = jnp.einsum("hts,shp->thp", scores[None] * decay_matrix, x_step, precision=precise)
    to_end = jnp.exp(
        jnp.where(
            (segment_ids == segment_ids[-1])[:, None], cum_decay[-1][None, :] - cum_decay, -jnp.inf
        )
    )
    state_out = jnp.einsum("shp,sn->hpn", x_step * to_end[:, :, None], b_rows, precision=precise)
    carried = segment_ids == seg_before
    carry_in = jnp.exp(jnp.where(carried[:, None], cum_decay, -jnp.inf))
    block_decay = jnp.where(carried[-1], jnp.exp(cum_decay[-1]), 0.0)
    return (intra, state_out, carry_in, block_decay)


def combine(earlier, later):
    return (earlier[0] * later[0], later[0][:, None, None] * earlier[1] + later[1])


def per_device(
    tokens,
    deal_order,
    lengths,
    x_weight,
    z_weight,
    shared_weight,
    step_weight,
    conv_heads,
    conv_shared,
    step_bias,
    decay_log,
    skip_gain,
):
    seq_count = lax.axis_size("seq")
    own_index = lax.axis_index("seq")
    tok_dev = tokens.shape[0]
    piece_rows = tok_dev // seq_count
    slot_rows = tokens.reshape(seq_count, piece_rows, tokens.shape[1])
    arrived = lax.all_to_all(slot_rows, "seq", split_axis=0, concat_axis=0, tiled=True)
    dealt_row = lax.dynamic_slice_in_dim(deal_order, own_index, 1, 0)[0]
    inverse = jnp.argsort(dealt_row)
    stream_block = jnp.take(arrived, inverse, axis=0).reshape(tok_dev, tokens.shape[1])
    inner_dev = x_weight.shape[1]
    heads_dev = step_weight.shape[1]
    head_dim = inner_dev // heads_dev
    state_dim = shared_weight.shape[1] // 2
    w_full = lax.all_gather(shared_weight, "fsdp", axis=0, tiled=True)
    weight_list = (x_weight, z_weight, step_weight, w_full)
    feature_part = lax.all_gather(stream_block, "fsdp", axis=1, tiled=True)
    x_acc, z_acc, step_acc, bc_acc = tuple(
        (
            jnp.dot(feature_part, weight, preferred_element_type=jnp.float32)
            for weight in weight_list
        )
    )
    x_raw = x_acc.astype(jnp.bfloat16)
    z_raw = z_acc.astype(jnp.bfloat16)
    bc_raw = bc_acc.astype(jnp.bfloat16)
    step_size = jax.nn.softplus(step_acc + step_bias[None, :])
    mixed_in = jnp.concatenate([x_raw, bc_raw], axis=1)
    conv_width = conv_heads.shape[0]
    prior_rows = shifted(mixed_in[tok_dev - conv_width + 1 :], "seq", 1)
    first_pos = own_index * tok_dev
    positions = first_pos - (conv_width - 1) + jnp.arange(tok_dev + conv_width - 1, dtype=jnp.int32)
    seg_ext = segment_of(positions, lengths)
    extended = jnp.concatenate([prior_rows, mixed_in], axis=0).astype(jnp.float32)
    activated = jax.nn.silu(
        causal_conv(
            extended, seg_ext, jnp.concatenate([conv_heads, conv_shared], axis=1), conv_width
        )
    )
    segment_ids = seg_ext[conv_width - 1 :]
    seg_before = jnp.where(own_index == 0, -1, seg_ext[conv_width - 2])
    x_heads = activated[:, :inner_dev].reshape(tok_dev, heads_dev, head_dim)
    b_rows = activated[:, inner_dev : inner_dev + state_dim]
    c_rows = activated[:, inner_dev + state_dim :]
    intra, state_out, carry_in, block_decay = local_terms(
        x_heads, b_rows, c_rows, step_size, decay_log, segment_ids, seg_before
    )
    identity = (jnp.ones_like(block_decay), jnp.zeros_like(state_out))
    _, state_in = prefix((block_decay, state_out), "seq", combine, identity)
    incoming = jnp.einsum("tn,hpn->thp", c_rows, state_in, precision=precise)
    y_block = intra + carry_in[:, :, None] * incoming + skip_gain[None, :, None] * x_heads
    gated = (y_block.reshape(tok_dev, inner_dev) * jax.nn.silu(z_raw.astype(jnp.float32))).astype(
        jnp.bfloat16
    )
    ordered = gated.reshape(seq_count, piece_rows, inner_dev)
    outgoing = jnp.take(ordered, dealt_row, axis=0)
    returned = lax.all_to_all(outgoing, "seq", split_axis=0, concat_axis=0, tiled=True)
    return returned.reshape(tok_dev, inner_dev)


def solution(mesh):
    return jax.shard_map(
        per_device,
        mesh=mesh,
        in_specs=(
            P("seq", "fsdp"),
            P(),
            P(),
            P(None, "fsdp"),
            P(None, "fsdp"),
            P("fsdp", None),
            P(None, "fsdp"),
            P(None, "fsdp"),
            P(),
            P("fsdp"),
            P("fsdp"),
            P("fsdp"),
        ),
        out_specs=P("seq", "fsdp"),
        check_vma=False,
    )
```

profile of v0, /device:TPU:0, one launch (start us, length us, event | category | flops | bytes accessed | tf_op | source)
XLA Modules:
  0.0 173.2 jit_solution(6664324433288918847)
XLA Ops:
  6.6 7.4 %all-to-all-start = ((bf16[8,32,512]{2,1,0:T(8,128)(2,1)}), bf16[8,32,512]{2,1,0:T(8,128)(2,1)S(1)}, u32[]{:S(2)}, u32[]{:S(2)}) async-start(bf16[8,32,512]{2,1,0:T(8,128)(2,1)} %bitcast.90), calls=%async_computation | async-start | bytes 524288 | tf_op jit(solution)/shard_map/all_to_all | solution.py:96
  14.0 1.3 compare_and_fusion.1
  15.3 1.0 sort.17
  16.3 0.1 broadcast_in_dim.88
  16.4 0.1 broadcast_in_dim.89
  16.5 6.5 %all-to-all-done = bf16[8,32,512]{2,1,0:T(8,128)(2,1)S(1)} async-done(((bf16[8,32,512]{2,1,0:T(8,128)(2,1)}), bf16[8,32,512]{2,1,0:T(8,128)(2,1)S(1)}, u32[]{:S(2)}, u32[]{:S(2)}) %all-to-all-start) | async-done | bytes 262176 | tf_op jit(solution)/shard_map/all_to_all | solution.py:96
  22.9 0.6 gather_fusion
  23.5 0.8 bitcast_select_fusion
  24.3 0.0 all-gather.8.cloned.1.call-start
  24.4 0.7 all-gather.8.cloned.1.call-update
  25.2 0.2 reduce-window.18
  25.3 0.1 convert_reduce_fusion
  25.4 0.6 fusion.51
  26.6 0.7 broadcast_compare_fusion
  27.4 0.6 slice.89
  28.0 12.2 %all-gather.6.cloned.1.call-done = bf16[256,2048]{1,0:T(8,128)(2,1)} async-done(((bf16[256,512]{1,0:T(8,128)(2,1)}), bf16[256,2048]{1,0:T(8,128)(2,1)}) %all-gather.6.cloned.1.call-update) | async-done | bytes 1048592 | tf_op jit(solution)/shard_map/all_gather | solution.py:106
  40.3 1.6 fusion.41
  41.9 1.8 %reduce-window.19 = f32[6,2,128]{2,1,0:T(2,128)S(1)} reduce-window(f32[6,2,128]{2,1,0:T(2,128)S(1)} %reshape.175, f32[]{:T(128)} %constant.76.clone.1), window={size=1x1x128 pad=0_0x0_0x127_0}, to_apply=%region_3.4 | reduce-window | flops 195072 | bytes 12292 | tf_op jit(solution)/shard_map/reduce-window.1
  43.8 0.1 slice.107
  43.8 0.1 copy.47
  44.0 0.1 copy.48
  44.1 0.1 add_bitcast_fusion
  44.2 0.8 slice_reduce_fusion
  45.0 0.1 select_exponential_fusion.1
  45.1 1.9 %convolution_convert_fusion.2 = bf16[256,384]{1,0:T(8,128)(2,1)S(1)} fusion(bf16[256,2048]{1,0:T(8,128)(2,1)} %all-gather.6.cloned.1.call-done, bf16[2048,384]{1,0:T(8,128)(2,1)S(1)} %copy-done), kind=kOutput, calls=%fused_computation.16 | convolution fusion | flops 402751488 | bytes 2818048 | tf_op jit(solution)/shard_map/dot_general | solution.py:109
  47.0 17.4 %all-gather.8.cloned.1.call-done = bf16[2048,512]{1,0:T(8,128)(2,1)} async-done(((bf16[512,512]{1,0:T(8,128)(2,1)}), bf16[2048,512]{1,0:T(8,128)(2,1)}) %all-gather.8.cloned.1.call-update) | async-done | bytes 2097168 | tf_op jit(solution)/shard_map/all_gather | solution.py:104
  64.5 2.3 %convolution_convert_fusion = bf16[256,512]{1,0:T(8,128)(2,1)S(1)} fusion(bf16[256,2048]{1,0:T(8,128)(2,1)S(1)} %copy-done.1, bf16[2048,512]{1,0:T(8,128)(2,1)} %all-gather.8.cloned.1.call-done), kind=kOutput, calls=%fused_computation.12 | convolution fusion | flops 537001984 | bytes 3407872 | tf_op jit(solution)/shard_map/dot_general | solution.py:109
  66.8 3.4 %collective-permute-start = (bf16[3,896]{1,0:T(4,128)(2,1)S(1)}, bf16[3,896]{1,0:T(4,128)(2,1)S(1)}, u32[]{:S(2)}, u32[]{:S(2)}) collective-permute-start(bf16[3,896]{1,0:T(4,128)(2,1)S(1)} %pad_maximum_fusion), channel_id=1, source_target_pairs={{0,4},{4,8},{8,12},{12,16},{16,20},{20,24},{24,28},{1,5},{5,9},{9,... | collective-permute-start | bytes 16136 | tf_op jit(solution)/shard_map/ppermute | solution.py:12
  70.2 1.3 collective-permute-done
  71.5 0.1 maximum_convert_fusion
  71.6 0.7 divide_multiply_fusion
  72.3 0.2 copy.46
  72.5 1.2 fusion.26
  73.8 0.1 slice.74
  73.8 0.7 fusion.47
  74.5 0.6 pad_clamp_fusion
  75.1 0.7 fusion.32
  75.9 21.6 %all-gather.1 = f32[8,1,6]{2,1,0:T(1,128)} all-gather(f32[1,1,6]{2,1,0:T(1,128)S(1)} %bitcast.96), channel_id=1, replica_groups=mesh['seq'=8,'fsdp'=4] {'seq'}, dimensions={0}, use_global_device_ids=true | all-gather | bytes 216 | tf_op jit(solution)/shard_map/all_gather | solution.py:17
  97.5 0.4 fusion.34
  97.9 37.2 %all-gather.10.cloned.1.call-done = f32[48,64,256]{2,1,0:T(8,128)} async-done(((f32[6,64,256]{2,1,0:T(8,128)}), f32[48,64,256]{2,1,0:T(8,128)}) %all-gather.10.cloned.1.call-update) | async-done | bytes 3145744 | tf_op jit(solution)/shard_map/all_gather | solution.py:17
  135.2 0.5 convolution_multiply_fusion
  135.7 2.8 %fusion.11 = f32[256,6,64]{0,2,1:T(8,128)S(1)} fusion(f32[256,6,64]{0,2,1:T(8,128)S(1)} %convolution_multiply_fusion, f32[6,256]{1,0:T(8,128)} %bitcast.93, f32[256,256]{1,0:T(8,128)S(1)} %fusion.34, pred[256,256]{1,0:T(8,128)(4,1)} %fusion.32, f32[256,6,64]{0,2,1:T(8,128)S(1)} %bitcast.86, f32[6]{0:T(128)} %param.25, f32[256,6]{0,1:T(8,128)S(1)} %compare_select_fusion.1), kind=kOutput, calls=%fused_computation.11 | convolution fusion | flops 303562752 | bytes 1519640 | tf_op jit(solution)/shard_map/hts,shp->thp/dot_general | solution.py:60
  138.5 0.2 copy.49
  138.7 2.5 %multiply_convert_fusion = bf16[256,384]{1,0:T(8,128)(2,1)S(1)} fusion(f32[256,384]{1,0:T(8,128)S(1)} %copy.49, bf16[256,2048]{1,0:T(8,128)(2,1)} %all-gather.6.cloned.1.call-done, bf16[2048,384]{1,0:T(8,128)(2,1)} %param.18), kind=kOutput, calls=%fused_computation.35 | convolution fusion | flops 403439616 | bytes 3211264 | tf_op jit(solution)/shard_map/dot_general | solution.py:109
  141.2 0.7 gather_fusion.1
  141.9 0.1 broadcast_select_fusion
  142.0 24.0 %all_to_all.10 = bf16[8,32,384]{2,1,0:T(8,128)(2,1)S(1)} all-to-all(bf16[8,32,384]{2,1,0:T(8,128)(2,1)S(1)} %broadcast_select_fusion), channel_id=1, replica_groups=mesh['seq'=8,'fsdp'=4] {'seq'}, dimensions={0} | all-to-all | bytes 393216 | tf_op jit(solution)/shard_map/all_to_all | solution.py:146
  166.0 0.7 copy.67
  (42 shorter events, 0.4 us)
Async XLA Ops:
  6.5 38.6 %copy-start = (bf16[2048,384]{1,0:T(8,128)(2,1)S(1)}, bf16[2048,384]{1,0:T(8,128)(2,1)}, u32[]{:S(2)}) copy-start(bf16[2048,384]{1,0:T(8,128)(2,1)} %param.17) | copy-start | bytes 4718596
  6.5 18.6 %copy-start.8 = (s32[4]{0:T(128)S(1)}, s32[4]{0:T(128)}, u32[]{:S(2)}) copy-start(s32[4]{0:T(128)} %param.16) | copy-start | bytes 52
  6.5 21.4 %copy-start.5 = (f32[4,384]{1,0:T(4,128)S(1)}, f32[4,384]{1,0:T(4,128)}, u32[]{:S(2)}) copy-start(f32[4,384]{1,0:T(4,128)} %param.21) | copy-start | bytes 18436
  6.5 21.4 %copy-start.4 = (f32[4,512]{1,0:T(4,128)S(1)}, f32[4,512]{1,0:T(4,128)}, u32[]{:S(2)}) copy-start(f32[4,512]{1,0:T(4,128)} %param.22) | copy-start | bytes 24580
  6.5 21.5 %copy-start.9 = (f32[6]{0:T(128)S(1)}, f32[6]{0:T(128)}, u32[]{:S(2)}) copy-start(f32[6]{0:T(128)} %param.24) | copy-start | bytes 76
  6.5 33.7 %copy-start.2 = (bf16[2048,6]{0,1:T(8,128)(2,1)S(1)}, bf16[2048,6]{0,1:T(8,128)(2,1)}, u32[]{:S(2)}) copy-start(bf16[2048,6]{0,1:T(8,128)(2,1)} %param.20) | copy-start | bytes 73732
  6.6 33.7 %copy-start.7 = (f32[6]{0:T(128)S(1)}, f32[6]{0:T(128)}, u32[]{:S(2)}) copy-start(f32[6]{0:T(128)} %param.23) | copy-start | bytes 76
  6.6 16.3 %all-to-all-start = ((bf16[8,32,512]{2,1,0:T(8,128)(2,1)}), bf16[8,32,512]{2,1,0:T(8,128)(2,1)S(1)}, u32[]{:S(2)}, u32[]{:S(2)}) async-start(bf16[8,32,512]{2,1,0:T(8,128)(2,1)} %bitcast.90), calls=%async_computation | async-start | bytes 524288 | tf_op jit(solution)/shard_map/all_to_all | solution.py:96
  14.0 26.3 %all-gather.6.cloned.1.call-start = ((), (), s32[]{:S(2)}) async-start(), calls=%async_computation.2 | async-start | bytes 1310720 | tf_op jit(solution)/shard_map/all_gather | solution.py:106
  24.3 40.1 %all-gather.8.cloned.1.call-start = ((), (), s32[]{:S(2)}) async-start(), calls=%async_computation.3 | async-start | bytes 2621440 | tf_op jit(solution)/shard_map/all_gather | solution.py:104
  25.1 110.1 %all-gather.10.cloned.1.call-start = ((), (), s32[]{:S(2)}) async-start(), calls=%async_computation.4 | async-start | bytes 3538944 | tf_op jit(solution)/shard_map/all_gather | solution.py:17
  41.9 22.5 %copy-start.1 = (bf16[256,2048]{1,0:T(8,128)(2,1)S(1)}, bf16[256,2048]{1,0:T(8,128)(2,1)}, u32[]{:S(2)}) copy-start(bf16[256,2048]{1,0:T(8,128)(2,1)} %all-gather.6.cloned.1.call-done) | copy-start | bytes 3145732
  44.2 0.8 copy-start.3
  66.8 4.7 %collective-permute-start = (bf16[3,896]{1,0:T(4,128)(2,1)S(1)}, bf16[3,896]{1,0:T(4,128)(2,1)S(1)}, u32[]{:S(2)}, u32[]{:S(2)}) collective-permute-start(bf16[3,896]{1,0:T(4,128)(2,1)S(1)} %pad_maximum_fusion), channel_id=1, source_target_pairs={{0,4},{4,8},{8,12},{12,16},{16,20},{20,24},{24,28},{1,5},{5,9},{9,... | collective-permute-start | bytes 16136 | tf_op jit(solution)/shard_map/ppermute | solution.py:12
  138.7 3.2 %copy-start.6 = (pred[8]{0:T(512)(128)(4,1)S(1)}, pred[8]{0:T(512)(128)(4,1)}, u32[]{:S(2)}) copy-start(pred[8]{0:T(512)(128)(4,1)} %get-tuple-element.68) | copy-start | bytes 28
Sparse Core Ops, SparseCore 0:
  24.5 15.7 all-gather.5
  41.8 22.5 all-gather.7
  73.9 61.2 all-gather.9
where the time goes:
time: 174 us; the launch traced here: 173 us
  waiting for transfers between devices  75.4 us (43%)
  blocking collectives  45.7 us (26%)
  between operations  14 us (8%)
  matrix products  13.3 us (8%)
  starting transfers between devices  10.9 us (6%)
  other arithmetic  9.84 us (6%)
  local copies, waits for them, and re-layouts  4.14 us (2%)
    all_gather x1, waiting for transfers between devices, prefix(): gathered = jax.tree.map(lambda a: lax.all_gather(a, axis), part)  37.2 us
    all_to_all x1, blocking collectives, per_device(): lax.all_to_all(outgoing, 'seq', split_axis=0, concat_axis=0, tiled=True)  24 us
    all_gather x1, blocking collectives, prefix(): gathered = jax.tree.map(lambda a: lax.all_gather(a, axis), part)  21.6 us
    all_gather x1, waiting for transfers between devices, per_device(): w_full = lax.all_gather(shared_weight, 'fsdp', axis=0, tiled=True)  17.4 us
    all_gather x1, waiting for transfers between devices, per_device(): feature_part = lax.all_gather(stream_block, 'fsdp', axis=1, tiled=True)  12.2 us
    dot_general x4, matrix products, per_device(): jnp.dot(feature_part, weight, preferred_element_type=jnp.float32)  8.34 us
    all_to_all x1, starting transfers between devices, per_device(): lax.all_to_all(slot_rows, 'seq', split_axis=0, concat_axis=0, tiled=True)  7.42 us
    all_to_all x1, waiting for transfers between devices, per_device(): lax.all_to_all(slot_rows, 'seq', split_axis=0, concat_axis=0, tiled=True)  6.45 us
  transfers between devices with their start and end apart: 5, of which 5 were waited for; matrix products, arithmetic and copies ran while one was open for 8% of the time, Pallas kernels for 0%

commit v1 on v0

--- a/solution.py
+++ b/solution.py
@@ -12,17 +12,32 @@
     return lax.ppermute(array, axis, pairs)
 
 
-def prefix(part, axis, combine, identity):
+def combine_packed(earlier, later):
+    rows = later.shape[1] - 1
+    d_e, d_l = earlier[:, rows:, :], later[:, rows:, :]
+    return jnp.concatenate([d_l * earlier[:, :rows, :] + later[:, :rows, :], d_e * d_l], axis=1)
+
+
+def received(packed, axis, by):
     place = lax.axis_index(axis)
-    gathered = jax.tree.map(lambda a: lax.all_gather(a, axis), part)
-    state = jax.tree.map(lambda a, e: jnp.zeros_like(a) + jnp.asarray(e, a.dtype), part, identity)
+    got = shifted(packed, axis, by)
+    rows = packed.shape[1] - 1
+    missing = (place < by).astype(packed.dtype)
+    return got.at[:, rows:, :].add(missing)
 
-    def one(turn, state):
-        return combine(
-            state, jax.tree.map(lambda a: lax.dynamic_index_in_dim(a, turn, 0, False), gathered)
-        )
 
-    return lax.fori_loop(0, place, one, state)
+def exclusive_scan(packed, axis):
+    count = lax.axis_size(axis)
+    if count == 1:
+        return received(packed, axis, 1)
+    held = received(packed, axis, 1)
+    if count > 2:
+        held = combine_packed(received(packed, axis, 2), held)
+    cover = 2
+    while cover < count - 1:
+        held = combine_packed(received(held, axis, cover), held)
+        cover *= 2
+    return held
 
 
 def segment_of(positions, lengths):
@@ -68,10 +83,6 @@
     carry_in = jnp.exp(jnp.where(carried[:, None], cum_decay, -jnp.inf))
     block_decay = jnp.where(carried[-1], jnp.exp(cum_decay[-1]), 0.0)
     return (intra, state_out, carry_in, block_decay)
-
-
-def combine(earlier, later):
-    return (earlier[0] * later[0], later[0][:, None, None] * earlier[1] + later[1])
 
 
 def per_device(
@@ -134,8 +145,10 @@
     intra, state_out, carry_in, block_decay = local_terms(
         x_heads, b_rows, c_rows, step_size, decay_log, segment_ids, seg_before
     )
-    identity = (jnp.ones_like(block_decay), jnp.zeros_like(state_out))
-    _, state_in = prefix((block_decay, state_out), "seq", combine, identity)
+    packed = jnp.concatenate(
+        [state_out, jnp.broadcast_to(block_decay[:, None, None], (heads_dev, 1, state_dim))], axis=1
+    )
+    state_in = exclusive_scan(packed, "seq")[:, :head_dim, :]
     incoming = jnp.einsum("tn,hpn->thp", c_rows, state_in, precision=precise)
     y_block = intra + carry_in[:, :, None] * incoming + skip_gain[None, :, None] * x_heads
     gated = (y_block.reshape(tok_dev, inner_dev) * jax.nn.silu(z_raw.astype(jnp.float32))).astype(

time: 174 us -> 162 us (0.931)
  starting transfers between devices: 10.9 us -> 36.3 us
  waiting for transfers between devices: 75.4 us -> 51.2 us
  blocking collectives: 45.7 us -> 22.9 us
  other arithmetic: 9.84 us -> 15.7 us
  local copies, waits for them, and re-layouts: 4.14 us -> 9.22 us
    all_gather x1 -> x0, waiting for transfers between devices: 37.2 us -> none  [prefix(): gathered = jax.tree.map(lambda a: lax.all_gather(a, axis), part)]
    ppermute x1 -> x5, starting transfers between devices: 3.38 us -> 28.8 us  [shifted(): return lax.ppermute(array, axis, pairs)]
    all_gather x1 -> x0, blocking collectives: 21.6 us -> none  [prefix(): gathered = jax.tree.map(lambda a: lax.all_gather(a, axis), part)]
    ppermute x1 -> x5, waiting for transfers between devices: 1.32 us -> 15.9 us  [shifted(): return lax.ppermute(array, axis, pairs)]
    slice x2, local copies, waits for them, and re-layouts: 0.19 us -> 2.68 us  [per_device(): x_heads = activated[:, :inner_dev].reshape(tok_dev, heads_dev, head_dim)]
  transfers between devices with their start and end apart: 5 -> 8, of which waited for: 5 -> 8; matrix products, arithmetic and copies ran while one was open for 8% -> 13% of each run, Pallas kernels for 0% -> 0%
where the time goes in v1:
time: 162 us; the launch traced here: 161 us
  waiting for transfers between devices  51.2 us (32%)
  starting transfers between devices  36.3 us (22%)
  blocking collectives  22.9 us (14%)
  other arithmetic  15.7 us (10%)
  between operations  14.4 us (9%)
  matrix products  11.6 us (7%)
  local copies, waits for them, and re-layouts  9.22 us (6%)
    ppermute x5, starting transfers between devices, shifted(): return lax.ppermute(array, axis, pairs)  28.8 us
    all_to_all x1, blocking collectives, per_device(): lax.all_to_all(outgoing, 'seq', split_axis=0, concat_axis=0, tiled=True)  22.9 us
    all_gather x1, waiting for transfers between devices, per_device(): w_full = lax.all_gather(shared_weight, 'fsdp', axis=0, tiled=True)  17.1 us
    ppermute x5, waiting for transfers between devices, shifted(): return lax.ppermute(array, axis, pairs)  15.9 us
    all_gather x1, waiting for transfers between devices, per_device(): feature_part = lax.all_gather(stream_block, 'fsdp', axis=1, tiled=True)  11.1 us
    all_to_all x1, starting transfers between devices, per_device(): lax.all_to_all(slot_rows, 'seq', split_axis=0, concat_axis=0, tiled=True)  7.42 us
    dot_general x4, matrix products, per_device(): jnp.dot(feature_part, weight, preferred_element_type=jnp.float32)  7.29 us
    all_to_all x1, waiting for transfers between devices, per_device(): lax.all_to_all(slot_rows, 'seq', split_axis=0, concat_axis=0, tiled=True)  6.42 us
  transfers between devices with their start and end apart: 8, of which 8 were waited for; matrix products, arithmetic and copies ran while one was open for 13% of the time, Pallas kernels for 0%

profile of v1, /device:TPU:0, one launch (start us, length us, event | category | flops | bytes accessed | tf_op | source)
XLA Modules:
  0.0 161.2 jit_solution(1924981026122222076)
XLA Ops:
  6.6 7.4 %all-to-all-start = ((bf16[8,32,512]{2,1,0:T(8,128)(2,1)}), bf16[8,32,512]{2,1,0:T(8,128)(2,1)S(1)}, u32[]{:S(2)}, u32[]{:S(2)}) async-start(bf16[8,32,512]{2,1,0:T(8,128)(2,1)} %bitcast.85), calls=%async_computation | async-start | bytes 524288 | tf_op jit(solution)/shard_map/all_to_all | solution.py:107
  14.0 1.3 compare_and_fusion.1
  15.3 1.0 sort.17
  16.5 6.4 %all-to-all-done = bf16[8,32,512]{2,1,0:T(8,128)(2,1)S(1)} async-done(((bf16[8,32,512]{2,1,0:T(8,128)(2,1)}), bf16[8,32,512]{2,1,0:T(8,128)(2,1)S(1)}, u32[]{:S(2)}, u32[]{:S(2)}) %all-to-all-start) | async-done | bytes 262176 | tf_op jit(solution)/shard_map/all_to_all | solution.py:107
  22.9 0.6 gather_fusion
  23.5 0.8 bitcast_select_fusion
  24.4 0.7 all-gather.5.cloned.1.call-update
  25.4 0.6 fusion.53
  26.5 1.3 broadcast_compare_fusion
  27.9 0.7 slice.199
  28.5 0.6 slice_reduce_fusion.4
  29.2 11.1 %all-gather.3.cloned.1.call-done = bf16[256,2048]{1,0:T(8,128)(2,1)} async-done(((bf16[256,512]{1,0:T(8,128)(2,1)}), bf16[256,2048]{1,0:T(8,128)(2,1)}) %all-gather.3.cloned.1.call-update) | async-done | bytes 1048592 | tf_op jit(solution)/shard_map/all_gather | solution.py:117
  40.2 1.6 %fusion.41 = (f32[6,256]{1,0:T(8,128)S(1)}, f32[256,6]{0,1:T(8,128)S(1)}) fusion(f32[6]{0:T(128)S(1)} %exponential_negate_fusion, f32[6]{0:T(128)S(1)} %copy-done.19, bf16[256,2048]{1,0:T(8,128)(2,1)} %all-gather.3.cloned.1.call-done, bf16[2048,6]{0,1:T(8,128)(2,1)S(1)} %copy-done.4), kind=kOutput, calls=%fused_computation.64 | convolution fusion | flops 6303744 | bytes 1085488 | tf_op jit(solution)/shard_map/dot_general | solution.py:120
  41.9 1.8 %reduce-window.19 = f32[6,2,128]{2,1,0:T(2,128)S(1)} reduce-window(f32[6,2,128]{2,1,0:T(2,128)S(1)} %reshape.288, f32[]{:T(128)} %constant.149.clone.1), window={size=1x1x128 pad=0_0x0_0x127_0}, to_apply=%region_3.4 | reduce-window | flops 195072 | bytes 12292 | tf_op jit(solution)/shard_map/reduce-window.1
  44.3 0.4 copy-done.7
  44.7 0.7 select_exponential_fusion.1
  45.4 1.9 %convolution_convert_fusion.2 = bf16[256,384]{1,0:T(8,128)(2,1)S(1)} fusion(bf16[256,2048]{1,0:T(8,128)(2,1)} %all-gather.3.cloned.1.call-done, bf16[2048,384]{1,0:T(8,128)(2,1)S(1)} %copy-done), kind=kOutput, calls=%fused_computation.14 | convolution fusion | flops 402751488 | bytes 2818048 | tf_op jit(solution)/shard_map/dot_general | solution.py:120
  47.3 17.1 %all-gather.5.cloned.1.call-done = bf16[2048,512]{1,0:T(8,128)(2,1)} async-done(((bf16[512,512]{1,0:T(8,128)(2,1)}), bf16[2048,512]{1,0:T(8,128)(2,1)}) %all-gather.5.cloned.1.call-update) | async-done | bytes 2097168 | tf_op jit(solution)/shard_map/all_gather | solution.py:115
  64.4 2.3 %convolution_convert_fusion = bf16[256,512]{1,0:T(8,128)(2,1)S(1)} fusion(bf16[256,2048]{1,0:T(8,128)(2,1)S(1)} %copy-done.1, bf16[2048,512]{1,0:T(8,128)(2,1)} %all-gather.5.cloned.1.call-done), kind=kOutput, calls=%fused_computation.8 | convolution fusion | flops 537001984 | bytes 3407872 | tf_op jit(solution)/shard_map/dot_general | solution.py:120
  66.8 3.4 %collective-permute-start = (bf16[3,896]{1,0:T(4,128)(2,1)S(1)}, bf16[3,896]{1,0:T(4,128)(2,1)S(1)}, u32[]{:S(2)}, u32[]{:S(2)}) collective-permute-start(bf16[3,896]{1,0:T(4,128)(2,1)S(1)} %pad_maximum_fusion.3), channel_id=1, source_target_pairs={{0,4},{4,8},{8,12},{12,16},{16,20},{20,24},{24,28},{1,5},{5,9},{9,... | collective-permute-start | bytes 16136 | tf_op jit(solution)/shard_map/ppermute | solution.py:12
  70.2 1.2 broadcast_select_fusion.1
  71.7 0.7 divide_multiply_fusion
  72.4 0.8 slice.219
  73.1 1.9 %copy.39 = f32[256,384]{0,1:T(8,128)} copy(f32[256,384]{1,0:T(8,128)} %slice.219) | data formatting | bytes 786432 | tf_op jit(solution)/shard_map/slice | solution.py:142
  75.1 1.5 fusion.25
  76.5 0.7 broadcast_in_dim.104
  77.3 0.8 pad_maximum_fusion
  78.1 5.9 %collective-permute-start.2 = (f32[6,65,256]{2,1,0:T(8,128)}, f32[6,65,256]{2,1,0:T(8,128)}, u32[]{:S(2)}, u32[]{:S(2)}) collective-permute-start(f32[6,65,256]{2,1,0:T(8,128)} %pad_maximum_fusion), channel_id=1, source_target_pairs={{0,8},{4,12},{8,16},{12,20},{16,24},{20,28},{1,9},{5,13},{9,17},{1... | collective-permute-start | bytes 1198088 | tf_op jit(solution)/shard_map/ppermute | solution.py:12
  83.9 3.2 %collective-permute-start.1 = (f32[6,65,256]{2,1,0:T(8,128)}, f32[6,65,256]{2,1,0:T(8,128)}, u32[]{:S(2)}, u32[]{:S(2)}) collective-permute-start(f32[6,65,256]{2,1,0:T(8,128)} %pad_maximum_fusion), channel_id=1, source_target_pairs={{0,4},{4,8},{8,12},{12,16},{16,20},{20,24},{24,28},{1,5},{5,9},{9,... | collective-permute-start | bytes 1198088 | tf_op jit(solution)/shard_map/ppermute | solution.py:12
  87.2 0.7 slice.182
  87.8 0.8 fusion.49
  88.7 0.9 fusion.31
  89.5 2.6 %collective-permute-done.2 = f32[6,65,256]{2,1,0:T(8,128)} collective-permute-done((f32[6,65,256]{2,1,0:T(8,128)}, f32[6,65,256]{2,1,0:T(8,128)}, u32[]{:S(2)}, u32[]{:S(2)}) %collective-permute-start.2) | collective-permute-done | bytes 399392 | tf_op jit(solution)/shard_map/ppermute | solution.py:12
  92.1 3.0 %collective-permute-done.1 = f32[6,65,256]{2,1,0:T(8,128)} collective-permute-done((f32[6,65,256]{2,1,0:T(8,128)}, f32[6,65,256]{2,1,0:T(8,128)}, u32[]{:S(2)}, u32[]{:S(2)}) %collective-permute-start.1) | collective-permute-done | bytes 399392 | tf_op jit(solution)/shard_map/ppermute | solution.py:12
  95.1 0.8 fusion.47
  96.0 1.2 slice_add_fusion
  97.2 10.9 %collective-permute-start.3 = (f32[6,65,256]{2,1,0:T(8,128)S(1)}, f32[6,65,256]{2,1,0:T(8,128)S(1)}, u32[]{:S(2)}, u32[]{:S(2)}) collective-permute-start(f32[6,65,256]{2,1,0:T(8,128)S(1)} %pad_maximum_fusion.1), channel_id=1, source_target_pairs={{0,8},{4,12},{8,16},{12,20},{16,24},{20,28},{1,9},{5,13},{9,17},{1... | collective-permute-start | bytes 1198088 | tf_op jit(solution)/shard_map/ppermute | solution.py:12
  108.1 0.6 pad_clamp_fusion
  108.7 1.4 fusion.10
  110.2 5.7 %collective-permute-done.3 = f32[6,65,256]{2,1,0:T(8,128)S(1)} collective-permute-done((f32[6,65,256]{2,1,0:T(8,128)S(1)}, f32[6,65,256]{2,1,0:T(8,128)S(1)}, u32[]{:S(2)}, u32[]{:S(2)}) %collective-permute-start.3) | collective-permute-done | bytes 399392 | tf_op jit(solution)/shard_map/ppermute | solution.py:12
  116.0 5.3 %collective-permute-start.4 = (f32[6,65,256]{2,1,0:T(8,128)S(1)}, f32[6,65,256]{2,1,0:T(8,128)S(1)}, u32[]{:S(2)}, u32[]{:S(2)}) collective-permute-start(f32[6,65,256]{2,1,0:T(8,128)S(1)} %pad_maximum_fusion.2), channel_id=1, source_target_pairs={{0,16},{4,20},{8,24},{12,28},{1,17},{5,21},{9,25},{13,29},{2,18},{... | collective-permute-start | bytes 1198088 | tf_op jit(solution)/shard_map/ppermute | solution.py:12
  121.7 1.9 %fusion.5 = f32[256,6,64]{0,2,1:T(8,128)S(1)} fusion(f32[6,256]{1,0:T(8,128)S(1)} %bitcast.90, f32[256,256]{1,0:T(8,128)S(1)} %fusion.33, pred[256,256]{1,0:T(8,128)(4,1)S(1)} %fusion.31, f32[256,6,64]{0,2,1:T(8,128)S(1)} %bitcast.80, f32[256,6]{0,1:T(8,128)S(1)} %get-tuple-element.76), kind=kOutput, calls=%fused_computation.7 | convolution fusion | flops 303267840 | bytes 1126400 | tf_op jit(solution)/shard_map/hts,shp->thp/dot_general | solution.py:75
  123.6 4.5 %collective-permute-done.4 = f32[6,65,256]{2,1,0:T(8,128)S(1)} collective-permute-done((f32[6,65,256]{2,1,0:T(8,128)S(1)}, f32[6,65,256]{2,1,0:T(8,128)S(1)}, u32[]{:S(2)}, u32[]{:S(2)}) %collective-permute-start.4) | collective-permute-done | bytes 399392 | tf_op jit(solution)/shard_map/ppermute | solution.py:12
  128.1 0.5 fusion.9
  128.8 1.1 multiply_convert_fusion
  129.9 0.7 gather_fusion.1
  130.8 22.9 %all_to_all.10 = bf16[8,32,384]{2,1,0:T(8,128)(2,1)S(1)} all-to-all(bf16[8,32,384]{2,1,0:T(8,128)(2,1)S(1)} %broadcast_select_fusion), channel_id=1, replica_groups=mesh['seq'=8,'fsdp'=4] {'seq'}, dimensions={0} | all-to-all | bytes 393216 | tf_op jit(solution)/shard_map/all_to_all | solution.py:159
  153.7 0.7 copy.63
  (82 shorter events, 2.3 us)
Async XLA Ops:
  6.5 38.8 %copy-start = (bf16[2048,384]{1,0:T(8,128)(2,1)S(1)}, bf16[2048,384]{1,0:T(8,128)(2,1)}, u32[]{:S(2)}) copy-start(bf16[2048,384]{1,0:T(8,128)(2,1)} %param.23) | copy-start | bytes 4718596
  6.5 18.5 %copy-start.21 = (s32[4]{0:T(128)S(1)}, s32[4]{0:T(128)}, u32[]{:S(2)}) copy-start(s32[4]{0:T(128)} %param.22) | copy-start | bytes 52
  6.5 22.0 %copy-start.14 = (f32[4,384]{1,0:T(4,128)S(1)}, f32[4,384]{1,0:T(4,128)}, u32[]{:S(2)}) copy-start(f32[4,384]{1,0:T(4,128)} %param.27) | copy-start | bytes 18436
  6.5 22.0 %copy-start.13 = (f32[4,512]{1,0:T(4,128)S(1)}, f32[4,512]{1,0:T(4,128)}, u32[]{:S(2)}) copy-start(f32[4,512]{1,0:T(4,128)} %param.28) | copy-start | bytes 24580
  6.5 22.6 %copy-start.22 = (f32[6]{0:T(128)S(1)}, f32[6]{0:T(128)}, u32[]{:S(2)}) copy-start(f32[6]{0:T(128)} %param.30) | copy-start | bytes 76
  6.5 33.7 %copy-start.19 = (f32[6]{0:T(128)S(1)}, f32[6]{0:T(128)}, u32[]{:S(2)}) copy-start(f32[6]{0:T(128)} %param.29) | copy-start | bytes 76
  6.6 33.7 %copy-start.4 = (bf16[2048,6]{0,1:T(8,128)(2,1)S(1)}, bf16[2048,6]{0,1:T(8,128)(2,1)}, u32[]{:S(2)}) copy-start(bf16[2048,6]{0,1:T(8,128)(2,1)} %param.26) | copy-start | bytes 73732
  6.6 16.3 %all-to-all-start = ((bf16[8,32,512]{2,1,0:T(8,128)(2,1)}), bf16[8,32,512]{2,1,0:T(8,128)(2,1)S(1)}, u32[]{:S(2)}, u32[]{:S(2)}) async-start(bf16[8,32,512]{2,1,0:T(8,128)(2,1)} %bitcast.85), calls=%async_computation | async-start | bytes 524288 | tf_op jit(solution)/shard_map/all_to_all | solution.py:107
  14.0 26.2 %all-gather.3.cloned.1.call-start = ((), (), s32[]{:S(2)}) async-start(), calls=%async_computation.2 | async-start | bytes 1310720 | tf_op jit(solution)/shard_map/all_gather | solution.py:117
  24.3 40.1 %all-gather.5.cloned.1.call-start = ((), (), s32[]{:S(2)}) async-start(), calls=%async_computation.3 | async-start | bytes 2621440 | tf_op jit(solution)/shard_map/all_gather | solution.py:115
  25.4 14.9 %copy-start.5 = (s32[259]{0:T(512)}, s32[259]{0:T(512)S(1)}, u32[]{:S(2)}) copy-start(s32[259]{0:T(512)S(1)} %convert_reduce_fusion) | copy-start | bytes 3112
  41.9 22.5 %copy-start.1 = (bf16[256,2048]{1,0:T(8,128)(2,1)S(1)}, bf16[256,2048]{1,0:T(8,128)(2,1)}, u32[]{:S(2)}) copy-start(bf16[256,2048]{1,0:T(8,128)(2,1)} %all-gather.3.cloned.1.call-done) | copy-start | bytes 3145732
  44.1 0.6 copy-start.7
  66.7 4.9 %copy-start.9 = (f32[896]{0:T(1024)S(1)}, f32[896]{0:T(1024)}, u32[]{:S(2)}) copy-start(f32[896]{0:T(1024)} %get-tuple-element.55) | copy-start | bytes 10756
  66.7 4.9 %copy-start.10 = (f32[896]{0:T(1024)S(1)}, f32[896]{0:T(1024)}, u32[]{:S(2)}) copy-start(f32[896]{0:T(1024)} %get-tuple-element.56) | copy-start | bytes 10756
  66.7 4.9 %copy-start.11 = (f32[896]{0:T(1024)S(1)}, f32[896]{0:T(1024)}, u32[]{:S(2)}) copy-start(f32[896]{0:T(1024)} %get-tuple-element.57) | copy-start | bytes 10756
  66.7 4.9 %copy-start.12 = (f32[896]{0:T(1024)S(1)}, f32[896]{0:T(1024)}, u32[]{:S(2)}) copy-start(f32[896]{0:T(1024)} %get-tuple-element.58) | copy-start | bytes 10756
  66.7 4.9 %copy-start.15 = (f32[256]{0:T(256)S(1)}, f32[256]{0:T(256)}, u32[]{:S(2)}) copy-start(f32[256]{0:T(256)} %get-tuple-element.69) | copy-start | bytes 3076
  66.8 4.9 %copy-start.16 = (f32[256]{0:T(256)S(1)}, f32[256]{0:T(256)}, u32[]{:S(2)}) copy-start(f32[256]{0:T(256)} %get-tuple-element.70) | copy-start | bytes 3076
  66.8 4.9 %copy-start.17 = (f32[256]{0:T(256)S(1)}, f32[256]{0:T(256)}, u32[]{:S(2)}) copy-start(f32[256]{0:T(256)} %get-tuple-element.71) | copy-start | bytes 3076
  66.8 4.7 %collective-permute-start = (bf16[3,896]{1,0:T(4,128)(2,1)S(1)}, bf16[3,896]{1,0:T(4,128)(2,1)S(1)}, u32[]{:S(2)}, u32[]{:S(2)}) collective-permute-start(bf16[3,896]{1,0:T(4,128)(2,1)S(1)} %pad_maximum_fusion.3), channel_id=1, source_target_pairs={{0,4},{4,8},{8,12},{12,16},{16,20},{20,24},{24,28},{1,5},{5,9},{9,... | collective-permute-start | bytes 16136 | tf_op jit(solution)/shard_map/ppermute | solution.py:12
  75.0 12.1 %copy-start.6 = (s32[259]{0:T(512)S(1)}, s32[259]{0:T(512)}, u32[]{:S(2)}) copy-start(s32[259]{0:T(512)} %copy-done.5) | copy-start | bytes 3112
  78.1 14.1 %collective-permute-start.2 = (f32[6,65,256]{2,1,0:T(8,128)}, f32[6,65,256]{2,1,0:T(8,128)}, u32[]{:S(2)}, u32[]{:S(2)}) collective-permute-start(f32[6,65,256]{2,1,0:T(8,128)} %pad_maximum_fusion), channel_id=1, source_target_pairs={{0,8},{4,12},{8,16},{12,20},{16,24},{20,28},{1,9},{5,13},{9,17},{1... | collective-permute-start | bytes 1198088 | tf_op jit(solution)/shard_map/ppermute | solution.py:12
  83.9 11.2 %collective-permute-start.1 = (f32[6,65,256]{2,1,0:T(8,128)}, f32[6,65,256]{2,1,0:T(8,128)}, u32[]{:S(2)}, u32[]{:S(2)}) collective-permute-start(f32[6,65,256]{2,1,0:T(8,128)} %pad_maximum_fusion), channel_id=1, source_target_pairs={{0,4},{4,8},{8,12},{12,16},{16,20},{20,24},{24,28},{1,5},{5,9},{9,... | collective-permute-start | bytes 1198088 | tf_op jit(solution)/shard_map/ppermute | solution.py:12
  87.8 20.9 %copy-start.3 = (bf16[2048,384]{1,0:T(8,128)(2,1)S(1)}, bf16[2048,384]{1,0:T(8,128)(2,1)}, u32[]{:S(2)}) copy-start(bf16[2048,384]{1,0:T(8,128)(2,1)} %param.24) | copy-start | bytes 4718596
  97.2 18.7 %collective-permute-start.3 = (f32[6,65,256]{2,1,0:T(8,128)S(1)}, f32[6,65,256]{2,1,0:T(8,128)S(1)}, u32[]{:S(2)}, u32[]{:S(2)}) collective-permute-start(f32[6,65,256]{2,1,0:T(8,128)S(1)} %pad_maximum_fusion.1), channel_id=1, source_target_pairs={{0,8},{4,12},{8,16},{12,20},{16,24},{20,28},{1,9},{5,13},{9,17},{1... | collective-permute-start | bytes 1198088 | tf_op jit(solution)/shard_map/ppermute | solution.py:12
  110.2 11.6 %copy-start.2 = (f32[256,384]{0,1:T(8,128)S(1)}, f32[256,384]{0,1:T(8,128)}, u32[]{:S(2)}) copy-start(f32[256,384]{0,1:T(8,128)} %copy.39) | copy-start | bytes 1179652
  110.2 11.6 %copy-start.8 = (f32[1,6,2,128]{3,1,2,0:T(8,128)S(1)}, f32[1,6,2,128]{3,1,2,0:T(8,128)}, u32[]{:S(2)}) copy-start(f32[1,6,2,128]{3,1,2,0:T(8,128)} %copy-done.7) | copy-start | bytes 18436
  115.9 12.2 %copy-start.20 = (f32[6]{0:T(128)S(1)}, f32[6]{0:T(128)}, u32[]{:S(2)}) copy-start(f32[6]{0:T(128)} %param.31) | copy-start | bytes 76
  116.0 12.2 %collective-permute-start.4 = (f32[6,65,256]{2,1,0:T(8,128)S(1)}, f32[6,65,256]{2,1,0:T(8,128)S(1)}, u32[]{:S(2)}, u32[]{:S(2)}) collective-permute-start(f32[6,65,256]{2,1,0:T(8,128)S(1)} %pad_maximum_fusion.2), channel_id=1, source_target_pairs={{0,16},{4,20},{8,24},{12,28},{1,17},{5,21},{9,25},{13,29},{2,18},{... | collective-permute-start | bytes 1198088 | tf_op jit(solution)/shard_map/ppermute | solution.py:12
  128.7 2.0 %copy-start.18 = (pred[8]{0:T(512)(128)(4,1)S(1)}, pred[8]{0:T(512)(128)(4,1)}, u32[]{:S(2)}) copy-start(pred[8]{0:T(512)(128)(4,1)} %get-tuple-element.59) | copy-start | bytes 28
Sparse Core Ops, SparseCore 0:
  24.4 15.7 all-gather.2
  41.8 22.5 all-gather.4

commit v2 on v1

--- a/solution.py
+++ b/solution.py
@@ -20,10 +20,15 @@
 
 def received(packed, axis, by):
     place = lax.axis_index(axis)
-    got = shifted(packed, axis, by)
     rows = packed.shape[1] - 1
-    missing = (place < by).astype(packed.dtype)
-    return got.at[:, rows:, :].add(missing)
+    decay = packed[:, rows:, :]
+    high = decay.astype(jnp.bfloat16)
+    low = (decay - high.astype(jnp.float32)).astype(jnp.bfloat16)
+    wire = jnp.concatenate([packed[:, :rows, :].astype(jnp.bfloat16), high, low], axis=1)
+    got = shifted(wire, axis, by).astype(jnp.float32)
+    missing = (place < by).astype(jnp.float32)
+    decay_got = got[:, rows : rows + 1, :] + got[:, rows + 1 :, :] + missing
+    return jnp.concatenate([got[:, :rows, :], decay_got], axis=1)
 
 
 def exclusive_scan(packed, axis):

time: 162 us -> 135 us (0.83)
  starting transfers between devices: 36.3 us -> 28.5 us
  other arithmetic: 15.7 us -> 8.22 us
  local copies, waits for them, and re-layouts: 9.22 us -> 4.33 us
  blocking collectives: 22.9 us -> 19.4 us
  waiting for transfers between devices: 51.2 us -> 47.9 us
    ppermute x5, starting transfers between devices: 28.8 us -> 21 us  [shifted(): return lax.ppermute(array, axis, pairs)]
    ppermute x5, waiting for transfers between devices: 15.9 us -> 9.9 us  [shifted(): return lax.ppermute(array, axis, pairs)]
    all_to_all x1, blocking collectives: 22.9 us -> 19.4 us  [per_device(): lax.all_to_all(outgoing, 'seq', split_axis=0, concat_axis=0, tiled=True)]
    slice x2, local copies, waits for them, and re-layouts: 2.68 us -> 0.19 us  [per_device(): x_heads = activated[:, :inner_dev].reshape(tok_dev, heads_dev, head_dim)]
  transfers between devices with their start and end apart: 8 -> 8, of which waited for: 8 -> 7; matrix products, arithmetic and copies ran while one was open for 13% -> 9% of each run, Pallas kernels for 0% -> 0%
where the time goes in v2:
time: 135 us; the launch traced here: 134 us
  waiting for transfers between devices  47.9 us (35%)
  starting transfers between devices  28.5 us (21%)
  blocking collectives  19.4 us (14%)
  between operations  14.4 us (11%)
  matrix products  11.6 us (9%)
  other arithmetic  8.22 us (6%)
  local copies, waits for them, and re-layouts  4.33 us (3%)
    ppermute x5, starting transfers between devices, shifted(): return lax.ppermute(array, axis, pairs)  21 us
    all_to_all x1, blocking collectives, per_device(): lax.all_to_all(outgoing, 'seq', split_axis=0, concat_axis=0, tiled=True)  19.4 us
    all_gather x1, waiting for transfers between devices, per_device(): w_full = lax.all_gather(shared_weight, 'fsdp', axis=0, tiled=True)  18.1 us
    all_gather x1, waiting for transfers between devices, per_device(): feature_part = lax.all_gather(stream_block, 'fsdp', axis=1, tiled=True)  12.2 us
    ppermute x5, waiting for transfers between devices, shifted(): return lax.ppermute(array, axis, pairs)  9.9 us
    dot_general x4, matrix products, per_device(): jnp.dot(feature_part, weight, preferred_element_type=jnp.float32)  8.34 us
    all_to_all x1, starting transfers between devices, per_device(): lax.all_to_all(slot_rows, 'seq', split_axis=0, concat_axis=0, tiled=True)  7.42 us
    all_to_all x1, waiting for transfers between devices, per_device(): lax.all_to_all(slot_rows, 'seq', split_axis=0, concat_axis=0, tiled=True)  7.02 us
  transfers between devices with their start and end apart: 8, of which 7 were waited for; matrix products, arithmetic and copies ran while one was open for 9% of the time, Pallas kernels for 0%

profile of v2, /device:TPU:0, one launch (start us, length us, event | category | flops | bytes accessed | tf_op | source)
XLA Modules:
  0.0 134.3 jit_solution(6287457943463217837)
XLA Ops:
  6.6 7.4 %all-to-all-start = ((bf16[8,32,512]{2,1,0:T(8,128)(2,1)}), bf16[8,32,512]{2,1,0:T(8,128)(2,1)S(1)}, u32[]{:S(2)}, u32[]{:S(2)}) async-start(bf16[8,32,512]{2,1,0:T(8,128)(2,1)} %bitcast.86), calls=%async_computation | async-start | bytes 524288 | tf_op jit(solution)/shard_map/all_to_all | solution.py:112
  14.0 0.7 compare_and_fusion.1
  14.7 1.0 sort.17
  15.8 0.1 broadcast_in_dim.92
  15.9 7.0 %all-to-all-done = bf16[8,32,512]{2,1,0:T(8,128)(2,1)S(1)} async-done(((bf16[8,32,512]{2,1,0:T(8,128)(2,1)}), bf16[8,32,512]{2,1,0:T(8,128)(2,1)S(1)}, u32[]{:S(2)}, u32[]{:S(2)}) %all-to-all-start) | async-done | bytes 262176 | tf_op jit(solution)/shard_map/all_to_all | solution.py:112
  22.9 0.6 gather_fusion
  23.5 0.8 bitcast_select_fusion
  24.4 0.7 all-gather.5.cloned.1.call-update
  25.1 0.2 reduce-window.18
  25.3 0.1 convert_reduce_fusion
  25.4 0.6 fusion.70
  26.6 0.7 broadcast_compare_fusion
  27.3 0.6 slice.124
  28.0 12.2 %all-gather.3.cloned.1.call-done = bf16[256,2048]{1,0:T(8,128)(2,1)} async-done(((bf16[256,512]{1,0:T(8,128)(2,1)}), bf16[256,2048]{1,0:T(8,128)(2,1)}) %all-gather.3.cloned.1.call-update) | async-done | bytes 1048592 | tf_op jit(solution)/shard_map/all_gather | solution.py:122
  40.2 1.6 %fusion.48 = (f32[6,256]{1,0:T(8,128)S(1)}, f32[256,6]{0,1:T(8,128)S(1)}) fusion(f32[6]{0:T(128)S(1)} %exponential_negate_fusion, f32[6]{0:T(128)S(1)} %copy-done.5, bf16[256,2048]{1,0:T(8,128)(2,1)} %all-gather.3.cloned.1.call-done, bf16[2048,6]{0,1:T(8,128)(2,1)S(1)} %copy-done.2), kind=kOutput, calls=%fused_computation.67 | convolution fusion | flops 6303744 | bytes 1085488 | tf_op jit(solution)/shard_map/dot_general | solution.py:125
  41.9 1.8 %reduce-window.19 = f32[6,2,128]{2,1,0:T(2,128)S(1)} reduce-window(f32[6,2,128]{2,1,0:T(2,128)S(1)} %reshape.217, f32[]{:T(128)} %constant.61.clone.1), window={size=1x1x128 pad=0_0x0_0x127_0}, to_apply=%region_3.4 | reduce-window | flops 195072 | bytes 12292 | tf_op jit(solution)/shard_map/reduce-window.1
  43.7 0.1 slice.151
  43.8 0.1 copy.40
  43.9 0.1 copy.41
  44.1 0.2 slice_reduce_fusion
  44.4 1.9 %convolution_convert_fusion.3 = bf16[256,384]{1,0:T(8,128)(2,1)S(1)} fusion(bf16[256,2048]{1,0:T(8,128)(2,1)} %all-gather.3.cloned.1.call-done, bf16[2048,384]{1,0:T(8,128)(2,1)S(1)} %copy-done), kind=kOutput, calls=%fused_computation.15 | convolution fusion | flops 402751488 | bytes 2818048 | tf_op jit(solution)/shard_map/dot_general | solution.py:125
  46.3 18.1 %all-gather.5.cloned.1.call-done = bf16[2048,512]{1,0:T(8,128)(2,1)} async-done(((bf16[512,512]{1,0:T(8,128)(2,1)}), bf16[2048,512]{1,0:T(8,128)(2,1)}) %all-gather.5.cloned.1.call-update) | async-done | bytes 2097168 | tf_op jit(solution)/shard_map/all_gather | solution.py:120
  64.4 2.3 %convolution_convert_fusion = bf16[256,512]{1,0:T(8,128)(2,1)S(1)} fusion(bf16[256,2048]{1,0:T(8,128)(2,1)S(1)} %copy-done.1, bf16[2048,512]{1,0:T(8,128)(2,1)} %all-gather.5.cloned.1.call-done), kind=kOutput, calls=%fused_computation.10 | convolution fusion | flops 537001984 | bytes 3407872 | tf_op jit(solution)/shard_map/dot_general | solution.py:125
  66.7 3.4 %collective-permute-start = (bf16[3,896]{1,0:T(4,128)(2,1)S(1)}, bf16[3,896]{1,0:T(4,128)(2,1)S(1)}, u32[]{:S(2)}, u32[]{:S(2)}) collective-permute-start(bf16[3,896]{1,0:T(4,128)(2,1)S(1)} %pad_maximum_fusion.3), channel_id=1, source_target_pairs={{0,4},{4,8},{8,12},{12,16},{16,20},{20,24},{24,28},{1,5},{5,9},{9,... | collective-permute-start | bytes 16136 | tf_op jit(solution)/shard_map/ppermute | solution.py:12
  70.1 0.7 fusion.62
  70.8 0.7 collective-permute-done
  71.5 0.1 maximum_convert_fusion
  71.6 0.7 divide_multiply_fusion
  72.3 0.2 copy.39
  72.4 0.5 convolution_convert_fusion.2
  73.1 4.2 %collective-permute-start.1 = (bf16[6,66,256]{2,1,0:T(8,128)(2,1)S(1)}, bf16[6,66,256]{2,1,0:T(8,128)(2,1)S(1)}, u32[]{:S(2)}, u32[]{:S(2)}) collective-permute-start(bf16[6,66,256]{2,1,0:T(8,128)(2,1)S(1)} %pad_maximum_fusion), channel_id=1, source_target_pairs={{0,4},{4,8},{8,12},{12,16},{16,20},{20,24},{24,28},{1,5},{5,9},{9,... | collective-permute-start | bytes 608264 | tf_op jit(solution)/shard_map/ppermute | solution.py:12
  77.3 3.4 %collective-permute-start.2 = (bf16[6,66,256]{2,1,0:T(8,128)(2,1)S(1)}, bf16[6,66,256]{2,1,0:T(8,128)(2,1)S(1)}, u32[]{:S(2)}, u32[]{:S(2)}) collective-permute-start(bf16[6,66,256]{2,1,0:T(8,128)(2,1)S(1)} %pad_maximum_fusion), channel_id=1, source_target_pairs={{0,8},{4,12},{8,16},{12,20},{16,24},{20,28},{1,9},{5,13},{9,17},{1... | collective-permute-start | bytes 608264 | tf_op jit(solution)/shard_map/ppermute | solution.py:12
  80.7 0.7 fusion.59
  81.5 2.9 %collective-permute-done.2 = bf16[6,66,256]{2,1,0:T(8,128)(2,1)S(1)} collective-permute-done((bf16[6,66,256]{2,1,0:T(8,128)(2,1)S(1)}, bf16[6,66,256]{2,1,0:T(8,128)(2,1)S(1)}, u32[]{:S(2)}, u32[]{:S(2)}) %collective-permute-start.2) | collective-permute-done | bytes 202784 | tf_op jit(solution)/shard_map/ppermute | solution.py:12
  84.5 4.7 %collective-permute-start.3 = (bf16[6,66,256]{2,1,0:T(8,128)(2,1)S(1)}, bf16[6,66,256]{2,1,0:T(8,128)(2,1)S(1)}, u32[]{:S(2)}, u32[]{:S(2)}) collective-permute-start(bf16[6,66,256]{2,1,0:T(8,128)(2,1)S(1)} %pad_maximum_fusion.1), channel_id=1, source_target_pairs={{0,8},{4,12},{8,16},{12,20},{16,24},{20,28},{1,9},{5,13},{9,17},{1... | collective-permute-start | bytes 608264 | tf_op jit(solution)/shard_map/ppermute | solution.py:12
  89.3 0.1 fusion.35
  89.4 3.3 %collective-permute-done.3 = bf16[6,66,256]{2,1,0:T(8,128)(2,1)S(1)} collective-permute-done((bf16[6,66,256]{2,1,0:T(8,128)(2,1)S(1)}, bf16[6,66,256]{2,1,0:T(8,128)(2,1)S(1)}, u32[]{:S(2)}, u32[]{:S(2)}) %collective-permute-start.3) | collective-permute-done | bytes 202784 | tf_op jit(solution)/shard_map/ppermute | solution.py:12
  92.9 5.3 %collective-permute-start.4 = (bf16[6,66,256]{2,1,0:T(8,128)(2,1)S(1)}, bf16[6,66,256]{2,1,0:T(8,128)(2,1)S(1)}, u32[]{:S(2)}, u32[]{:S(2)}) collective-permute-start(bf16[6,66,256]{2,1,0:T(8,128)(2,1)S(1)} %pad_maximum_fusion.2), channel_id=1, source_target_pairs={{0,16},{4,20},{8,24},{12,28},{1,17},{5,21},{9,25},{13,29},{2,18},{... | collective-permute-start | bytes 608264 | tf_op jit(solution)/shard_map/ppermute | solution.py:12
  98.2 0.4 fusion.37
  98.6 3.0 %collective-permute-done.4 = bf16[6,66,256]{2,1,0:T(8,128)(2,1)S(1)} collective-permute-done((bf16[6,66,256]{2,1,0:T(8,128)(2,1)S(1)}, bf16[6,66,256]{2,1,0:T(8,128)(2,1)S(1)}, u32[]{:S(2)}, u32[]{:S(2)}) %collective-permute-start.4) | collective-permute-done | bytes 202784 | tf_op jit(solution)/shard_map/ppermute | solution.py:12
  101.7 0.5 convolution_multiply_fusion
  102.2 1.9 %fusion.11 = f32[256,6,64]{0,2,1:T(8,128)S(1)} fusion(f32[256,6,64]{0,2,1:T(8,128)S(1)} %convolution_multiply_fusion, f32[6,256]{1,0:T(8,128)S(1)} %bitcast.93, f32[256,256]{1,0:T(8,128)S(1)} %fusion.37, pred[256,256]{1,0:T(8,128)(4,1)S(1)} %fusion.35, f32[256,6,64]{0,2,1:T(8,128)S(1)} %bitcast.83, f32[6]{0:T(128)S(1)} %copy-done.8, ...), kind=kOutput, calls=%fused_computation.9 | convolution fusion | flops 303562752 | bytes 1519640 | tf_op jit(solution)/shard_map/hts,shp->thp/dot_general | solution.py:80
  104.1 0.2 copy.42
  104.3 2.5 %multiply_convert_fusion = bf16[256,384]{1,0:T(8,128)(2,1)S(1)} fusion(f32[256,384]{1,0:T(8,128)S(1)} %copy.42, bf16[256,2048]{1,0:T(8,128)(2,1)} %all-gather.3.cloned.1.call-done, bf16[2048,384]{1,0:T(8,128)(2,1)} %param.16), kind=kOutput, calls=%fused_computation.38 | convolution fusion | flops 403439616 | bytes 3211264 | tf_op jit(solution)/shard_map/dot_general | solution.py:125
  106.8 0.6 gather_fusion.1
  107.4 0.1 broadcast_select_fusion
  107.5 19.4 %all_to_all.10 = bf16[8,32,384]{2,1,0:T(8,128)(2,1)S(1)} all-to-all(bf16[8,32,384]{2,1,0:T(8,128)(2,1)S(1)} %broadcast_select_fusion), channel_id=1, replica_groups=mesh['seq'=8,'fsdp'=4] {'seq'}, dimensions={0} | all-to-all | bytes 393216 | tf_op jit(solution)/shard_map/all_to_all | solution.py:164
  126.8 0.7 copy.63
  (60 shorter events, 1.1 us)
Async XLA Ops:
  6.5 37.9 %copy-start = (bf16[2048,384]{1,0:T(8,128)(2,1)S(1)}, bf16[2048,384]{1,0:T(8,128)(2,1)}, u32[]{:S(2)}) copy-start(bf16[2048,384]{1,0:T(8,128)(2,1)} %param.15) | copy-start | bytes 4718596
  6.5 18.6 %copy-start.6 = (s32[4]{0:T(128)S(1)}, s32[4]{0:T(128)}, u32[]{:S(2)}) copy-start(s32[4]{0:T(128)} %param.14) | copy-start | bytes 52
  6.5 21.4 %copy-start.4 = (f32[4,384]{1,0:T(4,128)S(1)}, f32[4,384]{1,0:T(4,128)}, u32[]{:S(2)}) copy-start(f32[4,384]{1,0:T(4,128)} %param.19) | copy-start | bytes 18436
  6.5 21.4 %copy-start.3 = (f32[4,512]{1,0:T(4,128)S(1)}, f32[4,512]{1,0:T(4,128)}, u32[]{:S(2)}) copy-start(f32[4,512]{1,0:T(4,128)} %param.20) | copy-start | bytes 24580
  6.5 21.4 %copy-start.7 = (f32[6]{0:T(128)S(1)}, f32[6]{0:T(128)}, u32[]{:S(2)}) copy-start(f32[6]{0:T(128)} %param.22) | copy-start | bytes 76
  6.5 33.7 %copy-start.2 = (bf16[2048,6]{0,1:T(8,128)(2,1)S(1)}, bf16[2048,6]{0,1:T(8,128)(2,1)}, u32[]{:S(2)}) copy-start(bf16[2048,6]{0,1:T(8,128)(2,1)} %param.18) | copy-start | bytes 73732
  6.6 33.7 %copy-start.5 = (f32[6]{0:T(128)S(1)}, f32[6]{0:T(128)}, u32[]{:S(2)}) copy-start(f32[6]{0:T(128)} %param.21) | copy-start | bytes 76
  6.6 16.3 %all-to-all-start = ((bf16[8,32,512]{2,1,0:T(8,128)(2,1)}), bf16[8,32,512]{2,1,0:T(8,128)(2,1)S(1)}, u32[]{:S(2)}, u32[]{:S(2)}) async-start(bf16[8,32,512]{2,1,0:T(8,128)(2,1)} %bitcast.86), calls=%async_computation | async-start | bytes 524288 | tf_op jit(solution)/shard_map/all_to_all | solution.py:112
  14.0 26.2 %all-gather.3.cloned.1.call-start = ((), (), s32[]{:S(2)}) async-start(), calls=%async_computation.2 | async-start | bytes 1310720 | tf_op jit(solution)/shard_map/all_gather | solution.py:122
  24.3 40.1 %all-gather.5.cloned.1.call-start = ((), (), s32[]{:S(2)}) async-start(), calls=%async_computation.3 | async-start | bytes 2621440 | tf_op jit(solution)/shard_map/all_gather | solution.py:120
  41.9 22.5 %copy-start.1 = (bf16[256,2048]{1,0:T(8,128)(2,1)S(1)}, bf16[256,2048]{1,0:T(8,128)(2,1)}, u32[]{:S(2)}) copy-start(bf16[256,2048]{1,0:T(8,128)(2,1)} %all-gather.3.cloned.1.call-done) | copy-start | bytes 3145732
  66.7 4.7 %collective-permute-start = (bf16[3,896]{1,0:T(4,128)(2,1)S(1)}, bf16[3,896]{1,0:T(4,128)(2,1)S(1)}, u32[]{:S(2)}, u32[]{:S(2)}) collective-permute-start(bf16[3,896]{1,0:T(4,128)(2,1)S(1)} %pad_maximum_fusion.3), channel_id=1, source_target_pairs={{0,4},{4,8},{8,12},{12,16},{16,20},{20,24},{24,28},{1,5},{5,9},{9,... | collective-permute-start | bytes 16136 | tf_op jit(solution)/shard_map/ppermute | solution.py:12
  73.1 8.3 %collective-permute-start.1 = (bf16[6,66,256]{2,1,0:T(8,128)(2,1)S(1)}, bf16[6,66,256]{2,1,0:T(8,128)(2,1)S(1)}, u32[]{:S(2)}, u32[]{:S(2)}) collective-permute-start(bf16[6,66,256]{2,1,0:T(8,128)(2,1)S(1)} %pad_maximum_fusion), channel_id=1, source_target_pairs={{0,4},{4,8},{8,12},{12,16},{16,20},{20,24},{24,28},{1,5},{5,9},{9,... | collective-permute-start | bytes 608264 | tf_op jit(solution)/shard_map/ppermute | solution.py:12
  77.3 7.0 %collective-permute-start.2 = (bf16[6,66,256]{2,1,0:T(8,128)(2,1)S(1)}, bf16[6,66,256]{2,1,0:T(8,128)(2,1)S(1)}, u32[]{:S(2)}, u32[]{:S(2)}) collective-permute-start(bf16[6,66,256]{2,1,0:T(8,128)(2,1)S(1)} %pad_maximum_fusion), channel_id=1, source_target_pairs={{0,8},{4,12},{8,16},{12,20},{16,24},{20,28},{1,9},{5,13},{9,17},{1... | collective-permute-start | bytes 608264 | tf_op jit(solution)/shard_map/ppermute | solution.py:12
  84.5 8.2 %collective-permute-start.3 = (bf16[6,66,256]{2,1,0:T(8,128)(2,1)S(1)}, bf16[6,66,256]{2,1,0:T(8,128)(2,1)S(1)}, u32[]{:S(2)}, u32[]{:S(2)}) collective-permute-start(bf16[6,66,256]{2,1,0:T(8,128)(2,1)S(1)} %pad_maximum_fusion.1), channel_id=1, source_target_pairs={{0,8},{4,12},{8,16},{12,20},{16,24},{20,28},{1,9},{5,13},{9,17},{1... | collective-permute-start | bytes 608264 | tf_op jit(solution)/shard_map/ppermute | solution.py:12
  92.8 9.4 %copy-start.8 = (f32[6]{0:T(128)S(1)}, f32[6]{0:T(128)}, u32[]{:S(2)}) copy-start(f32[6]{0:T(128)} %param.23) | copy-start | bytes 76
  92.9 8.8 %collective-permute-start.4 = (bf16[6,66,256]{2,1,0:T(8,128)(2,1)S(1)}, bf16[6,66,256]{2,1,0:T(8,128)(2,1)S(1)}, u32[]{:S(2)}, u32[]{:S(2)}) collective-permute-start(bf16[6,66,256]{2,1,0:T(8,128)(2,1)S(1)} %pad_maximum_fusion.2), channel_id=1, source_target_pairs={{0,16},{4,20},{8,24},{12,28},{1,17},{5,21},{9,25},{13,29},{2,18},{... | collective-permute-start | bytes 608264 | tf_op jit(solution)/shard_map/ppermute | solution.py:12
Sparse Core Ops, SparseCore 0:
  24.5 15.7 all-gather.2
  41.8 22.5 all-gather.4

commit v3 on v2

--- a/solution.py
+++ b/solution.py
@@ -118,6 +118,7 @@
     head_dim = inner_dev // heads_dev
     state_dim = shared_weight.shape[1] // 2
     w_full = lax.all_gather(shared_weight, "fsdp", axis=0, tiled=True)
+    w_full, stream_block = lax.optimization_barrier((w_full, stream_block))
     weight_list = (x_weight, z_weight, step_weight, w_full)
     feature_part = lax.all_gather(stream_block, "fsdp", axis=1, tiled=True)
     x_acc, z_acc, step_acc, bc_acc = tuple(

time: 135 us -> 127 us (0.941)
  waiting for transfers between devices: 47.9 us -> 42.8 us
  matrix products: 11.6 us -> 9.61 us
    all_gather x1, waiting for transfers between devices: 18.1 us -> 9.39 us  [per_device(): w_full = lax.all_gather(shared_weight, 'fsdp', axis=0, tiled=True)]
    all_gather x1, waiting for transfers between devices: 12.2 us -> 15.4 us  [per_device(): feature_part = lax.all_gather(stream_block, 'fsdp', axis=1, tiled=True)]
    dot_general x4, matrix products: 8.34 us -> 6.3 us  [per_device(): jnp.dot(feature_part, weight, preferred_element_type=jnp.float32)]
  transfers between devices with their start and end apart: 8 -> 8, of which waited for: 7 -> 7; matrix products, arithmetic and copies ran while one was open for 9% -> 8% of each run, Pallas kernels for 0% -> 0%
where the time goes in v3:
time: 127 us
  waiting for transfers between devices  42.8 us (34%)
  starting transfers between devices  27.3 us (21%)
  blocking collectives  20.3 us (16%)
  between operations  14.4 us (11%)
  matrix products  9.61 us (8%)
  other arithmetic  8.29 us (7%)
  local copies, waits for them, and re-layouts  4.33 us (3%)
    all_to_all x1, blocking collectives, per_device(): lax.all_to_all(outgoing, 'seq', split_axis=0, concat_axis=0, tiled=True)  20.3 us
    ppermute x5, starting transfers between devices, shifted(): return lax.ppermute(array, axis, pairs)  19.9 us
    all_gather x1, waiting for transfers between devices, per_device(): feature_part = lax.all_gather(stream_block, 'fsdp', axis=1, tiled=True)  15.4 us
    ppermute x5, waiting for transfers between devices, shifted(): return lax.ppermute(array, axis, pairs)  10.3 us
    all_gather x1, waiting for transfers between devices, per_device(): w_full = lax.all_gather(shared_weight, 'fsdp', axis=0, tiled=True)  9.39 us
    all_to_all x1, starting transfers between devices, per_device(): lax.all_to_all(slot_rows, 'seq', split_axis=0, concat_axis=0, tiled=True)  7.29 us
    all_to_all x1, waiting for transfers between devices, per_device(): lax.all_to_all(slot_rows, 'seq', split_axis=0, concat_axis=0, tiled=True)  7.01 us
    dot_general x4, matrix products, per_device(): jnp.dot(feature_part, weight, preferred_element_type=jnp.float32)  6.3 us
  transfers between devices with their start and end apart: 8, of which 7 were waited for; matrix products, arithmetic and copies ran while one was open for 8% of the time, Pallas kernels for 0%

profile of v3, /device:TPU:0, one launch (start us, length us, event | category | flops | bytes accessed | tf_op | source)
XLA Modules:
  0.0 126.9 jit_solution(3129703581392175608)
XLA Ops:
  6.6 0.7 all-gather.3.cloned.1.call-update
  7.3 7.3 %all-to-all-start = ((bf16[8,32,512]{2,1,0:T(8,128)(2,1)}), bf16[8,32,512]{2,1,0:T(8,128)(2,1)S(1)}, u32[]{:S(2)}, u32[]{:S(2)}) async-start(bf16[8,32,512]{2,1,0:T(8,128)(2,1)} %bitcast.86), calls=%async_computation | async-start | bytes 524288 | tf_op jit(solution)/shard_map/all_to_all | solution.py:112
  14.6 0.7 compare_and_fusion.1
  15.3 1.0 sort.17
  16.4 0.1 broadcast_in_dim.92
  16.5 7.0 %all-to-all-done = bf16[8,32,512]{2,1,0:T(8,128)(2,1)S(1)} async-done(((bf16[8,32,512]{2,1,0:T(8,128)(2,1)}), bf16[8,32,512]{2,1,0:T(8,128)(2,1)S(1)}, u32[]{:S(2)}, u32[]{:S(2)}) %all-to-all-start) | async-done | bytes 262176 | tf_op jit(solution)/shard_map/all_to_all | solution.py:112
  23.5 0.6 gather_fusion
  24.1 0.8 bitcast_select_fusion
  24.9 9.4 %all-gather.3.cloned.1.call-done = bf16[2048,512]{1,0:T(8,128)(2,1)} async-done(((bf16[512,512]{1,0:T(8,128)(2,1)}), bf16[2048,512]{1,0:T(8,128)(2,1)}) %all-gather.3.cloned.1.call-update) | async-done | bytes 2097168 | tf_op jit(solution)/shard_map/all_gather | solution.py:120
  34.3 0.2 reduce-window.18
  34.5 0.1 convert_reduce_fusion
  34.7 0.6 fusion.70
  35.8 0.7 broadcast_compare_fusion
  36.5 0.6 slice.124
  37.2 15.4 %all-gather.5.cloned.1.call-done = bf16[256,2048]{1,0:T(8,128)(2,1)} async-done(((bf16[256,512]{1,0:T(8,128)(2,1)}), bf16[256,2048]{1,0:T(8,128)(2,1)}) %all-gather.5.cloned.1.call-update) | async-done | bytes 1048592 | tf_op jit(solution)/shard_map/all_gather | solution.py:123
  52.7 2.7 %convolution_convert_fusion = bf16[256,512]{1,0:T(8,128)(2,1)S(1)} fusion(bf16[256,2048]{1,0:T(8,128)(2,1)} %all-gather.5.cloned.1.call-done, bf16[2048,512]{1,0:T(8,128)(2,1)} %all-gather.3.cloned.1.call-done), kind=kOutput, calls=%fused_computation.10 | convolution fusion | flops 537001984 | bytes 3407872 | tf_op jit(solution)/shard_map/dot_general | solution.py:126
  55.4 0.7 convolution_convert_fusion.3
  56.2 3.4 %collective-permute-start = (bf16[3,896]{1,0:T(4,128)(2,1)S(1)}, bf16[3,896]{1,0:T(4,128)(2,1)S(1)}, u32[]{:S(2)}, u32[]{:S(2)}) collective-permute-start(bf16[3,896]{1,0:T(4,128)(2,1)S(1)} %pad_maximum_fusion.3), channel_id=1, source_target_pairs={{0,4},{4,8},{8,12},{12,16},{16,20},{20,24},{24,28},{1,5},{5,9},{9,... | collective-permute-start | bytes 16136 | tf_op jit(solution)/shard_map/ppermute | solution.py:12
  59.6 0.4 fusion.48
  60.0 1.8 %reduce-window.19 = f32[6,2,128]{2,1,0:T(2,128)S(1)} reduce-window(f32[6,2,128]{2,1,0:T(2,128)S(1)} %reshape.217, f32[]{:T(128)} %constant.61.clone.1), window={size=1x1x128 pad=0_0x0_0x127_0}, to_apply=%region_3.4 | reduce-window | flops 195072 | bytes 12292 | tf_op jit(solution)/shard_map/reduce-window.1
  61.9 0.1 copy.40
  62.0 0.1 copy.41
  62.2 0.2 slice_reduce_fusion
  62.5 0.7 fusion.62
  63.2 0.1 maximum_convert_fusion
  63.3 0.7 divide_multiply_fusion
  64.0 0.2 copy.39
  64.2 0.5 convolution_convert_fusion.2
  64.8 3.4 %collective-permute-start.1 = (bf16[6,66,256]{2,1,0:T(8,128)(2,1)S(1)}, bf16[6,66,256]{2,1,0:T(8,128)(2,1)S(1)}, u32[]{:S(2)}, u32[]{:S(2)}) collective-permute-start(bf16[6,66,256]{2,1,0:T(8,128)(2,1)S(1)} %pad_maximum_fusion), channel_id=1, source_target_pairs={{0,4},{4,8},{8,12},{12,16},{16,20},{20,24},{24,28},{1,5},{5,9},{9,... | collective-permute-start | bytes 608264 | tf_op jit(solution)/shard_map/ppermute | solution.py:12
  68.2 3.4 %collective-permute-start.2 = (bf16[6,66,256]{2,1,0:T(8,128)(2,1)S(1)}, bf16[6,66,256]{2,1,0:T(8,128)(2,1)S(1)}, u32[]{:S(2)}, u32[]{:S(2)}) collective-permute-start(bf16[6,66,256]{2,1,0:T(8,128)(2,1)S(1)} %pad_maximum_fusion), channel_id=1, source_target_pairs={{0,8},{4,12},{8,16},{12,20},{16,24},{20,28},{1,9},{5,13},{9,17},{1... | collective-permute-start | bytes 608264 | tf_op jit(solution)/shard_map/ppermute | solution.py:12
  71.6 0.7 fusion.59
  72.4 0.7 collective-permute-done.1
  73.1 3.1 %collective-permute-done.2 = bf16[6,66,256]{2,1,0:T(8,128)(2,1)S(1)} collective-permute-done((bf16[6,66,256]{2,1,0:T(8,128)(2,1)S(1)}, bf16[6,66,256]{2,1,0:T(8,128)(2,1)S(1)}, u32[]{:S(2)}, u32[]{:S(2)}) %collective-permute-start.2) | collective-permute-done | bytes 202784 | tf_op jit(solution)/shard_map/ppermute | solution.py:12
  76.2 0.1 fusion.66
  76.4 4.4 %collective-permute-start.3 = (bf16[6,66,256]{2,1,0:T(8,128)(2,1)S(1)}, bf16[6,66,256]{2,1,0:T(8,128)(2,1)S(1)}, u32[]{:S(2)}, u32[]{:S(2)}) collective-permute-start(bf16[6,66,256]{2,1,0:T(8,128)(2,1)S(1)} %pad_maximum_fusion.1), channel_id=1, source_target_pairs={{0,8},{4,12},{8,16},{12,20},{16,24},{20,28},{1,9},{5,13},{9,17},{1... | collective-permute-start | bytes 608264 | tf_op jit(solution)/shard_map/ppermute | solution.py:12
  80.8 0.1 fusion.35
  80.9 3.5 %collective-permute-done.3 = bf16[6,66,256]{2,1,0:T(8,128)(2,1)S(1)} collective-permute-done((bf16[6,66,256]{2,1,0:T(8,128)(2,1)S(1)}, bf16[6,66,256]{2,1,0:T(8,128)(2,1)S(1)}, u32[]{:S(2)}, u32[]{:S(2)}) %collective-permute-start.3) | collective-permute-done | bytes 202784 | tf_op jit(solution)/shard_map/ppermute | solution.py:12
  84.6 5.3 %collective-permute-start.4 = (bf16[6,66,256]{2,1,0:T(8,128)(2,1)S(1)}, bf16[6,66,256]{2,1,0:T(8,128)(2,1)S(1)}, u32[]{:S(2)}, u32[]{:S(2)}) collective-permute-start(bf16[6,66,256]{2,1,0:T(8,128)(2,1)S(1)} %pad_maximum_fusion.2), channel_id=1, source_target_pairs={{0,16},{4,20},{8,24},{12,28},{1,17},{5,21},{9,25},{13,29},{2,18},{... | collective-permute-start | bytes 608264 | tf_op jit(solution)/shard_map/ppermute | solution.py:12
  89.9 0.4 fusion.37
  90.3 3.0 %collective-permute-done.4 = bf16[6,66,256]{2,1,0:T(8,128)(2,1)S(1)} collective-permute-done((bf16[6,66,256]{2,1,0:T(8,128)(2,1)S(1)}, bf16[6,66,256]{2,1,0:T(8,128)(2,1)S(1)}, u32[]{:S(2)}, u32[]{:S(2)}) %collective-permute-start.4) | collective-permute-done | bytes 202784 | tf_op jit(solution)/shard_map/ppermute | solution.py:12
  93.4 0.5 convolution_multiply_fusion
  93.9 1.9 %fusion.11 = f32[256,6,64]{0,2,1:T(8,128)S(1)} fusion(f32[256,6,64]{0,2,1:T(8,128)S(1)} %convolution_multiply_fusion, f32[6,256]{1,0:T(8,128)S(1)} %bitcast.93, f32[256,256]{1,0:T(8,128)S(1)} %fusion.37, pred[256,256]{1,0:T(8,128)(4,1)S(1)} %fusion.35, f32[256,6,64]{0,2,1:T(8,128)S(1)} %bitcast.83, f32[6]{0:T(128)S(1)} %copy-done.8, ...), kind=kOutput, calls=%fused_computation.9 | convolution fusion | flops 303562752 | bytes 1519640 | tf_op jit(solution)/shard_map/hts,shp->thp/dot_general | solution.py:80
  95.8 0.2 copy.42
  96.0 2.5 %multiply_convert_fusion = bf16[256,384]{1,0:T(8,128)(2,1)S(1)} fusion(f32[256,384]{1,0:T(8,128)S(1)} %copy.42, bf16[256,2048]{1,0:T(8,128)(2,1)} %all-gather.5.cloned.1.call-done, bf16[2048,384]{1,0:T(8,128)(2,1)} %param.16), kind=kOutput, calls=%fused_computation.38 | convolution fusion | flops 403439616 | bytes 3211264 | tf_op jit(solution)/shard_map/dot_general | solution.py:126
  98.5 0.6 gather_fusion.1
  99.1 0.1 broadcast_select_fusion
  99.2 20.3 %all_to_all.10 = bf16[8,32,384]{2,1,0:T(8,128)(2,1)S(1)} all-to-all(bf16[8,32,384]{2,1,0:T(8,128)(2,1)S(1)} %broadcast_select_fusion), channel_id=1, replica_groups=mesh['seq'=8,'fsdp'=4] {'seq'}, dimensions={0} | all-to-all | bytes 393216 | tf_op jit(solution)/shard_map/all_to_all | solution.py:165
  119.4 0.7 copy.63
  (60 shorter events, 1.2 us)
Async XLA Ops:
  6.5 48.8 %copy-start = (bf16[2048,384]{1,0:T(8,128)(2,1)S(1)}, bf16[2048,384]{1,0:T(8,128)(2,1)}, u32[]{:S(2)}) copy-start(bf16[2048,384]{1,0:T(8,128)(2,1)} %param.15) | copy-start | bytes 4718596
  6.5 27.8 %copy-start.6 = (s32[4]{0:T(128)S(1)}, s32[4]{0:T(128)}, u32[]{:S(2)}) copy-start(s32[4]{0:T(128)} %param.14) | copy-start | bytes 52
  6.5 30.6 %copy-start.4 = (f32[4,384]{1,0:T(4,128)S(1)}, f32[4,384]{1,0:T(4,128)}, u32[]{:S(2)}) copy-start(f32[4,384]{1,0:T(4,128)} %param.19) | copy-start | bytes 18436
  6.5 30.6 %copy-start.3 = (f32[4,512]{1,0:T(4,128)S(1)}, f32[4,512]{1,0:T(4,128)}, u32[]{:S(2)}) copy-start(f32[4,512]{1,0:T(4,128)} %param.20) | copy-start | bytes 24580
  6.5 30.6 %copy-start.7 = (f32[6]{0:T(128)S(1)}, f32[6]{0:T(128)}, u32[]{:S(2)}) copy-start(f32[6]{0:T(128)} %param.22) | copy-start | bytes 76
  6.5 27.7 %all-gather.3.cloned.1.call-start = ((), (), s32[]{:S(2)}) async-start(), calls=%async_computation.2 | async-start | bytes 2621440 | tf_op jit(solution)/shard_map/all_gather | solution.py:120
  7.3 16.2 %all-to-all-start = ((bf16[8,32,512]{2,1,0:T(8,128)(2,1)}), bf16[8,32,512]{2,1,0:T(8,128)(2,1)S(1)}, u32[]{:S(2)}, u32[]{:S(2)}) async-start(bf16[8,32,512]{2,1,0:T(8,128)(2,1)} %bitcast.86), calls=%async_computation | async-start | bytes 524288 | tf_op jit(solution)/shard_map/all_to_all | solution.py:112
  14.6 38.1 %all-gather.5.cloned.1.call-start = ((), (), s32[]{:S(2)}) async-start(), calls=%async_computation.3 | async-start | bytes 1310720 | tf_op jit(solution)/shard_map/all_gather | solution.py:123
  52.7 2.7 %copy-start.1 = (bf16[256,2048]{1,0:T(8,128)(2,1)S(1)}, bf16[256,2048]{1,0:T(8,128)(2,1)}, u32[]{:S(2)}) copy-start(bf16[256,2048]{1,0:T(8,128)(2,1)} %all-gather.5.cloned.1.call-done) | copy-start | bytes 3145732
  55.4 4.2 %copy-start.2 = (bf16[2048,6]{0,1:T(8,128)(2,1)S(1)}, bf16[2048,6]{0,1:T(8,128)(2,1)}, u32[]{:S(2)}) copy-start(bf16[2048,6]{0,1:T(8,128)(2,1)} %param.18) | copy-start | bytes 73732
  55.4 4.2 %copy-start.5 = (f32[6]{0:T(128)S(1)}, f32[6]{0:T(128)}, u32[]{:S(2)}) copy-start(f32[6]{0:T(128)} %param.21) | copy-start | bytes 76
  56.2 7.0 %collective-permute-start = (bf16[3,896]{1,0:T(4,128)(2,1)S(1)}, bf16[3,896]{1,0:T(4,128)(2,1)S(1)}, u32[]{:S(2)}, u32[]{:S(2)}) collective-permute-start(bf16[3,896]{1,0:T(4,128)(2,1)S(1)} %pad_maximum_fusion.3), channel_id=1, source_target_pairs={{0,4},{4,8},{8,12},{12,16},{16,20},{20,24},{24,28},{1,5},{5,9},{9,... | collective-permute-start | bytes 16136 | tf_op jit(solution)/shard_map/ppermute | solution.py:12
  64.8 8.2 %collective-permute-start.1 = (bf16[6,66,256]{2,1,0:T(8,128)(2,1)S(1)}, bf16[6,66,256]{2,1,0:T(8,128)(2,1)S(1)}, u32[]{:S(2)}, u32[]{:S(2)}) collective-permute-start(bf16[6,66,256]{2,1,0:T(8,128)(2,1)S(1)} %pad_maximum_fusion), channel_id=1, source_target_pairs={{0,4},{4,8},{8,12},{12,16},{16,20},{20,24},{24,28},{1,5},{5,9},{9,... | collective-permute-start | bytes 608264 | tf_op jit(solution)/shard_map/ppermute | solution.py:12
  68.2 7.9 %collective-permute-start.2 = (bf16[6,66,256]{2,1,0:T(8,128)(2,1)S(1)}, bf16[6,66,256]{2,1,0:T(8,128)(2,1)S(1)}, u32[]{:S(2)}, u32[]{:S(2)}) collective-permute-start(bf16[6,66,256]{2,1,0:T(8,128)(2,1)S(1)} %pad_maximum_fusion), channel_id=1, source_target_pairs={{0,8},{4,12},{8,16},{12,20},{16,24},{20,28},{1,9},{5,13},{9,17},{1... | collective-permute-start | bytes 608264 | tf_op jit(solution)/shard_map/ppermute | solution.py:12
  76.4 8.0 %collective-permute-start.3 = (bf16[6,66,256]{2,1,0:T(8,128)(2,1)S(1)}, bf16[6,66,256]{2,1,0:T(8,128)(2,1)S(1)}, u32[]{:S(2)}, u32[]{:S(2)}) collective-permute-start(bf16[6,66,256]{2,1,0:T(8,128)(2,1)S(1)} %pad_maximum_fusion.1), channel_id=1, source_target_pairs={{0,8},{4,12},{8,16},{12,20},{16,24},{20,28},{1,9},{5,13},{9,17},{1... | collective-permute-start | bytes 608264 | tf_op jit(solution)/shard_map/ppermute | solution.py:12
  84.5 9.4 %copy-start.8 = (f32[6]{0:T(128)S(1)}, f32[6]{0:T(128)}, u32[]{:S(2)}) copy-start(f32[6]{0:T(128)} %param.23) | copy-start | bytes 76
  84.6 8.8 %collective-permute-start.4 = (bf16[6,66,256]{2,1,0:T(8,128)(2,1)S(1)}, bf16[6,66,256]{2,1,0:T(8,128)(2,1)S(1)}, u32[]{:S(2)}, u32[]{:S(2)}) collective-permute-start(bf16[6,66,256]{2,1,0:T(8,128)(2,1)S(1)} %pad_maximum_fusion.2), channel_id=1, source_target_pairs={{0,16},{4,20},{8,24},{12,28},{1,17},{5,21},{9,25},{13,29},{2,18},{... | collective-permute-start | bytes 608264 | tf_op jit(solution)/shard_map/ppermute | solution.py:12
Sparse Core Ops, SparseCore 0:
  8.9 25.2 all-gather.2
  35.8 16.7 all-gather.4

commit v4 on v2

--- a/solution.py
+++ b/solution.py
@@ -43,6 +43,26 @@
         held = combine_packed(received(held, axis, cover), held)
         cover *= 2
     return held
+
+
+def gather_columns(block, axis):
+    count = lax.axis_size(axis)
+    if count & (count - 1):
+        return lax.all_gather(block, axis, axis=1, tiled=True)
+    place = lax.axis_index(axis)
+    held, codes = block[None], [0]
+    bit = count // 2
+    while bit >= 1:
+        other = lax.ppermute(held, axis, [(i, i ^ bit) for i in range(count)])
+        held = jnp.concatenate([held, other], axis=0)
+        codes = codes + [c ^ bit for c in codes]
+        bit //= 2
+    where_code = [0] * count
+    for position, code in enumerate(codes):
+        where_code[code] = position
+    order = jnp.asarray(where_code, jnp.int32)[jnp.bitwise_xor(jnp.arange(count, dtype=jnp.int32), place)]
+    ordered = jnp.take(held, order, axis=0)
+    return ordered.transpose(1, 0, 2).reshape(block.shape[0], count * block.shape[1])
 
 
 def segment_of(positions, lengths):
@@ -119,7 +139,7 @@
     state_dim = shared_weight.shape[1] // 2
     w_full = lax.all_gather(shared_weight, "fsdp", axis=0, tiled=True)
     weight_list = (x_weight, z_weight, step_weight, w_full)
-    feature_part = lax.all_gather(stream_block, "fsdp", axis=1, tiled=True)
+    feature_part = gather_columns(stream_block, "fsdp")
     x_acc, z_acc, step_acc, bc_acc = tuple(
         (
             jnp.dot(feature_part, weight, preferred_element_type=jnp.float32)

time: 135 us -> 127 us (0.941)
  waiting for transfers between devices: 47.9 us -> 20.4 us
  local copies, waits for them, and re-layouts: 4.33 us -> 15 us
  other arithmetic: 8.22 us -> 16 us
  starting transfers between devices: 28.5 us -> 32.1 us
  matrix products: 11.6 us -> 9.83 us
    all_gather x1, waiting for transfers between devices: 18.1 us -> 0.02 us  [per_device(): w_full = lax.all_gather(shared_weight, 'fsdp', axis=0, tiled=True)]
    all_gather x1 -> x0, waiting for transfers between devices: 12.2 us -> none  [per_device(): feature_part = lax.all_gather(stream_block, 'fsdp', axis=1, tiled=True)]
    ppermute x0 -> x2, waiting for transfers between devices: none -> 11.8 us  [gather_columns(): other = lax.ppermute(held, axis, [(i, i ^ bit) for i in range(count)])]
    all_to_all x1, waiting for transfers between devices: 7.02 us -> 0.01 us  [per_device(): lax.all_to_all(slot_rows, 'seq', split_axis=0, concat_axis=0, tiled=True)]
    dot_general x4, matrix products: 8.34 us -> 5.53 us  [per_device(): jnp.dot(feature_part, weight, preferred_element_type=jnp.float32)]
    slice x2, local copies, waits for them, and re-layouts: 0.19 us -> 2.69 us  [per_device(): x_heads = activated[:, :inner_dev].reshape(tok_dev, heads_dev, head_dim)]
    gather x0 -> x2, local copies, waits for them, and re-layouts: none -> 2.5 us  [the longest x1 1.86 us: gather_columns(): ordered = jnp.take(held, order, axis=0)]
    ppermute x5, waiting for transfers between devices: 9.9 us -> 7.86 us  [shifted(): return lax.ppermute(array, axis, pairs)]
  transfers between devices with their start and end apart: 8 -> 9, of which waited for: 7 -> 6; matrix products, arithmetic and copies ran while one was open for 9% -> 19% of each run, Pallas kernels for 0% -> 0%
where the time goes in v4:
time: 127 us; the launch traced here: 126 us
  starting transfers between devices  32.1 us (25%)
  waiting for transfers between devices  20.4 us (16%)
  blocking collectives  18.3 us (14%)
  other arithmetic  16 us (13%)
  local copies, waits for them, and re-layouts  15 us (12%)
  between operations  14.6 us (11%)
  matrix products  9.83 us (8%)
    ppermute x5, starting transfers between devices, shifted(): return lax.ppermute(array, axis, pairs)  23 us
    all_to_all x1, blocking collectives, per_device(): lax.all_to_all(outgoing, 'seq', split_axis=0, concat_axis=0, tiled=True)  18.3 us
    ppermute x2, waiting for transfers between devices, gather_columns(): other = lax.ppermute(held, axis, [(i, i ^ bit) for i in range(count)])  11.8 us
    ppermute x5, waiting for transfers between devices, shifted(): return lax.ppermute(array, axis, pairs)  7.86 us
    all_to_all x1, starting transfers between devices, per_device(): lax.all_to_all(slot_rows, 'seq', split_axis=0, concat_axis=0, tiled=True)  7.41 us
    dot_general x4, matrix products, per_device(): jnp.dot(feature_part, weight, preferred_element_type=jnp.float32)  5.53 us
    another operation x3, other arithmetic  2.69 us
    slice x2, local copies, waits for them, and re-layouts, per_device(): x_heads = activated[:, :inner_dev].reshape(tok_dev, heads_dev, head_dim)  2.69 us
  transfers between devices with their start and end apart: 9, of which 6 were waited for; matrix products, arithmetic and copies ran while one was open for 19% of the time, Pallas kernels for 0%

profile of v4, /device:TPU:0, one launch (start us, length us, event | category | flops | bytes accessed | tf_op | source)
XLA Modules:
  0.0 126.2 jit_solution(851981250091203117)
XLA Ops:
  6.5 7.4 %all-to-all-start = ((bf16[8,32,512]{2,1,0:T(8,128)(2,1)}), bf16[8,32,512]{2,1,0:T(8,128)(2,1)S(1)}, u32[]{:S(2)}, u32[]{:S(2)}) async-start(bf16[8,32,512]{2,1,0:T(8,128)(2,1)} %bitcast.101), calls=%async_computation | async-start | bytes 524288 | tf_op jit(solution)/shard_map/all_to_all | solution.py:132
  14.0 0.7 all-gather.2.cloned.1.call-update
  14.7 1.3 %compare_and_fusion.2 = (pred[8]{0:T(512)(128)(4,1)}, s32[8]{0:T(128)S(1)}) fusion(s32[8,8]{1,0:T(8,128)} %param.14, s32[]{:T(128)S(6)} %select_n.114), kind=kLoop, calls=%fused_computation.121 | loop fusion | flops 48 | bytes 76 | tf_op jit(solution)/shard_map/jit(_take)/and | solution.py:183
  16.0 1.0 sort.17
  17.0 0.8 reduce-window.18
  17.9 0.6 fusion.72
  18.5 0.7 constant_dynamic-update-slice_fusion.1
  19.2 0.7 constant_dynamic-update-slice_fusion
  19.9 0.7 fusion.61
  21.2 1.3 %broadcast_compare_fusion = (pred[256]{0:T(512)(128)(4,1)S(1)}, pred[256]{0:T(512)(128)(4,1)S(1)}, f32[256]{0:T(256)}, f32[256]{0:T(256)}, f32[256]{0:T(256)}) fusion(s32[]{:T(128)} %bitcast.17, s32[259]{0:T(512)S(1)} %convert_reduce_fusion, s32[]{:T(128)S(6)} %select_n.126), kind=kLoop, calls=%fused_computation.128 | loop fusion | flops 2048 | bytes 7688 | tf_op jit(solution)/shard_map/eq | solution.py:103
  22.7 0.6 slice_reduce_fusion.4
  24.0 1.6 %collective-permute-start = (bf16[1,256,512]{2,1,0:T(8,128)(2,1)S(1)}, bf16[1,256,512]{2,1,0:T(8,128)(2,1)S(1)}, u32[]{:S(2)}, u32[]{:S(2)}) collective-permute-start(bf16[1,256,512]{2,1,0:T(8,128)(2,1)S(1)} %bitcast_select_fusion), channel_id=1, source_target_pairs={{0,2},{1,3},{2,0},{3,1},{4,6},{5,7},{6,4},{7,5},{8,10},{9,11},{10,... | collective-permute-start | bytes 786440 | tf_op jit(solution)/shard_map/ppermute | solution.py:56
  26.2 0.7 slice.124
  26.8 0.6 gather_fusion
  27.5 10.0 %collective-permute-done = bf16[1,256,512]{2,1,0:T(8,128)(2,1)S(1)} collective-permute-done((bf16[1,256,512]{2,1,0:T(8,128)(2,1)S(1)}, bf16[1,256,512]{2,1,0:T(8,128)(2,1)S(1)}, u32[]{:S(2)}, u32[]{:S(2)}) %collective-permute-start) | collective-permute-done | bytes 262176 | tf_op jit(solution)/shard_map/ppermute | solution.py:56
  37.6 1.8 %collective-permute-done.1 = bf16[2,256,512]{2,1,0:T(8,128)(2,1)S(1)} collective-permute-done((bf16[2,256,512]{2,1,0:T(8,128)(2,1)S(1)}, bf16[2,256,512]{2,1,0:T(8,128)(2,1)S(1)}, u32[]{:S(2)}, u32[]{:S(2)}) %collective-permute-start.1) | collective-permute-done | bytes 524320 | tf_op jit(solution)/shard_map/ppermute | solution.py:56
  39.5 1.1 pad_maximum_fusion
  40.6 1.9 %gather_fusion.2 = bf16[4,256,512]{2,1,0:T(8,128)(2,1)S(1)} fusion(bf16[4,256,512]{2,1,0:T(8,128)(2,1)} %pad_maximum_fusion, s32[1024]{0:T(1024)S(1)} %pad_clamp_fusion.1), kind=kCustom, calls=%fused_computation.2 | custom fusion | bytes 2097168 | tf_op jit(solution)/shard_map/jit(_take)/gather | solution.py:64
  42.4 1.2 select_bitcast_fusion
  43.6 1.5 %copy.50 = bf16[256,4,512]{0,2,1:T(8,128)(2,1)S(1)} copy(bf16[256,4,512]{2,0,1:T(8,128)(2,1)} %select_bitcast_fusion) | data formatting | bytes 2097152 | tf_op jit(solution)/shard_map/jit(_take)/select_n | solution.py:64
  45.4 1.8 %reduce-window.19 = f32[6,2,128]{2,1,0:T(2,128)S(1)} reduce-window(f32[6,2,128]{2,1,0:T(2,128)S(1)} %reshape.284, f32[]{:T(128)} %constant.82.clone.1), window={size=1x1x128 pad=0_0x0_0x127_0}, to_apply=%region_3.4 | reduce-window | flops 195072 | bytes 12292 | tf_op jit(solution)/shard_map/reduce-window.1
  47.8 0.6 compare_select_fusion.1
  48.5 0.7 convolution_convert_fusion.3
  49.3 2.3 %convolution_convert_fusion = bf16[256,512]{1,0:T(8,128)(2,1)S(1)} fusion(bf16[256,2048]{0,1:T(8,128)(2,1)S(1)} %bitcast.94, bf16[2048,512]{1,0:T(8,128)(2,1)} %all-gather.2.cloned.1.call-done), kind=kOutput, calls=%fused_computation.12 | convolution fusion | flops 537001984 | bytes 3407872 | tf_op jit(solution)/shard_map/dot_general | solution.py:145
  51.7 3.6 %collective-permute-start.2 = (bf16[3,896]{1,0:T(4,128)(2,1)S(1)}, bf16[3,896]{1,0:T(4,128)(2,1)S(1)}, u32[]{:S(2)}, u32[]{:S(2)}) collective-permute-start(bf16[3,896]{1,0:T(4,128)(2,1)S(1)} %pad_maximum_fusion.5), channel_id=1, source_target_pairs={{0,4},{4,8},{8,12},{12,16},{16,20},{20,24},{24,28},{1,5},{5,9},{9,... | collective-permute-start | bytes 16136 | tf_op jit(solution)/shard_map/ppermute | solution.py:12
  55.4 1.3 %fusion.64 = (bf16[6]{0:T(256)(128)(2,1)}, bf16[6]{0:T(256)(128)(2,1)}) fusion(f32[6]{0:T(128)S(1)} %slice_reduce_fusion, pred[]{:T(512)} %bitcast.19), kind=kLoop, calls=%fused_computation.134 | loop fusion | flops 30 | bytes 49 | tf_op jit(solution)/shard_map/convert_element_type | solution.py:25
  56.9 0.7 divide_multiply_fusion
  57.5 0.8 slice.152
  58.3 1.9 %copy.51 = f32[256,384]{0,1:T(8,128)} copy(f32[256,384]{1,0:T(8,128)} %slice.152) | data formatting | bytes 786432 | tf_op jit(solution)/shard_map/slice | solution.py:167
  60.2 1.5 %convolution_convert_fusion.2 = bf16[6,64,256]{2,1,0:T(8,128)(2,1)S(1)} fusion(f32[256,6,64]{0,2,1:T(8,128)} %bitcast.96, f32[256,896]{1,0:T(8,128)S(1)} %divide_multiply_fusion, f32[256,6]{0,1:T(8,128)S(1)} %get-tuple-element.23, f32[256,6]{0,1:T(8,128)} %compare_select_fusion.1), kind=kOutput, calls=%fused_computation.16 | convolution fusion | flops 302284800 | bytes 866304 | tf_op jit(solution)/shard_map/shp,sn->hpn/dot_general | solution.py:106
  61.7 0.7 broadcast_in_dim.115
  62.5 0.7 broadcast_in_dim.116
  63.2 0.7 pad_maximum_fusion.2
  63.9 4.9 %collective-permute-start.3 = (bf16[6,66,256]{2,1,0:T(8,128)(2,1)}, bf16[6,66,256]{2,1,0:T(8,128)(2,1)}, u32[]{:S(2)}, u32[]{:S(2)}) collective-permute-start(bf16[6,66,256]{2,1,0:T(8,128)(2,1)} %pad_maximum_fusion.2), channel_id=1, source_target_pairs={{0,4},{4,8},{8,12},{12,16},{16,20},{20,24},{24,28},{1,5},{5,9},{9,... | collective-permute-start | bytes 608264 | tf_op jit(solution)/shard_map/ppermute | solution.py:12
  68.8 3.4 %collective-permute-start.4 = (bf16[6,66,256]{2,1,0:T(8,128)(2,1)}, bf16[6,66,256]{2,1,0:T(8,128)(2,1)}, u32[]{:S(2)}, u32[]{:S(2)}) collective-permute-start(bf16[6,66,256]{2,1,0:T(8,128)(2,1)} %pad_maximum_fusion.2), channel_id=1, source_target_pairs={{0,8},{4,12},{8,16},{12,20},{16,24},{20,28},{1,9},{5,13},{9,17},{1... | collective-permute-start | bytes 608264 | tf_op jit(solution)/shard_map/ppermute | solution.py:12
  72.2 0.7 slice.107
  72.9 1.0 convert_element_type.123
  73.9 1.5 %collective-permute-done.4 = bf16[6,66,256]{2,1,0:T(8,128)(2,1)} collective-permute-done((bf16[6,66,256]{2,1,0:T(8,128)(2,1)}, bf16[6,66,256]{2,1,0:T(8,128)(2,1)}, u32[]{:S(2)}, u32[]{:S(2)}) %collective-permute-start.4) | collective-permute-done | bytes 202784 | tf_op jit(solution)/shard_map/ppermute | solution.py:12
  75.3 1.0 convert_element_type.125
  76.5 5.7 %collective-permute-start.5 = (bf16[6,66,256]{2,1,0:T(8,128)(2,1)S(1)}, bf16[6,66,256]{2,1,0:T(8,128)(2,1)S(1)}, u32[]{:S(2)}, u32[]{:S(2)}) collective-permute-start(bf16[6,66,256]{2,1,0:T(8,128)(2,1)S(1)} %pad_maximum_fusion.3), channel_id=1, source_target_pairs={{0,8},{4,12},{8,16},{12,20},{16,24},{20,28},{1,9},{5,13},{9,17},{1... | collective-permute-start | bytes 608264 | tf_op jit(solution)/shard_map/ppermute | solution.py:12
  82.3 3.3 %collective-permute-done.5 = bf16[6,66,256]{2,1,0:T(8,128)(2,1)S(1)} collective-permute-done((bf16[6,66,256]{2,1,0:T(8,128)(2,1)S(1)}, bf16[6,66,256]{2,1,0:T(8,128)(2,1)S(1)}, u32[]{:S(2)}, u32[]{:S(2)}) %collective-permute-start.5) | collective-permute-done | bytes 202784 | tf_op jit(solution)/shard_map/ppermute | solution.py:12
  85.8 5.4 %collective-permute-start.6 = (bf16[6,66,256]{2,1,0:T(8,128)(2,1)S(1)}, bf16[6,66,256]{2,1,0:T(8,128)(2,1)S(1)}, u32[]{:S(2)}, u32[]{:S(2)}) collective-permute-start(bf16[6,66,256]{2,1,0:T(8,128)(2,1)S(1)} %pad_maximum_fusion.4), channel_id=1, source_target_pairs={{0,16},{4,20},{8,24},{12,28},{1,17},{5,21},{9,25},{13,29},{2,18},{... | collective-permute-start | bytes 608264 | tf_op jit(solution)/shard_map/ppermute | solution.py:12
  91.7 3.0 %collective-permute-done.6 = bf16[6,66,256]{2,1,0:T(8,128)(2,1)S(1)} collective-permute-done((bf16[6,66,256]{2,1,0:T(8,128)(2,1)S(1)}, bf16[6,66,256]{2,1,0:T(8,128)(2,1)S(1)}, u32[]{:S(2)}, u32[]{:S(2)}) %collective-permute-start.6) | collective-permute-done | bytes 202784 | tf_op jit(solution)/shard_map/ppermute | solution.py:12
  95.3 1.9 %fusion.11 = f32[256,6,64]{0,2,1:T(8,128)S(1)} fusion(f32[256,6,64]{0,2,1:T(8,128)S(1)} %convolution_multiply_fusion, f32[6,256]{1,0:T(8,128)S(1)} %bitcast.108, f32[256,256]{1,0:T(8,128)S(1)} %fusion.37, pred[256,256]{1,0:T(8,128)(4,1)S(1)} %fusion.35, f32[256,6,64]{0,2,1:T(8,128)S(1)} %bitcast.97, f32[6]{0:T(128)S(1)} %copy-done.18, ...), kind=kOutput, calls=%fused_computation.11 | convolution fusion | flops 303562752 | bytes 1519640 | tf_op jit(solution)/shard_map/hts,shp->thp/dot_general | solution.py:100
  97.3 2.2 %multiply_convert_fusion = bf16[256,384]{1,0:T(8,128)(2,1)S(1)} fusion(f32[256,384]{1,0:T(8,128)S(1)} %copy.54, bf16[256,2048]{0,1:T(8,128)(2,1)S(1)} %bitcast.95, bf16[2048,384]{1,0:T(8,128)(2,1)} %param.17), kind=kOutput, calls=%fused_computation.43 | convolution fusion | flops 403439616 | bytes 3211264 | tf_op jit(solution)/shard_map/dot_general | solution.py:145
  99.5 0.7 gather_fusion.3
  100.4 18.3 %all_to_all.10 = bf16[8,32,384]{2,1,0:T(8,128)(2,1)S(1)} all-to-all(bf16[8,32,384]{2,1,0:T(8,128)(2,1)S(1)} %broadcast_select_fusion), channel_id=1, replica_groups=mesh['seq'=8,'fsdp'=4] {'seq'}, dimensions={0} | all-to-all | bytes 393216 | tf_op jit(solution)/shard_map/all_to_all | solution.py:184
  118.7 0.7 copy.75
  (91 shorter events, 4.5 us)
Async XLA Ops:
  6.5 42.0 %copy-start = (bf16[2048,384]{1,0:T(8,128)(2,1)S(1)}, bf16[2048,384]{1,0:T(8,128)(2,1)}, u32[]{:S(2)}) copy-start(bf16[2048,384]{1,0:T(8,128)(2,1)} %param.16) | copy-start | bytes 4718596
  6.5 20.3 %copy-start.1 = (s32[4]{0:T(128)S(1)}, s32[4]{0:T(128)}, u32[]{:S(2)}) copy-start(s32[4]{0:T(128)} %constant.87.clone) | copy-start | bytes 52
  6.5 16.8 %all-to-all-start = ((bf16[8,32,512]{2,1,0:T(8,128)(2,1)}), bf16[8,32,512]{2,1,0:T(8,128)(2,1)S(1)}, u32[]{:S(2)}, u32[]{:S(2)}) async-start(bf16[8,32,512]{2,1,0:T(8,128)(2,1)} %bitcast.101), calls=%async_computation | async-start | bytes 524288 | tf_op jit(solution)/shard_map/all_to_all | solution.py:132
  14.0 23.7 %copy-start.17 = (f32[6]{0:T(128)S(1)}, f32[6]{0:T(128)}, u32[]{:S(2)}) copy-start(f32[6]{0:T(128)} %param.23) | copy-start | bytes 76
  14.0 35.3 %all-gather.2.cloned.1.call-start = ((), (), s32[]{:S(2)}) async-start(), calls=%async_computation.2 | async-start | bytes 2621440 | tf_op jit(solution)/shard_map/all_gather | solution.py:140
  17.9 5.4 %copy-start.5 = (s32[259]{0:T(512)}, s32[259]{0:T(512)S(1)}, u32[]{:S(2)}) copy-start(s32[259]{0:T(512)S(1)} %convert_reduce_fusion) | copy-start | bytes 3112
  24.0 13.4 %collective-permute-start = (bf16[1,256,512]{2,1,0:T(8,128)(2,1)S(1)}, bf16[1,256,512]{2,1,0:T(8,128)(2,1)S(1)}, u32[]{:S(2)}, u32[]{:S(2)}) collective-permute-start(bf16[1,256,512]{2,1,0:T(8,128)(2,1)S(1)} %bitcast_select_fusion), channel_id=1, source_target_pairs={{0,2},{1,3},{2,0},{3,1},{4,6},{5,7},{6,4},{7,5},{8,10},{9,11},{10,... | collective-permute-start | bytes 786440 | tf_op jit(solution)/shard_map/ppermute | solution.py:56
  37.5 2.0 %collective-permute-start.1 = (bf16[2,256,512]{2,1,0:T(8,128)(2,1)S(1)}, bf16[2,256,512]{2,1,0:T(8,128)(2,1)S(1)}, u32[]{:S(2)}, u32[]{:S(2)}) collective-permute-start(bf16[2,256,512]{2,1,0:T(8,128)(2,1)S(1)} %pad_maximum_fusion.1), channel_id=1, source_target_pairs={{0,1},{1,0},{2,3},{3,2},{4,5},{5,4},{6,7},{7,6},{8,9},{9,8},{10,11... | collective-permute-start | bytes 1572872 | tf_op jit(solution)/shard_map/ppermute | solution.py:56
  43.6 1.5 %copy-start.4 = (bf16[2048,6]{0,1:T(8,128)(2,1)S(1)}, bf16[2048,6]{0,1:T(8,128)(2,1)}, u32[]{:S(2)}) copy-start(bf16[2048,6]{0,1:T(8,128)(2,1)} %param.19) | copy-start | bytes 73732
  43.6 1.5 %copy-start.16 = (f32[6]{0:T(128)S(1)}, f32[6]{0:T(128)}, u32[]{:S(2)}) copy-start(f32[6]{0:T(128)} %param.22) | copy-start | bytes 76
  47.6 0.8 copy-start.6
  51.6 5.2 %copy-start.8 = (f32[896]{0:T(1024)S(1)}, f32[896]{0:T(1024)}, u32[]{:S(2)}) copy-start(f32[896]{0:T(1024)} %get-tuple-element.7) | copy-start | bytes 10756
  51.6 5.2 %copy-start.9 = (f32[896]{0:T(1024)S(1)}, f32[896]{0:T(1024)}, u32[]{:S(2)}) copy-start(f32[896]{0:T(1024)} %get-tuple-element.8) | copy-start | bytes 10756
  51.6 5.2 %copy-start.10 = (f32[896]{0:T(1024)S(1)}, f32[896]{0:T(1024)}, u32[]{:S(2)}) copy-start(f32[896]{0:T(1024)} %get-tuple-element.9) | copy-start | bytes 10756
  51.6 5.2 %copy-start.11 = (f32[896]{0:T(1024)S(1)}, f32[896]{0:T(1024)}, u32[]{:S(2)}) copy-start(f32[896]{0:T(1024)} %get-tuple-element.10) | copy-start | bytes 10756
  51.6 5.2 %copy-start.12 = (f32[256]{0:T(256)S(1)}, f32[256]{0:T(256)}, u32[]{:S(2)}) copy-start(f32[256]{0:T(256)} %get-tuple-element.26) | copy-start | bytes 3076
  51.7 5.2 %copy-start.13 = (f32[256]{0:T(256)S(1)}, f32[256]{0:T(256)}, u32[]{:S(2)}) copy-start(f32[256]{0:T(256)} %get-tuple-element.27) | copy-start | bytes 3076
  51.7 5.2 %copy-start.14 = (f32[256]{0:T(256)S(1)}, f32[256]{0:T(256)}, u32[]{:S(2)}) copy-start(f32[256]{0:T(256)} %get-tuple-element.28) | copy-start | bytes 3076
  51.7 5.0 %collective-permute-start.2 = (bf16[3,896]{1,0:T(4,128)(2,1)S(1)}, bf16[3,896]{1,0:T(4,128)(2,1)S(1)}, u32[]{:S(2)}, u32[]{:S(2)}) collective-permute-start(bf16[3,896]{1,0:T(4,128)(2,1)S(1)} %pad_maximum_fusion.5), channel_id=1, source_target_pairs={{0,4},{4,8},{8,12},{12,16},{16,20},{20,24},{24,28},{1,5},{5,9},{9,... | collective-permute-start | bytes 16136 | tf_op jit(solution)/shard_map/ppermute | solution.py:12
  63.9 9.0 %collective-permute-start.3 = (bf16[6,66,256]{2,1,0:T(8,128)(2,1)}, bf16[6,66,256]{2,1,0:T(8,128)(2,1)}, u32[]{:S(2)}, u32[]{:S(2)}) collective-permute-start(bf16[6,66,256]{2,1,0:T(8,128)(2,1)} %pad_maximum_fusion.2), channel_id=1, source_target_pairs={{0,4},{4,8},{8,12},{12,16},{16,20},{20,24},{24,28},{1,5},{5,9},{9,... | collective-permute-start | bytes 608264 | tf_op jit(solution)/shard_map/ppermute | solution.py:12
  68.8 6.5 %collective-permute-start.4 = (bf16[6,66,256]{2,1,0:T(8,128)(2,1)}, bf16[6,66,256]{2,1,0:T(8,128)(2,1)}, u32[]{:S(2)}, u32[]{:S(2)}) collective-permute-start(bf16[6,66,256]{2,1,0:T(8,128)(2,1)} %pad_maximum_fusion.2), channel_id=1, source_target_pairs={{0,8},{4,12},{8,16},{12,20},{16,24},{20,28},{1,9},{5,13},{9,17},{1... | collective-permute-start | bytes 608264 | tf_op jit(solution)/shard_map/ppermute | solution.py:12
  76.5 9.1 %collective-permute-start.5 = (bf16[6,66,256]{2,1,0:T(8,128)(2,1)S(1)}, bf16[6,66,256]{2,1,0:T(8,128)(2,1)S(1)}, u32[]{:S(2)}, u32[]{:S(2)}) collective-permute-start(bf16[6,66,256]{2,1,0:T(8,128)(2,1)S(1)} %pad_maximum_fusion.3), channel_id=1, source_target_pairs={{0,8},{4,12},{8,16},{12,20},{16,24},{20,28},{1,9},{5,13},{9,17},{1... | collective-permute-start | bytes 608264 | tf_op jit(solution)/shard_map/ppermute | solution.py:12
  85.7 9.5 %copy-start.2 = (f32[256,384]{0,1:T(8,128)S(1)}, f32[256,384]{0,1:T(8,128)}, u32[]{:S(2)}) copy-start(f32[256,384]{0,1:T(8,128)} %copy.51) | copy-start | bytes 1179652
  85.7 9.5 %copy-start.3 = (f32[256,6]{0,1:T(8,128)S(1)}, f32[256,6]{0,1:T(8,128)}, u32[]{:S(2)}) copy-start(f32[256,6]{0,1:T(8,128)} %compare_select_fusion.1) | copy-start | bytes 18436
  85.7 9.5 %copy-start.7 = (f32[1,6,2,128]{3,1,2,0:T(8,128)S(1)}, f32[1,6,2,128]{3,1,2,0:T(8,128)}, u32[]{:S(2)}) copy-start(f32[1,6,2,128]{3,1,2,0:T(8,128)} %copy-done.6) | copy-start | bytes 18436
  85.8 9.5 %copy-start.18 = (f32[6]{0:T(128)S(1)}, f32[6]{0:T(128)}, u32[]{:S(2)}) copy-start(f32[6]{0:T(128)} %param.24) | copy-start | bytes 76
  85.8 8.9 %collective-permute-start.6 = (bf16[6,66,256]{2,1,0:T(8,128)(2,1)S(1)}, bf16[6,66,256]{2,1,0:T(8,128)(2,1)S(1)}, u32[]{:S(2)}, u32[]{:S(2)}) collective-permute-start(bf16[6,66,256]{2,1,0:T(8,128)(2,1)S(1)} %pad_maximum_fusion.4), channel_id=1, source_target_pairs={{0,16},{4,20},{8,24},{12,28},{1,17},{5,21},{9,25},{13,29},{2,18},{... | collective-permute-start | bytes 608264 | tf_op jit(solution)/shard_map/ppermute | solution.py:12
  97.3 2.9 %copy-start.15 = (pred[8]{0:T(512)(128)(4,1)S(1)}, pred[8]{0:T(512)(128)(4,1)}, u32[]{:S(2)}) copy-start(pred[8]{0:T(512)(128)(4,1)} %get-tuple-element.11) | copy-start | bytes 28
Sparse Core Ops, SparseCore 0:
  16.4 28.2 all-gather.1

commit v5 on v4

--- a/solution.py
+++ b/solution.py
@@ -45,10 +45,10 @@
     return held
 
 
-def gather_columns(block, axis):
+def gather_blocks(block, axis):
     count = lax.axis_size(axis)
     if count & (count - 1):
-        return lax.all_gather(block, axis, axis=1, tiled=True)
+        return lax.all_gather(block, axis, axis=0, tiled=False)
     place = lax.axis_index(axis)
     held, codes = block[None], [0]
     bit = count // 2
@@ -61,8 +61,12 @@
     for position, code in enumerate(codes):
         where_code[code] = position
     order = jnp.asarray(where_code, jnp.int32)[jnp.bitwise_xor(jnp.arange(count, dtype=jnp.int32), place)]
-    ordered = jnp.take(held, order, axis=0)
-    return ordered.transpose(1, 0, 2).reshape(block.shape[0], count * block.shape[1])
+    return jnp.take(held, order, axis=0)
+
+
+def gather_columns(block, axis):
+    stacked = gather_blocks(block, axis)
+    return stacked.transpose(1, 0, 2).reshape(block.shape[0], stacked.shape[0] * block.shape[1])
 
 
 def segment_of(positions, lengths):
@@ -137,7 +141,7 @@
     heads_dev = step_weight.shape[1]
     head_dim = inner_dev // heads_dev
     state_dim = shared_weight.shape[1] // 2
-    w_full = lax.all_gather(shared_weight, "fsdp", axis=0, tiled=True)
+    w_full = gather_blocks(shared_weight, "fsdp").reshape(-1, shared_weight.shape[1])
     weight_list = (x_weight, z_weight, step_weight, w_full)
     feature_part = gather_columns(stream_block, "fsdp")
     x_acc, z_acc, step_acc, bc_acc = tuple(

time: 127 us -> 115 us (0.906)
  between operations: 14.6 us -> 1.25 us
  waiting for transfers between devices: 20.4 us -> 12.4 us
  local copies, waits for them, and re-layouts: 15 us -> 20.1 us
  other arithmetic: 16 us -> 19.7 us
  blocking collectives: 18.3 us -> 16 us
  starting transfers between devices: 32.1 us -> 34.2 us
    ppermute x2 -> x4, waiting for transfers between devices: 11.8 us -> 3.21 us  [gather_blocks(): other = lax.ppermute(held, axis, [(i, i ^ bit) for i in range(count)])]
    gather x2 -> x3, local copies, waits for them, and re-layouts: 2.5 us -> 6.72 us  [the longest x2 5.42 us: gather_blocks(): return jnp.take(held, order, axis=0)]
    concatenate x2 -> x4, other arithmetic: 1.14 us -> 5.04 us  [gather_blocks(): held = jnp.concatenate([held, other], axis=0)]
    ppermute x2 -> x4, starting transfers between devices: 1.63 us -> 4.1 us  [gather_blocks(): other = lax.ppermute(held, axis, [(i, i ^ bit) for i in range(count)])]
    all_to_all x1, blocking collectives: 18.3 us -> 16 us  [per_device(): lax.all_to_all(outgoing, 'seq', split_axis=0, concat_axis=0, tiled=True)]
    all_to_all x1, starting transfers between devices: 7.41 us -> 5.97 us  [per_device(): lax.all_to_all(slot_rows, 'seq', split_axis=0, concat_axis=0, tiled=True)]
  transfers between devices with their start and end apart: 9 -> 10, of which waited for: 6 -> 6; matrix products, arithmetic and copies ran while one was open for 19% -> 22% of each run, Pallas kernels for 0% -> 0%
where the time goes in v5:
time: 115 us; the launch traced here: 114 us
  starting transfers between devices  34.2 us (30%)
  local copies, waits for them, and re-layouts  20.1 us (17%)
  other arithmetic  19.7 us (17%)
  blocking collectives  16 us (14%)
  waiting for transfers between devices  12.4 us (11%)
  matrix products  10.2 us (9%)
  between operations  1.25 us (1%)
    ppermute x5, starting transfers between devices, shifted(): return lax.ppermute(array, axis, pairs)  24.1 us
    all_to_all x1, blocking collectives, per_device(): lax.all_to_all(outgoing, 'seq', split_axis=0, concat_axis=0, tiled=True)  16 us
    ppermute x5, waiting for transfers between devices, shifted(): return lax.ppermute(array, axis, pairs)  7.88 us
    all_to_all x1, starting transfers between devices, per_device(): lax.all_to_all(slot_rows, 'seq', split_axis=0, concat_axis=0, tiled=True)  5.97 us
    dot_general x4, matrix products, per_device(): jnp.dot(feature_part, weight, preferred_element_type=jnp.float32)  5.91 us
    gather x2, local copies, waits for them, and re-layouts, gather_blocks(): return jnp.take(held, order, axis=0)  5.42 us
    concatenate x4, other arithmetic, gather_blocks(): held = jnp.concatenate([held, other], axis=0)  5.04 us
    ppermute x4, starting transfers between devices, gather_blocks(): other = lax.ppermute(held, axis, [(i, i ^ bit) for i in range(count)])  4.1 us
  transfers between devices with their start and end apart: 10, of which 6 were waited for; matrix products, arithmetic and copies ran while one was open for 22% of the time, Pallas kernels for 0%

profile of v5, /device:TPU:0, one launch (start us, length us, event | category | flops | bytes accessed | tf_op | source)
XLA Modules:
  0.0 113.9 jit_solution(16122949836369039611)
XLA Ops:
  0.0 2.9 %collective-permute-start.2 = (bf16[1,512,512]{2,1,0:T(8,128)(2,1)}, bf16[1,512,512]{2,1,0:T(8,128)(2,1)S(1)}, u32[]{:S(2)}, u32[]{:S(2)}) collective-permute-start(bf16[1,512,512]{2,1,0:T(8,128)(2,1)} %bitcast.99), channel_id=1, source_target_pairs={{0,2},{1,3},{2,0},{3,1},{4,6},{5,7},{6,4},{7,5},{8,10},{9,11},{10,... | collective-permute-start | bytes 1572872 | tf_op jit(solution)/shard_map/ppermute | solution.py:56
  2.9 6.0 %all-to-all-start = ((bf16[8,32,512]{2,1,0:T(8,128)(2,1)}), bf16[8,32,512]{2,1,0:T(8,128)(2,1)S(1)}, u32[]{:S(2)}, u32[]{:S(2)}) async-start(bf16[8,32,512]{2,1,0:T(8,128)(2,1)} %bitcast.107), calls=%async_computation | async-start | bytes 524288 | tf_op jit(solution)/shard_map/all_to_all | solution.py:136
  8.9 0.7 fusion.71
  9.6 1.3 %compare_and_fusion.2 = (pred[8]{0:T(512)(128)(4,1)}, s32[8]{0:T(128)S(1)}) fusion(s32[8,8]{1,0:T(8,128)} %param.15, s32[]{:T(128)S(6)} %select_n.134), kind=kLoop, calls=%fused_computation.129 | loop fusion | flops 48 | bytes 76 | tf_op jit(solution)/shard_map/jit(_take)/and | solution.py:187
  10.9 1.0 sort.17
  11.9 0.7 constant_dynamic-update-slice_fusion.1
  12.6 0.8 reduce-window.18
  14.0 0.7 constant_dynamic-update-slice_fusion
  15.0 1.3 %gather_fusion = s32[4]{0:T(128)S(1)} fusion(s32[4]{0:T(128)} %constant.99.clone, s32[1024]{0:T(1024)S(1)} %get-tuple-element.36), kind=kCustom, calls=%fused_computation | custom fusion | bytes 48 | tf_op jit(solution)/shard_map/gather | solution.py:63
  16.3 1.3 %all-to-all-done = bf16[8,32,512]{2,1,0:T(8,128)(2,1)S(1)} async-done(((bf16[8,32,512]{2,1,0:T(8,128)(2,1)}), bf16[8,32,512]{2,1,0:T(8,128)(2,1)S(1)}, u32[]{:S(2)}, u32[]{:S(2)}) %all-to-all-start) | async-done | bytes 262176 | tf_op jit(solution)/shard_map/all_to_all | solution.py:136
  18.8 0.7 fusion.83
  20.2 1.3 %broadcast_compare_fusion = (pred[256]{0:T(512)(128)(4,1)S(1)}, pred[256]{0:T(512)(128)(4,1)S(1)}, f32[256]{0:T(256)}, f32[256]{0:T(256)}, f32[256]{0:T(256)}) fusion(s32[]{:T(128)} %bitcast.19, s32[259]{0:T(512)S(1)} %convert_reduce_fusion, s32[]{:T(128)S(6)} %select_n.149), kind=kLoop, calls=%fused_computation.136 | loop fusion | flops 2048 | bytes 7688 | tf_op jit(solution)/shard_map/eq | solution.py:107
  21.5 3.2 %collective-permute-done = bf16[1,256,512]{2,1,0:T(8,128)(2,1)S(1)} collective-permute-done((bf16[1,256,512]{2,1,0:T(8,128)(2,1)S(1)}, bf16[1,256,512]{2,1,0:T(8,128)(2,1)S(1)}, u32[]{:S(2)}, u32[]{:S(2)}) %collective-permute-start) | collective-permute-done | bytes 262176 | tf_op jit(solution)/shard_map/ppermute | solution.py:56
  26.1 1.2 %pad_maximum_fusion.2 = bf16[2,512,512]{2,1,0:T(8,128)(2,1)} fusion(bf16[1,512,512]{2,1,0:T(8,128)(2,1)S(1)} %collective-permute-done.2, bf16[1,512,512]{2,1,0:T(8,128)(2,1)S(1)} %bitcast.100), kind=kLoop, calls=%fused_computation.26 | loop fusion | flops 524288 | bytes 2097152 | tf_op jit(solution)/shard_map/concatenate | solution.py:57
  27.7 1.1 pad_maximum_fusion.1
  28.8 1.8 %gather_fusion.2 = bf16[4,256,512]{2,1,0:T(8,128)(2,1)S(1)} fusion(bf16[4,256,512]{2,1,0:T(8,128)(2,1)} %pad_maximum_fusion.1, s32[1024]{0:T(1024)S(1)} %pad_clamp_fusion.1), kind=kCustom, calls=%fused_computation.2 | custom fusion | bytes 2097168 | tf_op jit(solution)/shard_map/jit(_take)/gather | solution.py:64
  30.6 1.0 copy-done.1
  31.6 1.1 select_bitcast_fusion
  32.7 1.5 %copy.52 = bf16[256,4,512]{0,2,1:T(8,128)(2,1)S(1)} copy(bf16[256,4,512]{2,0,1:T(8,128)(2,1)} %select_bitcast_fusion) | data formatting | bytes 2097152 | tf_op jit(solution)/shard_map/jit(_take)/select_n | solution.py:64
  34.5 1.8 %reduce-window.19 = f32[6,2,128]{2,1,0:T(2,128)S(1)} reduce-window(f32[6,2,128]{2,1,0:T(2,128)S(1)} %reshape.303, f32[]{:T(128)} %constant.94.clone.1), window={size=1x1x128 pad=0_0x0_0x127_0}, to_apply=%region_3.4 | reduce-window | flops 195072 | bytes 12292 | tf_op jit(solution)/shard_map/reduce-window.1
  37.6 0.7 convolution_convert_fusion.2
  38.4 2.8 %pad_maximum_fusion = bf16[4,512,512]{2,1,0:T(8,128)(2,1)} fusion(bf16[2,512,512]{2,1,0:T(8,128)(2,1)} %collective-permute-done.3, bf16[1,512,512]{2,1,0:T(8,128)(2,1)S(1)} %copy-done.4, bf16[1,512,512]{2,1,0:T(8,128)(2,1)S(1)} %bitcast.101), kind=kLoop, calls=%fused_computation.5 | loop fusion | flops 2097152 | bytes 4194304 | tf_op jit(solution)/shard_map/concatenate | solution.py:57
  41.2 3.6 %gather_fusion.3 = bf16[4,512,512]{2,1,0:T(8,128)(2,1)} fusion(bf16[4,512,512]{2,1,0:T(8,128)(2,1)} %pad_maximum_fusion, s32[1024]{0:T(1024)S(1)} %pad_clamp_fusion.1), kind=kCustom, calls=%fused_computation.3 | custom fusion | bytes 4194320 | tf_op jit(solution)/shard_map/jit(_take)/gather | solution.py:64
  44.8 2.7 %fusion.11 = bf16[256,512]{1,0:T(8,128)(2,1)S(1)} fusion(bf16[4,512,512]{2,1,0:T(8,128)(2,1)} %gather_fusion.3, pred[4]{0:T(512)(128)(4,1)S(1)} %compare_and_fusion.1, bf16[4,256,512]{2,1,0:T(8,128)(2,1)} %copy-done.1), kind=kOutput, calls=%fused_computation.15 | convolution fusion | flops 538574848 | bytes 3407876 | tf_op jit(solution)/shard_map/dot_general | solution.py:149
  47.5 3.5 %collective-permute-start.4 = (bf16[3,896]{1,0:T(4,128)(2,1)S(1)}, bf16[3,896]{1,0:T(4,128)(2,1)S(1)}, u32[]{:S(2)}, u32[]{:S(2)}) collective-permute-start(bf16[3,896]{1,0:T(4,128)(2,1)S(1)} %pad_maximum_fusion.7), channel_id=1, source_target_pairs={{0,4},{4,8},{8,12},{12,16},{16,20},{20,24},{24,28},{1,5},{5,9},{9,... | collective-permute-start | bytes 16136 | tf_op jit(solution)/shard_map/ppermute | solution.py:12
  51.1 1.1 %fusion.75 = (bf16[6]{0:T(256)(128)(2,1)}, bf16[6]{0:T(256)(128)(2,1)}) fusion(f32[6]{0:T(128)S(1)} %slice_reduce_fusion, pred[]{:T(512)} %bitcast.21), kind=kLoop, calls=%fused_computation.143 | loop fusion | flops 30 | bytes 49 | tf_op jit(solution)/shard_map/convert_element_type | solution.py:25
  52.6 0.7 divide_multiply_fusion
  53.3 0.8 slice.154
  54.0 1.9 %copy.53 = f32[256,384]{0,1:T(8,128)} copy(f32[256,384]{1,0:T(8,128)} %slice.154) | data formatting | bytes 786432 | tf_op jit(solution)/shard_map/slice | solution.py:171
  55.9 1.5 %convolution_convert_fusion.1 = bf16[6,64,256]{2,1,0:T(8,128)(2,1)S(1)} fusion(f32[256,6,64]{0,2,1:T(8,128)} %bitcast.102, f32[256,896]{1,0:T(8,128)S(1)} %divide_multiply_fusion, f32[256,6]{0,1:T(8,128)S(1)} %get-tuple-element.23, f32[256,6]{0,1:T(8,128)} %compare_select_fusion.1), kind=kOutput, calls=%fused_computation.22 | convolution fusion | flops 302284800 | bytes 866304 | tf_op jit(solution)/shard_map/shp,sn->hpn/dot_general | solution.py:110
  57.4 0.7 broadcast_in_dim.133
  58.1 0.7 broadcast_in_dim.132
  58.9 0.7 pad_maximum_fusion.4
  59.6 5.8 %collective-permute-start.6 = (bf16[6,66,256]{2,1,0:T(8,128)(2,1)}, bf16[6,66,256]{2,1,0:T(8,128)(2,1)}, u32[]{:S(2)}, u32[]{:S(2)}) collective-permute-start(bf16[6,66,256]{2,1,0:T(8,128)(2,1)} %pad_maximum_fusion.4), channel_id=1, source_target_pairs={{0,8},{4,12},{8,16},{12,20},{16,24},{20,28},{1,9},{5,13},{9,17},{1... | collective-permute-start | bytes 608264 | tf_op jit(solution)/shard_map/ppermute | solution.py:12
  65.3 3.1 %collective-permute-start.5 = (bf16[6,66,256]{2,1,0:T(8,128)(2,1)}, bf16[6,66,256]{2,1,0:T(8,128)(2,1)}, u32[]{:S(2)}, u32[]{:S(2)}) collective-permute-start(bf16[6,66,256]{2,1,0:T(8,128)(2,1)} %pad_maximum_fusion.4), channel_id=1, source_target_pairs={{0,4},{4,8},{8,12},{12,16},{16,20},{20,24},{24,28},{1,5},{5,9},{9,... | collective-permute-start | bytes 608264 | tf_op jit(solution)/shard_map/ppermute | solution.py:12
  68.5 0.8 slice.107
  69.2 1.0 convert_element_type.125
  70.2 1.3 %collective-permute-done.5 = bf16[6,66,256]{2,1,0:T(8,128)(2,1)} collective-permute-done((bf16[6,66,256]{2,1,0:T(8,128)(2,1)}, bf16[6,66,256]{2,1,0:T(8,128)(2,1)}, u32[]{:S(2)}, u32[]{:S(2)}) %collective-permute-start.5) | collective-permute-done | bytes 202784 | tf_op jit(solution)/shard_map/ppermute | solution.py:12
  71.6 1.0 convert_element_type.123
  72.7 6.3 %collective-permute-start.7 = (bf16[6,66,256]{2,1,0:T(8,128)(2,1)S(1)}, bf16[6,66,256]{2,1,0:T(8,128)(2,1)S(1)}, u32[]{:S(2)}, u32[]{:S(2)}) collective-permute-start(bf16[6,66,256]{2,1,0:T(8,128)(2,1)S(1)} %pad_maximum_fusion.5), channel_id=1, source_target_pairs={{0,8},{4,12},{8,16},{12,20},{16,24},{20,28},{1,9},{5,13},{9,17},{1... | collective-permute-start | bytes 608264 | tf_op jit(solution)/shard_map/ppermute | solution.py:12
  79.1 3.3 %collective-permute-done.7 = bf16[6,66,256]{2,1,0:T(8,128)(2,1)S(1)} collective-permute-done((bf16[6,66,256]{2,1,0:T(8,128)(2,1)S(1)}, bf16[6,66,256]{2,1,0:T(8,128)(2,1)S(1)}, u32[]{:S(2)}, u32[]{:S(2)}) %collective-permute-start.7) | collective-permute-done | bytes 202784 | tf_op jit(solution)/shard_map/ppermute | solution.py:12
  82.6 5.4 %collective-permute-start.8 = (bf16[6,66,256]{2,1,0:T(8,128)(2,1)S(1)}, bf16[6,66,256]{2,1,0:T(8,128)(2,1)S(1)}, u32[]{:S(2)}, u32[]{:S(2)}) collective-permute-start(bf16[6,66,256]{2,1,0:T(8,128)(2,1)S(1)} %pad_maximum_fusion.6), channel_id=1, source_target_pairs={{0,16},{4,20},{8,24},{12,28},{1,17},{5,21},{9,25},{13,29},{2,18},{... | collective-permute-start | bytes 608264 | tf_op jit(solution)/shard_map/ppermute | solution.py:12
  88.5 3.0 %collective-permute-done.8 = bf16[6,66,256]{2,1,0:T(8,128)(2,1)S(1)} collective-permute-done((bf16[6,66,256]{2,1,0:T(8,128)(2,1)S(1)}, bf16[6,66,256]{2,1,0:T(8,128)(2,1)S(1)}, u32[]{:S(2)}, u32[]{:S(2)}) %collective-permute-start.8) | collective-permute-done | bytes 202784 | tf_op jit(solution)/shard_map/ppermute | solution.py:12
  92.1 1.9 %fusion.20 = f32[256,6,64]{0,2,1:T(8,128)S(1)} fusion(f32[256,6,64]{0,2,1:T(8,128)S(1)} %convolution_multiply_fusion, f32[6,256]{1,0:T(8,128)S(1)} %bitcast.114, f32[256,256]{1,0:T(8,128)S(1)} %fusion.47, pred[256,256]{1,0:T(8,128)(4,1)S(1)} %fusion.45, f32[256,6,64]{0,2,1:T(8,128)S(1)} %bitcast.103, f32[6]{0:T(128)S(1)} %copy-done.21, ...), kind=kOutput, calls=%fused_computation.18 | convolution fusion | flops 303562752 | bytes 1519640 | tf_op jit(solution)/shard_map/hts,shp->thp/dot_general | solution.py:104
  94.1 2.2 %multiply_convert_fusion = bf16[256,384]{1,0:T(8,128)(2,1)S(1)} fusion(f32[256,384]{1,0:T(8,128)S(1)} %copy.56, bf16[256,2048]{0,1:T(8,128)(2,1)S(1)} %bitcast.98, bf16[2048,384]{1,0:T(8,128)(2,1)} %param.18), kind=kOutput, calls=%fused_computation.51 | convolution fusion | flops 403439616 | bytes 3211264 | tf_op jit(solution)/shard_map/dot_general | solution.py:149
  96.3 0.7 gather_fusion.4
  97.2 16.0 %all_to_all.10 = bf16[8,32,384]{2,1,0:T(8,128)(2,1)S(1)} all-to-all(bf16[8,32,384]{2,1,0:T(8,128)(2,1)S(1)} %broadcast_select_fusion), channel_id=1, replica_groups=mesh['seq'=8,'fsdp'=4] {'seq'}, dimensions={0} | all-to-all | bytes 393216 | tf_op jit(solution)/shard_map/all_to_all | solution.py:188
  113.2 0.7 copy.77
  (101 shorter events, 7.5 us)
Async XLA Ops:
  0.0 37.6 %copy-start = (bf16[2048,384]{1,0:T(8,128)(2,1)S(1)}, bf16[2048,384]{1,0:T(8,128)(2,1)}, u32[]{:S(2)}) copy-start(bf16[2048,384]{1,0:T(8,128)(2,1)} %param.17) | copy-start | bytes 4718596
  0.0 26.0 %collective-permute-start.2 = (bf16[1,512,512]{2,1,0:T(8,128)(2,1)}, bf16[1,512,512]{2,1,0:T(8,128)(2,1)S(1)}, u32[]{:S(2)}, u32[]{:S(2)}) collective-permute-start(bf16[1,512,512]{2,1,0:T(8,128)(2,1)} %bitcast.99), channel_id=1, source_target_pairs={{0,2},{1,3},{2,0},{3,1},{4,6},{5,7},{6,4},{7,5},{8,10},{9,11},{10,... | collective-permute-start | bytes 1572872 | tf_op jit(solution)/shard_map/ppermute | solution.py:56
  2.9 23.1 %copy-start.20 = (f32[6]{0:T(128)S(1)}, f32[6]{0:T(128)}, u32[]{:S(2)}) copy-start(f32[6]{0:T(128)} %param.24) | copy-start | bytes 76
  2.9 23.1 %copy-start.2 = (bf16[512,512]{1,0:T(8,128)(2,1)S(1)}, bf16[512,512]{1,0:T(8,128)(2,1)}, u32[]{:S(2)}) copy-start(bf16[512,512]{1,0:T(8,128)(2,1)} %param.19) | copy-start | bytes 1572868
  2.9 14.6 %all-to-all-start = ((bf16[8,32,512]{2,1,0:T(8,128)(2,1)}), bf16[8,32,512]{2,1,0:T(8,128)(2,1)S(1)}, u32[]{:S(2)}, u32[]{:S(2)}) async-start(bf16[8,32,512]{2,1,0:T(8,128)(2,1)} %bitcast.107), calls=%async_computation | async-start | bytes 524288 | tf_op jit(solution)/shard_map/all_to_all | solution.py:136
  14.8 12.4 %copy-start.8 = (s32[259]{0:T(512)}, s32[259]{0:T(512)S(1)}, u32[]{:S(2)}) copy-start(s32[259]{0:T(512)S(1)} %convert_reduce_fusion) | copy-start | bytes 3112
  18.2 6.4 %collective-permute-start = (bf16[1,256,512]{2,1,0:T(8,128)(2,1)S(1)}, bf16[1,256,512]{2,1,0:T(8,128)(2,1)S(1)}, u32[]{:S(2)}, u32[]{:S(2)}) collective-permute-start(bf16[1,256,512]{2,1,0:T(8,128)(2,1)S(1)} %bitcast_select_fusion), channel_id=1, source_target_pairs={{0,2},{1,3},{2,0},{3,1},{4,6},{5,7},{6,4},{7,5},{8,10},{9,11},{10,... | collective-permute-start | bytes 786440 | tf_op jit(solution)/shard_map/ppermute | solution.py:56
  24.7 3.0 %collective-permute-start.1 = (bf16[2,256,512]{2,1,0:T(8,128)(2,1)S(1)}, bf16[2,256,512]{2,1,0:T(8,128)(2,1)S(1)}, u32[]{:S(2)}, u32[]{:S(2)}) collective-permute-start(bf16[2,256,512]{2,1,0:T(8,128)(2,1)S(1)} %pad_maximum_fusion.3), channel_id=1, source_target_pairs={{0,1},{1,0},{2,3},{3,2},{4,5},{5,4},{6,7},{7,6},{8,9},{9,8},{10,11... | collective-permute-start | bytes 1572872 | tf_op jit(solution)/shard_map/ppermute | solution.py:56
  26.1 1.7 %copy-start.3 = (bf16[1,512,512]{2,1,0:T(8,128)(2,1)}, bf16[1,512,512]{2,1,0:T(8,128)(2,1)S(1)}, u32[]{:S(2)}) copy-start(bf16[1,512,512]{2,1,0:T(8,128)(2,1)S(1)} %collective-permute-done.2) | copy-start | bytes 1572868
  27.2 11.2 %collective-permute-start.3 = (bf16[2,512,512]{2,1,0:T(8,128)(2,1)}, bf16[2,512,512]{2,1,0:T(8,128)(2,1)}, u32[]{:S(2)}, u32[]{:S(2)}) collective-permute-start(bf16[2,512,512]{2,1,0:T(8,128)(2,1)} %pad_maximum_fusion.2), channel_id=1, source_target_pairs={{0,1},{1,0},{2,3},{3,2},{4,5},{5,4},{6,7},{7,6},{8,9},{9,8},{10,11... | collective-permute-start | bytes 3145736 | tf_op jit(solution)/shard_map/ppermute | solution.py:56
  30.6 1.0 copy-start.1
  32.7 1.5 %copy-start.7 = (bf16[2048,6]{0,1:T(8,128)(2,1)S(1)}, bf16[2048,6]{0,1:T(8,128)(2,1)}, u32[]{:S(2)}) copy-start(bf16[2048,6]{0,1:T(8,128)(2,1)} %param.20) | copy-start | bytes 73732
  32.7 1.5 %copy-start.19 = (f32[6]{0:T(128)S(1)}, f32[6]{0:T(128)}, u32[]{:S(2)}) copy-start(f32[6]{0:T(128)} %param.23) | copy-start | bytes 76
  36.7 1.7 %copy-start.4 = (bf16[1,512,512]{2,1,0:T(8,128)(2,1)S(1)}, bf16[1,512,512]{2,1,0:T(8,128)(2,1)}, u32[]{:S(2)}) copy-start(bf16[1,512,512]{2,1,0:T(8,128)(2,1)} %copy-done.3) | copy-start | bytes 1572868
  36.7 0.8 copy-start.9
  47.5 5.0 %copy-start.11 = (f32[896]{0:T(1024)S(1)}, f32[896]{0:T(1024)}, u32[]{:S(2)}) copy-start(f32[896]{0:T(1024)} %get-tuple-element.7) | copy-start | bytes 10756
  47.5 5.0 %copy-start.12 = (f32[896]{0:T(1024)S(1)}, f32[896]{0:T(1024)}, u32[]{:S(2)}) copy-start(f32[896]{0:T(1024)} %get-tuple-element.8) | copy-start | bytes 10756
  47.5 5.0 %copy-start.13 = (f32[896]{0:T(1024)S(1)}, f32[896]{0:T(1024)}, u32[]{:S(2)}) copy-start(f32[896]{0:T(1024)} %get-tuple-element.9) | copy-start | bytes 10756
  47.5 5.0 %copy-start.14 = (f32[896]{0:T(1024)S(1)}, f32[896]{0:T(1024)}, u32[]{:S(2)}) copy-start(f32[896]{0:T(1024)} %get-tuple-element.10) | copy-start | bytes 10756
  47.5 5.0 %copy-start.15 = (f32[256]{0:T(256)S(1)}, f32[256]{0:T(256)}, u32[]{:S(2)}) copy-start(f32[256]{0:T(256)} %get-tuple-element.26) | copy-start | bytes 3076
  47.5 5.0 %copy-start.16 = (f32[256]{0:T(256)S(1)}, f32[256]{0:T(256)}, u32[]{:S(2)}) copy-start(f32[256]{0:T(256)} %get-tuple-element.27) | copy-start | bytes 3076
  47.5 5.0 %copy-start.17 = (f32[256]{0:T(256)S(1)}, f32[256]{0:T(256)}, u32[]{:S(2)}) copy-start(f32[256]{0:T(256)} %get-tuple-element.28) | copy-start | bytes 3076
  47.5 4.9 %collective-permute-start.4 = (bf16[3,896]{1,0:T(4,128)(2,1)S(1)}, bf16[3,896]{1,0:T(4,128)(2,1)S(1)}, u32[]{:S(2)}, u32[]{:S(2)}) collective-permute-start(bf16[3,896]{1,0:T(4,128)(2,1)S(1)} %pad_maximum_fusion.7), channel_id=1, source_target_pairs={{0,4},{4,8},{8,12},{12,16},{16,20},{20,24},{24,28},{1,5},{5,9},{9,... | collective-permute-start | bytes 16136 | tf_op jit(solution)/shard_map/ppermute | solution.py:12
  59.6 9.7 %collective-permute-start.6 = (bf16[6,66,256]{2,1,0:T(8,128)(2,1)}, bf16[6,66,256]{2,1,0:T(8,128)(2,1)}, u32[]{:S(2)}, u32[]{:S(2)}) collective-permute-start(bf16[6,66,256]{2,1,0:T(8,128)(2,1)} %pad_maximum_fusion.4), channel_id=1, source_target_pairs={{0,8},{4,12},{8,16},{12,20},{16,24},{20,28},{1,9},{5,13},{9,17},{1... | collective-permute-start | bytes 608264 | tf_op jit(solution)/shard_map/ppermute | solution.py:12
  65.3 6.2 %collective-permute-start.5 = (bf16[6,66,256]{2,1,0:T(8,128)(2,1)}, bf16[6,66,256]{2,1,0:T(8,128)(2,1)}, u32[]{:S(2)}, u32[]{:S(2)}) collective-permute-start(bf16[6,66,256]{2,1,0:T(8,128)(2,1)} %pad_maximum_fusion.4), channel_id=1, source_target_pairs={{0,4},{4,8},{8,12},{12,16},{16,20},{20,24},{24,28},{1,5},{5,9},{9,... | collective-permute-start | bytes 608264 | tf_op jit(solution)/shard_map/ppermute | solution.py:12
  72.7 9.7 %collective-permute-start.7 = (bf16[6,66,256]{2,1,0:T(8,128)(2,1)S(1)}, bf16[6,66,256]{2,1,0:T(8,128)(2,1)S(1)}, u32[]{:S(2)}, u32[]{:S(2)}) collective-permute-start(bf16[6,66,256]{2,1,0:T(8,128)(2,1)S(1)} %pad_maximum_fusion.5), channel_id=1, source_target_pairs={{0,8},{4,12},{8,16},{12,20},{16,24},{20,28},{1,9},{5,13},{9,17},{1... | collective-permute-start | bytes 608264 | tf_op jit(solution)/shard_map/ppermute | solution.py:12
  82.5 9.5 %copy-start.5 = (f32[256,384]{0,1:T(8,128)S(1)}, f32[256,384]{0,1:T(8,128)}, u32[]{:S(2)}) copy-start(f32[256,384]{0,1:T(8,128)} %copy.53) | copy-start | bytes 1179652
  82.5 9.5 %copy-start.6 = (f32[256,6]{0,1:T(8,128)S(1)}, f32[256,6]{0,1:T(8,128)}, u32[]{:S(2)}) copy-start(f32[256,6]{0,1:T(8,128)} %compare_select_fusion.1) | copy-start | bytes 18436
  82.5 9.5 %copy-start.10 = (f32[1,6,2,128]{3,1,2,0:T(8,128)S(1)}, f32[1,6,2,128]{3,1,2,0:T(8,128)}, u32[]{:S(2)}) copy-start(f32[1,6,2,128]{3,1,2,0:T(8,128)} %copy-done.9) | copy-start | bytes 18436
  82.5 9.5 %copy-start.21 = (f32[6]{0:T(128)S(1)}, f32[6]{0:T(128)}, u32[]{:S(2)}) copy-start(f32[6]{0:T(128)} %param.25) | copy-start | bytes 76
  82.6 8.9 %collective-permute-start.8 = (bf16[6,66,256]{2,1,0:T(8,128)(2,1)S(1)}, bf16[6,66,256]{2,1,0:T(8,128)(2,1)S(1)}, u32[]{:S(2)}, u32[]{:S(2)}) collective-permute-start(bf16[6,66,256]{2,1,0:T(8,128)(2,1)S(1)} %pad_maximum_fusion.6), channel_id=1, source_target_pairs={{0,16},{4,20},{8,24},{12,28},{1,17},{5,21},{9,25},{13,29},{2,18},{... | collective-permute-start | bytes 608264 | tf_op jit(solution)/shard_map/ppermute | solution.py:12
  94.1 2.9 %copy-start.18 = (pred[8]{0:T(512)(128)(4,1)S(1)}, pred[8]{0:T(512)(128)(4,1)}, u32[]{:S(2)}) copy-start(pred[8]{0:T(512)(128)(4,1)} %get-tuple-element.11) | copy-start | bytes 28

commit v6 on v4

--- a/solution.py
+++ b/solution.py
@@ -45,24 +45,35 @@
     return held
 
 
-def gather_columns(block, axis):
+def exchange(block, axis, dim):
     count = lax.axis_size(axis)
     if count & (count - 1):
-        return lax.all_gather(block, axis, axis=1, tiled=True)
-    place = lax.axis_index(axis)
-    held, codes = block[None], [0]
+        return lax.all_gather(block, axis, axis=dim, tiled=True), None
+    held, codes = block, [0]
     bit = count // 2
     while bit >= 1:
         other = lax.ppermute(held, axis, [(i, i ^ bit) for i in range(count)])
-        held = jnp.concatenate([held, other], axis=0)
+        held = jnp.concatenate([held, other], axis=dim)
         codes = codes + [c ^ bit for c in codes]
         bit //= 2
+    return held, codes
+
+
+def to_natural(held, codes, axis, dim):
+    if codes is None:
+        return held
+    count = len(codes)
+    width = held.shape[dim] // count
     where_code = [0] * count
     for position, code in enumerate(codes):
         where_code[code] = position
-    order = jnp.asarray(where_code, jnp.int32)[jnp.bitwise_xor(jnp.arange(count, dtype=jnp.int32), place)]
-    ordered = jnp.take(held, order, axis=0)
-    return ordered.transpose(1, 0, 2).reshape(block.shape[0], count * block.shape[1])
+    table = jnp.asarray(where_code, jnp.int32)
+    place = lax.axis_index(axis)
+    parts = [
+        lax.dynamic_slice_in_dim(held, table[jnp.bitwise_xor(index, place)] * width, width, axis=dim)
+        for index in range(count)
+    ]
+    return jnp.concatenate(parts, axis=dim)
 
 
 def segment_of(positions, lengths):
@@ -137,15 +148,16 @@
     heads_dev = step_weight.shape[1]
     head_dim = inner_dev // heads_dev
     state_dim = shared_weight.shape[1] // 2
-    w_full = lax.all_gather(shared_weight, "fsdp", axis=0, tiled=True)
-    weight_list = (x_weight, z_weight, step_weight, w_full)
-    feature_part = gather_columns(stream_block, "fsdp")
-    x_acc, z_acc, step_acc, bc_acc = tuple(
+    w_held, _ = exchange(shared_weight, "fsdp", 0)
+    feature_held, codes = exchange(stream_block, "fsdp", 1)
+    feature_part = to_natural(feature_held, codes, "fsdp", 1)
+    x_acc, z_acc, step_acc = tuple(
         (
             jnp.dot(feature_part, weight, preferred_element_type=jnp.float32)
-            for weight in weight_list
-        )
-    )
+            for weight in (x_weight, z_weight, step_weight)
+        )
+    )
+    bc_acc = jnp.dot(feature_held, w_held, preferred_element_type=jnp.float32)
     x_raw = x_acc.astype(jnp.bfloat16)
     z_raw = z_acc.astype(jnp.bfloat16)
     bc_raw = bc_acc.astype(jnp.bfloat16)

time: 127 us -> 103 us (0.81)
  between operations: 14.6 us -> 3.71 us
  local copies, waits for them, and re-layouts: 15 us -> 8.32 us
  other arithmetic: 16 us -> 13.2 us
  waiting for transfers between devices: 20.4 us -> 17.9 us
  blocking collectives: 18.3 us -> 16.4 us
    ppermute x2 -> x4, waiting for transfers between devices: 11.8 us -> 3.84 us  [exchange(): other = lax.ppermute(held, axis, [(i, i ^ bit) for i in range(count)])]
    all_to_all x1, waiting for transfers between devices: 0.01 us -> 4.61 us  [per_device(): lax.all_to_all(slot_rows, 'seq', split_axis=0, concat_axis=0, tiled=True)]
    ppermute x2 -> x4, starting transfers between devices: 1.63 us -> 4.29 us  [exchange(): other = lax.ppermute(held, axis, [(i, i ^ bit) for i in range(count)])]
    slice x2, local copies, waits for them, and re-layouts: 2.69 us -> 0.19 us  [per_device(): x_heads = activated[:, :inner_dev].reshape(tok_dev, heads_dev, head_dim)]
    gather x2 -> x0, local copies, waits for them, and re-layouts: 2.5 us -> none  [the longest x1 1.86 us: gather_columns(): ordered = jnp.take(held, order, axis=0)]
    dot_general x0 -> x1, matrix products: none -> 2.22 us  [per_device(): bc_acc = jnp.dot(feature_held, w_held, preferred_element_type=jnp.float32)]
    concatenate x2 -> x3, other arithmetic: 1.14 us -> 3.28 us  [exchange(): held = jnp.concatenate([held, other], axis=dim)]
    convert_element_type x3, other arithmetic: 1.96 us -> 0.09 us  [received(): got = shifted(wire, axis, by).astype(jnp.float32)]
  transfers between devices with their start and end apart: 9 -> 10, of which waited for: 6 -> 7; matrix products, arithmetic and copies ran while one was open for 19% -> 19% of each run, Pallas kernels for 0% -> 0%
where the time goes in v6:
time: 103 us; the launch traced here: 102 us
  starting transfers between devices  32 us (31%)
  waiting for transfers between devices  17.9 us (17%)
  blocking collectives  16.4 us (16%)
  other arithmetic  13.2 us (13%)
  matrix products  10.8 us (10%)
  local copies, waits for them, and re-layouts  8.32 us (8%)
  between operations  3.71 us (4%)
    ppermute x5, starting transfers between devices, shifted(): return lax.ppermute(array, axis, pairs)  21.8 us
    all_to_all x1, blocking collectives, per_device(): lax.all_to_all(outgoing, 'seq', split_axis=0, concat_axis=0, tiled=True)  16.4 us
    ppermute x5, waiting for transfers between devices, shifted(): return lax.ppermute(array, axis, pairs)  9.44 us
    all_to_all x1, starting transfers between devices, per_device(): lax.all_to_all(slot_rows, 'seq', split_axis=0, concat_axis=0, tiled=True)  5.83 us
    all_to_all x1, waiting for transfers between devices, per_device(): lax.all_to_all(slot_rows, 'seq', split_axis=0, concat_axis=0, tiled=True)  4.61 us
    dot_general x3, matrix products, per_device(): jnp.dot(feature_part, weight, preferred_element_type=jnp.float32)  4.61 us
    ppermute x4, starting transfers between devices, exchange(): other = lax.ppermute(held, axis, [(i, i ^ bit) for i in range(count)])  4.29 us
    ppermute x4, waiting for transfers between devices, exchange(): other = lax.ppermute(held, axis, [(i, i ^ bit) for i in range(count)])  3.84 us
  transfers between devices with their start and end apart: 10, of which 7 were waited for; matrix products, arithmetic and copies ran while one was open for 19% of the time, Pallas kernels for 0%

profile of v6, /device:TPU:0, one launch (start us, length us, event | category | flops | bytes accessed | tf_op | source)
XLA Modules:
  0.0 102.3 jit_solution(9854872894236134481)
XLA Ops:
  0.0 3.0 %collective-permute-start.2 = (bf16[512,512]{1,0:T(8,128)(2,1)}, bf16[512,512]{1,0:T(8,128)(2,1)}, u32[]{:S(2)}, u32[]{:S(2)}) collective-permute-start(bf16[512,512]{1,0:T(8,128)(2,1)} %param.18), channel_id=1, source_target_pairs={{0,2},{1,3},{2,0},{3,1},{4,6},{5,7},{6,4},{7,5},{8,10},{9,11},{10,... | collective-permute-start | bytes 1572872 | tf_op jit(solution)/shard_map/ppermute | solution.py:55
  3.0 5.8 %all-to-all-start = ((bf16[8,32,512]{2,1,0:T(8,128)(2,1)}), bf16[8,32,512]{2,1,0:T(8,128)(2,1)S(1)}, u32[]{:S(2)}, u32[]{:S(2)}) async-start(bf16[8,32,512]{2,1,0:T(8,128)(2,1)} %bitcast.85), calls=%async_computation | async-start | bytes 524288 | tf_op jit(solution)/shard_map/all_to_all | solution.py:143
  8.9 1.3 %compare_and_fusion.1 = (pred[8]{0:T(512)(128)(4,1)}, s32[8]{0:T(128)S(1)}) fusion(s32[8,8]{1,0:T(8,128)} %param.14, s32[]{:T(128)S(6)} %select_n.98), kind=kLoop, calls=%fused_computation.120 | loop fusion | flops 48 | bytes 76 | tf_op jit(solution)/shard_map/jit(_take)/and | solution.py:195
  10.1 1.0 sort.17
  11.3 0.8 reduce-window.18
  12.1 0.7 constant_dynamic-update-slice_fusion.1
  12.9 4.6 %all-to-all-done = bf16[8,32,512]{2,1,0:T(8,128)(2,1)S(1)} async-done(((bf16[8,32,512]{2,1,0:T(8,128)(2,1)}), bf16[8,32,512]{2,1,0:T(8,128)(2,1)S(1)}, u32[]{:S(2)}, u32[]{:S(2)}) %all-to-all-start) | async-done | bytes 262176 | tf_op jit(solution)/shard_map/all_to_all | solution.py:143
  17.5 0.6 gather_fusion
  18.2 0.7 collective-permute-start
  18.9 0.6 fusion.80
  20.1 0.7 broadcast_compare_fusion
  20.8 3.8 %collective-permute-done = bf16[256,512]{1,0:T(8,128)(2,1)S(1)} collective-permute-done((bf16[256,512]{1,0:T(8,128)(2,1)S(1)}, bf16[256,512]{1,0:T(8,128)(2,1)S(1)}, u32[]{:S(2)}, u32[]{:S(2)}) %collective-permute-start) | collective-permute-done | bytes 262176 | tf_op jit(solution)/shard_map/ppermute | solution.py:55
  24.6 0.9 pad_maximum_fusion.3
  25.5 0.7 fusion.81
  28.8 0.6 slice.107
  29.4 0.6 slice.124
  30.1 1.3 %pad_maximum_fusion.2 = bf16[1024,512]{1,0:T(8,128)(2,1)S(1)} fusion(bf16[512,512]{1,0:T(8,128)(2,1)} %collective-permute-done.2, bf16[512,512]{1,0:T(8,128)(2,1)} %param.18), kind=kLoop, calls=%fused_computation.25 | loop fusion | flops 2097152 | bytes 2097152 | tf_op jit(solution)/shard_map/concatenate | solution.py:56
  31.3 0.5 collective-permute-start.3
  31.9 1.1 %pad_maximum_fusion = bf16[256,2048]{1,0:T(8,128)(2,1)S(1)} fusion(bf16[256,1024]{1,0:T(8,128)(2,1)} %collective-permute-done.1, bf16[256,512]{1,0:T(8,128)(2,1)S(1)} %collective-permute-done, bf16[256,512]{1,0:T(8,128)(2,1)S(1)} %bitcast_select_fusion), kind=kLoop, calls=%fused_computation.23 | loop fusion | flops 3145728 | bytes 2097152 | tf_op jit(solution)/shard_map/concatenate | solution.py:56
  33.2 0.7 copy-done.2
  33.9 0.4 fusion.57
  34.3 1.8 %reduce-window.19 = f32[6,2,128]{2,1,0:T(2,128)S(1)} reduce-window(f32[6,2,128]{2,1,0:T(2,128)S(1)} %reshape.225, f32[]{:T(128)} %constant.79.clone.1), window={size=1x1x128 pad=0_0x0_0x127_0}, to_apply=%region_3.4 | reduce-window | flops 195072 | bytes 12292 | tf_op jit(solution)/shard_map/reduce-window.1
  36.6 0.2 slice_reduce_fusion
  36.8 0.6 compare_select_fusion.1
  37.5 1.9 %convolution_convert_fusion.2 = bf16[256,384]{1,0:T(8,128)(2,1)S(1)} fusion(bf16[2048,384]{1,0:T(8,128)(2,1)S(1)} %copy-done, bf16[256,512]{1,0:T(8,128)(2,1)} %copy-done.2, bf16[256,512]{1,0:T(8,128)(2,1)} %copy-done.4, bf16[256,512]{1,0:T(8,128)(2,1)} %copy-done.5, bf16[256,512]{1,0:T(8,128)(2,1)S(1)} %get-tuple-element.20), kind=kOutput, calls=%fused_computation.21 | convolution fusion | flops 406945792 | bytes 2818048 | tf_op jit(solution)/shard_map/dot_general | solution.py:156
  39.4 2.2 %fusion.20 = bf16[256,512]{1,0:T(8,128)(2,1)S(1)} fusion(bf16[1024,512]{1,0:T(8,128)(2,1)} %collective-permute-done.3, bf16[512,512]{1,0:T(8,128)(2,1)} %collective-permute-done.2, bf16[512,512]{1,0:T(8,128)(2,1)S(1)} %copy-done.1, bf16[256,1024]{1,0:T(8,128)(2,1)} %collective-permute-done.1, bf16[256,512]{1,0:T(8,128)(2,1)S(1)} %collective-permute-done, ...), kind=kOutput, calls=%fused_computation.16 | convolution fusion | flops 546439168 | bytes 3407872 | tf_op jit(solution)/shard_map/dot_general | solution.py:160
  41.6 3.4 %collective-permute-start.4 = (bf16[3,896]{1,0:T(4,128)(2,1)S(1)}, bf16[3,896]{1,0:T(4,128)(2,1)S(1)}, u32[]{:S(2)}, u32[]{:S(2)}) collective-permute-start(bf16[3,896]{1,0:T(4,128)(2,1)S(1)} %pad_maximum_fusion.7), channel_id=1, source_target_pairs={{0,4},{4,8},{8,12},{12,16},{16,20},{20,24},{24,28},{1,5},{5,9},{9,... | collective-permute-start | bytes 16136 | tf_op jit(solution)/shard_map/ppermute | solution.py:12
  45.0 1.2 %fusion.72 = (bf16[6]{0:T(256)(128)(2,1)}, bf16[6]{0:T(256)(128)(2,1)}) fusion(f32[6]{0:T(128)S(1)} %slice_reduce_fusion, pred[]{:T(512)} %bitcast.18), kind=kLoop, calls=%fused_computation.136 | loop fusion | flops 30 | bytes 49 | tf_op jit(solution)/shard_map/convert_element_type | solution.py:25
  46.4 0.7 divide_multiply_fusion
  47.3 1.2 %convolution_convert_fusion.1 = bf16[6,64,256]{2,1,0:T(8,128)(2,1)S(1)} fusion(f32[256,6,64]{0,2,1:T(8,128)S(1)} %bitcast.81, f32[256,896]{1,0:T(8,128)S(1)} %divide_multiply_fusion, f32[256,6]{0,1:T(8,128)S(1)} %get-tuple-element.27, f32[256,6]{0,1:T(8,128)} %compare_select_fusion.1), kind=kOutput, calls=%fused_computation.20 | convolution fusion | flops 302284800 | bytes 866304 | tf_op jit(solution)/shard_map/shp,sn->hpn/dot_general | solution.py:117
  48.5 0.8 broadcast_in_dim.103
  49.3 0.7 broadcast_in_dim.102
  50.0 4.7 %collective-permute-start.6 = (bf16[6,66,256]{2,1,0:T(8,128)(2,1)S(1)}, bf16[6,66,256]{2,1,0:T(8,128)(2,1)S(1)}, u32[]{:S(2)}, u32[]{:S(2)}) collective-permute-start(bf16[6,66,256]{2,1,0:T(8,128)(2,1)S(1)} %pad_maximum_fusion.4), channel_id=1, source_target_pairs={{0,8},{4,12},{8,16},{12,20},{16,24},{20,28},{1,9},{5,13},{9,17},{1... | collective-permute-start | bytes 608264 | tf_op jit(solution)/shard_map/ppermute | solution.py:12
  54.7 1.4 %collective-permute-start.5 = (bf16[6,66,256]{2,1,0:T(8,128)(2,1)S(1)}, bf16[6,66,256]{2,1,0:T(8,128)(2,1)S(1)}, u32[]{:S(2)}, u32[]{:S(2)}) collective-permute-start(bf16[6,66,256]{2,1,0:T(8,128)(2,1)S(1)} %pad_maximum_fusion.4), channel_id=1, source_target_pairs={{0,4},{4,8},{8,12},{12,16},{16,20},{20,24},{24,28},{1,5},{5,9},{9,... | collective-permute-start | bytes 608264 | tf_op jit(solution)/shard_map/ppermute | solution.py:12
  56.1 0.7 fusion.68
  56.8 1.6 %collective-permute-done.6 = bf16[6,66,256]{2,1,0:T(8,128)(2,1)S(1)} collective-permute-done((bf16[6,66,256]{2,1,0:T(8,128)(2,1)S(1)}, bf16[6,66,256]{2,1,0:T(8,128)(2,1)S(1)}, u32[]{:S(2)}, u32[]{:S(2)}) %collective-permute-start.6) | collective-permute-done | bytes 202784 | tf_op jit(solution)/shard_map/ppermute | solution.py:12
  58.5 1.4 %collective-permute-done.5 = bf16[6,66,256]{2,1,0:T(8,128)(2,1)S(1)} collective-permute-done((bf16[6,66,256]{2,1,0:T(8,128)(2,1)S(1)}, bf16[6,66,256]{2,1,0:T(8,128)(2,1)S(1)}, u32[]{:S(2)}, u32[]{:S(2)}) %collective-permute-start.5) | collective-permute-done | bytes 202784 | tf_op jit(solution)/shard_map/ppermute | solution.py:12
  60.1 6.9 %collective-permute-start.7 = (bf16[6,66,256]{2,1,0:T(8,128)(2,1)S(1)}, bf16[6,66,256]{2,1,0:T(8,128)(2,1)S(1)}, u32[]{:S(2)}, u32[]{:S(2)}) collective-permute-start(bf16[6,66,256]{2,1,0:T(8,128)(2,1)S(1)} %pad_maximum_fusion.5), channel_id=1, source_target_pairs={{0,8},{4,12},{8,16},{12,20},{16,24},{20,28},{1,9},{5,13},{9,17},{1... | collective-permute-start | bytes 608264 | tf_op jit(solution)/shard_map/ppermute | solution.py:12
  67.1 3.3 %collective-permute-done.7 = bf16[6,66,256]{2,1,0:T(8,128)(2,1)S(1)} collective-permute-done((bf16[6,66,256]{2,1,0:T(8,128)(2,1)S(1)}, bf16[6,66,256]{2,1,0:T(8,128)(2,1)S(1)}, u32[]{:S(2)}, u32[]{:S(2)}) %collective-permute-start.7) | collective-permute-done | bytes 202784 | tf_op jit(solution)/shard_map/ppermute | solution.py:12
  70.6 5.4 %collective-permute-start.8 = (bf16[6,66,256]{2,1,0:T(8,128)(2,1)S(1)}, bf16[6,66,256]{2,1,0:T(8,128)(2,1)S(1)}, u32[]{:S(2)}, u32[]{:S(2)}) collective-permute-start(bf16[6,66,256]{2,1,0:T(8,128)(2,1)S(1)} %pad_maximum_fusion.6), channel_id=1, source_target_pairs={{0,16},{4,20},{8,24},{12,28},{1,17},{5,21},{9,25},{13,29},{2,18},{... | collective-permute-start | bytes 608264 | tf_op jit(solution)/shard_map/ppermute | solution.py:12
  76.1 0.4 fusion.46
  76.5 3.0 %collective-permute-done.8 = bf16[6,66,256]{2,1,0:T(8,128)(2,1)S(1)} collective-permute-done((bf16[6,66,256]{2,1,0:T(8,128)(2,1)S(1)}, bf16[6,66,256]{2,1,0:T(8,128)(2,1)S(1)}, u32[]{:S(2)}, u32[]{:S(2)}) %collective-permute-start.8) | collective-permute-done | bytes 202784 | tf_op jit(solution)/shard_map/ppermute | solution.py:12
  79.5 0.5 convolution_multiply_fusion
  80.1 1.9 %fusion.17 = f32[256,6,64]{0,2,1:T(8,128)S(1)} fusion(f32[256,6,64]{0,2,1:T(8,128)S(1)} %convolution_multiply_fusion, f32[6,256]{1,0:T(8,128)S(1)} %bitcast.92, f32[256,256]{1,0:T(8,128)S(1)} %fusion.46, pred[256,256]{1,0:T(8,128)(4,1)S(1)} %fusion.44, f32[256,6,64]{0,2,1:T(8,128)S(1)} %bitcast.82, f32[6]{0:T(128)S(1)} %copy-done.16, f32[256,6]{0,1:T(8,128)S(1)} %copy-done.6), kind=kOutput, calls=%fused_computation.15 | convolution fusion | flops 303562752 | bytes 1519640 | tf_op jit(solution)/shard_map/hts,shp->thp/dot_general | solution.py:111
  82.2 2.3 %multiply_convert_fusion = bf16[256,384]{1,0:T(8,128)(2,1)S(1)} fusion(f32[256,384]{1,0:T(8,128)S(1)} %copy.43, bf16[2048,384]{1,0:T(8,128)(2,1)} %param.17, bf16[256,512]{1,0:T(8,128)(2,1)S(1)} %copy-done.3, bf16[256,512]{1,0:T(8,128)(2,1)} %copy-done.4, bf16[256,512]{1,0:T(8,128)(2,1)} %copy-done.5, bf16[256,512]{1,0:T(8,128)(2,1)S(1)} %get-tuple-element.20), kind=kOutput, calls=%fused_computation.48 | convolution fusion | flops 407633920 | bytes 3211264 | tf_op jit(solution)/shard_map/dot_general | solution.py:156
  84.5 0.6 gather_fusion.1
  85.2 16.4 %all_to_all.10 = bf16[8,32,384]{2,1,0:T(8,128)(2,1)S(1)} all-to-all(bf16[8,32,384]{2,1,0:T(8,128)(2,1)S(1)} %broadcast_select_fusion), channel_id=1, replica_groups=mesh['seq'=8,'fsdp'=4] {'seq'}, dimensions={0} | all-to-all | bytes 393216 | tf_op jit(solution)/shard_map/all_to_all | solution.py:196
  101.6 0.7 copy.64
  (83 shorter events, 2.2 us)
Async XLA Ops:
  0.0 37.5 %copy-start = (bf16[2048,384]{1,0:T(8,128)(2,1)S(1)}, bf16[2048,384]{1,0:T(8,128)(2,1)}, u32[]{:S(2)}) copy-start(bf16[2048,384]{1,0:T(8,128)(2,1)} %param.16) | copy-start | bytes 4718596
  0.0 25.5 %copy-start.10 = (s32[4]{0:T(128)S(1)}, s32[4]{0:T(128)}, u32[]{:S(2)}) copy-start(s32[4]{0:T(128)} %constant.82.clone) | copy-start | bytes 52
  0.0 25.5 %copy-start.11 = (f32[4,512]{1,0:T(4,128)S(1)}, f32[4,512]{1,0:T(4,128)}, u32[]{:S(2)}) copy-start(f32[4,512]{1,0:T(4,128)} %param.21) | copy-start | bytes 24580
  0.0 30.0 %copy-start.14 = (f32[6]{0:T(128)S(1)}, f32[6]{0:T(128)}, u32[]{:S(2)}) copy-start(f32[6]{0:T(128)} %param.23) | copy-start | bytes 76
  0.0 30.0 %collective-permute-start.2 = (bf16[512,512]{1,0:T(8,128)(2,1)}, bf16[512,512]{1,0:T(8,128)(2,1)}, u32[]{:S(2)}, u32[]{:S(2)}) collective-permute-start(bf16[512,512]{1,0:T(8,128)(2,1)} %param.18), channel_id=1, source_target_pairs={{0,2},{1,3},{2,0},{3,1},{4,6},{5,7},{6,4},{7,5},{8,10},{9,11},{10,... | collective-permute-start | bytes 1572872 | tf_op jit(solution)/shard_map/ppermute | solution.py:55
  3.0 14.5 %all-to-all-start = ((bf16[8,32,512]{2,1,0:T(8,128)(2,1)}), bf16[8,32,512]{2,1,0:T(8,128)(2,1)S(1)}, u32[]{:S(2)}, u32[]{:S(2)}) async-start(bf16[8,32,512]{2,1,0:T(8,128)(2,1)} %bitcast.85), calls=%async_computation | async-start | bytes 524288 | tf_op jit(solution)/shard_map/all_to_all | solution.py:143
  18.2 6.4 %collective-permute-start = (bf16[256,512]{1,0:T(8,128)(2,1)S(1)}, bf16[256,512]{1,0:T(8,128)(2,1)S(1)}, u32[]{:S(2)}, u32[]{:S(2)}) collective-permute-start(bf16[256,512]{1,0:T(8,128)(2,1)S(1)} %bitcast_select_fusion), channel_id=1, source_target_pairs={{0,2},{1,3},{2,0},{3,1},{4,6},{5,7},{6,4},{7,5},{8,10},{9,11},{10,... | collective-permute-start | bytes 786440 | tf_op jit(solution)/shard_map/ppermute | solution.py:55
  25.5 6.4 %collective-permute-start.1 = (bf16[256,1024]{1,0:T(8,128)(2,1)}, bf16[256,1024]{1,0:T(8,128)(2,1)}, u32[]{:S(2)}, u32[]{:S(2)}) collective-permute-start(bf16[256,1024]{1,0:T(8,128)(2,1)} %pad_maximum_fusion.3), channel_id=1, source_target_pairs={{0,1},{1,0},{2,3},{3,2},{4,5},{5,4},{6,7},{7,6},{8,9},{9,8},{10,11... | collective-permute-start | bytes 1572872 | tf_op jit(solution)/shard_map/ppermute | solution.py:55
  31.3 8.0 %collective-permute-start.3 = (bf16[1024,512]{1,0:T(8,128)(2,1)S(1)}, bf16[1024,512]{1,0:T(8,128)(2,1)}, u32[]{:S(2)}, u32[]{:S(2)}) collective-permute-start(bf16[1024,512]{1,0:T(8,128)(2,1)S(1)} %pad_maximum_fusion.2), channel_id=1, source_target_pairs={{0,1},{1,0},{2,3},{3,2},{4,5},{5,4},{6,7},{7,6},{8,9},{9,8},{10,11... | collective-permute-start | bytes 3145736 | tf_op jit(solution)/shard_map/ppermute | solution.py:55
  33.0 0.9 copy-start.13
  33.1 0.8 copy-start.15
  33.2 0.7 copy-start.2
  33.2 1.1 %copy-start.4 = (bf16[256,512]{1,0:T(8,128)(2,1)}, bf16[256,512]{1,0:T(8,128)(2,1)S(1)}, u32[]{:S(2)}) copy-start(bf16[256,512]{1,0:T(8,128)(2,1)S(1)} %get-tuple-element.22) | copy-start | bytes 786436
  33.2 1.1 %copy-start.5 = (bf16[256,512]{1,0:T(8,128)(2,1)}, bf16[256,512]{1,0:T(8,128)(2,1)S(1)}, u32[]{:S(2)}) copy-start(bf16[256,512]{1,0:T(8,128)(2,1)S(1)} %get-tuple-element.23) | copy-start | bytes 786436
  36.6 2.8 %copy-start.7 = (f32[1,6,2,128]{3,1,2,0:T(8,128)}, f32[1,6,2,128]{3,1,2,0:T(8,128)S(1)}, u32[]{:S(2)}) copy-start(f32[1,6,2,128]{3,1,2,0:T(8,128)S(1)} %copy.58) | copy-start | bytes 18436
  37.5 1.9 %copy-start.1 = (bf16[512,512]{1,0:T(8,128)(2,1)S(1)}, bf16[512,512]{1,0:T(8,128)(2,1)}, u32[]{:S(2)}) copy-start(bf16[512,512]{1,0:T(8,128)(2,1)} %param.18) | copy-start | bytes 1572868
  41.6 4.7 %collective-permute-start.4 = (bf16[3,896]{1,0:T(4,128)(2,1)S(1)}, bf16[3,896]{1,0:T(4,128)(2,1)S(1)}, u32[]{:S(2)}, u32[]{:S(2)}) collective-permute-start(bf16[3,896]{1,0:T(4,128)(2,1)S(1)} %pad_maximum_fusion.7), channel_id=1, source_target_pairs={{0,4},{4,8},{8,12},{12,16},{16,20},{20,24},{24,28},{1,5},{5,9},{9,... | collective-permute-start | bytes 16136 | tf_op jit(solution)/shard_map/ppermute | solution.py:12
  50.0 8.5 %collective-permute-start.6 = (bf16[6,66,256]{2,1,0:T(8,128)(2,1)S(1)}, bf16[6,66,256]{2,1,0:T(8,128)(2,1)S(1)}, u32[]{:S(2)}, u32[]{:S(2)}) collective-permute-start(bf16[6,66,256]{2,1,0:T(8,128)(2,1)S(1)} %pad_maximum_fusion.4), channel_id=1, source_target_pairs={{0,8},{4,12},{8,16},{12,20},{16,24},{20,28},{1,9},{5,13},{9,17},{1... | collective-permute-start | bytes 608264 | tf_op jit(solution)/shard_map/ppermute | solution.py:12
  54.7 5.2 %collective-permute-start.5 = (bf16[6,66,256]{2,1,0:T(8,128)(2,1)S(1)}, bf16[6,66,256]{2,1,0:T(8,128)(2,1)S(1)}, u32[]{:S(2)}, u32[]{:S(2)}) collective-permute-start(bf16[6,66,256]{2,1,0:T(8,128)(2,1)S(1)} %pad_maximum_fusion.4), channel_id=1, source_target_pairs={{0,4},{4,8},{8,12},{12,16},{16,20},{20,24},{24,28},{1,5},{5,9},{9,... | collective-permute-start | bytes 608264 | tf_op jit(solution)/shard_map/ppermute | solution.py:12
  56.8 10.2 %copy-start.9 = (s32[256]{0:T(256)S(1)}, s32[256]{0:T(256)}, u32[]{:S(2)}) copy-start(s32[256]{0:T(256)} %slice.107) | copy-start | bytes 3076
  60.1 10.4 %collective-permute-start.7 = (bf16[6,66,256]{2,1,0:T(8,128)(2,1)S(1)}, bf16[6,66,256]{2,1,0:T(8,128)(2,1)S(1)}, u32[]{:S(2)}, u32[]{:S(2)}) collective-permute-start(bf16[6,66,256]{2,1,0:T(8,128)(2,1)S(1)} %pad_maximum_fusion.5), channel_id=1, source_target_pairs={{0,8},{4,12},{8,16},{12,20},{16,24},{20,28},{1,9},{5,13},{9,17},{1... | collective-permute-start | bytes 608264 | tf_op jit(solution)/shard_map/ppermute | solution.py:12
  70.6 9.5 %copy-start.6 = (f32[256,6]{0,1:T(8,128)S(1)}, f32[256,6]{0,1:T(8,128)}, u32[]{:S(2)}) copy-start(f32[256,6]{0,1:T(8,128)} %compare_select_fusion.1) | copy-start | bytes 18436
  70.6 9.5 %copy-start.8 = (f32[1,6,2,128]{3,1,2,0:T(8,128)S(1)}, f32[1,6,2,128]{3,1,2,0:T(8,128)}, u32[]{:S(2)}) copy-start(f32[1,6,2,128]{3,1,2,0:T(8,128)} %copy-done.7) | copy-start | bytes 18436
  70.6 9.5 %copy-start.16 = (f32[6]{0:T(128)S(1)}, f32[6]{0:T(128)}, u32[]{:S(2)}) copy-start(f32[6]{0:T(128)} %param.24) | copy-start | bytes 76
  70.6 8.9 %collective-permute-start.8 = (bf16[6,66,256]{2,1,0:T(8,128)(2,1)S(1)}, bf16[6,66,256]{2,1,0:T(8,128)(2,1)S(1)}, u32[]{:S(2)}, u32[]{:S(2)}) collective-permute-start(bf16[6,66,256]{2,1,0:T(8,128)(2,1)S(1)} %pad_maximum_fusion.6), channel_id=1, source_target_pairs={{0,16},{4,20},{8,24},{12,28},{1,17},{5,21},{9,25},{13,29},{2,18},{... | collective-permute-start | bytes 608264 | tf_op jit(solution)/shard_map/ppermute | solution.py:12
  80.1 2.1 %copy-start.3 = (bf16[256,512]{1,0:T(8,128)(2,1)S(1)}, bf16[256,512]{1,0:T(8,128)(2,1)}, u32[]{:S(2)}) copy-start(bf16[256,512]{1,0:T(8,128)(2,1)} %copy-done.2) | copy-start | bytes 786436
  82.2 2.9 %copy-start.12 = (pred[8]{0:T(512)(128)(4,1)S(1)}, pred[8]{0:T(512)(128)(4,1)}, u32[]{:S(2)}) copy-start(pred[8]{0:T(512)(128)(4,1)} %get-tuple-element.11) | copy-start | bytes 28

commit v7 on v6

--- a/solution.py
+++ b/solution.py
@@ -21,7 +21,7 @@
 def received(packed, axis, by):
     place = lax.axis_index(axis)
     rows = packed.shape[1] - 1
-    decay = packed[:, rows:, :]
+    decay = jnp.broadcast_to(packed[:, rows:, :1], (packed.shape[0], 1, packed.shape[2]))
     high = decay.astype(jnp.bfloat16)
     low = (decay - high.astype(jnp.float32)).astype(jnp.bfloat16)
     wire = jnp.concatenate([packed[:, :rows, :].astype(jnp.bfloat16), high, low], axis=1)
@@ -31,18 +31,20 @@
     return jnp.concatenate([got[:, :rows, :], decay_got], axis=1)
 
 
-def exclusive_scan(packed, axis):
+def exclusive_scan(packed, axis, side):
     count = lax.axis_size(axis)
     if count == 1:
-        return received(packed, axis, 1)
+        return received(packed, axis, 1), side
     held = received(packed, axis, 1)
     if count > 2:
         held = combine_packed(received(packed, axis, 2), held)
     cover = 2
     while cover < count - 1:
+        if cover * 2 >= count - 1:
+            held, side = lax.optimization_barrier((held, side))
         held = combine_packed(received(held, axis, cover), held)
         cover *= 2
-    return held
+    return held, side
 
 
 def exchange(block, axis, dim):
@@ -99,8 +101,9 @@
 
 def local_terms(x_heads, b_rows, c_rows, step_size, decay_log, segment_ids, seg_before):
     log_decay = -jnp.exp(decay_log)[None, :] * step_size
-    cum_decay = jnp.cumsum(log_decay, axis=0)
     positions_in = jnp.arange(x_heads.shape[0], dtype=jnp.int32)
+    lower = (positions_in[:, None] >= positions_in[None, :]).astype(jnp.float32)
+    cum_decay = jnp.dot(lower, log_decay, precision=precise)
     same_prompt = (segment_ids[:, None] == segment_ids[None, :]) & (
         positions_in[:, None] >= positions_in[None, :]
     )
@@ -185,12 +188,13 @@
     packed = jnp.concatenate(
         [state_out, jnp.broadcast_to(block_decay[:, None, None], (heads_dev, 1, state_dim))], axis=1
     )
-    state_in = exclusive_scan(packed, "seq")[:, :head_dim, :]
+    local_y = intra + skip_gain[None, :, None] * x_heads
+    gate = jax.nn.silu(z_raw.astype(jnp.float32)).reshape(tok_dev, heads_dev, head_dim)
+    scanned, (local_y, gate, carry_in) = exclusive_scan(packed, "seq", (local_y, gate, carry_in))
+    state_in = scanned[:, :head_dim, :]
     incoming = jnp.einsum("tn,hpn->thp", c_rows, state_in, precision=precise)
-    y_block = intra + carry_in[:, :, None] * incoming + skip_gain[None, :, None] * x_heads
-    gated = (y_block.reshape(tok_dev, inner_dev) * jax.nn.silu(z_raw.astype(jnp.float32))).astype(
-        jnp.bfloat16
-    )
+    y_block = local_y + carry_in[:, :, None] * incoming
+    gated = (y_block * gate).reshape(tok_dev, inner_dev).astype(jnp.bfloat16)
     ordered = gated.reshape(seq_count, piece_rows, inner_dev)
     outgoing = jnp.take(ordered, dealt_row, axis=0)
     returned = lax.all_to_all(outgoing, "seq", split_axis=0, concat_axis=0, tiled=True)

time: 103 us -> 99.2 us (0.963)
  matrix products: 10.8 us -> 7.23 us
  other arithmetic: 13.2 us -> 10.3 us
  starting transfers between devices: 32 us -> 34.5 us
  local copies, waits for them, and re-layouts: 8.32 us -> 10.4 us
  waiting for transfers between devices: 17.9 us -> 16 us
    dot_general x3, matrix products: 4.61 us -> 1.85 us  [per_device(): jnp.dot(feature_part, weight, preferred_element_type=jnp.float32)]
    another operation x3 -> x1, other arithmetic: 2.69 us -> 0.83 us
    all_to_all x1, waiting for transfers between devices: 4.61 us -> 2.75 us  [per_device(): lax.all_to_all(slot_rows, 'seq', split_axis=0, concat_axis=0, tiled=True)]
    slice x2, local copies, waits for them, and re-layouts: 0.19 us -> 1.93 us  [per_device(): x_heads = activated[:, :inner_dev].reshape(tok_dev, heads_dev, head_dim)]
    ppermute x5, waiting for transfers between devices: 9.44 us -> 7.75 us  [shifted(): return lax.ppermute(array, axis, pairs)]
    ppermute x4, waiting for transfers between devices: 3.84 us -> 5.52 us  [exchange(): other = lax.ppermute(held, axis, [(i, i ^ bit) for i in range(count)])]
    ppermute x5, starting transfers between devices: 21.8 us -> 23.5 us  [shifted(): return lax.ppermute(array, axis, pairs)]
    all_to_all x1, starting transfers between devices: 5.83 us -> 7.43 us  [per_device(): lax.all_to_all(slot_rows, 'seq', split_axis=0, concat_axis=0, tiled=True)]
  transfers between devices with their start and end apart: 10 -> 10, of which waited for: 7 -> 7; matrix products, arithmetic and copies ran while one was open for 19% -> 18% of each run, Pallas kernels for 0% -> 0%
where the time goes in v7:
time: 99.2 us; the launch traced here: 98.4 us
  starting transfers between devices  34.5 us (35%)
  blocking collectives  16.1 us (16%)
  waiting for transfers between devices  16 us (16%)
  local copies, waits for them, and re-layouts  10.4 us (10%)
  other arithmetic  10.3 us (10%)
  matrix products  7.23 us (7%)
  between operations  3.79 us (4%)
    ppermute x5, starting transfers between devices, shifted(): return lax.ppermute(array, axis, pairs)  23.5 us
    all_to_all x1, blocking collectives, per_device(): lax.all_to_all(outgoing, 'seq', split_axis=0, concat_axis=0, tiled=True)  16.1 us
    ppermute x5, waiting for transfers between devices, shifted(): return lax.ppermute(array, axis, pairs)  7.75 us
    all_to_all x1, starting transfers between devices, per_device(): lax.all_to_all(slot_rows, 'seq', split_axis=0, concat_axis=0, tiled=True)  7.43 us
    ppermute x4, waiting for transfers between devices, exchange(): other = lax.ppermute(held, axis, [(i, i ^ bit) for i in range(count)])  5.52 us
    ppermute x4, starting transfers between devices, exchange(): other = lax.ppermute(held, axis, [(i, i ^ bit) for i in range(count)])  3.64 us
    unnamed x45, local copies, waits for them, and re-layouts  2.75 us
    all_to_all x1, waiting for transfers between devices, per_device(): lax.all_to_all(slot_rows, 'seq', split_axis=0, concat_axis=0, tiled=True)  2.75 us
  transfers between devices with their start and end apart: 10, of which 7 were waited for; matrix products, arithmetic and copies ran while one was open for 18% of the time, Pallas kernels for 0%

profile of v7, /device:TPU:0, one launch (start us, length us, event | category | flops | bytes accessed | tf_op | source)
XLA Modules:
  0.0 98.4 jit_solution(15906179220758004056)
XLA Ops:
  0.0 7.4 %all-to-all-start = ((bf16[8,32,512]{2,1,0:T(8,128)(2,1)}), bf16[8,32,512]{2,1,0:T(8,128)(2,1)S(1)}, u32[]{:S(2)}, u32[]{:S(2)}) async-start(bf16[8,32,512]{2,1,0:T(8,128)(2,1)} %bitcast.49), calls=%async_computation | async-start | bytes 524288 | tf_op jit(solution)/shard_map/all_to_all | solution.py:146
  7.4 1.5 %collective-permute-start.2 = (bf16[512,512]{1,0:T(8,128)(2,1)}, bf16[512,512]{1,0:T(8,128)(2,1)}, u32[]{:S(2)}, u32[]{:S(2)}) collective-permute-start(bf16[512,512]{1,0:T(8,128)(2,1)} %param.18), channel_id=1, source_target_pairs={{0,2},{1,3},{2,0},{3,1},{4,6},{5,7},{6,4},{7,5},{8,10},{9,11},{10,... | collective-permute-start | bytes 1572872 | tf_op jit(solution)/shard_map/ppermute | solution.py:57
  8.9 1.2 %compare_and_fusion.1 = (pred[8]{0:T(512)(128)(4,1)}, s32[8]{0:T(128)S(1)}) fusion(s32[8,8]{1,0:T(8,128)} %param.14, s32[]{:T(128)S(6)} %select_n.95), kind=kLoop, calls=%fused_computation.118 | loop fusion | flops 48 | bytes 76 | tf_op jit(solution)/shard_map/jit(_take)/and | solution.py:199
  10.2 1.0 sort.17
  11.3 0.8 reduce-window.8
  12.2 0.7 constant_dynamic-update-slice_fusion.1
  13.0 0.7 exponential_negate_fusion
  13.6 2.8 %all-to-all-done = bf16[8,32,512]{2,1,0:T(8,128)(2,1)S(1)} async-done(((bf16[8,32,512]{2,1,0:T(8,128)(2,1)}), bf16[8,32,512]{2,1,0:T(8,128)(2,1)S(1)}, u32[]{:S(2)}, u32[]{:S(2)}) %all-to-all-start) | async-done | bytes 262176 | tf_op jit(solution)/shard_map/all_to_all | solution.py:146
  16.4 0.6 gather_fusion
  17.0 1.6 %collective-permute-start = (bf16[256,512]{1,0:T(8,128)(2,1)S(1)}, bf16[256,512]{1,0:T(8,128)(2,1)S(1)}, u32[]{:S(2)}, u32[]{:S(2)}) collective-permute-start(bf16[256,512]{1,0:T(8,128)(2,1)S(1)} %bitcast_select_fusion), channel_id=1, source_target_pairs={{0,2},{1,3},{2,0},{3,1},{4,6},{5,7},{6,4},{7,5},{8,10},{9,11},{10,... | collective-permute-start | bytes 786440 | tf_op jit(solution)/shard_map/ppermute | solution.py:57
  18.6 0.6 fusion.72
  19.8 1.3 %broadcast_compare_fusion.1 = (pred[256]{0:T(512)(128)(4,1)S(1)}, pred[256]{0:T(512)(128)(4,1)S(1)}, f32[256]{0:T(256)}, f32[256]{0:T(256)}, f32[256]{0:T(256)}) fusion(s32[]{:T(128)} %bitcast.10, s32[259]{0:T(512)S(1)} %convert_reduce_fusion, s32[]{:T(128)S(6)} %select_n.109), kind=kLoop, calls=%fused_computation.131 | loop fusion | flops 2048 | bytes 7688 | tf_op jit(solution)/shard_map/eq | solution.py:117
  21.1 5.5 %collective-permute-done = bf16[256,512]{1,0:T(8,128)(2,1)S(1)} collective-permute-done((bf16[256,512]{1,0:T(8,128)(2,1)S(1)}, bf16[256,512]{1,0:T(8,128)(2,1)S(1)}, u32[]{:S(2)}, u32[]{:S(2)}) %collective-permute-start) | collective-permute-done | bytes 262176 | tf_op jit(solution)/shard_map/ppermute | solution.py:57
  26.9 0.6 fusion.75
  30.1 0.6 slice.130
  30.7 0.6 slice_reduce_fusion.4
  31.4 1.1 %pad_maximum_fusion.2 = bf16[1024,512]{1,0:T(8,128)(2,1)S(1)} fusion(bf16[512,512]{1,0:T(8,128)(2,1)} %collective-permute-done.2, bf16[512,512]{1,0:T(8,128)(2,1)S(1)} %copy-done.1), kind=kLoop, calls=%fused_computation.27 | loop fusion | flops 2097152 | bytes 2097152 | tf_op jit(solution)/shard_map/concatenate | solution.py:58
  32.6 0.5 collective-permute-start.3
  33.1 1.1 %pad_maximum_fusion = bf16[256,2048]{1,0:T(8,128)(2,1)S(1)} fusion(bf16[256,1024]{1,0:T(8,128)(2,1)} %collective-permute-done.1, bf16[256,512]{1,0:T(8,128)(2,1)S(1)} %collective-permute-done, bf16[256,512]{1,0:T(8,128)(2,1)S(1)} %bitcast_select_fusion), kind=kLoop, calls=%fused_computation.25 | loop fusion | flops 3145728 | bytes 2097152 | tf_op jit(solution)/shard_map/concatenate | solution.py:58
  34.4 0.6 copy-done.17
  35.0 0.4 compare_select_fusion
  35.9 0.7 convolution_convert_fusion.2
  36.7 0.7 copy-done.16
  37.4 0.7 divide_multiply_fusion.1
  38.1 1.9 %fusion.17 = bf16[256,512]{1,0:T(8,128)(2,1)S(1)} fusion(bf16[1024,512]{1,0:T(8,128)(2,1)S(1)} %collective-permute-done.3, bf16[512,512]{1,0:T(8,128)(2,1)} %collective-permute-done.2, bf16[512,512]{1,0:T(8,128)(2,1)S(1)} %copy-done.1, bf16[256,1024]{1,0:T(8,128)(2,1)} %collective-permute-done.1, bf16[256,512]{1,0:T(8,128)(2,1)S(1)} %collective-permute-done, ...), kind=kOutput, calls=%fused_computation.15 | convolution fusion | flops 546439168 | bytes 3407872 | tf_op jit(solution)/shard_map/dot_general | solution.py:163
  40.1 3.6 %collective-permute-start.4 = (bf16[3,896]{1,0:T(4,128)(2,1)S(1)}, bf16[3,896]{1,0:T(4,128)(2,1)S(1)}, u32[]{:S(2)}, u32[]{:S(2)}) collective-permute-start(bf16[3,896]{1,0:T(4,128)(2,1)S(1)} %pad_maximum_fusion.8), channel_id=1, source_target_pairs={{0,4},{4,8},{8,12},{12,16},{16,20},{20,24},{24,28},{1,5},{5,9},{9,... | collective-permute-start | bytes 16136 | tf_op jit(solution)/shard_map/ppermute | solution.py:12
  43.8 0.6 fusion.69
  44.6 0.5 collective-permute-done.4
  45.3 0.7 divide_multiply_fusion
  46.0 0.8 slice.159
  46.7 1.2 %copy.21 = f32[256,384]{0,1:T(8,128)S(1)} copy(f32[256,384]{1,0:T(8,128)} %slice.159) | data formatting | bytes 786432 | tf_op jit(solution)/shard_map/slice | solution.py:182
  47.9 0.5 convolution_convert_fusion.1
  48.6 5.1 %collective-permute-start.5 = (bf16[6,66,256]{2,1,0:T(8,128)(2,1)S(1)}, bf16[6,66,256]{2,1,0:T(8,128)(2,1)S(1)}, u32[]{:S(2)}, u32[]{:S(2)}) collective-permute-start(bf16[6,66,256]{2,1,0:T(8,128)(2,1)S(1)} %pad_maximum_fusion.5), channel_id=1, source_target_pairs={{0,8},{4,12},{8,16},{12,20},{16,24},{20,28},{1,9},{5,13},{9,17},{1... | collective-permute-start | bytes 608264 | tf_op jit(solution)/shard_map/ppermute | solution.py:12
  53.7 2.5 %collective-permute-start.6 = (bf16[6,66,256]{2,1,0:T(8,128)(2,1)S(1)}, bf16[6,66,256]{2,1,0:T(8,128)(2,1)S(1)}, u32[]{:S(2)}, u32[]{:S(2)}) collective-permute-start(bf16[6,66,256]{2,1,0:T(8,128)(2,1)S(1)} %pad_maximum_fusion.5), channel_id=1, source_target_pairs={{0,4},{4,8},{8,12},{12,16},{16,20},{20,24},{24,28},{1,5},{5,9},{9,... | collective-permute-start | bytes 608264 | tf_op jit(solution)/shard_map/ppermute | solution.py:12
  56.2 0.4 fusion.48
  56.6 0.8 collective-permute-done.5
  57.5 2.2 %collective-permute-done.6 = bf16[6,66,256]{2,1,0:T(8,128)(2,1)S(1)} collective-permute-done((bf16[6,66,256]{2,1,0:T(8,128)(2,1)S(1)}, bf16[6,66,256]{2,1,0:T(8,128)(2,1)S(1)}, u32[]{:S(2)}, u32[]{:S(2)}) %collective-permute-start.6) | collective-permute-done | bytes 202784 | tf_op jit(solution)/shard_map/ppermute | solution.py:12
  60.1 6.9 %collective-permute-start.7 = (bf16[6,66,256]{2,1,0:T(8,128)(2,1)S(1)}, bf16[6,66,256]{2,1,0:T(8,128)(2,1)S(1)}, u32[]{:S(2)}, u32[]{:S(2)}) collective-permute-start(bf16[6,66,256]{2,1,0:T(8,128)(2,1)S(1)} %pad_maximum_fusion.6), channel_id=1, source_target_pairs={{0,8},{4,12},{8,16},{12,20},{16,24},{20,28},{1,9},{5,13},{9,17},{1... | collective-permute-start | bytes 608264 | tf_op jit(solution)/shard_map/ppermute | solution.py:12
  67.0 1.9 %fusion.14 = f32[256,6,64]{0,2,1:T(8,128)S(1)} fusion(f32[6,256]{1,0:T(8,128)S(1)} %bitcast.54, f32[256,256]{1,0:T(8,128)S(1)} %fusion.48, pred[256,256]{1,0:T(8,128)(4,1)S(1)} %fusion.45, f32[256,6,64]{0,2,1:T(8,128)S(1)} %bitcast.47, f32[6]{0:T(128)S(1)} %copy-done.19, f32[256,6]{0,1:T(8,128)S(1)} %copy-done.9), kind=kOutput, calls=%fused_computation.14 | convolution fusion | flops 303464448 | bytes 1126424 | tf_op jit(solution)/shard_map/hts,shp->thp/dot_general | solution.py:114
  68.9 1.5 %collective-permute-done.7 = bf16[6,66,256]{2,1,0:T(8,128)(2,1)S(1)} collective-permute-done((bf16[6,66,256]{2,1,0:T(8,128)(2,1)S(1)}, bf16[6,66,256]{2,1,0:T(8,128)(2,1)S(1)}, u32[]{:S(2)}, u32[]{:S(2)}) %collective-permute-start.7) | collective-permute-done | bytes 202784 | tf_op jit(solution)/shard_map/ppermute | solution.py:12
  71.0 5.3 %collective-permute-start.8 = (bf16[6,66,256]{2,1,0:T(8,128)(2,1)S(1)}, bf16[6,66,256]{2,1,0:T(8,128)(2,1)S(1)}, u32[]{:S(2)}, u32[]{:S(2)}) collective-permute-start(bf16[6,66,256]{2,1,0:T(8,128)(2,1)S(1)} %pad_maximum_fusion.7), channel_id=1, source_target_pairs={{0,16},{4,20},{8,24},{12,28},{1,17},{5,21},{9,25},{13,29},{2,18},{... | collective-permute-start | bytes 608264 | tf_op jit(solution)/shard_map/ppermute | solution.py:12
  76.3 0.7 fusion.65
  77.0 2.7 %collective-permute-done.8 = bf16[6,66,256]{2,1,0:T(8,128)(2,1)S(1)} collective-permute-done((bf16[6,66,256]{2,1,0:T(8,128)(2,1)S(1)}, bf16[6,66,256]{2,1,0:T(8,128)(2,1)S(1)}, u32[]{:S(2)}, u32[]{:S(2)}) %collective-permute-start.8) | collective-permute-done | bytes 202784 | tf_op jit(solution)/shard_map/ppermute | solution.py:12
  79.8 0.5 fusion.22
  80.6 0.3 convert_element_type.188
  80.9 0.6 gather_fusion.1
  81.6 16.1 %all_to_all.10 = bf16[8,32,384]{2,1,0:T(8,128)(2,1)S(1)} all-to-all(bf16[8,32,384]{2,1,0:T(8,128)(2,1)S(1)} %broadcast_select_fusion), channel_id=1, replica_groups=mesh['seq'=8,'fsdp'=4] {'seq'}, dimensions={0} | all-to-all | bytes 393216 | tf_op jit(solution)/shard_map/all_to_all | solution.py:200
  97.7 0.7 copy.35
  (91 shorter events, 3.2 us)
Async XLA Ops:
  0.0 35.9 %copy-start = (bf16[2048,384]{1,0:T(8,128)(2,1)S(1)}, bf16[2048,384]{1,0:T(8,128)(2,1)}, u32[]{:S(2)}) copy-start(bf16[2048,384]{1,0:T(8,128)(2,1)} %param.16) | copy-start | bytes 4718596
  0.0 26.8 %copy-start.10 = (s32[4]{0:T(128)S(1)}, s32[4]{0:T(128)}, u32[]{:S(2)}) copy-start(s32[4]{0:T(128)} %constant.79.clone) | copy-start | bytes 52
  0.0 31.4 %copy-start.1 = (bf16[512,512]{1,0:T(8,128)(2,1)S(1)}, bf16[512,512]{1,0:T(8,128)(2,1)}, u32[]{:S(2)}) copy-start(bf16[512,512]{1,0:T(8,128)(2,1)} %param.18) | copy-start | bytes 1572868
  0.0 26.8 %copy-start.11 = (f32[4,512]{1,0:T(4,128)S(1)}, f32[4,512]{1,0:T(4,128)}, u32[]{:S(2)}) copy-start(f32[4,512]{1,0:T(4,128)} %param.21) | copy-start | bytes 24580
  0.0 16.4 %all-to-all-start = ((bf16[8,32,512]{2,1,0:T(8,128)(2,1)}), bf16[8,32,512]{2,1,0:T(8,128)(2,1)S(1)}, u32[]{:S(2)}, u32[]{:S(2)}) async-start(bf16[8,32,512]{2,1,0:T(8,128)(2,1)} %bitcast.49), calls=%async_computation | async-start | bytes 524288 | tf_op jit(solution)/shard_map/all_to_all | solution.py:146
  7.4 24.0 %collective-permute-start.2 = (bf16[512,512]{1,0:T(8,128)(2,1)}, bf16[512,512]{1,0:T(8,128)(2,1)}, u32[]{:S(2)}, u32[]{:S(2)}) collective-permute-start(bf16[512,512]{1,0:T(8,128)(2,1)} %param.18), channel_id=1, source_target_pairs={{0,2},{1,3},{2,0},{3,1},{4,6},{5,7},{6,4},{7,5},{8,10},{9,11},{10,... | collective-permute-start | bytes 1572872 | tf_op jit(solution)/shard_map/ppermute | solution.py:57
  17.0 9.6 %collective-permute-start = (bf16[256,512]{1,0:T(8,128)(2,1)S(1)}, bf16[256,512]{1,0:T(8,128)(2,1)S(1)}, u32[]{:S(2)}, u32[]{:S(2)}) collective-permute-start(bf16[256,512]{1,0:T(8,128)(2,1)S(1)} %bitcast_select_fusion), channel_id=1, source_target_pairs={{0,2},{1,3},{2,0},{3,1},{4,6},{5,7},{6,4},{7,5},{8,10},{9,11},{10,... | collective-permute-start | bytes 786440 | tf_op jit(solution)/shard_map/ppermute | solution.py:57
  26.7 6.4 %collective-permute-start.1 = (bf16[256,1024]{1,0:T(8,128)(2,1)S(1)}, bf16[256,1024]{1,0:T(8,128)(2,1)}, u32[]{:S(2)}, u32[]{:S(2)}) collective-permute-start(bf16[256,1024]{1,0:T(8,128)(2,1)S(1)} %pad_maximum_fusion.3), channel_id=1, source_target_pairs={{0,1},{1,0},{2,3},{3,2},{4,5},{5,4},{6,7},{7,6},{8,9},{9,8},{10,11... | collective-permute-start | bytes 1572872 | tf_op jit(solution)/shard_map/ppermute | solution.py:57
  32.6 5.6 %collective-permute-start.3 = (bf16[1024,512]{1,0:T(8,128)(2,1)S(1)}, bf16[1024,512]{1,0:T(8,128)(2,1)S(1)}, u32[]{:S(2)}, u32[]{:S(2)}) collective-permute-start(bf16[1024,512]{1,0:T(8,128)(2,1)S(1)} %pad_maximum_fusion.2), channel_id=1, source_target_pairs={{0,1},{1,0},{2,3},{3,2},{4,5},{5,4},{6,7},{7,6},{8,9},{9,8},{10,11... | collective-permute-start | bytes 3145736 | tf_op jit(solution)/shard_map/ppermute | solution.py:57
  34.2 0.8 copy-start.17
  34.2 0.8 copy-start.18
  35.4 1.3 %copy-start.8 = (f32[256,6]{0,1:T(8,128)}, f32[256,6]{0,1:T(8,128)S(1)}, u32[]{:S(2)}) copy-start(f32[256,6]{0,1:T(8,128)S(1)} %compare_select_fusion) | copy-start | bytes 18436
  35.6 1.1 %copy-start.2 = (f32[256,6]{0,1:T(8,128)}, f32[256,6]{0,1:T(8,128)S(1)}, u32[]{:S(2)}) copy-start(f32[256,6]{0,1:T(8,128)S(1)} %fusion.46) | copy-start | bytes 18436
  35.9 1.4 %copy-start.16 = (bf16[2048,384]{1,0:T(8,128)(2,1)S(1)}, bf16[2048,384]{1,0:T(8,128)(2,1)}, u32[]{:S(2)}) copy-start(bf16[2048,384]{1,0:T(8,128)(2,1)} %param.17) | copy-start | bytes 4718596
  40.0 5.2 %copy-start.4 = (f32[896]{0:T(1024)S(1)}, f32[896]{0:T(1024)}, u32[]{:S(2)}) copy-start(f32[896]{0:T(1024)} %get-tuple-element.15) | copy-start | bytes 10756
  40.0 5.2 %copy-start.5 = (f32[896]{0:T(1024)S(1)}, f32[896]{0:T(1024)}, u32[]{:S(2)}) copy-start(f32[896]{0:T(1024)} %get-tuple-element.16) | copy-start | bytes 10756
  40.0 5.2 %copy-start.6 = (f32[896]{0:T(1024)S(1)}, f32[896]{0:T(1024)}, u32[]{:S(2)}) copy-start(f32[896]{0:T(1024)} %get-tuple-element.17) | copy-start | bytes 10756
  40.1 5.2 %copy-start.7 = (f32[896]{0:T(1024)S(1)}, f32[896]{0:T(1024)}, u32[]{:S(2)}) copy-start(f32[896]{0:T(1024)} %get-tuple-element.18) | copy-start | bytes 10756
  40.1 5.2 %copy-start.12 = (f32[256]{0:T(256)S(1)}, f32[256]{0:T(256)}, u32[]{:S(2)}) copy-start(f32[256]{0:T(256)} %get-tuple-element.31) | copy-start | bytes 3076
  40.1 5.2 %copy-start.13 = (f32[256]{0:T(256)S(1)}, f32[256]{0:T(256)}, u32[]{:S(2)}) copy-start(f32[256]{0:T(256)} %get-tuple-element.32) | copy-start | bytes 3076
  40.1 5.2 %copy-start.14 = (f32[256]{0:T(256)S(1)}, f32[256]{0:T(256)}, u32[]{:S(2)}) copy-start(f32[256]{0:T(256)} %get-tuple-element.33) | copy-start | bytes 3076
  40.1 5.0 %collective-permute-start.4 = (bf16[3,896]{1,0:T(4,128)(2,1)S(1)}, bf16[3,896]{1,0:T(4,128)(2,1)S(1)}, u32[]{:S(2)}, u32[]{:S(2)}) collective-permute-start(bf16[3,896]{1,0:T(4,128)(2,1)S(1)} %pad_maximum_fusion.8), channel_id=1, source_target_pairs={{0,4},{4,8},{8,12},{12,16},{16,20},{20,24},{24,28},{1,5},{5,9},{9,... | collective-permute-start | bytes 16136 | tf_op jit(solution)/shard_map/ppermute | solution.py:12
  46.0 1.9 %copy-start.9 = (f32[256,6]{0,1:T(8,128)S(1)}, f32[256,6]{0,1:T(8,128)}, u32[]{:S(2)}) copy-start(f32[256,6]{0,1:T(8,128)} %copy-done.8) | copy-start | bytes 18436
  48.6 8.8 %collective-permute-start.5 = (bf16[6,66,256]{2,1,0:T(8,128)(2,1)S(1)}, bf16[6,66,256]{2,1,0:T(8,128)(2,1)S(1)}, u32[]{:S(2)}, u32[]{:S(2)}) collective-permute-start(bf16[6,66,256]{2,1,0:T(8,128)(2,1)S(1)} %pad_maximum_fusion.5), channel_id=1, source_target_pairs={{0,8},{4,12},{8,16},{12,20},{16,24},{20,28},{1,9},{5,13},{9,17},{1... | collective-permute-start | bytes 608264 | tf_op jit(solution)/shard_map/ppermute | solution.py:12
  53.7 5.9 %collective-permute-start.6 = (bf16[6,66,256]{2,1,0:T(8,128)(2,1)S(1)}, bf16[6,66,256]{2,1,0:T(8,128)(2,1)S(1)}, u32[]{:S(2)}, u32[]{:S(2)}) collective-permute-start(bf16[6,66,256]{2,1,0:T(8,128)(2,1)S(1)} %pad_maximum_fusion.5), channel_id=1, source_target_pairs={{0,4},{4,8},{8,12},{12,16},{16,20},{20,24},{24,28},{1,5},{5,9},{9,... | collective-permute-start | bytes 608264 | tf_op jit(solution)/shard_map/ppermute | solution.py:12
  56.6 10.4 %copy-start.3 = (f32[256,6]{0,1:T(8,128)S(1)}, f32[256,6]{0,1:T(8,128)}, u32[]{:S(2)}) copy-start(f32[256,6]{0,1:T(8,128)} %copy-done.2) | copy-start | bytes 18436
  56.6 10.4 %copy-start.19 = (f32[6]{0:T(128)S(1)}, f32[6]{0:T(128)}, u32[]{:S(2)}) copy-start(f32[6]{0:T(128)} %param.24) | copy-start | bytes 76
  60.1 10.4 %collective-permute-start.7 = (bf16[6,66,256]{2,1,0:T(8,128)(2,1)S(1)}, bf16[6,66,256]{2,1,0:T(8,128)(2,1)S(1)}, u32[]{:S(2)}, u32[]{:S(2)}) collective-permute-start(bf16[6,66,256]{2,1,0:T(8,128)(2,1)S(1)} %pad_maximum_fusion.6), channel_id=1, source_target_pairs={{0,8},{4,12},{8,16},{12,20},{16,24},{20,28},{1,9},{5,13},{9,17},{1... | collective-permute-start | bytes 608264 | tf_op jit(solution)/shard_map/ppermute | solution.py:12
  71.0 8.8 %collective-permute-start.8 = (bf16[6,66,256]{2,1,0:T(8,128)(2,1)S(1)}, bf16[6,66,256]{2,1,0:T(8,128)(2,1)S(1)}, u32[]{:S(2)}, u32[]{:S(2)}) collective-permute-start(bf16[6,66,256]{2,1,0:T(8,128)(2,1)S(1)} %pad_maximum_fusion.7), channel_id=1, source_target_pairs={{0,16},{4,20},{8,24},{12,28},{1,17},{5,21},{9,25},{13,29},{2,18},{... | collective-permute-start | bytes 608264 | tf_op jit(solution)/shard_map/ppermute | solution.py:12
  79.8 1.8 %copy-start.15 = (pred[8]{0:T(512)(128)(4,1)S(1)}, pred[8]{0:T(512)(128)(4,1)}, u32[]{:S(2)}) copy-start(pred[8]{0:T(512)(128)(4,1)} %get-tuple-element.19) | copy-start | bytes 28

commit v8 on v7

--- a/solution.py
+++ b/solution.py
@@ -142,36 +142,50 @@
     own_index = lax.axis_index("seq")
     tok_dev = tokens.shape[0]
     piece_rows = tok_dev // seq_count
+    conv_width = conv_heads.shape[0]
+    halo = conv_width - 1
     slot_rows = tokens.reshape(seq_count, piece_rows, tokens.shape[1])
-    arrived = lax.all_to_all(slot_rows, "seq", split_axis=0, concat_axis=0, tiled=True)
+    tail = min(halo, piece_rows)
+    tail_pad = 16 if piece_rows % 16 == 0 and tail <= 16 else tail
+    tails = jnp.roll(slot_rows[:, piece_rows - tail :, :], 1, axis=0)
+    tails = jnp.pad(tails, ((0, 0), (0, tail_pad - tail), (0, 0)))
+    outgoing_rows = jnp.concatenate([slot_rows, tails], axis=1)
+    arrived = lax.all_to_all(outgoing_rows, "seq", split_axis=0, concat_axis=0, tiled=True)
     dealt_row = lax.dynamic_slice_in_dim(deal_order, own_index, 1, 0)[0]
     inverse = jnp.argsort(dealt_row)
-    stream_block = jnp.take(arrived, inverse, axis=0).reshape(tok_dev, tokens.shape[1])
+    stream_block = jnp.take(arrived[:, :piece_rows, :], inverse, axis=0).reshape(tok_dev, tokens.shape[1])
+    prior_row = lax.dynamic_slice_in_dim(deal_order, (own_index + seq_count - 1) % seq_count, 1, 0)[0]
+    inverse_prior = jnp.argsort(prior_row)
+    block_rows = [tok_dev - halo + r for r in range(halo)]
+    pieces = jnp.asarray([b // piece_rows for b in block_rows], jnp.int32)
+    within = jnp.asarray([b % piece_rows - (piece_rows - tail) for b in block_rows], jnp.int32)
+    tail_in = arrived[:, piece_rows : piece_rows + tail, :].reshape(seq_count * tail, tokens.shape[1])
+    halo_rows = jnp.take(tail_in, inverse_prior[pieces] * tail + within, axis=0)
+    halo_rows = jnp.where(own_index > 0, halo_rows, jnp.zeros_like(halo_rows))
+    extended_rows = jnp.concatenate([stream_block, halo_rows], axis=0)
     inner_dev = x_weight.shape[1]
     heads_dev = step_weight.shape[1]
     head_dim = inner_dev // heads_dev
     state_dim = shared_weight.shape[1] // 2
     w_held, _ = exchange(shared_weight, "fsdp", 0)
-    feature_held, codes = exchange(stream_block, "fsdp", 1)
-    feature_part = to_natural(feature_held, codes, "fsdp", 1)
-    x_acc, z_acc, step_acc = tuple(
+    feature_held, codes = exchange(extended_rows, "fsdp", 1)
+    feature_ext = to_natural(feature_held, codes, "fsdp", 1)
+    feature_part = feature_ext[:tok_dev]
+    x_ext = jnp.dot(feature_ext, x_weight, preferred_element_type=jnp.float32)
+    z_acc, step_acc = tuple(
         (
             jnp.dot(feature_part, weight, preferred_element_type=jnp.float32)
-            for weight in (x_weight, z_weight, step_weight)
-        )
-    )
-    bc_acc = jnp.dot(feature_held, w_held, preferred_element_type=jnp.float32)
-    x_raw = x_acc.astype(jnp.bfloat16)
+            for weight in (z_weight, step_weight)
+        )
+    )
+    bc_ext = jnp.dot(feature_held, w_held, preferred_element_type=jnp.float32)
     z_raw = z_acc.astype(jnp.bfloat16)
-    bc_raw = bc_acc.astype(jnp.bfloat16)
     step_size = jax.nn.softplus(step_acc + step_bias[None, :])
-    mixed_in = jnp.concatenate([x_raw, bc_raw], axis=1)
-    conv_width = conv_heads.shape[0]
-    prior_rows = shifted(mixed_in[tok_dev - conv_width + 1 :], "seq", 1)
+    mixed_ext = jnp.concatenate([x_ext.astype(jnp.bfloat16), bc_ext.astype(jnp.bfloat16)], axis=1)
     first_pos = own_index * tok_dev
     positions = first_pos - (conv_width - 1) + jnp.arange(tok_dev + conv_width - 1, dtype=jnp.int32)
     seg_ext = segment_of(positions, lengths)
-    extended = jnp.concatenate([prior_rows, mixed_in], axis=0).astype(jnp.float32)
+    extended = jnp.concatenate([mixed_ext[tok_dev:], mixed_ext[:tok_dev]], axis=0).astype(jnp.float32)
     activated = jax.nn.silu(
         causal_conv(
             extended, seg_ext, jnp.concatenate([conv_heads, conv_shared], axis=1), conv_width

time: 99.2 us -> 110 us (1.11)
  starting transfers between devices: 34.5 us -> 27.2 us
  other arithmetic: 10.3 us -> 15.2 us
  local copies, waits for them, and re-layouts: 10.4 us -> 14.9 us
  blocking collectives: 16.1 us -> 20.5 us
  matrix products: 7.23 us -> 11.6 us
    ppermute x5 -> x4, starting transfers between devices: 23.5 us -> 16.2 us  [shifted(): return lax.ppermute(array, axis, pairs)]
    all_to_all x1, blocking collectives: 16.1 us -> 20.5 us  [per_device(): lax.all_to_all(outgoing, 'seq', split_axis=0, concat_axis=0, tiled=True)]
    ppermute x4, waiting for transfers between devices: 5.52 us -> 2.42 us  [exchange(): other = lax.ppermute(held, axis, [(i, i ^ bit) for i in range(count)])]
    dot_general x3 -> x2, matrix products: 1.85 us -> 4.11 us  [per_device(): jnp.dot(feature_part, weight, preferred_element_type=jnp.float32)]
    dot_general x1 -> x2, matrix products: 1.9 us -> 3.99 us  [the longest x1 2.24 us: per_device(): bc_ext = jnp.dot(feature_held, w_held, preferred_element_type=jnp.float32)]
    all_to_all x1, waiting for transfers between devices: 2.75 us -> 4.52 us  [per_device(): lax.all_to_all(outgoing_rows, 'seq', split_axis=0, concat_axis=0, tiled=T...]
    concatenate x1 -> x3, other arithmetic: 0.01 us -> 1.77 us  [the longest x1 1.72 us: per_device(): outgoing_rows = jnp.concatenate([slot_rows, tails], axis=1)]
    slice x0 -> x4, local copies, waits for them, and re-layouts: none -> 1.72 us  [the longest x2 1.69 us: per_device(): tails = jnp.roll(slot_rows[:, piece_rows - tail:, :], 1, axis=0)]
  transfers between devices with their start and end apart: 10 -> 9, of which waited for: 7 -> 6; matrix products, arithmetic and copies ran while one was open for 18% -> 26% of each run, Pallas kernels for 0% -> 0%
where the time goes in v8:
time: 110 us; the launch traced here: 109 us
  starting transfers between devices  27.2 us (25%)
  blocking collectives  20.5 us (19%)
  waiting for transfers between devices  15.5 us (14%)
  other arithmetic  15.2 us (14%)
  local copies, waits for them, and re-layouts  14.9 us (14%)
  matrix products  11.6 us (11%)
  between operations  3.95 us (4%)
    all_to_all x1, blocking collectives, per_device(): lax.all_to_all(outgoing, 'seq', split_axis=0, concat_axis=0, tiled=True)  20.5 us
    ppermute x4, starting transfers between devices, shifted(): return lax.ppermute(array, axis, pairs)  16.2 us
    ppermute x4, waiting for transfers between devices, shifted(): return lax.ppermute(array, axis, pairs)  8.6 us
    all_to_all x1, starting transfers between devices, per_device(): lax.all_to_all(outgoing_rows, 'seq', split_axis=0, concat_axis=0, tiled=T...  7.29 us
    all_to_all x1, waiting for transfers between devices, per_device(): lax.all_to_all(outgoing_rows, 'seq', split_axis=0, concat_axis=0, tiled=T...  4.52 us
    dot_general x2, matrix products, per_device(): jnp.dot(feature_part, weight, preferred_element_type=jnp.float32)  4.11 us
    ppermute x4, starting transfers between devices, exchange(): other = lax.ppermute(held, axis, [(i, i ^ bit) for i in range(count)])  3.66 us
    concatenate x3, other arithmetic, exchange(): held = jnp.concatenate([held, other], axis=dim)  3.3 us
  transfers between devices with their start and end apart: 9, of which 6 were waited for; matrix products, arithmetic and copies ran while one was open for 26% of the time, Pallas kernels for 0%

profile of v8, /device:TPU:0, one launch (start us, length us, event | category | flops | bytes accessed | tf_op | source)
XLA Modules:
  0.0 108.8 jit_solution(4150458136292827719)
XLA Ops:
  0.0 0.9 slice.185
  0.9 0.8 slice.186
  1.7 1.7 %pad_maximum_fusion.7 = bf16[8,48,512]{2,1,0:T(8,128)(2,1)} fusion(bf16[8,16,512]{2,1,0:T(8,128)(2,1)S(1)} %fusion.68, bf16[8,32,512]{2,1,0:T(8,128)(2,1)} %bitcast.53), kind=kLoop, calls=%fused_computation.63 | loop fusion | flops 786432 | bytes 786432 | tf_op jit(solution)/shard_map/concatenate | solution.py:152
  3.5 7.3 %all-to-all-start = ((bf16[8,48,512]{2,1,0:T(8,128)(2,1)}), bf16[8,48,512]{2,1,0:T(8,128)(2,1)S(1)}, u32[]{:S(2)}, u32[]{:S(2)}) async-start(bf16[8,48,512]{2,1,0:T(8,128)(2,1)} %pad_maximum_fusion.7), calls=%async_computation | async-start | bytes 786432 | tf_op jit(solution)/shard_map/all_to_all | solution.py:153
  10.8 1.6 %collective-permute-start.2 = (bf16[512,512]{1,0:T(8,128)(2,1)S(1)}, bf16[512,512]{1,0:T(8,128)(2,1)}, u32[]{:S(2)}, u32[]{:S(2)}) collective-permute-start(bf16[512,512]{1,0:T(8,128)(2,1)S(1)} %copy-done.1), channel_id=1, source_target_pairs={{0,2},{1,3},{2,0},{3,1},{4,6},{5,7},{6,4},{7,5},{8,10},{9,11},{10,... | collective-permute-start | bytes 1572872 | tf_op jit(solution)/shard_map/ppermute | solution.py:57
  12.3 1.2 %compare_and_fusion.2 = (pred[8]{0:T(512)(128)(4,1)}, s32[8]{0:T(128)S(1)}) fusion(s32[8,8]{1,0:T(8,128)} %param.16, s32[]{:T(128)S(6)} %select_n.125), kind=kLoop, calls=%fused_computation.140 | loop fusion | flops 48 | bytes 76 | tf_op jit(solution)/shard_map/jit(_take)/and | solution.py:213
  13.5 1.0 sort.31
  14.6 0.7 fusion.77
  15.6 1.0 sort.32
  16.6 0.6 gather_fusion.1
  17.3 0.6 exponential_negate_fusion
  17.9 4.5 %all-to-all-done = bf16[8,48,512]{2,1,0:T(8,128)(2,1)S(1)} async-done(((bf16[8,48,512]{2,1,0:T(8,128)(2,1)}), bf16[8,48,512]{2,1,0:T(8,128)(2,1)S(1)}, u32[]{:S(2)}, u32[]{:S(2)}) %all-to-all-start) | async-done | bytes 393248 | tf_op jit(solution)/shard_map/all_to_all | solution.py:153
  23.9 1.6 %collective-permute-start = (bf16[259,512]{1,0:T(8,128)(2,1)S(1)}, bf16[259,512]{1,0:T(8,128)(2,1)S(1)}, u32[]{:S(2)}, u32[]{:S(2)}) collective-permute-start(bf16[259,512]{1,0:T(8,128)(2,1)S(1)} %pad_maximum_fusion.8), channel_id=1, source_target_pairs={{0,2},{1,3},{2,0},{3,1},{4,6},{5,7},{6,4},{7,5},{8,10},{9,11},{10,... | collective-permute-start | bytes 795656 | tf_op jit(solution)/shard_map/ppermute | solution.py:57
  25.5 0.6 fusion.88
  26.7 1.3 %broadcast_compare_fusion.1 = (pred[256]{0:T(512)(128)(4,1)}, pred[256]{0:T(512)(128)(4,1)S(1)}, f32[256]{0:T(256)}, f32[256]{0:T(256)}, f32[256]{0:T(256)}) fusion(s32[]{:T(128)} %bitcast.11, s32[259]{0:T(512)S(1)} %convert_reduce_fusion, s32[]{:T(128)S(6)} %select_n.146), kind=kLoop, calls=%fused_computation.155 | loop fusion | flops 2048 | bytes 7688 | tf_op jit(solution)/shard_map/eq | solution.py:117
  28.0 2.4 %collective-permute-done = bf16[259,512]{1,0:T(8,128)(2,1)S(1)} collective-permute-done((bf16[259,512]{1,0:T(8,128)(2,1)S(1)}, bf16[259,512]{1,0:T(8,128)(2,1)S(1)}, u32[]{:S(2)}, u32[]{:S(2)}) %collective-permute-start) | collective-permute-done | bytes 265248 | tf_op jit(solution)/shard_map/ppermute | solution.py:57
  30.4 0.9 pad_maximum_fusion.3
  31.4 0.7 fusion.91
  34.6 0.7 slice.159
  35.3 0.6 slice_reduce_fusion.4
  35.9 0.7 fusion.56
  36.6 1.3 %pad_maximum_fusion.2 = bf16[1024,512]{1,0:T(8,128)(2,1)S(1)} fusion(bf16[512,512]{1,0:T(8,128)(2,1)} %collective-permute-done.2, bf16[512,512]{1,0:T(8,128)(2,1)} %param.20), kind=kLoop, calls=%fused_computation.36 | loop fusion | flops 2097152 | bytes 2097152 | tf_op jit(solution)/shard_map/concatenate | solution.py:58
  38.5 1.1 %pad_maximum_fusion = bf16[259,2048]{1,0:T(8,128)(2,1)S(1)} fusion(bf16[259,1024]{1,0:T(8,128)(2,1)} %collective-permute-done.1, bf16[259,512]{1,0:T(8,128)(2,1)S(1)} %collective-permute-done, bf16[3,512]{1,0:T(4,128)(2,1)S(1)} %select_select_fusion, bf16[256,512]{1,0:T(8,128)(2,1)S(1)} %bitcast_select_fusion), kind=kLoop, calls=%fused_computation.27 | loop fusion | flops 4243456 | bytes 2121728 | tf_op jit(solution)/shard_map/concatenate | solution.py:58
  39.6 0.8 constant_dynamic-slice_fusion.3
  40.5 0.7 copy-done.3
  41.4 2.4 %divide_multiply_fusion.1 = f32[256,384]{1,0:T(8,128)} fusion(bf16[2048,384]{1,0:T(8,128)(2,1)S(1)} %copy-done.31, bf16[259,512]{1,0:T(8,128)(2,1)S(1)} %get-tuple-element.28, bf16[259,512]{1,0:T(8,128)(2,1)S(1)} %get-tuple-element.29, bf16[259,512]{1,0:T(8,128)(2,1)S(1)} %get-tuple-element.30, bf16[259,512]{1,0:T(8,128)(2,1)} %get-tuple-element.27), kind=kOutput, calls=%fused_computation.67 | convolution fusion | flops 407437312 | bytes 3026944 | tf_op jit(solution)/shard_map/dot_general | solution.py:177
  43.8 1.2 %copy.24 = f32[256,384]{0,1:T(8,128)S(1)} copy(f32[256,384]{1,0:T(8,128)} %divide_multiply_fusion.1) | data formatting | bytes 786432 | tf_op jit(solution)/shard_map/jit(silu)/mul | solution.py:206
  45.1 1.7 %compare_select_fusion = f32[256,6]{0,1:T(8,128)S(1)} fusion(bf16[2048,6]{0,1:T(8,128)(2,1)} %param.21, bf16[259,512]{1,0:T(8,128)(2,1)} %copy-done.3, bf16[259,512]{1,0:T(8,128)(2,1)} %copy-done.5, bf16[259,512]{1,0:T(8,128)(2,1)} %copy-done.7, bf16[259,512]{1,0:T(8,128)(2,1)} %get-tuple-element.27, f32[6]{0:T(128)} %param.24), kind=kOutput, calls=%fused_computation.99 | convolution fusion | flops 10496512 | bytes 1091608 | tf_op jit(solution)/shard_map/dot_general | solution.py:177
  47.2 1.2 %fusion.85 = (bf16[6]{0:T(256)(128)(2,1)}, bf16[6]{0:T(256)(128)(2,1)}) fusion(f32[6]{0:T(128)S(1)} %slice_reduce_fusion, pred[]{:T(512)} %bitcast.14), kind=kLoop, calls=%fused_computation.162 | loop fusion | flops 30 | bytes 49 | tf_op jit(solution)/shard_map/convert_element_type | solution.py:25
  48.4 0.7 select_exponential_fusion
  49.1 1.7 %convolution_convert_fusion = bf16[259,384]{1,0:T(8,128)(2,1)S(1)} fusion(bf16[2048,384]{1,0:T(8,128)(2,1)S(1)} %copy-done, bf16[259,512]{1,0:T(8,128)(2,1)S(1)} %copy-done.4, bf16[259,512]{1,0:T(8,128)(2,1)S(1)} %copy-done.6, bf16[259,512]{1,0:T(8,128)(2,1)S(1)} %copy-done.8, bf16[259,512]{1,0:T(8,128)(2,1)} %get-tuple-element.27), kind=kOutput, calls=%fused_computation.21 | convolution fusion | flops 411714688 | bytes 2832640 | tf_op jit(solution)/shard_map/dot_general | solution.py:174
  51.0 2.2 %fusion.11 = bf16[259,512]{1,0:T(8,128)(2,1)S(1)} fusion(bf16[1024,512]{1,0:T(8,128)(2,1)} %collective-permute-done.3, bf16[512,512]{1,0:T(8,128)(2,1)} %collective-permute-done.2, bf16[512,512]{1,0:T(8,128)(2,1)S(1)} %copy-done.2, bf16[259,1024]{1,0:T(8,128)(2,1)} %collective-permute-done.1, bf16[259,512]{1,0:T(8,128)(2,1)S(1)} %collective-permute-done, ...), kind=kOutput, calls=%fused_computation.15 | convolution fusion | flops 553829888 | bytes 3423232 | tf_op jit(solution)/shard_map/dot_general | solution.py:181
  53.4 0.7 divide_multiply_fusion
  54.1 0.8 slice.196
  54.9 1.2 %copy.23 = f32[256,384]{0,1:T(8,128)S(1)} copy(f32[256,384]{1,0:T(8,128)} %slice.196) | data formatting | bytes 786432 | tf_op jit(solution)/shard_map/slice | solution.py:196
  56.8 4.1 %collective-permute-start.5 = (bf16[6,66,256]{2,1,0:T(8,128)(2,1)S(1)}, bf16[6,66,256]{2,1,0:T(8,128)(2,1)S(1)}, u32[]{:S(2)}, u32[]{:S(2)}) collective-permute-start(bf16[6,66,256]{2,1,0:T(8,128)(2,1)S(1)} %pad_maximum_fusion.9), channel_id=1, source_target_pairs={{0,4},{4,8},{8,12},{12,16},{16,20},{20,24},{24,28},{1,5},{5,9},{9,... | collective-permute-start | bytes 608264 | tf_op jit(solution)/shard_map/ppermute | solution.py:12
  60.8 2.5 %collective-permute-start.4 = (bf16[6,66,256]{2,1,0:T(8,128)(2,1)S(1)}, bf16[6,66,256]{2,1,0:T(8,128)(2,1)S(1)}, u32[]{:S(2)}, u32[]{:S(2)}) collective-permute-start(bf16[6,66,256]{2,1,0:T(8,128)(2,1)S(1)} %pad_maximum_fusion.9), channel_id=1, source_target_pairs={{0,8},{4,12},{8,16},{12,20},{16,24},{20,28},{1,9},{5,13},{9,17},{1... | collective-permute-start | bytes 608264 | tf_op jit(solution)/shard_map/ppermute | solution.py:12
  63.8 1.9 %collective-permute-done.5 = bf16[6,66,256]{2,1,0:T(8,128)(2,1)S(1)} collective-permute-done((bf16[6,66,256]{2,1,0:T(8,128)(2,1)S(1)}, bf16[6,66,256]{2,1,0:T(8,128)(2,1)S(1)}, u32[]{:S(2)}, u32[]{:S(2)}) %collective-permute-start.5) | collective-permute-done | bytes 202784 | tf_op jit(solution)/shard_map/ppermute | solution.py:12
  65.7 2.2 %collective-permute-done.4 = bf16[6,66,256]{2,1,0:T(8,128)(2,1)S(1)} collective-permute-done((bf16[6,66,256]{2,1,0:T(8,128)(2,1)S(1)}, bf16[6,66,256]{2,1,0:T(8,128)(2,1)S(1)}, u32[]{:S(2)}, u32[]{:S(2)}) %collective-permute-start.4) | collective-permute-done | bytes 202784 | tf_op jit(solution)/shard_map/ppermute | solution.py:12
  68.3 4.4 %collective-permute-start.6 = (bf16[6,66,256]{2,1,0:T(8,128)(2,1)S(1)}, bf16[6,66,256]{2,1,0:T(8,128)(2,1)S(1)}, u32[]{:S(2)}, u32[]{:S(2)}) collective-permute-start(bf16[6,66,256]{2,1,0:T(8,128)(2,1)S(1)} %pad_maximum_fusion.10), channel_id=1, source_target_pairs={{0,8},{4,12},{8,16},{12,20},{16,24},{20,28},{1,9},{5,13},{9,17},{1... | collective-permute-start | bytes 608264 | tf_op jit(solution)/shard_map/ppermute | solution.py:12
  72.8 1.9 %fusion.17 = f32[256,6,64]{0,2,1:T(8,128)S(1)} fusion(f32[6,256]{1,0:T(8,128)S(1)} %bitcast.58, f32[256,256]{1,0:T(8,128)S(1)} %fusion.59, pred[256,256]{1,0:T(8,128)(4,1)S(1)} %copy-done.9, f32[256,6,64]{0,2,1:T(8,128)S(1)} %bitcast.49, f32[6]{0:T(128)S(1)} %copy-done.34, f32[256,6]{0,1:T(8,128)S(1)} %copy-done.18), kind=kOutput, calls=%fused_computation.17 | convolution fusion | flops 303464448 | bytes 1126424 | tf_op jit(solution)/shard_map/hts,shp->thp/dot_general | solution.py:114
  74.7 1.8 %collective-permute-done.6 = bf16[6,66,256]{2,1,0:T(8,128)(2,1)S(1)} collective-permute-done((bf16[6,66,256]{2,1,0:T(8,128)(2,1)S(1)}, bf16[6,66,256]{2,1,0:T(8,128)(2,1)S(1)}, u32[]{:S(2)}, u32[]{:S(2)}) %collective-permute-start.6) | collective-permute-done | bytes 202784 | tf_op jit(solution)/shard_map/ppermute | solution.py:12
  77.0 5.3 %collective-permute-start.7 = (bf16[6,66,256]{2,1,0:T(8,128)(2,1)S(1)}, bf16[6,66,256]{2,1,0:T(8,128)(2,1)S(1)}, u32[]{:S(2)}, u32[]{:S(2)}) collective-permute-start(bf16[6,66,256]{2,1,0:T(8,128)(2,1)S(1)} %pad_maximum_fusion.11), channel_id=1, source_target_pairs={{0,16},{4,20},{8,24},{12,28},{1,17},{5,21},{9,25},{13,29},{2,18},{... | collective-permute-start | bytes 608264 | tf_op jit(solution)/shard_map/ppermute | solution.py:12
  82.3 0.7 fusion.78
  83.0 2.7 %collective-permute-done.7 = bf16[6,66,256]{2,1,0:T(8,128)(2,1)S(1)} collective-permute-done((bf16[6,66,256]{2,1,0:T(8,128)(2,1)S(1)}, bf16[6,66,256]{2,1,0:T(8,128)(2,1)S(1)}, u32[]{:S(2)}, u32[]{:S(2)}) %collective-permute-start.7) | collective-permute-done | bytes 202784 | tf_op jit(solution)/shard_map/ppermute | solution.py:12
  86.9 0.6 gather_fusion.3
  87.6 20.5 %all_to_all.10 = bf16[8,32,384]{2,1,0:T(8,128)(2,1)S(1)} all-to-all(bf16[8,32,384]{2,1,0:T(8,128)(2,1)S(1)} %broadcast_select_fusion), channel_id=1, replica_groups=mesh['seq'=8,'fsdp'=4] {'seq'}, dimensions={0} | all-to-all | bytes 393216 | tf_op jit(solution)/shard_map/all_to_all | solution.py:214
  108.1 0.7 copy.37
  (137 shorter events, 6.7 us)
Async XLA Ops:
  0.0 49.1 %copy-start = (bf16[2048,384]{1,0:T(8,128)(2,1)S(1)}, bf16[2048,384]{1,0:T(8,128)(2,1)}, u32[]{:S(2)}) copy-start(bf16[2048,384]{1,0:T(8,128)(2,1)} %param.18) | copy-start | bytes 4718596
  0.0 10.8 %copy-start.1 = (bf16[512,512]{1,0:T(8,128)(2,1)S(1)}, bf16[512,512]{1,0:T(8,128)(2,1)}, u32[]{:S(2)}) copy-start(bf16[512,512]{1,0:T(8,128)(2,1)} %param.20) | copy-start | bytes 1572868
  0.0 14.6 %copy-start.21 = (f32[4,384]{1,0:T(4,128)S(1)}, f32[4,384]{1,0:T(4,128)}, u32[]{:S(2)}) copy-start(f32[4,384]{1,0:T(4,128)} %param.22) | copy-start | bytes 18436
  0.0 15.3 %copy-start.32 = (s32[4]{0:T(128)S(1)}, s32[4]{0:T(128)}, u32[]{:S(2)}) copy-start(s32[4]{0:T(128)} %param.17) | copy-start | bytes 52
  0.0 17.3 %copy-start.33 = (f32[6]{0:T(128)S(1)}, f32[6]{0:T(128)}, u32[]{:S(2)}) copy-start(f32[6]{0:T(128)} %param.25) | copy-start | bytes 76
  3.5 19.0 %all-to-all-start = ((bf16[8,48,512]{2,1,0:T(8,128)(2,1)}), bf16[8,48,512]{2,1,0:T(8,128)(2,1)S(1)}, u32[]{:S(2)}, u32[]{:S(2)}) async-start(bf16[8,48,512]{2,1,0:T(8,128)(2,1)} %pad_maximum_fusion.7), calls=%async_computation | async-start | bytes 786432 | tf_op jit(solution)/shard_map/all_to_all | solution.py:153
  10.8 25.9 %collective-permute-start.2 = (bf16[512,512]{1,0:T(8,128)(2,1)S(1)}, bf16[512,512]{1,0:T(8,128)(2,1)}, u32[]{:S(2)}, u32[]{:S(2)}) collective-permute-start(bf16[512,512]{1,0:T(8,128)(2,1)S(1)} %copy-done.1), channel_id=1, source_target_pairs={{0,2},{1,3},{2,0},{3,1},{4,6},{5,7},{6,4},{7,5},{8,10},{9,11},{10,... | collective-permute-start | bytes 1572872 | tf_op jit(solution)/shard_map/ppermute | solution.py:57
  23.1 8.3 %copy-start.20 = (f32[4,512]{1,0:T(4,128)S(1)}, f32[4,512]{1,0:T(4,128)}, u32[]{:S(2)}) copy-start(f32[4,512]{1,0:T(4,128)} %param.23) | copy-start | bytes 24580
  23.1 8.3 %copy-start.19 = (s32[4]{0:T(128)S(1)}, s32[4]{0:T(128)}, u32[]{:S(2)}) copy-start(s32[4]{0:T(128)} %constant.115.clone) | copy-start | bytes 52
  23.9 6.5 %collective-permute-start = (bf16[259,512]{1,0:T(8,128)(2,1)S(1)}, bf16[259,512]{1,0:T(8,128)(2,1)S(1)}, u32[]{:S(2)}, u32[]{:S(2)}) collective-permute-start(bf16[259,512]{1,0:T(8,128)(2,1)S(1)} %pad_maximum_fusion.8), channel_id=1, source_target_pairs={{0,2},{1,3},{2,0},{3,1},{4,6},{5,7},{6,4},{7,5},{8,10},{9,11},{10,... | collective-permute-start | bytes 795656 | tf_op jit(solution)/shard_map/ppermute | solution.py:57
  28.0 9.9 %copy-start.27 = (pred[256]{0:T(512)(128)(4,1)}, pred[256]{0:T(512)(128)(4,1)S(1)}, u32[]{:S(2)}) copy-start(pred[256]{0:T(512)(128)(4,1)S(1)} %get-tuple-element.34) | copy-start | bytes 772
  31.3 7.2 %collective-permute-start.1 = (bf16[259,1024]{1,0:T(8,128)(2,1)}, bf16[259,1024]{1,0:T(8,128)(2,1)}, u32[]{:S(2)}, u32[]{:S(2)}) collective-permute-start(bf16[259,1024]{1,0:T(8,128)(2,1)} %pad_maximum_fusion.3), channel_id=1, source_target_pairs={{0,1},{1,0},{2,3},{3,2},{4,5},{5,4},{6,7},{7,6},{8,9},{9,8},{10,11... | collective-permute-start | bytes 1591304 | tf_op jit(solution)/shard_map/ppermute | solution.py:57
  37.9 13.0 %collective-permute-start.3 = (bf16[1024,512]{1,0:T(8,128)(2,1)S(1)}, bf16[1024,512]{1,0:T(8,128)(2,1)}, u32[]{:S(2)}, u32[]{:S(2)}) collective-permute-start(bf16[1024,512]{1,0:T(8,128)(2,1)S(1)} %pad_maximum_fusion.2), channel_id=1, source_target_pairs={{0,1},{1,0},{2,3},{3,2},{4,5},{5,4},{6,7},{7,6},{8,9},{9,8},{10,11... | collective-permute-start | bytes 3145736 | tf_op jit(solution)/shard_map/ppermute | solution.py:57
  39.6 1.8 %copy-start.31 = (bf16[2048,384]{1,0:T(8,128)(2,1)S(1)}, bf16[2048,384]{1,0:T(8,128)(2,1)}, u32[]{:S(2)}) copy-start(bf16[2048,384]{1,0:T(8,128)(2,1)} %param.19) | copy-start | bytes 4718596
  40.5 0.7 copy-start.3
  40.5 0.8 copy-start.5
  40.5 0.9 copy-start.7
  45.0 1.7 %copy-start.35 = (f32[6]{0:T(128)S(1)}, f32[6]{0:T(128)}, u32[]{:S(2)}) copy-start(f32[6]{0:T(128)} %exponential_negate_fusion) | copy-start | bytes 76
  45.0 3.4 %copy-start.26 = (pred[256]{0:T(512)(128)(4,1)S(1)}, pred[256]{0:T(512)(128)(4,1)}, u32[]{:S(2)}) copy-start(pred[256]{0:T(512)(128)(4,1)} %get-tuple-element.33) | copy-start | bytes 772
  45.0 3.4 %copy-start.28 = (pred[256]{0:T(512)(128)(4,1)S(1)}, pred[256]{0:T(512)(128)(4,1)}, u32[]{:S(2)}) copy-start(pred[256]{0:T(512)(128)(4,1)} %copy-done.27) | copy-start | bytes 772
  45.0 4.1 %copy-start.4 = (bf16[259,512]{1,0:T(8,128)(2,1)S(1)}, bf16[259,512]{1,0:T(8,128)(2,1)}, u32[]{:S(2)}) copy-start(bf16[259,512]{1,0:T(8,128)(2,1)} %copy-done.3) | copy-start | bytes 795652
  45.0 4.1 %copy-start.6 = (bf16[259,512]{1,0:T(8,128)(2,1)S(1)}, bf16[259,512]{1,0:T(8,128)(2,1)}, u32[]{:S(2)}) copy-start(bf16[259,512]{1,0:T(8,128)(2,1)} %copy-done.5) | copy-start | bytes 795652
  45.0 4.1 %copy-start.8 = (bf16[259,512]{1,0:T(8,128)(2,1)S(1)}, bf16[259,512]{1,0:T(8,128)(2,1)}, u32[]{:S(2)}) copy-start(bf16[259,512]{1,0:T(8,128)(2,1)} %copy-done.7) | copy-start | bytes 795652
  46.7 1.7 %copy-start.17 = (f32[256,6]{0,1:T(8,128)}, f32[256,6]{0,1:T(8,128)S(1)}, u32[]{:S(2)}) copy-start(f32[256,6]{0,1:T(8,128)S(1)} %compare_select_fusion) | copy-start | bytes 18436
  46.9 1.5 %copy-start.12 = (f32[256,6]{0,1:T(8,128)}, f32[256,6]{0,1:T(8,128)S(1)}, u32[]{:S(2)}) copy-start(f32[256,6]{0,1:T(8,128)S(1)} %fusion.57) | copy-start | bytes 18436
  49.1 1.8 %copy-start.2 = (bf16[512,512]{1,0:T(8,128)(2,1)S(1)}, bf16[512,512]{1,0:T(8,128)(2,1)}, u32[]{:S(2)}) copy-start(bf16[512,512]{1,0:T(8,128)(2,1)} %param.20) | copy-start | bytes 1572868
  50.9 2.4 %copy-start.14 = (f32[896]{0:T(1024)S(1)}, f32[896]{0:T(1024)}, u32[]{:S(2)}) copy-start(f32[896]{0:T(1024)} %get-tuple-element.18) | copy-start | bytes 10756
  50.9 2.4 %copy-start.15 = (f32[896]{0:T(1024)S(1)}, f32[896]{0:T(1024)}, u32[]{:S(2)}) copy-start(f32[896]{0:T(1024)} %get-tuple-element.19) | copy-start | bytes 10756
  50.9 2.4 %copy-start.16 = (f32[896]{0:T(1024)S(1)}, f32[896]{0:T(1024)}, u32[]{:S(2)}) copy-start(f32[896]{0:T(1024)} %get-tuple-element.20) | copy-start | bytes 10756
  50.9 2.4 %copy-start.22 = (f32[256]{0:T(256)S(1)}, f32[256]{0:T(256)}, u32[]{:S(2)}) copy-start(f32[256]{0:T(256)} %get-tuple-element.35) | copy-start | bytes 3076
  50.9 2.4 %copy-start.23 = (f32[256]{0:T(256)S(1)}, f32[256]{0:T(256)}, u32[]{:S(2)}) copy-start(f32[256]{0:T(256)} %get-tuple-element.36) | copy-start | bytes 3076
  50.9 2.4 %copy-start.24 = (f32[256]{0:T(256)S(1)}, f32[256]{0:T(256)}, u32[]{:S(2)}) copy-start(f32[256]{0:T(256)} %get-tuple-element.37) | copy-start | bytes 3076
  54.1 2.0 %copy-start.11 = (f32[256,6]{0,1:T(8,128)S(1)}, f32[256,6]{0,1:T(8,128)}, u32[]{:S(2)}) copy-start(f32[256,6]{0,1:T(8,128)} %get-tuple-element.32) | copy-start | bytes 18436
  54.1 2.0 %copy-start.18 = (f32[256,6]{0,1:T(8,128)S(1)}, f32[256,6]{0,1:T(8,128)}, u32[]{:S(2)}) copy-start(f32[256,6]{0,1:T(8,128)} %copy-done.17) | copy-start | bytes 18436
  54.1 2.5 %copy-start.30 = (bf16[6]{0:T(256)(128)(2,1)S(1)}, bf16[6]{0:T(256)(128)(2,1)}, u32[]{:S(2)}) copy-start(bf16[6]{0:T(256)(128)(2,1)} %get-tuple-element.44) | copy-start | bytes 40
  54.1 2.5 %copy-start.29 = (bf16[6]{0:T(256)(128)(2,1)S(1)}, bf16[6]{0:T(256)(128)(2,1)}, u32[]{:S(2)}) copy-start(bf16[6]{0:T(256)(128)(2,1)} %get-tuple-element.45) | copy-start | bytes 40
  56.8 8.9 %collective-permute-start.5 = (bf16[6,66,256]{2,1,0:T(8,128)(2,1)S(1)}, bf16[6,66,256]{2,1,0:T(8,128)(2,1)S(1)}, u32[]{:S(2)}, u32[]{:S(2)}) collective-permute-start(bf16[6,66,256]{2,1,0:T(8,128)(2,1)S(1)} %pad_maximum_fusion.9), channel_id=1, source_target_pairs={{0,4},{4,8},{8,12},{12,16},{16,20},{20,24},{24,28},{1,5},{5,9},{9,... | collective-permute-start | bytes 608264 | tf_op jit(solution)/shard_map/ppermute | solution.py:12
  60.8 7.1 %collective-permute-start.4 = (bf16[6,66,256]{2,1,0:T(8,128)(2,1)S(1)}, bf16[6,66,256]{2,1,0:T(8,128)(2,1)S(1)}, u32[]{:S(2)}, u32[]{:S(2)}) collective-permute-start(bf16[6,66,256]{2,1,0:T(8,128)(2,1)S(1)} %pad_maximum_fusion.9), channel_id=1, source_target_pairs={{0,8},{4,12},{8,16},{12,20},{16,24},{20,28},{1,9},{5,13},{9,17},{1... | collective-permute-start | bytes 608264 | tf_op jit(solution)/shard_map/ppermute | solution.py:12
  63.7 9.0 %copy-start.9 = (pred[256,256]{1,0:T(8,128)(4,1)S(1)}, pred[256,256]{1,0:T(8,128)(4,1)}, u32[]{:S(2)}) copy-start(pred[256,256]{1,0:T(8,128)(4,1)} %fusion.56) | copy-start | bytes 196612
  63.7 9.0 %copy-start.13 = (f32[256,6]{0,1:T(8,128)S(1)}, f32[256,6]{0,1:T(8,128)}, u32[]{:S(2)}) copy-start(f32[256,6]{0,1:T(8,128)} %copy-done.12) | copy-start | bytes 18436
  63.7 9.0 %copy-start.34 = (f32[6]{0:T(128)S(1)}, f32[6]{0:T(128)}, u32[]{:S(2)}) copy-start(f32[6]{0:T(128)} %param.26) | copy-start | bytes 76
  68.3 8.1 %collective-permute-start.6 = (bf16[6,66,256]{2,1,0:T(8,128)(2,1)S(1)}, bf16[6,66,256]{2,1,0:T(8,128)(2,1)S(1)}, u32[]{:S(2)}, u32[]{:S(2)}) collective-permute-start(bf16[6,66,256]{2,1,0:T(8,128)(2,1)S(1)} %pad_maximum_fusion.10), channel_id=1, source_target_pairs={{0,8},{4,12},{8,16},{12,20},{16,24},{20,28},{1,9},{5,13},{9,17},{1... | collective-permute-start | bytes 608264 | tf_op jit(solution)/shard_map/ppermute | solution.py:12
  76.5 9.3 %copy-start.10 = (f32[256,6]{0,1:T(8,128)S(1)}, f32[256,6]{0,1:T(8,128)}, u32[]{:S(2)}) copy-start(f32[256,6]{0,1:T(8,128)} %get-tuple-element.14) | copy-start | bytes 18436
  77.0 8.8 %collective-permute-start.7 = (bf16[6,66,256]{2,1,0:T(8,128)(2,1)S(1)}, bf16[6,66,256]{2,1,0:T(8,128)(2,1)S(1)}, u32[]{:S(2)}, u32[]{:S(2)}) collective-permute-start(bf16[6,66,256]{2,1,0:T(8,128)(2,1)S(1)} %pad_maximum_fusion.11), channel_id=1, source_target_pairs={{0,16},{4,20},{8,24},{12,28},{1,17},{5,21},{9,25},{13,29},{2,18},{... | collective-permute-start | bytes 608264 | tf_op jit(solution)/shard_map/ppermute | solution.py:12
  85.8 1.8 %copy-start.25 = (pred[8]{0:T(512)(128)(4,1)S(1)}, pred[8]{0:T(512)(128)(4,1)}, u32[]{:S(2)}) copy-start(pred[8]{0:T(512)(128)(4,1)} %get-tuple-element.21) | copy-start | bytes 28

commit v9 on v7

--- a/solution.py
+++ b/solution.py
@@ -13,22 +13,24 @@
 
 
 def combine_packed(earlier, later):
-    rows = later.shape[1] - 1
-    d_e, d_l = earlier[:, rows:, :], later[:, rows:, :]
-    return jnp.concatenate([d_l * earlier[:, :rows, :] + later[:, :rows, :], d_e * d_l], axis=1)
+    rows = later.shape[1] - 2
+    d_e, d_l = earlier[:, rows : rows + 1, :], later[:, rows : rows + 1, :]
+    state = d_l * earlier[:, :rows, :] + later[:, :rows, :]
+    decay = d_e * d_l
+    return jnp.concatenate([state, decay, decay], axis=1)
 
 
 def received(packed, axis, by):
     place = lax.axis_index(axis)
-    rows = packed.shape[1] - 1
-    decay = jnp.broadcast_to(packed[:, rows:, :1], (packed.shape[0], 1, packed.shape[2]))
-    high = decay.astype(jnp.bfloat16)
-    low = (decay - high.astype(jnp.float32)).astype(jnp.bfloat16)
-    wire = jnp.concatenate([packed[:, :rows, :].astype(jnp.bfloat16), high, low], axis=1)
+    rows = packed.shape[1] - 2
+    row = lax.broadcasted_iota(jnp.int32, packed.shape, 1)
+    high = packed.astype(jnp.bfloat16)
+    low = (packed - high.astype(jnp.float32)).astype(jnp.bfloat16)
+    wire = jnp.where(row == rows + 1, low, high)
     got = shifted(wire, axis, by).astype(jnp.float32)
     missing = (place < by).astype(jnp.float32)
-    decay_got = got[:, rows : rows + 1, :] + got[:, rows + 1 :, :] + missing
-    return jnp.concatenate([got[:, :rows, :], decay_got], axis=1)
+    decay = got[:, rows : rows + 1, :] + got[:, rows + 1 :, :] + missing
+    return jnp.concatenate([got[:, :rows, :], decay, decay], axis=1)
 
 
 def exclusive_scan(packed, axis, side):
@@ -185,9 +187,8 @@
     intra, state_out, carry_in, block_decay = local_terms(
         x_heads, b_rows, c_rows, step_size, decay_log, segment_ids, seg_before
     )
-    packed = jnp.concatenate(
-        [state_out, jnp.broadcast_to(block_decay[:, None, None], (heads_dev, 1, state_dim))], axis=1
-    )
+    decay_rows = jnp.broadcast_to(block_decay[:, None, None], (heads_dev, 2, state_dim))
+    packed = jnp.concatenate([state_out, decay_rows], axis=1)
     local_y = intra + skip_gain[None, :, None] * x_heads
     gate = jax.nn.silu(z_raw.astype(jnp.float32)).reshape(tok_dev, heads_dev, head_dim)
     scanned, (local_y, gate, carry_in) = exclusive_scan(packed, "seq", (local_y, gate, carry_in))

time: 99.2 us -> 99.9 us (level)
  other arithmetic: 10.3 us -> 12.5 us
  waiting for transfers between devices: 16 us -> 14.8 us
    select_n x0 -> x4, other arithmetic: none -> 1.64 us  [the longest x1 1.29 us: local_terms(): block_decay = jnp.where(carried[-1], jnp.exp(cum_decay[-1]), 0.0)]
    unnamed x45 -> x33, local copies, waits for them, and re-layouts: 2.75 us -> 2.73 us
  transfers between devices with their start and end apart: 10 -> 10, of which waited for: 7 -> 6; matrix products, arithmetic and copies ran while one was open for 18% -> 20% of each run, Pallas kernels for 0% -> 0%
where the time goes in v9:
time: 99.9 us; the launch traced here: 99.1 us
  starting transfers between devices  34.4 us (34%)
  blocking collectives  15.8 us (16%)
  waiting for transfers between devices  14.8 us (15%)
  other arithmetic  12.5 us (13%)
  local copies, waits for them, and re-layouts  10.6 us (11%)
  matrix products  7.24 us (7%)
  between operations  3.71 us (4%)
    ppermute x5, starting transfers between devices, shifted(): return lax.ppermute(array, axis, pairs)  23.3 us
    all_to_all x1, blocking collectives, per_device(): lax.all_to_all(outgoing, 'seq', split_axis=0, concat_axis=0, tiled=True)  15.8 us
    all_to_all x1, starting transfers between devices, per_device(): lax.all_to_all(slot_rows, 'seq', split_axis=0, concat_axis=0, tiled=True)  7.43 us
    ppermute x5, waiting for transfers between devices, shifted(): return lax.ppermute(array, axis, pairs)  7.38 us
    ppermute x4, waiting for transfers between devices, exchange(): other = lax.ppermute(held, axis, [(i, i ^ bit) for i in range(count)])  5.41 us
    ppermute x4, starting transfers between devices, exchange(): other = lax.ppermute(held, axis, [(i, i ^ bit) for i in range(count)])  3.68 us
    unnamed x33, local copies, waits for them, and re-layouts  2.73 us
    concatenate x3, other arithmetic, exchange(): held = jnp.concatenate([held, other], axis=dim)  2.31 us
  transfers between devices with their start and end apart: 10, of which 6 were waited for; matrix products, arithmetic and copies ran while one was open for 20% of the time, Pallas kernels for 0%

profile of v9, /device:TPU:0, one launch (start us, length us, event | category | flops | bytes accessed | tf_op | source)
XLA Modules:
  0.0 99.1 jit_solution(14675748212482397102)
XLA Ops:
  0.0 7.4 %all-to-all-start = ((bf16[8,32,512]{2,1,0:T(8,128)(2,1)}), bf16[8,32,512]{2,1,0:T(8,128)(2,1)S(1)}, u32[]{:S(2)}, u32[]{:S(2)}) async-start(bf16[8,32,512]{2,1,0:T(8,128)(2,1)} %bitcast.49), calls=%async_computation | async-start | bytes 524288 | tf_op jit(solution)/shard_map/all_to_all | solution.py:148
  7.4 1.5 %collective-permute-start.2 = (bf16[512,512]{1,0:T(8,128)(2,1)}, bf16[512,512]{1,0:T(8,128)(2,1)}, u32[]{:S(2)}, u32[]{:S(2)}) collective-permute-start(bf16[512,512]{1,0:T(8,128)(2,1)} %param.18), channel_id=1, source_target_pairs={{0,2},{1,3},{2,0},{3,1},{4,6},{5,7},{6,4},{7,5},{8,10},{9,11},{10,... | collective-permute-start | bytes 1572872 | tf_op jit(solution)/shard_map/ppermute | solution.py:59
  8.9 1.3 %compare_and_fusion.1 = (pred[8]{0:T(512)(128)(4,1)}, s32[8]{0:T(128)S(1)}) fusion(s32[8,8]{1,0:T(8,128)} %param.14, s32[]{:T(128)S(6)} %select_n.98), kind=kLoop, calls=%fused_computation.121 | loop fusion | flops 48 | bytes 76 | tf_op jit(solution)/shard_map/jit(_take)/and | solution.py:200
  10.2 1.0 sort.17
  11.2 0.7 constant_dynamic-update-slice_fusion.1
  11.9 0.8 reduce-window.8
  12.9 0.7 constant_dynamic-update-slice_fusion
  13.7 0.7 exponential_negate_fusion
  14.3 2.0 %all-to-all-done = bf16[8,32,512]{2,1,0:T(8,128)(2,1)S(1)} async-done(((bf16[8,32,512]{2,1,0:T(8,128)(2,1)}), bf16[8,32,512]{2,1,0:T(8,128)(2,1)S(1)}, u32[]{:S(2)}, u32[]{:S(2)}) %all-to-all-start) | async-done | bytes 262176 | tf_op jit(solution)/shard_map/all_to_all | solution.py:148
  16.4 0.6 gather_fusion
  17.0 1.6 %collective-permute-start = (bf16[256,512]{1,0:T(8,128)(2,1)S(1)}, bf16[256,512]{1,0:T(8,128)(2,1)S(1)}, u32[]{:S(2)}, u32[]{:S(2)}) collective-permute-start(bf16[256,512]{1,0:T(8,128)(2,1)S(1)} %bitcast_select_fusion), channel_id=1, source_target_pairs={{0,2},{1,3},{2,0},{3,1},{4,6},{5,7},{6,4},{7,5},{8,10},{9,11},{10,... | collective-permute-start | bytes 786440 | tf_op jit(solution)/shard_map/ppermute | solution.py:59
  18.6 0.6 fusion.76
  19.9 1.3 %broadcast_compare_fusion.1 = (pred[256]{0:T(512)(128)(4,1)S(1)}, pred[256]{0:T(512)(128)(4,1)S(1)}, f32[256]{0:T(256)}, f32[256]{0:T(256)}, f32[256]{0:T(256)}) fusion(s32[]{:T(128)} %bitcast.10, s32[259]{0:T(512)S(1)} %convert_reduce_fusion, s32[]{:T(128)S(6)} %select_n.112), kind=kLoop, calls=%fused_computation.131 | loop fusion | flops 2048 | bytes 7688 | tf_op jit(solution)/shard_map/eq | solution.py:119
  21.2 5.4 %collective-permute-done = bf16[256,512]{1,0:T(8,128)(2,1)S(1)} collective-permute-done((bf16[256,512]{1,0:T(8,128)(2,1)S(1)}, bf16[256,512]{1,0:T(8,128)(2,1)S(1)}, u32[]{:S(2)}, u32[]{:S(2)}) %collective-permute-start) | collective-permute-done | bytes 262176 | tf_op jit(solution)/shard_map/ppermute | solution.py:59
  26.8 0.5 iota_compare_fusion.2
  27.3 0.7 fusion.77
  30.6 0.7 slice.121
  31.2 0.6 slice_reduce_fusion.4
  32.0 1.1 %pad_maximum_fusion.2 = bf16[1024,512]{1,0:T(8,128)(2,1)S(1)} fusion(bf16[512,512]{1,0:T(8,128)(2,1)} %collective-permute-done.2, bf16[512,512]{1,0:T(8,128)(2,1)S(1)} %copy-done.1), kind=kLoop, calls=%fused_computation.26 | loop fusion | flops 2097152 | bytes 2097152 | tf_op jit(solution)/shard_map/concatenate | solution.py:60
  33.1 0.6 collective-permute-start.3
  33.7 1.1 %pad_maximum_fusion = bf16[256,2048]{1,0:T(8,128)(2,1)S(1)} fusion(bf16[256,1024]{1,0:T(8,128)(2,1)} %collective-permute-done.1, bf16[256,512]{1,0:T(8,128)(2,1)S(1)} %collective-permute-done, bf16[256,512]{1,0:T(8,128)(2,1)S(1)} %bitcast_select_fusion), kind=kLoop, calls=%fused_computation.24 | loop fusion | flops 3145728 | bytes 2097152 | tf_op jit(solution)/shard_map/concatenate | solution.py:60
  35.0 0.6 copy-done.11
  35.6 0.4 compare_select_fusion
  36.5 0.7 convolution_convert_fusion.1
  37.3 0.7 copy-done.10
  38.0 0.7 divide_multiply_fusion.1
  38.7 1.9 %fusion.17 = bf16[256,512]{1,0:T(8,128)(2,1)S(1)} fusion(bf16[1024,512]{1,0:T(8,128)(2,1)S(1)} %collective-permute-done.3, bf16[512,512]{1,0:T(8,128)(2,1)} %collective-permute-done.2, bf16[512,512]{1,0:T(8,128)(2,1)S(1)} %copy-done.1, bf16[256,1024]{1,0:T(8,128)(2,1)} %collective-permute-done.1, bf16[256,512]{1,0:T(8,128)(2,1)S(1)} %collective-permute-done, ...), kind=kOutput, calls=%fused_computation.15 | convolution fusion | flops 546439168 | bytes 3407872 | tf_op jit(solution)/shard_map/dot_general | solution.py:165
  40.6 3.6 %collective-permute-start.4 = (bf16[3,896]{1,0:T(4,128)(2,1)S(1)}, bf16[3,896]{1,0:T(4,128)(2,1)S(1)}, u32[]{:S(2)}, u32[]{:S(2)}) collective-permute-start(bf16[3,896]{1,0:T(4,128)(2,1)S(1)} %pad_maximum_fusion.7), channel_id=1, source_target_pairs={{0,4},{4,8},{8,12},{12,16},{16,20},{20,24},{24,28},{1,5},{5,9},{9,... | collective-permute-start | bytes 16136 | tf_op jit(solution)/shard_map/ppermute | solution.py:12
  44.3 1.3 %broadcast_select_fusion.1 = f32[6]{0:T(128)} fusion(pred[]{:T(512)} %bitcast.13, f32[6]{0:T(128)S(1)} %slice_reduce_fusion), kind=kLoop, calls=%fused_computation.127 | loop fusion | flops 6 | bytes 49 | tf_op jit(solution)/shard_map/jit(_where)/select_n | solution.py:125
  45.9 1.4 %divide_multiply_fusion = f32[256,896]{1,0:T(8,128)S(1)} fusion(f32[259,896]{1,0:T(8,128)S(1)} %maximum_convert_fusion, f32[896]{0:T(1024)} %get-tuple-element.16, f32[256]{0:T(256)} %get-tuple-element.31, f32[896]{0:T(1024)} %get-tuple-element.17, f32[256]{0:T(256)} %get-tuple-element.32, f32[896]{0:T(1024)} %get-tuple-element.18, ...), kind=kLoop, calls=%fused_computation.37 | loop fusion | flops 3211264 | bytes 4604928 | tf_op jit(solution)/shard_map/jit(silu)/mul | solution.py:177
  47.3 0.8 slice.148
  48.1 1.2 %copy.21 = f32[256,384]{0,1:T(8,128)S(1)} copy(f32[256,384]{1,0:T(8,128)} %slice.148) | data formatting | bytes 786432 | tf_op jit(solution)/shard_map/slice | solution.py:184
  49.2 0.5 fusion.40
  49.9 5.0 %collective-permute-start.5 = (bf16[6,66,256]{2,1,0:T(8,128)(2,1)S(1)}, bf16[6,66,256]{2,1,0:T(8,128)(2,1)S(1)}, u32[]{:S(2)}, u32[]{:S(2)}) collective-permute-start(bf16[6,66,256]{2,1,0:T(8,128)(2,1)S(1)} %fusion.46), channel_id=1, source_target_pairs={{0,8},{4,12},{8,16},{12,20},{16,24},{20,28},{1,9},{5,13},{9,17},{1... | collective-permute-start | bytes 608264 | tf_op jit(solution)/shard_map/ppermute | solution.py:12
  54.9 2.5 %collective-permute-start.6 = (bf16[6,66,256]{2,1,0:T(8,128)(2,1)S(1)}, bf16[6,66,256]{2,1,0:T(8,128)(2,1)S(1)}, u32[]{:S(2)}, u32[]{:S(2)}) collective-permute-start(bf16[6,66,256]{2,1,0:T(8,128)(2,1)S(1)} %fusion.46), channel_id=1, source_target_pairs={{0,4},{4,8},{8,12},{12,16},{16,20},{20,24},{24,28},{1,5},{5,9},{9,... | collective-permute-start | bytes 608264 | tf_op jit(solution)/shard_map/ppermute | solution.py:12
  57.4 0.4 fusion.54
  57.8 0.8 collective-permute-done.5
  58.6 2.4 %collective-permute-done.6 = bf16[6,66,256]{2,1,0:T(8,128)(2,1)S(1)} collective-permute-done((bf16[6,66,256]{2,1,0:T(8,128)(2,1)S(1)}, bf16[6,66,256]{2,1,0:T(8,128)(2,1)S(1)}, u32[]{:S(2)}, u32[]{:S(2)}) %collective-permute-start.6) | collective-permute-done | bytes 202784 | tf_op jit(solution)/shard_map/ppermute | solution.py:12
  61.3 6.9 %collective-permute-start.7 = (bf16[6,66,256]{2,1,0:T(8,128)(2,1)S(1)}, bf16[6,66,256]{2,1,0:T(8,128)(2,1)S(1)}, u32[]{:S(2)}, u32[]{:S(2)}) collective-permute-start(bf16[6,66,256]{2,1,0:T(8,128)(2,1)S(1)} %fusion.47), channel_id=1, source_target_pairs={{0,8},{4,12},{8,16},{12,20},{16,24},{20,28},{1,9},{5,13},{9,17},{1... | collective-permute-start | bytes 608264 | tf_op jit(solution)/shard_map/ppermute | solution.py:12
  68.2 1.9 %fusion.14 = f32[256,6,64]{0,2,1:T(8,128)S(1)} fusion(f32[6,256]{1,0:T(8,128)S(1)} %bitcast.53, f32[256,256]{1,0:T(8,128)S(1)} %fusion.54, pred[256,256]{1,0:T(8,128)(4,1)S(1)} %fusion.51, f32[256,6,64]{0,2,1:T(8,128)S(1)} %bitcast.47, f32[6]{0:T(128)S(1)} %copy-done.13, f32[256,6]{0,1:T(8,128)S(1)} %copy-done.5), kind=kOutput, calls=%fused_computation.14 | convolution fusion | flops 303464448 | bytes 1126424 | tf_op jit(solution)/shard_map/hts,shp->thp/dot_general | solution.py:116
  70.1 1.5 %collective-permute-done.7 = bf16[6,66,256]{2,1,0:T(8,128)(2,1)S(1)} collective-permute-done((bf16[6,66,256]{2,1,0:T(8,128)(2,1)S(1)}, bf16[6,66,256]{2,1,0:T(8,128)(2,1)S(1)}, u32[]{:S(2)}, u32[]{:S(2)}) %collective-permute-start.7) | collective-permute-done | bytes 202784 | tf_op jit(solution)/shard_map/ppermute | solution.py:12
  71.9 5.3 %collective-permute-start.8 = (bf16[6,66,256]{2,1,0:T(8,128)(2,1)S(1)}, bf16[6,66,256]{2,1,0:T(8,128)(2,1)S(1)}, u32[]{:S(2)}, u32[]{:S(2)}) collective-permute-start(bf16[6,66,256]{2,1,0:T(8,128)(2,1)S(1)} %fusion.48), channel_id=1, source_target_pairs={{0,16},{4,20},{8,24},{12,28},{1,17},{5,21},{9,25},{13,29},{2,18},{... | collective-permute-start | bytes 608264 | tf_op jit(solution)/shard_map/ppermute | solution.py:12
  77.2 0.7 fusion.70
  77.9 2.7 %collective-permute-done.8 = bf16[6,66,256]{2,1,0:T(8,128)(2,1)S(1)} collective-permute-done((bf16[6,66,256]{2,1,0:T(8,128)(2,1)S(1)}, bf16[6,66,256]{2,1,0:T(8,128)(2,1)S(1)}, u32[]{:S(2)}, u32[]{:S(2)}) %collective-permute-start.8) | collective-permute-done | bytes 202784 | tf_op jit(solution)/shard_map/ppermute | solution.py:12
  80.7 0.5 fusion.22
  81.8 0.6 gather_fusion.1
  82.6 15.8 %all_to_all.10 = bf16[8,32,384]{2,1,0:T(8,128)(2,1)S(1)} all-to-all(bf16[8,32,384]{2,1,0:T(8,128)(2,1)S(1)} %broadcast_select_fusion), channel_id=1, replica_groups=mesh['seq'=8,'fsdp'=4] {'seq'}, dimensions={0} | all-to-all | bytes 393216 | tf_op jit(solution)/shard_map/all_to_all | solution.py:201
  98.4 0.7 copy.35
  (70 shorter events, 3.1 us)
Async XLA Ops:
  0.0 36.5 %copy-start = (bf16[2048,384]{1,0:T(8,128)(2,1)S(1)}, bf16[2048,384]{1,0:T(8,128)(2,1)}, u32[]{:S(2)}) copy-start(bf16[2048,384]{1,0:T(8,128)(2,1)} %param.16) | copy-start | bytes 4718596
  0.0 27.3 %copy-start.6 = (s32[4]{0:T(128)S(1)}, s32[4]{0:T(128)}, u32[]{:S(2)}) copy-start(s32[4]{0:T(128)} %constant.81.clone) | copy-start | bytes 52
  0.0 32.0 %copy-start.1 = (bf16[512,512]{1,0:T(8,128)(2,1)S(1)}, bf16[512,512]{1,0:T(8,128)(2,1)}, u32[]{:S(2)}) copy-start(bf16[512,512]{1,0:T(8,128)(2,1)} %param.18) | copy-start | bytes 1572868
  0.0 16.3 %all-to-all-start = ((bf16[8,32,512]{2,1,0:T(8,128)(2,1)}), bf16[8,32,512]{2,1,0:T(8,128)(2,1)S(1)}, u32[]{:S(2)}, u32[]{:S(2)}) async-start(bf16[8,32,512]{2,1,0:T(8,128)(2,1)} %bitcast.49), calls=%async_computation | async-start | bytes 524288 | tf_op jit(solution)/shard_map/all_to_all | solution.py:148
  7.4 24.5 %collective-permute-start.2 = (bf16[512,512]{1,0:T(8,128)(2,1)}, bf16[512,512]{1,0:T(8,128)(2,1)}, u32[]{:S(2)}, u32[]{:S(2)}) collective-permute-start(bf16[512,512]{1,0:T(8,128)(2,1)} %param.18), channel_id=1, source_target_pairs={{0,2},{1,3},{2,0},{3,1},{4,6},{5,7},{6,4},{7,5},{8,10},{9,11},{10,... | collective-permute-start | bytes 1572872 | tf_op jit(solution)/shard_map/ppermute | solution.py:59
  17.0 9.6 %collective-permute-start = (bf16[256,512]{1,0:T(8,128)(2,1)S(1)}, bf16[256,512]{1,0:T(8,128)(2,1)S(1)}, u32[]{:S(2)}, u32[]{:S(2)}) collective-permute-start(bf16[256,512]{1,0:T(8,128)(2,1)S(1)} %bitcast_select_fusion), channel_id=1, source_target_pairs={{0,2},{1,3},{2,0},{3,1},{4,6},{5,7},{6,4},{7,5},{8,10},{9,11},{10,... | collective-permute-start | bytes 786440 | tf_op jit(solution)/shard_map/ppermute | solution.py:59
  26.7 7.0 %collective-permute-start.1 = (bf16[256,1024]{1,0:T(8,128)(2,1)S(1)}, bf16[256,1024]{1,0:T(8,128)(2,1)}, u32[]{:S(2)}, u32[]{:S(2)}) collective-permute-start(bf16[256,1024]{1,0:T(8,128)(2,1)S(1)} %pad_maximum_fusion.3), channel_id=1, source_target_pairs={{0,1},{1,0},{2,3},{3,2},{4,5},{5,4},{6,7},{7,6},{8,9},{9,8},{10,11... | collective-permute-start | bytes 1572872 | tf_op jit(solution)/shard_map/ppermute | solution.py:59
  33.1 5.6 %collective-permute-start.3 = (bf16[1024,512]{1,0:T(8,128)(2,1)S(1)}, bf16[1024,512]{1,0:T(8,128)(2,1)S(1)}, u32[]{:S(2)}, u32[]{:S(2)}) collective-permute-start(bf16[1024,512]{1,0:T(8,128)(2,1)S(1)} %pad_maximum_fusion.2), channel_id=1, source_target_pairs={{0,1},{1,0},{2,3},{3,2},{4,5},{5,4},{6,7},{7,6},{8,9},{9,8},{10,11... | collective-permute-start | bytes 3145736 | tf_op jit(solution)/shard_map/ppermute | solution.py:59
  34.8 0.8 copy-start.11
  34.8 0.8 copy-start.12
  36.0 1.3 %copy-start.4 = (f32[256,6]{0,1:T(8,128)}, f32[256,6]{0,1:T(8,128)S(1)}, u32[]{:S(2)}) copy-start(f32[256,6]{0,1:T(8,128)S(1)} %compare_select_fusion) | copy-start | bytes 18436
  36.2 1.1 %copy-start.2 = (f32[256,6]{0,1:T(8,128)}, f32[256,6]{0,1:T(8,128)S(1)}, u32[]{:S(2)}) copy-start(f32[256,6]{0,1:T(8,128)S(1)} %fusion.52) | copy-start | bytes 18436
  36.5 1.4 %copy-start.10 = (bf16[2048,384]{1,0:T(8,128)(2,1)S(1)}, bf16[2048,384]{1,0:T(8,128)(2,1)}, u32[]{:S(2)}) copy-start(bf16[2048,384]{1,0:T(8,128)(2,1)} %param.17) | copy-start | bytes 4718596
  40.6 5.1 %collective-permute-start.4 = (bf16[3,896]{1,0:T(4,128)(2,1)S(1)}, bf16[3,896]{1,0:T(4,128)(2,1)S(1)}, u32[]{:S(2)}, u32[]{:S(2)}) collective-permute-start(bf16[3,896]{1,0:T(4,128)(2,1)S(1)} %pad_maximum_fusion.7), channel_id=1, source_target_pairs={{0,4},{4,8},{8,12},{12,16},{16,20},{20,24},{24,28},{1,5},{5,9},{9,... | collective-permute-start | bytes 16136 | tf_op jit(solution)/shard_map/ppermute | solution.py:12
  47.3 2.0 %copy-start.5 = (f32[256,6]{0,1:T(8,128)S(1)}, f32[256,6]{0,1:T(8,128)}, u32[]{:S(2)}) copy-start(f32[256,6]{0,1:T(8,128)} %copy-done.4) | copy-start | bytes 18436
  47.3 2.5 %copy-start.9 = (f32[6]{0:T(128)S(1)}, f32[6]{0:T(128)}, u32[]{:S(2)}) copy-start(f32[6]{0:T(128)} %broadcast_select_fusion.1) | copy-start | bytes 76
  47.3 2.5 %copy-start.7 = (pred[66]{0:T(512)(128)(4,1)S(1)}, pred[66]{0:T(512)(128)(4,1)}, u32[]{:S(2)}) copy-start(pred[66]{0:T(512)(128)(4,1)} %iota_compare_fusion.2) | copy-start | bytes 202
  49.9 8.7 %collective-permute-start.5 = (bf16[6,66,256]{2,1,0:T(8,128)(2,1)S(1)}, bf16[6,66,256]{2,1,0:T(8,128)(2,1)S(1)}, u32[]{:S(2)}, u32[]{:S(2)}) collective-permute-start(bf16[6,66,256]{2,1,0:T(8,128)(2,1)S(1)} %fusion.46), channel_id=1, source_target_pairs={{0,8},{4,12},{8,16},{12,20},{16,24},{20,28},{1,9},{5,13},{9,17},{1... | collective-permute-start | bytes 608264 | tf_op jit(solution)/shard_map/ppermute | solution.py:12
  54.9 6.1 %collective-permute-start.6 = (bf16[6,66,256]{2,1,0:T(8,128)(2,1)S(1)}, bf16[6,66,256]{2,1,0:T(8,128)(2,1)S(1)}, u32[]{:S(2)}, u32[]{:S(2)}) collective-permute-start(bf16[6,66,256]{2,1,0:T(8,128)(2,1)S(1)} %fusion.46), channel_id=1, source_target_pairs={{0,4},{4,8},{8,12},{12,16},{16,20},{20,24},{24,28},{1,5},{5,9},{9,... | collective-permute-start | bytes 608264 | tf_op jit(solution)/shard_map/ppermute | solution.py:12
  57.8 10.4 %copy-start.3 = (f32[256,6]{0,1:T(8,128)S(1)}, f32[256,6]{0,1:T(8,128)}, u32[]{:S(2)}) copy-start(f32[256,6]{0,1:T(8,128)} %copy-done.2) | copy-start | bytes 18436
  57.8 10.4 %copy-start.13 = (f32[6]{0:T(128)S(1)}, f32[6]{0:T(128)}, u32[]{:S(2)}) copy-start(f32[6]{0:T(128)} %param.24) | copy-start | bytes 76
  61.3 10.4 %collective-permute-start.7 = (bf16[6,66,256]{2,1,0:T(8,128)(2,1)S(1)}, bf16[6,66,256]{2,1,0:T(8,128)(2,1)S(1)}, u32[]{:S(2)}, u32[]{:S(2)}) collective-permute-start(bf16[6,66,256]{2,1,0:T(8,128)(2,1)S(1)} %fusion.47), channel_id=1, source_target_pairs={{0,8},{4,12},{8,16},{12,20},{16,24},{20,28},{1,9},{5,13},{9,17},{1... | collective-permute-start | bytes 608264 | tf_op jit(solution)/shard_map/ppermute | solution.py:12
  71.9 8.8 %collective-permute-start.8 = (bf16[6,66,256]{2,1,0:T(8,128)(2,1)S(1)}, bf16[6,66,256]{2,1,0:T(8,128)(2,1)S(1)}, u32[]{:S(2)}, u32[]{:S(2)}) collective-permute-start(bf16[6,66,256]{2,1,0:T(8,128)(2,1)S(1)} %fusion.48), channel_id=1, source_target_pairs={{0,16},{4,20},{8,24},{12,28},{1,17},{5,21},{9,25},{13,29},{2,18},{... | collective-permute-start | bytes 608264 | tf_op jit(solution)/shard_map/ppermute | solution.py:12
  80.7 1.8 %copy-start.8 = (pred[8]{0:T(512)(128)(4,1)S(1)}, pred[8]{0:T(512)(128)(4,1)}, u32[]{:S(2)}) copy-start(pred[8]{0:T(512)(128)(4,1)} %get-tuple-element.19) | copy-start | bytes 28

commit v10 on v9

--- a/solution.py
+++ b/solution.py
@@ -78,6 +78,28 @@
         for index in range(count)
     ]
     return jnp.concatenate(parts, axis=dim)
+
+
+def summed_columns(partial, axis):
+    count = lax.axis_size(axis)
+    if count & (count - 1) or partial.shape[1] % 2:
+        return lax.psum(partial, axis).astype(jnp.bfloat16)
+    if count == 1:
+        return partial.astype(jnp.bfloat16)
+    place = lax.axis_index(axis)
+    half = partial.shape[1] // 2
+    side = place % 2
+    kept = lax.dynamic_slice_in_dim(partial, side * half, half, axis=1)
+    sent = lax.dynamic_slice_in_dim(partial, (1 - side) * half, half, axis=1)
+    kept = kept + lax.ppermute(sent, axis, [(i, i ^ 1) for i in range(count)])
+    bit = 2
+    while bit < count:
+        kept = kept + lax.ppermute(kept, axis, [(i, i ^ bit) for i in range(count)])
+        bit *= 2
+    kept = kept.astype(jnp.bfloat16)
+    other = lax.ppermute(kept, axis, [(i, i ^ 1) for i in range(count)])
+    both = jnp.concatenate([kept, other], axis=1)
+    return jnp.where(side == 0, both, jnp.concatenate([other, kept], axis=1))
 
 
 def segment_of(positions, lengths):
@@ -153,7 +175,8 @@
     heads_dev = step_weight.shape[1]
     head_dim = inner_dev // heads_dev
     state_dim = shared_weight.shape[1] // 2
-    w_held, _ = exchange(shared_weight, "fsdp", 0)
+    bc_partial = jnp.dot(stream_block, shared_weight, preferred_element_type=jnp.float32)
+    bc_raw = summed_columns(bc_partial, "fsdp")
     feature_held, codes = exchange(stream_block, "fsdp", 1)
     feature_part = to_natural(feature_held, codes, "fsdp", 1)
     x_acc, z_acc, step_acc = tuple(
@@ -162,10 +185,8 @@
             for weight in (x_weight, z_weight, step_weight)
         )
     )
-    bc_acc = jnp.dot(feature_held, w_held, preferred_element_type=jnp.float32)
     x_raw = x_acc.astype(jnp.bfloat16)
     z_raw = z_acc.astype(jnp.bfloat16)
-    bc_raw = bc_acc.astype(jnp.bfloat16)
     step_size = jax.nn.softplus(step_acc + step_bias[None, :])
     mixed_in = jnp.concatenate([x_raw, bc_raw], axis=1)
     conv_width = conv_heads.shape[0]

time: 99.9 us -> 98.8 us (0.989)
  waiting for transfers between devices: 14.8 us -> 23.8 us
  other arithmetic: 12.5 us -> 7.83 us
  starting transfers between devices: 34.4 us -> 30 us
  blocking collectives: 15.8 us -> 18.6 us
  local copies, waits for them, and re-layouts: 10.6 us -> 8.56 us
  matrix products: 7.24 us -> 5.63 us
    ppermute x0 -> x3, waiting for transfers between devices: none -> 5.06 us  [the longest x1 5.06 us: summed_columns(): kept = kept + lax.ppermute(kept, axis, [(i, i ^ bit) for i in range(count)])]
    ppermute x5, starting transfers between devices: 23.3 us -> 19.5 us  [shifted(): return lax.ppermute(array, axis, pairs)]
    all_to_all x1, blocking collectives: 15.8 us -> 18.6 us  [per_device(): lax.all_to_all(outgoing, 'seq', split_axis=0, concat_axis=0, tiled=True)]
    all_to_all x1, waiting for transfers between devices: 2.02 us -> 4.13 us  [per_device(): lax.all_to_all(slot_rows, 'seq', split_axis=0, concat_axis=0, tiled=True)]
    ppermute x4 -> x2, starting transfers between devices: 3.68 us -> 1.63 us  [exchange(): other = lax.ppermute(held, axis, [(i, i ^ bit) for i in range(count)])]
    dot_general x1, matrix products: 1.9 us -> 0.29 us  [per_device(): jnp.dot(stream_block, shared_weight, preferred_element_type=jnp.float32)]
    ppermute x0 -> x3, starting transfers between devices: none -> 1.45 us  [the longest x1 1.31 us: summed_columns(): kept = kept + lax.ppermute(kept, axis, [(i, i ^ bit) for i in range(count)])]
    concatenate x3 -> x2, other arithmetic: 2.31 us -> 1.2 us  [exchange(): held = jnp.concatenate([held, other], axis=dim)]
  transfers between devices with their start and end apart: 10 -> 11, of which waited for: 6 -> 8; matrix products, arithmetic and copies ran while one was open for 20% -> 10% of each run, Pallas kernels for 0% -> 0%
where the time goes in v10:
time: 98.8 us; the launch traced here: 98.2 us
  starting transfers between devices  30 us (30%)
  waiting for transfers between devices  23.8 us (24%)
  blocking collectives  18.6 us (19%)
  local copies, waits for them, and re-layouts  8.56 us (9%)
  other arithmetic  7.83 us (8%)
  matrix products  5.63 us (6%)
  between operations  3.71 us (4%)
    ppermute x5, starting transfers between devices, shifted(): return lax.ppermute(array, axis, pairs)  19.5 us
    all_to_all x1, blocking collectives, per_device(): lax.all_to_all(outgoing, 'seq', split_axis=0, concat_axis=0, tiled=True)  18.6 us
    ppermute x5, waiting for transfers between devices, shifted(): return lax.ppermute(array, axis, pairs)  8.39 us
    all_to_all x1, starting transfers between devices, per_device(): lax.all_to_all(slot_rows, 'seq', split_axis=0, concat_axis=0, tiled=True)  7.41 us
    ppermute x2, waiting for transfers between devices, exchange(): other = lax.ppermute(held, axis, [(i, i ^ bit) for i in range(count)])  6.25 us
    ppermute x1, waiting for transfers between devices, summed_columns(): kept = kept + lax.ppermute(kept, axis, [(i, i ^ bit) for i in range(count)])  5.06 us
    all_to_all x1, waiting for transfers between devices, per_device(): lax.all_to_all(slot_rows, 'seq', split_axis=0, concat_axis=0, tiled=True)  4.13 us
    unnamed x25, local copies, waits for them, and re-layouts  2.04 us
  transfers between devices with their start and end apart: 11, of which 8 were waited for; matrix products, arithmetic and copies ran while one was open for 10% of the time, Pallas kernels for 0%

profile of v10, /device:TPU:0, one launch (start us, length us, event | category | flops | bytes accessed | tf_op | source)
XLA Modules:
  0.0 98.2 jit_solution(2667492736511522776)
XLA Ops:
  0.0 7.4 %all-to-all-start = ((bf16[8,32,512]{2,1,0:T(8,128)(2,1)}), bf16[8,32,512]{2,1,0:T(8,128)(2,1)S(1)}, u32[]{:S(2)}, u32[]{:S(2)}) async-start(bf16[8,32,512]{2,1,0:T(8,128)(2,1)} %bitcast.51), calls=%async_computation | async-start | bytes 524288 | tf_op jit(solution)/shard_map/all_to_all | solution.py:170
  7.4 0.8 reduce-window.8
  8.3 0.7 compare_and_fusion.1
  9.0 1.0 sort.17
  10.2 0.6 fusion.66
  11.5 0.7 broadcast_compare_fusion.1
  12.2 4.1 %all-to-all-done = bf16[8,32,512]{2,1,0:T(8,128)(2,1)S(1)} async-done(((bf16[8,32,512]{2,1,0:T(8,128)(2,1)}), bf16[8,32,512]{2,1,0:T(8,128)(2,1)S(1)}, u32[]{:S(2)}, u32[]{:S(2)}) %all-to-all-start) | async-done | bytes 262176 | tf_op jit(solution)/shard_map/all_to_all | solution.py:170
  16.3 0.6 gather_fusion
  17.1 0.3 fusion.68
  17.7 1.6 %collective-permute-start = (bf16[256,512]{1,0:T(8,128)(2,1)S(1)}, bf16[256,512]{1,0:T(8,128)(2,1)S(1)}, u32[]{:S(2)}, u32[]{:S(2)}) collective-permute-start(bf16[256,512]{1,0:T(8,128)(2,1)S(1)} %bitcast_select_fusion), channel_id=1, source_target_pairs={{0,2},{1,3},{2,0},{3,1},{4,6},{5,7},{6,4},{7,5},{8,10},{9,11},{10,... | collective-permute-start | bytes 786440 | tf_op jit(solution)/shard_map/ppermute | solution.py:59
  19.3 1.3 %collective-permute-start.3 = (f32[256,256]{1,0:T(8,128)S(1)}, f32[256,256]{1,0:T(8,128)S(1)}, u32[]{:S(2)}, u32[]{:S(2)}) collective-permute-start(f32[256,256]{1,0:T(8,128)S(1)} %dynamic-slice_add_fusion), channel_id=1, source_target_pairs={{0,2},{1,3},{2,0},{3,1},{4,6},{5,7},{6,4},{7,5},{8,10},{9,11},{10,... | collective-permute-start | bytes 786440 | tf_op jit(solution)/shard_map/ppermute | solution.py:97
  20.6 6.2 %collective-permute-done = bf16[256,512]{1,0:T(8,128)(2,1)S(1)} collective-permute-done((bf16[256,512]{1,0:T(8,128)(2,1)S(1)}, bf16[256,512]{1,0:T(8,128)(2,1)S(1)}, u32[]{:S(2)}, u32[]{:S(2)}) %collective-permute-start) | collective-permute-done | bytes 262176 | tf_op jit(solution)/shard_map/ppermute | solution.py:59
  27.0 5.1 %collective-permute-done.3 = f32[256,256]{1,0:T(8,128)S(1)} collective-permute-done((f32[256,256]{1,0:T(8,128)S(1)}, f32[256,256]{1,0:T(8,128)S(1)}, u32[]{:S(2)}, u32[]{:S(2)}) %collective-permute-start.3) | collective-permute-done | bytes 262176 | tf_op jit(solution)/shard_map/ppermute | solution.py:97
  32.2 0.7 fusion.67
  35.4 0.6 slice.121
  36.2 1.1 %pad_maximum_fusion = bf16[256,2048]{1,0:T(8,128)(2,1)S(1)} fusion(bf16[256,1024]{1,0:T(8,128)(2,1)} %collective-permute-done.1, bf16[256,512]{1,0:T(8,128)(2,1)S(1)} %collective-permute-done, bf16[256,512]{1,0:T(8,128)(2,1)S(1)} %bitcast_select_fusion), kind=kLoop, calls=%fused_computation.17 | loop fusion | flops 3145728 | bytes 2097152 | tf_op jit(solution)/shard_map/concatenate | solution.py:60
  37.5 0.6 copy-done.6
  38.1 0.4 compare_select_fusion
  38.5 0.2 fusion.43
  38.7 0.2 slice_reduce_fusion
  39.0 0.7 convolution_convert_fusion.1
  39.7 0.7 copy-done.5
  40.4 0.7 divide_multiply_fusion.1
  41.2 3.3 %collective-permute-start.5 = (bf16[3,896]{1,0:T(4,128)(2,1)S(1)}, bf16[3,896]{1,0:T(4,128)(2,1)S(1)}, u32[]{:S(2)}, u32[]{:S(2)}) collective-permute-start(bf16[3,896]{1,0:T(4,128)(2,1)S(1)} %pad_maximum_fusion.6), channel_id=1, source_target_pairs={{0,4},{4,8},{8,12},{12,16},{16,20},{20,24},{24,28},{1,5},{5,9},{9,... | collective-permute-start | bytes 16136 | tf_op jit(solution)/shard_map/ppermute | solution.py:12
  44.6 0.6 broadcast_select_fusion.1
  45.2 0.2 copy.22
  45.4 0.5 collective-permute-done.5
  45.9 0.7 divide_multiply_fusion
  46.6 0.8 slice.148
  47.4 1.2 %copy.21 = f32[256,384]{0,1:T(8,128)S(1)} copy(f32[256,384]{1,0:T(8,128)} %slice.148) | data formatting | bytes 786432 | tf_op jit(solution)/shard_map/slice | solution.py:205
  48.5 0.5 fusion.31
  49.2 4.2 %collective-permute-start.7 = (bf16[6,66,256]{2,1,0:T(8,128)(2,1)S(1)}, bf16[6,66,256]{2,1,0:T(8,128)(2,1)S(1)}, u32[]{:S(2)}, u32[]{:S(2)}) collective-permute-start(bf16[6,66,256]{2,1,0:T(8,128)(2,1)S(1)} %fusion.37), channel_id=1, source_target_pairs={{0,4},{4,8},{8,12},{12,16},{16,20},{20,24},{24,28},{1,5},{5,9},{9,... | collective-permute-start | bytes 608264 | tf_op jit(solution)/shard_map/ppermute | solution.py:12
  53.5 2.5 %collective-permute-start.6 = (bf16[6,66,256]{2,1,0:T(8,128)(2,1)S(1)}, bf16[6,66,256]{2,1,0:T(8,128)(2,1)S(1)}, u32[]{:S(2)}, u32[]{:S(2)}) collective-permute-start(bf16[6,66,256]{2,1,0:T(8,128)(2,1)S(1)} %fusion.37), channel_id=1, source_target_pairs={{0,8},{4,12},{8,16},{12,20},{16,24},{20,28},{1,9},{5,13},{9,17},{1... | collective-permute-start | bytes 608264 | tf_op jit(solution)/shard_map/ppermute | solution.py:12
  55.9 0.4 fusion.45
  56.4 1.2 %collective-permute-done.7 = bf16[6,66,256]{2,1,0:T(8,128)(2,1)S(1)} collective-permute-done((bf16[6,66,256]{2,1,0:T(8,128)(2,1)S(1)}, bf16[6,66,256]{2,1,0:T(8,128)(2,1)S(1)}, u32[]{:S(2)}, u32[]{:S(2)}) %collective-permute-start.7) | collective-permute-done | bytes 202784 | tf_op jit(solution)/shard_map/ppermute | solution.py:12
  57.6 2.4 %collective-permute-done.6 = bf16[6,66,256]{2,1,0:T(8,128)(2,1)S(1)} collective-permute-done((bf16[6,66,256]{2,1,0:T(8,128)(2,1)S(1)}, bf16[6,66,256]{2,1,0:T(8,128)(2,1)S(1)}, u32[]{:S(2)}, u32[]{:S(2)}) %collective-permute-start.6) | collective-permute-done | bytes 202784 | tf_op jit(solution)/shard_map/ppermute | solution.py:12
  60.3 5.2 %collective-permute-start.8 = (bf16[6,66,256]{2,1,0:T(8,128)(2,1)S(1)}, bf16[6,66,256]{2,1,0:T(8,128)(2,1)S(1)}, u32[]{:S(2)}, u32[]{:S(2)}) collective-permute-start(bf16[6,66,256]{2,1,0:T(8,128)(2,1)S(1)} %fusion.38), channel_id=1, source_target_pairs={{0,8},{4,12},{8,16},{12,20},{16,24},{20,28},{1,9},{5,13},{9,17},{1... | collective-permute-start | bytes 608264 | tf_op jit(solution)/shard_map/ppermute | solution.py:12
  65.5 1.9 %fusion.8 = f32[256,6,64]{0,2,1:T(8,128)S(1)} fusion(f32[6,256]{1,0:T(8,128)S(1)} %bitcast.55, f32[256,256]{1,0:T(8,128)S(1)} %fusion.45, pred[256,256]{1,0:T(8,128)(4,1)S(1)} %fusion.42, f32[256,6,64]{0,2,1:T(8,128)S(1)} %bitcast.49, f32[6]{0:T(128)S(1)} %copy-done.9, f32[256,6]{0,1:T(8,128)S(1)} %compare_select_fusion), kind=kOutput, calls=%fused_computation.8 | convolution fusion | flops 303464448 | bytes 1126424 | tf_op jit(solution)/shard_map/hts,shp->thp/dot_general | solution.py:138
  67.4 1.5 %collective-permute-done.8 = bf16[6,66,256]{2,1,0:T(8,128)(2,1)S(1)} collective-permute-done((bf16[6,66,256]{2,1,0:T(8,128)(2,1)S(1)}, bf16[6,66,256]{2,1,0:T(8,128)(2,1)S(1)}, u32[]{:S(2)}, u32[]{:S(2)}) %collective-permute-start.8) | collective-permute-done | bytes 202784 | tf_op jit(solution)/shard_map/ppermute | solution.py:12
  69.2 4.4 %collective-permute-start.9 = (bf16[6,66,256]{2,1,0:T(8,128)(2,1)S(1)}, bf16[6,66,256]{2,1,0:T(8,128)(2,1)S(1)}, u32[]{:S(2)}, u32[]{:S(2)}) collective-permute-start(bf16[6,66,256]{2,1,0:T(8,128)(2,1)S(1)} %fusion.39), channel_id=1, source_target_pairs={{0,16},{4,20},{8,24},{12,28},{1,17},{5,21},{9,25},{13,29},{2,18},{... | collective-permute-start | bytes 608264 | tf_op jit(solution)/shard_map/ppermute | solution.py:12
  73.6 0.7 fusion.61
  74.3 2.7 %collective-permute-done.9 = bf16[6,66,256]{2,1,0:T(8,128)(2,1)S(1)} collective-permute-done((bf16[6,66,256]{2,1,0:T(8,128)(2,1)S(1)}, bf16[6,66,256]{2,1,0:T(8,128)(2,1)S(1)}, u32[]{:S(2)}, u32[]{:S(2)}) %collective-permute-start.9) | collective-permute-done | bytes 202784 | tf_op jit(solution)/shard_map/ppermute | solution.py:12
  77.0 0.5 fusion.13
  77.6 0.3 copy.23
  77.9 0.3 convert_element_type.109
  78.2 0.6 gather_fusion.1
  78.9 18.6 %all_to_all.10 = bf16[8,32,384]{2,1,0:T(8,128)(2,1)S(1)} all-to-all(bf16[8,32,384]{2,1,0:T(8,128)(2,1)S(1)} %broadcast_select_fusion), channel_id=1, replica_groups=mesh['seq'=8,'fsdp'=4] {'seq'}, dimensions={0} | all-to-all | bytes 393216 | tf_op jit(solution)/shard_map/all_to_all | solution.py:222
  97.5 0.7 copy.35
  (67 shorter events, 2.3 us)
Async XLA Ops:
  0.0 39.0 %copy-start = (bf16[2048,384]{1,0:T(8,128)(2,1)S(1)}, bf16[2048,384]{1,0:T(8,128)(2,1)}, u32[]{:S(2)}) copy-start(bf16[2048,384]{1,0:T(8,128)(2,1)} %param.16) | copy-start | bytes 4718596
  0.0 17.0 %copy-start.1 = (bf16[512,512]{1,0:T(8,128)(2,1)S(1)}, bf16[512,512]{1,0:T(8,128)(2,1)}, u32[]{:S(2)}) copy-start(bf16[512,512]{1,0:T(8,128)(2,1)} %param.18) | copy-start | bytes 1572868
  0.0 16.3 %all-to-all-start = ((bf16[8,32,512]{2,1,0:T(8,128)(2,1)}), bf16[8,32,512]{2,1,0:T(8,128)(2,1)S(1)}, u32[]{:S(2)}, u32[]{:S(2)}) async-start(bf16[8,32,512]{2,1,0:T(8,128)(2,1)} %bitcast.51), calls=%async_computation | async-start | bytes 524288 | tf_op jit(solution)/shard_map/all_to_all | solution.py:170
  7.4 10.1 %copy-start.7 = (f32[6]{0:T(128)S(1)}, f32[6]{0:T(128)}, u32[]{:S(2)}) copy-start(f32[6]{0:T(128)} %param.23) | copy-start | bytes 76
  16.9 3.7 %copy-start.4 = (f32[4,384]{1,0:T(4,128)S(1)}, f32[4,384]{1,0:T(4,128)}, u32[]{:S(2)}) copy-start(f32[4,384]{1,0:T(4,128)} %param.20) | copy-start | bytes 18436
  16.9 3.7 %copy-start.3 = (f32[4,512]{1,0:T(4,128)S(1)}, f32[4,512]{1,0:T(4,128)}, u32[]{:S(2)}) copy-start(f32[4,512]{1,0:T(4,128)} %param.21) | copy-start | bytes 24580
  17.4 14.9 %copy-start.2 = (s32[4]{0:T(128)S(1)}, s32[4]{0:T(128)}, u32[]{:S(2)}) copy-start(s32[4]{0:T(128)} %constant.91.clone) | copy-start | bytes 52
  17.4 1.9 %collective-permute-start.2 = (f32[256,256]{1,0:T(8,128)S(1)}, f32[256,256]{1,0:T(8,128)S(1)}, u32[]{:S(2)}, u32[]{:S(2)}) collective-permute-start(f32[256,256]{1,0:T(8,128)S(1)} %constant_dynamic-slice_fusion), channel_id=1, source_target_pairs={{0,1},{1,0},{2,3},{3,2},{4,5},{5,4},{6,7},{7,6},{8,9},{9,8},{10,11... | collective-permute-start | bytes 786440 | tf_op jit(solution)/shard_map/ppermute | solution.py:94
  17.7 9.2 %collective-permute-start = (bf16[256,512]{1,0:T(8,128)(2,1)S(1)}, bf16[256,512]{1,0:T(8,128)(2,1)S(1)}, u32[]{:S(2)}, u32[]{:S(2)}) collective-permute-start(bf16[256,512]{1,0:T(8,128)(2,1)S(1)} %bitcast_select_fusion), channel_id=1, source_target_pairs={{0,2},{1,3},{2,0},{3,1},{4,6},{5,7},{6,4},{7,5},{8,10},{9,11},{10,... | collective-permute-start | bytes 786440 | tf_op jit(solution)/shard_map/ppermute | solution.py:59
  19.3 12.8 %collective-permute-start.3 = (f32[256,256]{1,0:T(8,128)S(1)}, f32[256,256]{1,0:T(8,128)S(1)}, u32[]{:S(2)}, u32[]{:S(2)}) collective-permute-start(f32[256,256]{1,0:T(8,128)S(1)} %dynamic-slice_add_fusion), channel_id=1, source_target_pairs={{0,2},{1,3},{2,0},{3,1},{4,6},{5,7},{6,4},{7,5},{8,10},{9,11},{10,... | collective-permute-start | bytes 786440 | tf_op jit(solution)/shard_map/ppermute | solution.py:97
  26.9 9.3 %collective-permute-start.1 = (bf16[256,1024]{1,0:T(8,128)(2,1)S(1)}, bf16[256,1024]{1,0:T(8,128)(2,1)}, u32[]{:S(2)}, u32[]{:S(2)}) collective-permute-start(bf16[256,1024]{1,0:T(8,128)(2,1)S(1)} %pad_maximum_fusion.2), channel_id=1, source_target_pairs={{0,1},{1,0},{2,3},{3,2},{4,5},{5,4},{6,7},{7,6},{8,9},{9,8},{10,11... | collective-permute-start | bytes 1572872 | tf_op jit(solution)/shard_map/ppermute | solution.py:59
  32.1 4.0 %collective-permute-start.4 = (bf16[256,256]{1,0:T(8,128)(2,1)S(1)}, bf16[256,256]{1,0:T(8,128)(2,1)S(1)}, u32[]{:S(2)}, u32[]{:S(2)}) collective-permute-start(bf16[256,256]{1,0:T(8,128)(2,1)S(1)} %add_convert_fusion), channel_id=1, source_target_pairs={{0,1},{1,0},{2,3},{3,2},{4,5},{5,4},{6,7},{7,6},{8,9},{9,8},{10,11... | collective-permute-start | bytes 393224 | tf_op jit(solution)/shard_map/ppermute | solution.py:100
  37.4 0.8 copy-start.6
  37.4 0.8 copy-start.8
  39.0 1.4 %copy-start.5 = (bf16[2048,384]{1,0:T(8,128)(2,1)S(1)}, bf16[2048,384]{1,0:T(8,128)(2,1)}, u32[]{:S(2)}) copy-start(bf16[2048,384]{1,0:T(8,128)(2,1)} %param.17) | copy-start | bytes 4718596
  41.2 4.7 %collective-permute-start.5 = (bf16[3,896]{1,0:T(4,128)(2,1)S(1)}, bf16[3,896]{1,0:T(4,128)(2,1)S(1)}, u32[]{:S(2)}, u32[]{:S(2)}) collective-permute-start(bf16[3,896]{1,0:T(4,128)(2,1)S(1)} %pad_maximum_fusion.6), channel_id=1, source_target_pairs={{0,4},{4,8},{8,12},{12,16},{16,20},{20,24},{24,28},{1,5},{5,9},{9,... | collective-permute-start | bytes 16136 | tf_op jit(solution)/shard_map/ppermute | solution.py:12
  49.2 8.3 %collective-permute-start.7 = (bf16[6,66,256]{2,1,0:T(8,128)(2,1)S(1)}, bf16[6,66,256]{2,1,0:T(8,128)(2,1)S(1)}, u32[]{:S(2)}, u32[]{:S(2)}) collective-permute-start(bf16[6,66,256]{2,1,0:T(8,128)(2,1)S(1)} %fusion.37), channel_id=1, source_target_pairs={{0,4},{4,8},{8,12},{12,16},{16,20},{20,24},{24,28},{1,5},{5,9},{9,... | collective-permute-start | bytes 608264 | tf_op jit(solution)/shard_map/ppermute | solution.py:12
  53.5 6.6 %collective-permute-start.6 = (bf16[6,66,256]{2,1,0:T(8,128)(2,1)S(1)}, bf16[6,66,256]{2,1,0:T(8,128)(2,1)S(1)}, u32[]{:S(2)}, u32[]{:S(2)}) collective-permute-start(bf16[6,66,256]{2,1,0:T(8,128)(2,1)S(1)} %fusion.37), channel_id=1, source_target_pairs={{0,8},{4,12},{8,16},{12,20},{16,24},{20,28},{1,9},{5,13},{9,17},{1... | collective-permute-start | bytes 608264 | tf_op jit(solution)/shard_map/ppermute | solution.py:12
  56.3 9.1 %copy-start.9 = (f32[6]{0:T(128)S(1)}, f32[6]{0:T(128)}, u32[]{:S(2)}) copy-start(f32[6]{0:T(128)} %param.24) | copy-start | bytes 76
  60.3 8.6 %collective-permute-start.8 = (bf16[6,66,256]{2,1,0:T(8,128)(2,1)S(1)}, bf16[6,66,256]{2,1,0:T(8,128)(2,1)S(1)}, u32[]{:S(2)}, u32[]{:S(2)}) collective-permute-start(bf16[6,66,256]{2,1,0:T(8,128)(2,1)S(1)} %fusion.38), channel_id=1, source_target_pairs={{0,8},{4,12},{8,16},{12,20},{16,24},{20,28},{1,9},{5,13},{9,17},{1... | collective-permute-start | bytes 608264 | tf_op jit(solution)/shard_map/ppermute | solution.py:12
  69.2 7.9 %collective-permute-start.9 = (bf16[6,66,256]{2,1,0:T(8,128)(2,1)S(1)}, bf16[6,66,256]{2,1,0:T(8,128)(2,1)S(1)}, u32[]{:S(2)}, u32[]{:S(2)}) collective-permute-start(bf16[6,66,256]{2,1,0:T(8,128)(2,1)S(1)} %fusion.39), channel_id=1, source_target_pairs={{0,16},{4,20},{8,24},{12,28},{1,17},{5,21},{9,25},{13,29},{2,18},{... | collective-permute-start | bytes 608264 | tf_op jit(solution)/shard_map/ppermute | solution.py:12

commit v11 on v10

--- a/solution.py
+++ b/solution.py
@@ -102,6 +102,30 @@
     return jnp.where(side == 0, both, jnp.concatenate([other, kept], axis=1))
 
 
+def scattered_columns(partial, axis):
+    count = lax.axis_size(axis)
+    place = lax.axis_index(axis)
+    bit = 1
+    while bit < count:
+        half = partial.shape[1] // 2
+        side = (place // bit) % 2
+        kept = lax.dynamic_slice_in_dim(partial, side * half, half, axis=1)
+        sent = lax.dynamic_slice_in_dim(partial, (1 - side) * half, half, axis=1)
+        partial = kept + lax.ppermute(sent, axis, [(i, i ^ bit) for i in range(count)])
+        bit *= 2
+    return partial.astype(jnp.bfloat16)
+
+
+def bit_reversed(index, count):
+    out, bit, top = 0, 1, count // 2
+    while bit < count:
+        if index & bit:
+            out += top
+        bit *= 2
+        top //= 2
+    return out
+
+
 def segment_of(positions, lengths):
     prompt_ends = jnp.cumsum(lengths)
     counted = (positions[:, None] >= prompt_ends[None, :]).astype(jnp.int32)
@@ -166,19 +190,59 @@
     own_index = lax.axis_index("seq")
     tok_dev = tokens.shape[0]
     piece_rows = tok_dev // seq_count
-    slot_rows = tokens.reshape(seq_count, piece_rows, tokens.shape[1])
+    model_cols = tokens.shape[1]
+    fsdp_count = lax.axis_size("fsdp")
+    fsdp_place = lax.axis_index("fsdp")
+    split_ok = fsdp_count & (fsdp_count - 1) == 0 and shared_weight.shape[1] % fsdp_count == 0
+    if split_ok:
+        bc_quarter = scattered_columns(
+            jnp.dot(tokens, shared_weight, preferred_element_type=jnp.float32), "fsdp"
+        )
+        quarter = bc_quarter.shape[1]
+        sent_rows = jnp.concatenate([tokens, bc_quarter], axis=1)
+    else:
+        quarter = 0
+        sent_rows = tokens
+    width = sent_rows.shape[1]
+    slot_rows = sent_rows.reshape(seq_count, piece_rows, width)
     arrived = lax.all_to_all(slot_rows, "seq", split_axis=0, concat_axis=0, tiled=True)
     dealt_row = lax.dynamic_slice_in_dim(deal_order, own_index, 1, 0)[0]
     inverse = jnp.argsort(dealt_row)
-    stream_block = jnp.take(arrived, inverse, axis=0).reshape(tok_dev, tokens.shape[1])
+    stream_block = jnp.take(arrived, inverse, axis=0).reshape(tok_dev, width)
     inner_dev = x_weight.shape[1]
     heads_dev = step_weight.shape[1]
     head_dim = inner_dev // heads_dev
     state_dim = shared_weight.shape[1] // 2
-    bc_partial = jnp.dot(stream_block, shared_weight, preferred_element_type=jnp.float32)
-    bc_raw = summed_columns(bc_partial, "fsdp")
     feature_held, codes = exchange(stream_block, "fsdp", 1)
-    feature_part = to_natural(feature_held, codes, "fsdp", 1)
+    if codes is None:
+        codes = list(range(fsdp_count))
+        fsdp_place = 0
+    where_code = [0] * fsdp_count
+    for position, code in enumerate(codes):
+        where_code[code] = position
+    table = jnp.asarray(where_code, jnp.int32)
+
+    def piece_of(source, start, size):
+        position = table[jnp.bitwise_xor(source, fsdp_place)]
+        return lax.dynamic_slice_in_dim(feature_held, position * width + start, size, axis=1)
+
+    feature_part = jnp.concatenate(
+        [piece_of(index, 0, model_cols) for index in range(fsdp_count)], axis=1
+    )
+    if split_ok:
+        bc_raw = jnp.concatenate(
+            [
+                piece_of(bit_reversed(block, fsdp_count), model_cols, quarter)
+                for block in range(fsdp_count)
+            ],
+            axis=1,
+        )
+    else:
+        bc_raw = jnp.dot(
+            feature_part,
+            lax.all_gather(shared_weight, "fsdp", axis=0, tiled=True),
+            preferred_element_type=jnp.float32,
+        ).astype(jnp.bfloat16)
     x_acc, z_acc, step_acc = tuple(
         (
             jnp.dot(feature_part, weight, preferred_element_type=jnp.float32)

time: 98.8 us -> 100 us (1.012)
  starting transfers between devices: 30 us -> 32 us
  matrix products: 5.63 us -> 6.89 us
  other arithmetic: 7.83 us -> 6.75 us
    all_to_all x1, waiting for transfers between devices: 4.13 us -> 8.42 us  [per_device(): lax.all_to_all(slot_rows, 'seq', split_axis=0, concat_axis=0, tiled=True)]
    ppermute x2, waiting for transfers between devices: 6.25 us -> 2.84 us  [exchange(): other = lax.ppermute(held, axis, [(i, i ^ bit) for i in range(count)])]
    ppermute x3 -> x2, starting transfers between devices: 1.45 us -> 3.14 us  [scattered_columns(): lax.ppermute(sent, axis, [(i, i ^ bit) for i in range(count)])]
    ppermute x5, starting transfers between devices: 19.5 us -> 21.1 us  [shifted(): return lax.ppermute(array, axis, pairs)]
    all_to_all x1, starting transfers between devices: 7.41 us -> 6.08 us  [per_device(): lax.all_to_all(slot_rows, 'seq', split_axis=0, concat_axis=0, tiled=True)]
    dot_general x1, matrix products: 0.29 us -> 1.55 us  [per_device(): jnp.dot(tokens, shared_weight, preferred_element_type=jnp.float32)]
    concatenate x2, other arithmetic: 1.2 us -> 0.14 us  [exchange(): held = jnp.concatenate([held, other], axis=dim)]
    ppermute x3 -> x2, waiting for transfers between devices: 5.06 us -> 4.1 us  [scattered_columns(): lax.ppermute(sent, axis, [(i, i ^ bit) for i in range(count)])]
  transfers between devices with their start and end apart: 11 -> 10, of which waited for: 8 -> 9; matrix products, arithmetic and copies ran while one was open for 10% -> 9% of each run, Pallas kernels for 0% -> 0%
where the time goes in v11:
time: 100 us; the launch traced here: 99.6 us
  starting transfers between devices  32 us (32%)
  waiting for transfers between devices  23.4 us (23%)
  blocking collectives  18.2 us (18%)
  local copies, waits for them, and re-layouts  8.64 us (9%)
  matrix products  6.89 us (7%)
  other arithmetic  6.75 us (7%)
  between operations  3.66 us (4%)
    ppermute x5, starting transfers between devices, shifted(): return lax.ppermute(array, axis, pairs)  21.1 us
    all_to_all x1, blocking collectives, per_device(): lax.all_to_all(outgoing, 'seq', split_axis=0, concat_axis=0, tiled=True)  18.2 us
    all_to_all x1, waiting for transfers between devices, per_device(): lax.all_to_all(slot_rows, 'seq', split_axis=0, concat_axis=0, tiled=True)  8.42 us
    ppermute x5, waiting for transfers between devices, shifted(): return lax.ppermute(array, axis, pairs)  8.03 us
    all_to_all x1, starting transfers between devices, per_device(): lax.all_to_all(slot_rows, 'seq', split_axis=0, concat_axis=0, tiled=True)  6.08 us
    ppermute x2, waiting for transfers between devices, scattered_columns(): lax.ppermute(sent, axis, [(i, i ^ bit) for i in range(count)])  4.1 us
    ppermute x2, starting transfers between devices, scattered_columns(): lax.ppermute(sent, axis, [(i, i ^ bit) for i in range(count)])  3.14 us
    ppermute x2, waiting for transfers between devices, exchange(): other = lax.ppermute(held, axis, [(i, i ^ bit) for i in range(count)])  2.84 us
  transfers between devices with their start and end apart: 10, of which 9 were waited for; matrix products, arithmetic and copies ran while one was open for 9% of the time, Pallas kernels for 0%

profile of v11, /device:TPU:0, one launch (start us, length us, event | category | flops | bytes accessed | tf_op | source)
XLA Modules:
  0.0 99.6 jit_solution(15639379563483895082)
XLA Ops:
  0.0 1.5 %fusion.69 = f32[256,512]{1,0:T(8,128)S(1)} fusion(bf16[256,512]{1,0:T(8,128)(2,1)} %param.13, bf16[512,512]{1,0:T(8,128)(2,1)} %param.18), kind=kOutput, calls=%fused_computation.138 | convolution fusion | flops 134217728 | bytes 1310720 | tf_op jit(solution)/shard_map/dot_general | solution.py:199
  1.6 0.5 collective-permute-start
  2.1 0.7 compare_and_fusion.1
  2.8 1.0 sort.17
  3.9 2.6 %collective-permute-start.1 = (f32[256,128]{1,0:T(8,128)S(1)}, f32[256,128]{1,0:T(8,128)S(1)}, u32[]{:S(2)}, u32[]{:S(2)}) collective-permute-start(f32[256,128]{1,0:T(8,128)S(1)} %constant_dynamic-slice_fusion.4), channel_id=1, source_target_pairs={{0,2},{1,3},{2,0},{3,1},{4,6},{5,7},{6,4},{7,5},{8,10},{9,11},{10,... | collective-permute-start | bytes 393224 | tf_op jit(solution)/shard_map/ppermute | solution.py:114
  6.5 4.1 %collective-permute-done.1 = f32[256,128]{1,0:T(8,128)S(1)} collective-permute-done((f32[256,128]{1,0:T(8,128)S(1)}, f32[256,128]{1,0:T(8,128)S(1)}, u32[]{:S(2)}, u32[]{:S(2)}) %collective-permute-start.1) | collective-permute-done | bytes 131104 | tf_op jit(solution)/shard_map/ppermute | solution.py:114
  10.7 0.7 pad_maximum_fusion.6
  11.4 6.1 %all-to-all-start = ((bf16[8,32,640]{2,1,0:T(8,128)(2,1)}), bf16[8,32,640]{2,1,0:T(8,128)(2,1)S(1)}, u32[]{:S(2)}, u32[]{:S(2)}) async-start(bf16[8,32,640]{2,1,0:T(8,128)(2,1)} %bitcast.1), calls=%async_computation | async-start | bytes 655360 | tf_op jit(solution)/shard_map/all_to_all | solution.py:208
  17.9 0.6 fusion.67
  19.2 8.4 %all-to-all-done = bf16[8,32,640]{2,1,0:T(8,128)(2,1)S(1)} async-done(((bf16[8,32,640]{2,1,0:T(8,128)(2,1)}), bf16[8,32,640]{2,1,0:T(8,128)(2,1)S(1)}, u32[]{:S(2)}, u32[]{:S(2)}) %all-to-all-start) | async-done | bytes 327712 | tf_op jit(solution)/shard_map/all_to_all | solution.py:208
  27.6 0.6 gather_fusion
  28.4 1.6 %collective-permute-start.2 = (bf16[256,640]{1,0:T(8,128)(2,1)S(1)}, bf16[256,640]{1,0:T(8,128)(2,1)S(1)}, u32[]{:S(2)}, u32[]{:S(2)}) collective-permute-start(bf16[256,640]{1,0:T(8,128)(2,1)S(1)} %bitcast_select_fusion), channel_id=1, source_target_pairs={{0,2},{1,3},{2,0},{3,1},{4,6},{5,7},{6,4},{7,5},{8,10},{9,11},{10,... | collective-permute-start | bytes 983048 | tf_op jit(solution)/shard_map/ppermute | solution.py:59
  29.9 0.7 broadcast_compare_fusion.1
  30.6 0.7 fusion.68
  33.9 0.6 slice.121
  34.6 0.9 collective-permute-done.2
  35.8 1.9 %collective-permute-done.3 = bf16[256,1280]{1,0:T(8,128)(2,1)S(1)} collective-permute-done((bf16[256,1280]{1,0:T(8,128)(2,1)S(1)}, bf16[256,1280]{1,0:T(8,128)(2,1)S(1)}, u32[]{:S(2)}, u32[]{:S(2)}) %collective-permute-start.3) | collective-permute-done | bytes 655392 | tf_op jit(solution)/shard_map/ppermute | solution.py:59
  37.9 0.6 copy-done.6
  38.6 0.4 compare_select_fusion
  39.0 0.2 fusion.44
  39.2 0.2 slice_reduce_fusion
  39.4 0.6 copy-done.5
  40.0 0.7 divide_multiply_fusion.1
  40.7 0.7 fusion.15
  41.6 3.8 %collective-permute-start.4 = (bf16[3,896]{1,0:T(4,128)(2,1)S(1)}, bf16[3,896]{1,0:T(4,128)(2,1)S(1)}, u32[]{:S(2)}, u32[]{:S(2)}) collective-permute-start(bf16[3,896]{1,0:T(4,128)(2,1)S(1)} %slice.141), channel_id=1, source_target_pairs={{0,4},{4,8},{8,12},{12,16},{16,20},{20,24},{24,28},{1,5},{5,9},{9,... | collective-permute-start | bytes 16136 | tf_op jit(solution)/shard_map/ppermute | solution.py:12
  45.5 0.6 broadcast_select_fusion.1
  46.3 0.4 collective-permute-done.4
  46.9 0.7 divide_multiply_fusion
  47.6 0.8 slice.149
  48.3 1.2 %copy.21 = f32[256,384]{0,1:T(8,128)S(1)} copy(f32[256,384]{1,0:T(8,128)} %slice.149) | data formatting | bytes 786432 | tf_op jit(solution)/shard_map/slice | solution.py:269
  49.5 0.5 fusion.32
  50.2 4.2 %collective-permute-start.6 = (bf16[6,66,256]{2,1,0:T(8,128)(2,1)S(1)}, bf16[6,66,256]{2,1,0:T(8,128)(2,1)S(1)}, u32[]{:S(2)}, u32[]{:S(2)}) collective-permute-start(bf16[6,66,256]{2,1,0:T(8,128)(2,1)S(1)} %fusion.38), channel_id=1, source_target_pairs={{0,4},{4,8},{8,12},{12,16},{16,20},{20,24},{24,28},{1,5},{5,9},{9,... | collective-permute-start | bytes 608264 | tf_op jit(solution)/shard_map/ppermute | solution.py:12
  54.4 2.3 %collective-permute-start.5 = (bf16[6,66,256]{2,1,0:T(8,128)(2,1)S(1)}, bf16[6,66,256]{2,1,0:T(8,128)(2,1)S(1)}, u32[]{:S(2)}, u32[]{:S(2)}) collective-permute-start(bf16[6,66,256]{2,1,0:T(8,128)(2,1)S(1)} %fusion.38), channel_id=1, source_target_pairs={{0,8},{4,12},{8,16},{12,20},{16,24},{20,28},{1,9},{5,13},{9,17},{1... | collective-permute-start | bytes 608264 | tf_op jit(solution)/shard_map/ppermute | solution.py:12
  56.7 0.4 fusion.46
  57.1 1.1 %collective-permute-done.6 = bf16[6,66,256]{2,1,0:T(8,128)(2,1)S(1)} collective-permute-done((bf16[6,66,256]{2,1,0:T(8,128)(2,1)S(1)}, bf16[6,66,256]{2,1,0:T(8,128)(2,1)S(1)}, u32[]{:S(2)}, u32[]{:S(2)}) %collective-permute-start.6) | collective-permute-done | bytes 202784 | tf_op jit(solution)/shard_map/ppermute | solution.py:12
  58.2 2.2 %collective-permute-done.5 = bf16[6,66,256]{2,1,0:T(8,128)(2,1)S(1)} collective-permute-done((bf16[6,66,256]{2,1,0:T(8,128)(2,1)S(1)}, bf16[6,66,256]{2,1,0:T(8,128)(2,1)S(1)}, u32[]{:S(2)}, u32[]{:S(2)}) %collective-permute-start.5) | collective-permute-done | bytes 202784 | tf_op jit(solution)/shard_map/ppermute | solution.py:12
  60.7 4.4 %collective-permute-start.7 = (bf16[6,66,256]{2,1,0:T(8,128)(2,1)S(1)}, bf16[6,66,256]{2,1,0:T(8,128)(2,1)S(1)}, u32[]{:S(2)}, u32[]{:S(2)}) collective-permute-start(bf16[6,66,256]{2,1,0:T(8,128)(2,1)S(1)} %fusion.39), channel_id=1, source_target_pairs={{0,8},{4,12},{8,16},{12,20},{16,24},{20,28},{1,9},{5,13},{9,17},{1... | collective-permute-start | bytes 608264 | tf_op jit(solution)/shard_map/ppermute | solution.py:12
  65.1 1.9 %fusion.8 = f32[256,6,64]{0,2,1:T(8,128)S(1)} fusion(f32[6,256]{1,0:T(8,128)S(1)} %bitcast.54, f32[256,256]{1,0:T(8,128)S(1)} %fusion.46, pred[256,256]{1,0:T(8,128)(4,1)S(1)} %fusion.43, f32[256,6,64]{0,2,1:T(8,128)S(1)} %bitcast.49, f32[6]{0:T(128)S(1)} %copy-done.10, f32[256,6]{0,1:T(8,128)S(1)} %compare_select_fusion), kind=kOutput, calls=%fused_computation.9 | convolution fusion | flops 303464448 | bytes 1126424 | tf_op jit(solution)/shard_map/hts,shp->thp/dot_general | solution.py:162
  67.0 1.5 %collective-permute-done.7 = bf16[6,66,256]{2,1,0:T(8,128)(2,1)S(1)} collective-permute-done((bf16[6,66,256]{2,1,0:T(8,128)(2,1)S(1)}, bf16[6,66,256]{2,1,0:T(8,128)(2,1)S(1)}, u32[]{:S(2)}, u32[]{:S(2)}) %collective-permute-start.7) | collective-permute-done | bytes 202784 | tf_op jit(solution)/shard_map/ppermute | solution.py:12
  68.8 6.5 %collective-permute-start.8 = (bf16[6,66,256]{2,1,0:T(8,128)(2,1)S(1)}, bf16[6,66,256]{2,1,0:T(8,128)(2,1)S(1)}, u32[]{:S(2)}, u32[]{:S(2)}) collective-permute-start(bf16[6,66,256]{2,1,0:T(8,128)(2,1)S(1)} %fusion.40), channel_id=1, source_target_pairs={{0,16},{4,20},{8,24},{12,28},{1,17},{5,21},{9,25},{13,29},{2,18},{... | collective-permute-start | bytes 608264 | tf_op jit(solution)/shard_map/ppermute | solution.py:12
  75.3 0.7 fusion.62
  76.0 2.7 %collective-permute-done.8 = bf16[6,66,256]{2,1,0:T(8,128)(2,1)S(1)} collective-permute-done((bf16[6,66,256]{2,1,0:T(8,128)(2,1)S(1)}, bf16[6,66,256]{2,1,0:T(8,128)(2,1)S(1)}, u32[]{:S(2)}, u32[]{:S(2)}) %collective-permute-start.8) | collective-permute-done | bytes 202784 | tf_op jit(solution)/shard_map/ppermute | solution.py:12
  78.8 0.5 fusion.13
  79.3 0.3 copy.23
  79.6 0.3 convert_element_type.109
  79.9 0.6 gather_fusion.1
  80.6 18.2 %all_to_all.10 = bf16[8,32,384]{2,1,0:T(8,128)(2,1)S(1)} all-to-all(bf16[8,32,384]{2,1,0:T(8,128)(2,1)S(1)} %broadcast_select_fusion), channel_id=1, replica_groups=mesh['seq'=8,'fsdp'=4] {'seq'}, dimensions={0} | all-to-all | bytes 393216 | tf_op jit(solution)/shard_map/all_to_all | solution.py:286
  98.9 0.7 copy.39
  (72 shorter events, 2.5 us)
Async XLA Ops:
  0.0 40.7 %copy-start = (bf16[2048,384]{1,0:T(8,128)(2,1)S(1)}, bf16[2048,384]{1,0:T(8,128)(2,1)}, u32[]{:S(2)}) copy-start(bf16[2048,384]{1,0:T(8,128)(2,1)} %param.16) | copy-start | bytes 4718596
  0.0 10.6 %copy-start.1 = (bf16[256,512]{1,0:T(8,128)(2,1)S(1)}, bf16[256,512]{1,0:T(8,128)(2,1)}, u32[]{:S(2)}) copy-start(bf16[256,512]{1,0:T(8,128)(2,1)} %param.13) | copy-start | bytes 786436
  1.6 16.0 %copy-start.7 = (s32[4]{0:T(128)S(1)}, s32[4]{0:T(128)}, u32[]{:S(2)}) copy-start(s32[4]{0:T(128)} %param.15) | copy-start | bytes 52
  1.6 2.2 %collective-permute-start = (f32[256,256]{1,0:T(8,128)S(1)}, f32[256,256]{1,0:T(8,128)S(1)}, u32[]{:S(2)}, u32[]{:S(2)}) collective-permute-start(f32[256,256]{1,0:T(8,128)S(1)} %constant_dynamic-slice_fusion.5), channel_id=1, source_target_pairs={{0,1},{1,0},{2,3},{3,2},{4,5},{5,4},{6,7},{7,6},{8,9},{9,8},{10,11... | collective-permute-start | bytes 786440 | tf_op jit(solution)/shard_map/ppermute | solution.py:114
  3.9 26.8 %copy-start.2 = (s32[4]{0:T(128)S(1)}, s32[4]{0:T(128)}, u32[]{:S(2)}) copy-start(s32[4]{0:T(128)} %constant.121.clone) | copy-start | bytes 52
  3.9 30.7 %copy-start.4 = (f32[4,384]{1,0:T(4,128)S(1)}, f32[4,384]{1,0:T(4,128)}, u32[]{:S(2)}) copy-start(f32[4,384]{1,0:T(4,128)} %param.20) | copy-start | bytes 18436
  3.9 30.7 %copy-start.3 = (f32[4,512]{1,0:T(4,128)S(1)}, f32[4,512]{1,0:T(4,128)}, u32[]{:S(2)}) copy-start(f32[4,512]{1,0:T(4,128)} %param.21) | copy-start | bytes 24580
  3.9 6.7 %collective-permute-start.1 = (f32[256,128]{1,0:T(8,128)S(1)}, f32[256,128]{1,0:T(8,128)S(1)}, u32[]{:S(2)}, u32[]{:S(2)}) collective-permute-start(f32[256,128]{1,0:T(8,128)S(1)} %constant_dynamic-slice_fusion.4), channel_id=1, source_target_pairs={{0,2},{1,3},{2,0},{3,1},{4,6},{5,7},{6,4},{7,5},{8,10},{9,11},{10,... | collective-permute-start | bytes 393224 | tf_op jit(solution)/shard_map/ppermute | solution.py:114
  11.4 16.2 %all-to-all-start = ((bf16[8,32,640]{2,1,0:T(8,128)(2,1)}), bf16[8,32,640]{2,1,0:T(8,128)(2,1)S(1)}, u32[]{:S(2)}, u32[]{:S(2)}) async-start(bf16[8,32,640]{2,1,0:T(8,128)(2,1)} %bitcast.1), calls=%async_computation | async-start | bytes 655360 | tf_op jit(solution)/shard_map/all_to_all | solution.py:208
  17.5 18.2 %copy-start.8 = (f32[6]{0:T(128)S(1)}, f32[6]{0:T(128)}, u32[]{:S(2)}) copy-start(f32[6]{0:T(128)} %param.23) | copy-start | bytes 76
  28.4 7.1 %collective-permute-start.2 = (bf16[256,640]{1,0:T(8,128)(2,1)S(1)}, bf16[256,640]{1,0:T(8,128)(2,1)S(1)}, u32[]{:S(2)}, u32[]{:S(2)}) collective-permute-start(bf16[256,640]{1,0:T(8,128)(2,1)S(1)} %bitcast_select_fusion), channel_id=1, source_target_pairs={{0,2},{1,3},{2,0},{3,1},{4,6},{5,7},{6,4},{7,5},{8,10},{9,11},{10,... | collective-permute-start | bytes 983048 | tf_op jit(solution)/shard_map/ppermute | solution.py:59
  35.6 2.2 %collective-permute-start.3 = (bf16[256,1280]{1,0:T(8,128)(2,1)S(1)}, bf16[256,1280]{1,0:T(8,128)(2,1)S(1)}, u32[]{:S(2)}, u32[]{:S(2)}) collective-permute-start(bf16[256,1280]{1,0:T(8,128)(2,1)S(1)} %pad_maximum_fusion.2), channel_id=1, source_target_pairs={{0,1},{1,0},{2,3},{3,2},{4,5},{5,4},{6,7},{7,6},{8,9},{9,8},{10,11... | collective-permute-start | bytes 1966088 | tf_op jit(solution)/shard_map/ppermute | solution.py:59
  37.8 0.8 copy-start.6
  37.8 0.8 copy-start.9
  38.6 1.4 %copy-start.5 = (bf16[2048,384]{1,0:T(8,128)(2,1)S(1)}, bf16[2048,384]{1,0:T(8,128)(2,1)}, u32[]{:S(2)}) copy-start(bf16[2048,384]{1,0:T(8,128)(2,1)} %param.17) | copy-start | bytes 4718596
  41.6 5.2 %collective-permute-start.4 = (bf16[3,896]{1,0:T(4,128)(2,1)S(1)}, bf16[3,896]{1,0:T(4,128)(2,1)S(1)}, u32[]{:S(2)}, u32[]{:S(2)}) collective-permute-start(bf16[3,896]{1,0:T(4,128)(2,1)S(1)} %slice.141), channel_id=1, source_target_pairs={{0,4},{4,8},{8,12},{12,16},{16,20},{20,24},{24,28},{1,5},{5,9},{9,... | collective-permute-start | bytes 16136 | tf_op jit(solution)/shard_map/ppermute | solution.py:12
  50.2 8.0 %collective-permute-start.6 = (bf16[6,66,256]{2,1,0:T(8,128)(2,1)S(1)}, bf16[6,66,256]{2,1,0:T(8,128)(2,1)S(1)}, u32[]{:S(2)}, u32[]{:S(2)}) collective-permute-start(bf16[6,66,256]{2,1,0:T(8,128)(2,1)S(1)} %fusion.38), channel_id=1, source_target_pairs={{0,4},{4,8},{8,12},{12,16},{16,20},{20,24},{24,28},{1,5},{5,9},{9,... | collective-permute-start | bytes 608264 | tf_op jit(solution)/shard_map/ppermute | solution.py:12
  54.4 6.1 %collective-permute-start.5 = (bf16[6,66,256]{2,1,0:T(8,128)(2,1)S(1)}, bf16[6,66,256]{2,1,0:T(8,128)(2,1)S(1)}, u32[]{:S(2)}, u32[]{:S(2)}) collective-permute-start(bf16[6,66,256]{2,1,0:T(8,128)(2,1)S(1)} %fusion.38), channel_id=1, source_target_pairs={{0,8},{4,12},{8,16},{12,20},{16,24},{20,28},{1,9},{5,13},{9,17},{1... | collective-permute-start | bytes 608264 | tf_op jit(solution)/shard_map/ppermute | solution.py:12
  57.1 8.0 %copy-start.10 = (f32[6]{0:T(128)S(1)}, f32[6]{0:T(128)}, u32[]{:S(2)}) copy-start(f32[6]{0:T(128)} %param.24) | copy-start | bytes 76
  60.7 7.8 %collective-permute-start.7 = (bf16[6,66,256]{2,1,0:T(8,128)(2,1)S(1)}, bf16[6,66,256]{2,1,0:T(8,128)(2,1)S(1)}, u32[]{:S(2)}, u32[]{:S(2)}) collective-permute-start(bf16[6,66,256]{2,1,0:T(8,128)(2,1)S(1)} %fusion.39), channel_id=1, source_target_pairs={{0,8},{4,12},{8,16},{12,20},{16,24},{20,28},{1,9},{5,13},{9,17},{1... | collective-permute-start | bytes 608264 | tf_op jit(solution)/shard_map/ppermute | solution.py:12
  68.8 9.9 %collective-permute-start.8 = (bf16[6,66,256]{2,1,0:T(8,128)(2,1)S(1)}, bf16[6,66,256]{2,1,0:T(8,128)(2,1)S(1)}, u32[]{:S(2)}, u32[]{:S(2)}) collective-permute-start(bf16[6,66,256]{2,1,0:T(8,128)(2,1)S(1)} %fusion.40), channel_id=1, source_target_pairs={{0,16},{4,20},{8,24},{12,28},{1,17},{5,21},{9,25},{13,29},{2,18},{... | collective-permute-start | bytes 608264 | tf_op jit(solution)/shard_map/ppermute | solution.py:12

commit v12 on v11

--- a/solution.py
+++ b/solution.py
@@ -204,16 +204,40 @@
         quarter = 0
         sent_rows = tokens
     width = sent_rows.shape[1]
+    conv_width = conv_heads.shape[0]
+    halo = conv_width - 1
+    tail = min(halo, piece_rows)
     slot_rows = sent_rows.reshape(seq_count, piece_rows, width)
-    arrived = lax.all_to_all(slot_rows, "seq", split_axis=0, concat_axis=0, tiled=True)
+    tails = jnp.roll(slot_rows[:, piece_rows - tail :, :], 1, axis=0).reshape(seq_count, tail * width)
+    tail_cols = -(-tail * width // piece_rows)
+    tail_pad = -(-tail_cols // 128) * 128
+    tails = jnp.pad(tails, ((0, 0), (0, tail_cols * piece_rows - tail * width)))
+    tails = jnp.pad(tails.reshape(seq_count, piece_rows, tail_cols), ((0, 0), (0, 0), (0, tail_pad - tail_cols)))
+    arrived = lax.all_to_all(
+        jnp.concatenate([slot_rows, tails], axis=2), "seq", split_axis=0, concat_axis=0, tiled=True
+    )
     dealt_row = lax.dynamic_slice_in_dim(deal_order, own_index, 1, 0)[0]
     inverse = jnp.argsort(dealt_row)
-    stream_block = jnp.take(arrived, inverse, axis=0).reshape(tok_dev, width)
+    stream_block = jnp.take(arrived[:, :, :width], inverse, axis=0).reshape(tok_dev, width)
+    tail_in = arrived[:, :, width : width + tail_cols].reshape(seq_count, piece_rows * tail_cols)
+    tail_in = tail_in[:, : tail * width].reshape(seq_count * tail, width)
+    prior_row = lax.dynamic_slice_in_dim(deal_order, (own_index + seq_count - 1) % seq_count, 1, 0)[0]
+    inverse_prior = jnp.argsort(prior_row)
+    block_rows = [tok_dev - halo + r for r in range(halo)]
+    pieces = jnp.asarray([b // piece_rows for b in block_rows], jnp.int32)
+    within = jnp.asarray([b % piece_rows - (piece_rows - tail) for b in block_rows], jnp.int32)
+    halo_rows = jnp.take(tail_in, inverse_prior[pieces] * tail + within, axis=0)
+    halo_rows = jnp.where(own_index > 0, halo_rows, jnp.zeros_like(halo_rows))
+    halo_cols = -(-halo * width // tok_dev)
+    halo_pad = -(-halo_cols // 128) * 128
+    halo_flat = jnp.pad(halo_rows.reshape(halo * width), (0, halo_cols * tok_dev - halo * width))
+    halo_block = jnp.pad(halo_flat.reshape(tok_dev, halo_cols), ((0, 0), (0, halo_pad - halo_cols)))
     inner_dev = x_weight.shape[1]
     heads_dev = step_weight.shape[1]
     head_dim = inner_dev // heads_dev
     state_dim = shared_weight.shape[1] // 2
-    feature_held, codes = exchange(stream_block, "fsdp", 1)
+    span = width + halo_pad
+    feature_held, codes = exchange(jnp.concatenate([stream_block, halo_block], axis=1), "fsdp", 1)
     if codes is None:
         codes = list(range(fsdp_count))
         fsdp_place = 0
@@ -224,11 +248,17 @@
 
     def piece_of(source, start, size):
         position = table[jnp.bitwise_xor(source, fsdp_place)]
-        return lax.dynamic_slice_in_dim(feature_held, position * width + start, size, axis=1)
+        return lax.dynamic_slice_in_dim(feature_held, position * span + start, size, axis=1)
+
+    def halo_of(source):
+        cols = piece_of(source, width, halo_cols).reshape(tok_dev * halo_cols)
+        return cols[: halo * width].reshape(halo, width)
 
     feature_part = jnp.concatenate(
         [piece_of(index, 0, model_cols) for index in range(fsdp_count)], axis=1
     )
+    halo_parts = [halo_of(index) for index in range(fsdp_count)]
+    halo_features = jnp.concatenate([part[:, :model_cols] for part in halo_parts], axis=1)
     if split_ok:
         bc_raw = jnp.concatenate(
             [
@@ -237,12 +267,16 @@
             ],
             axis=1,
         )
+        halo_bc = jnp.concatenate(
+            [halo_parts[bit_reversed(block, fsdp_count)][:, model_cols:] for block in range(fsdp_count)],
+            axis=1,
+        )
     else:
-        bc_raw = jnp.dot(
-            feature_part,
-            lax.all_gather(shared_weight, "fsdp", axis=0, tiled=True),
-            preferred_element_type=jnp.float32,
-        ).astype(jnp.bfloat16)
+        w_full = lax.all_gather(shared_weight, "fsdp", axis=0, tiled=True)
+        bc_raw = jnp.dot(feature_part, w_full, preferred_element_type=jnp.float32).astype(jnp.bfloat16)
+        halo_bc = jnp.dot(halo_features, w_full, preferred_element_type=jnp.float32).astype(jnp.bfloat16)
+    halo_x = jnp.dot(halo_features, x_weight, preferred_element_type=jnp.float32).astype(jnp.bfloat16)
+    prior_rows = jnp.concatenate([halo_x, halo_bc], axis=1)
     x_acc, z_acc, step_acc = tuple(
         (
             jnp.dot(feature_part, weight, preferred_element_type=jnp.float32)
@@ -253,8 +287,6 @@
     z_raw = z_acc.astype(jnp.bfloat16)
     step_size = jax.nn.softplus(step_acc + step_bias[None, :])
     mixed_in = jnp.concatenate([x_raw, bc_raw], axis=1)
-    conv_width = conv_heads.shape[0]
-    prior_rows = shifted(mixed_in[tok_dev - conv_width + 1 :], "seq", 1)
     first_pos = own_index * tok_dev
     positions = first_pos - (conv_width - 1) + jnp.arange(tok_dev + conv_width - 1, dtype=jnp.int32)
     seg_ext = segment_of(positions, lengths)

time: 100 us -> 107 us (1.070)
  other arithmetic: 6.75 us -> 15.1 us
  starting transfers between devices: 32 us -> 26.5 us
  waiting for transfers between devices: 23.4 us -> 18.4 us
  local copies, waits for them, and re-layouts: 8.64 us -> 11.9 us
  matrix products: 6.89 us -> 10.1 us
  blocking collectives: 18.2 us -> 19.8 us
    ppermute x5 -> x4, starting transfers between devices: 21.1 us -> 15.7 us  [shifted(): return lax.ppermute(array, axis, pairs)]
    ppermute x5 -> x4, waiting for transfers between devices: 8.03 us -> 5.07 us  [shifted(): return lax.ppermute(array, axis, pairs)]
    ppermute x2, waiting for transfers between devices: 2.84 us -> 0.34 us  [exchange(): other = lax.ppermute(held, axis, [(i, i ^ bit) for i in range(count)])]
    dot_general x3, matrix products: 1.85 us -> 4.01 us  [per_device(): jnp.dot(feature_part, weight, preferred_element_type=jnp.float32)]
    convert_element_type x3, other arithmetic: 0.09 us -> 1.99 us  [received(): got = shifted(wire, axis, by).astype(jnp.float32)]
    slice x2, local copies, waits for them, and re-layouts: 1.93 us -> 0.19 us  [per_device(): x_heads = activated[:, :inner_dev].reshape(tok_dev, heads_dev, head_dim)]
    all_to_all x1, blocking collectives: 18.2 us -> 19.8 us  [per_device(): lax.all_to_all(outgoing, 'seq', split_axis=0, concat_axis=0, tiled=True)]
    select_n x3, other arithmetic: 0.35 us -> 1.68 us  [received(): wire = jnp.where(row == rows + 1, low, high)]
  transfers between devices with their start and end apart: 10 -> 9, of which waited for: 9 -> 5; matrix products, arithmetic and copies ran while one was open for 9% -> 17% of each run, Pallas kernels for 0% -> 0%
where the time goes in v12:
time: 107 us; the launch traced here: 106 us
  starting transfers between devices  26.5 us (25%)
  blocking collectives  19.8 us (19%)
  waiting for transfers between devices  18.4 us (17%)
  other arithmetic  15.1 us (14%)
  local copies, waits for them, and re-layouts  11.9 us (11%)
  matrix products  10.1 us (9%)
  between operations  3.98 us (4%)
    all_to_all x1, blocking collectives, per_device(): lax.all_to_all(outgoing, 'seq', split_axis=0, concat_axis=0, tiled=True)  19.8 us
    ppermute x4, starting transfers between devices, shifted(): return lax.ppermute(array, axis, pairs)  15.7 us
    all_to_all x1, waiting for transfers between devices, per_device(): lax.all_to_all(jnp.concatenate([slot_rows, tails], axis=2), 'seq', split_...  8.83 us
    all_to_all x1, starting transfers between devices, per_device(): lax.all_to_all(jnp.concatenate([slot_rows, tails], axis=2), 'seq', split_...  6.08 us
    ppermute x4, waiting for transfers between devices, shifted(): return lax.ppermute(array, axis, pairs)  5.07 us
    ppermute x2, waiting for transfers between devices, scattered_columns(): lax.ppermute(sent, axis, [(i, i ^ bit) for i in range(count)])  4.14 us
    dot_general x3, matrix products, per_device(): jnp.dot(feature_part, weight, preferred_element_type=jnp.float32)  4.01 us
    ppermute x2, starting transfers between devices, scattered_columns(): lax.ppermute(sent, axis, [(i, i ^ bit) for i in range(count)])  3.09 us
  transfers between devices with their start and end apart: 9, of which 5 were waited for; matrix products, arithmetic and copies ran while one was open for 17% of the time, Pallas kernels for 0%

profile of v12, /device:TPU:0, one launch (start us, length us, event | category | flops | bytes accessed | tf_op | source)
XLA Modules:
  0.0 105.8 jit_solution(15692375683924679828)
XLA Ops:
  0.0 1.5 %fusion.81 = f32[256,512]{1,0:T(8,128)S(1)} fusion(bf16[256,512]{1,0:T(8,128)(2,1)} %param.15, bf16[512,512]{1,0:T(8,128)(2,1)} %param.20), kind=kOutput, calls=%fused_computation.170 | convolution fusion | flops 134217728 | bytes 1310720 | tf_op jit(solution)/shard_map/dot_general | solution.py:199
  1.6 0.5 collective-permute-start
  2.1 1.2 %compare_and_fusion.2 = (pred[8]{0:T(512)(128)(4,1)}, s32[8]{0:T(128)S(1)}) fusion(s32[8,8]{1,0:T(8,128)} %param.16, s32[]{:T(128)S(6)} %select_n.191), kind=kLoop, calls=%fused_computation.157 | loop fusion | flops 48 | bytes 76 | tf_op jit(solution)/shard_map/jit(_take)/and | solution.py:317
  3.3 1.0 sort.31
  4.4 2.6 %collective-permute-start.1 = (f32[256,128]{1,0:T(8,128)S(1)}, f32[256,128]{1,0:T(8,128)S(1)}, u32[]{:S(2)}, u32[]{:S(2)}) collective-permute-start(f32[256,128]{1,0:T(8,128)S(1)} %constant_dynamic-slice_fusion.9), channel_id=1, source_target_pairs={{0,2},{1,3},{2,0},{3,1},{4,6},{5,7},{6,4},{7,5},{8,10},{9,11},{10,... | collective-permute-start | bytes 393224 | tf_op jit(solution)/shard_map/ppermute | solution.py:114
  7.0 4.1 %collective-permute-done.1 = f32[256,128]{1,0:T(8,128)S(1)} collective-permute-done((f32[256,128]{1,0:T(8,128)S(1)}, f32[256,128]{1,0:T(8,128)S(1)}, u32[]{:S(2)}, u32[]{:S(2)}) %collective-permute-start.1) | collective-permute-done | bytes 131104 | tf_op jit(solution)/shard_map/ppermute | solution.py:114
  11.5 0.8 fusion.29
  12.3 6.1 %all-to-all-start = ((bf16[8,32,768]{2,1,0:T(8,128)(2,1)}), bf16[8,32,768]{2,1,0:T(8,128)(2,1)S(1)}, u32[]{:S(2)}, u32[]{:S(2)}) async-start(bf16[8,32,768]{2,1,0:T(8,128)(2,1)} %fusion.29), calls=%async_computation | async-start | bytes 786432 | tf_op jit(solution)/shard_map/all_to_all | solution.py:216
  18.3 0.7 fusion.73
  19.4 1.0 sort.32
  20.3 0.6 gather_fusion.1
  21.1 8.8 %all-to-all-done = bf16[8,32,768]{2,1,0:T(8,128)(2,1)S(1)} async-done(((bf16[8,32,768]{2,1,0:T(8,128)(2,1)}), bf16[8,32,768]{2,1,0:T(8,128)(2,1)S(1)}, u32[]{:S(2)}, u32[]{:S(2)}) %all-to-all-start) | async-done | bytes 393248 | tf_op jit(solution)/shard_map/all_to_all | solution.py:216
  30.1 0.6 gather_fusion.2
  31.0 0.6 gather_fusion
  31.8 1.6 %collective-permute-start.2 = (bf16[256,768]{1,0:T(8,128)(2,1)S(1)}, bf16[256,768]{1,0:T(8,128)(2,1)S(1)}, u32[]{:S(2)}, u32[]{:S(2)}) collective-permute-start(bf16[256,768]{1,0:T(8,128)(2,1)S(1)} %pad_maximum_fusion.6), channel_id=1, source_target_pairs={{0,2},{1,3},{2,0},{3,1},{4,6},{5,7},{6,4},{7,5},{8,10},{9,11},{10,... | collective-permute-start | bytes 1179656 | tf_op jit(solution)/shard_map/ppermute | solution.py:59
  33.3 0.6 fusion.79
  34.0 0.7 fusion.80
  37.8 1.3 %broadcast_compare_fusion.1 = (pred[256]{0:T(512)(128)(4,1)}, pred[256]{0:T(512)(128)(4,1)S(1)}, f32[256]{0:T(256)}, f32[256]{0:T(256)}, f32[256]{0:T(256)}) fusion(s32[]{:T(128)} %bitcast.11, s32[259]{0:T(512)S(1)} %convert_reduce_fusion, s32[]{:T(128)S(6)} %select_n.228), kind=kLoop, calls=%fused_computation.163 | loop fusion | flops 2048 | bytes 7688 | tf_op jit(solution)/shard_map/eq | solution.py:165
  39.1 0.6 copy-done.29
  39.7 0.6 slice.190
  40.5 0.5 iota_compare_fusion.3
  41.0 0.6 slice_reduce_fusion.4
  41.7 0.7 fusion.46
  42.7 1.2 %pad_maximum_fusion = bf16[256,3072]{1,0:T(8,128)(2,1)S(1)} fusion(bf16[256,1536]{1,0:T(8,128)(2,1)S(1)} %collective-permute-done.3, bf16[256,768]{1,0:T(8,128)(2,1)} %copy-done.1, bf16[256,128]{1,0:T(8,128)(2,1)S(1)} %pad.14, bf16[256,640]{1,0:T(8,128)(2,1)S(1)} %bitcast_select_fusion), kind=kLoop, calls=%fused_computation.4 | loop fusion | flops 6291456 | bytes 3145728 | tf_op jit(solution)/shard_map/concatenate | solution.py:60
  45.2 0.7 fusion.15
  46.1 0.4 compare_select_fusion
  47.0 1.2 %broadcast_select_fusion.1 = f32[6]{0:T(128)} fusion(pred[]{:T(512)} %bitcast.14, f32[6]{0:T(128)S(1)} %slice_reduce_fusion), kind=kLoop, calls=%fused_computation.158 | loop fusion | flops 6 | bytes 49 | tf_op jit(solution)/shard_map/jit(_where)/select_n | solution.py:171
  48.6 0.7 divide_multiply_fusion
  49.6 1.3 %fusion.35 = f32[6,64,256]{2,1,0:T(8,128)S(1)} fusion(f32[256,6,64]{0,2,1:T(8,128)S(1)} %bitcast.51, f32[256,896]{1,0:T(8,128)S(1)} %divide_multiply_fusion, f32[256,6]{0,1:T(8,128)S(1)} %get-tuple-element.36, f32[256,6]{0,1:T(8,128)} %copy-done.18), kind=kOutput, calls=%fused_computation.61 | convolution fusion | flops 302186496 | bytes 1062912 | tf_op jit(solution)/shard_map/shp,sn->hpn/dot_general | solution.py:168
  50.8 0.7 broadcast_in_dim.122
  51.5 1.5 %fusion.41 = bf16[6,66,256]{2,1,0:T(8,128)(2,1)} fusion(f32[6,2,256]{2,1,0:T(2,128)S(1)} %broadcast_in_dim.122, f32[6,64,256]{2,1,0:T(8,128)S(1)} %fusion.35, pred[66]{0:T(512)(128)(4,1)} %iota_compare_fusion.3), kind=kLoop, calls=%fused_computation.67 | loop fusion | flops 608256 | bytes 608322 | tf_op jit(solution)/shard_map/jit(_where)/select_n | solution.py:29
  52.9 5.3 %collective-permute-start.5 = (bf16[6,66,256]{2,1,0:T(8,128)(2,1)}, bf16[6,66,256]{2,1,0:T(8,128)(2,1)}, u32[]{:S(2)}, u32[]{:S(2)}) collective-permute-start(bf16[6,66,256]{2,1,0:T(8,128)(2,1)} %fusion.41), channel_id=1, source_target_pairs={{0,4},{4,8},{8,12},{12,16},{16,20},{20,24},{24,28},{1,5},{5,9},{9,... | collective-permute-start | bytes 608264 | tf_op jit(solution)/shard_map/ppermute | solution.py:12
  58.2 2.0 %collective-permute-start.4 = (bf16[6,66,256]{2,1,0:T(8,128)(2,1)}, bf16[6,66,256]{2,1,0:T(8,128)(2,1)}, u32[]{:S(2)}, u32[]{:S(2)}) collective-permute-start(bf16[6,66,256]{2,1,0:T(8,128)(2,1)} %fusion.41), channel_id=1, source_target_pairs={{0,8},{4,12},{8,16},{12,20},{16,24},{20,28},{1,9},{5,13},{9,17},{1... | collective-permute-start | bytes 608264 | tf_op jit(solution)/shard_map/ppermute | solution.py:12
  60.2 2.9 %divide_multiply_fusion.1 = f32[256,384]{1,0:T(8,128)} fusion(bf16[2048,384]{1,0:T(8,128)(2,1)} %param.19, bf16[256,512]{1,0:T(8,128)(2,1)S(1)} %copy-done.6, bf16[256,512]{1,0:T(8,128)(2,1)S(1)} %copy-done.8, bf16[256,512]{1,0:T(8,128)(2,1)S(1)} %copy-done.10, bf16[256,512]{1,0:T(8,128)(2,1)S(1)} %copy-done.4), kind=kOutput, calls=%fused_computation.60 | convolution fusion | flops 407437312 | bytes 3014656 | tf_op jit(solution)/shard_map/dot_general | solution.py:282
  63.1 1.2 %copy.24 = f32[256,384]{0,1:T(8,128)S(1)} copy(f32[256,384]{1,0:T(8,128)} %divide_multiply_fusion.1) | data formatting | bytes 786432 | tf_op jit(solution)/shard_map/jit(silu)/mul | solution.py:310
  64.3 0.4 fusion.49
  64.8 1.0 convert_element_type.107
  65.8 1.0 convert_element_type.105
  67.0 3.4 %collective-permute-start.6 = (bf16[6,66,256]{2,1,0:T(8,128)(2,1)S(1)}, bf16[6,66,256]{2,1,0:T(8,128)(2,1)S(1)}, u32[]{:S(2)}, u32[]{:S(2)}) collective-permute-start(bf16[6,66,256]{2,1,0:T(8,128)(2,1)S(1)} %fusion.42), channel_id=1, source_target_pairs={{0,8},{4,12},{8,16},{12,20},{16,24},{20,28},{1,9},{5,13},{9,17},{1... | collective-permute-start | bytes 608264 | tf_op jit(solution)/shard_map/ppermute | solution.py:12
  70.5 1.9 %fusion.8 = f32[256,6,64]{0,2,1:T(8,128)S(1)} fusion(f32[6,256]{1,0:T(8,128)S(1)} %bitcast.60, f32[256,256]{1,0:T(8,128)S(1)} %fusion.49, pred[256,256]{1,0:T(8,128)(4,1)S(1)} %copy-done.11, f32[256,6,64]{0,2,1:T(8,128)S(1)} %bitcast.52, f32[6]{0:T(128)S(1)} %copy-done.35, f32[256,6]{0,1:T(8,128)S(1)} %copy-done.19), kind=kOutput, calls=%fused_computation.11 | convolution fusion | flops 303464448 | bytes 1126424 | tf_op jit(solution)/shard_map/hts,shp->thp/dot_general | solution.py:162
  72.4 2.2 %collective-permute-done.6 = bf16[6,66,256]{2,1,0:T(8,128)(2,1)S(1)} collective-permute-done((bf16[6,66,256]{2,1,0:T(8,128)(2,1)S(1)}, bf16[6,66,256]{2,1,0:T(8,128)(2,1)S(1)}, u32[]{:S(2)}, u32[]{:S(2)}) %collective-permute-start.6) | collective-permute-done | bytes 202784 | tf_op jit(solution)/shard_map/ppermute | solution.py:12
  74.9 5.0 %collective-permute-start.7 = (bf16[6,66,256]{2,1,0:T(8,128)(2,1)S(1)}, bf16[6,66,256]{2,1,0:T(8,128)(2,1)S(1)}, u32[]{:S(2)}, u32[]{:S(2)}) collective-permute-start(bf16[6,66,256]{2,1,0:T(8,128)(2,1)S(1)} %fusion.43), channel_id=1, source_target_pairs={{0,16},{4,20},{8,24},{12,28},{1,17},{5,21},{9,25},{13,29},{2,18},{... | collective-permute-start | bytes 608264 | tf_op jit(solution)/shard_map/ppermute | solution.py:12
  79.9 0.7 fusion.72
  80.6 2.8 %collective-permute-done.7 = bf16[6,66,256]{2,1,0:T(8,128)(2,1)S(1)} collective-permute-done((bf16[6,66,256]{2,1,0:T(8,128)(2,1)S(1)}, bf16[6,66,256]{2,1,0:T(8,128)(2,1)S(1)}, u32[]{:S(2)}, u32[]{:S(2)}) %collective-permute-start.7) | collective-permute-done | bytes 202784 | tf_op jit(solution)/shard_map/ppermute | solution.py:12
  83.5 0.5 fusion.13
  84.7 0.6 gather_fusion.3
  85.4 19.8 %all_to_all.10 = bf16[8,32,384]{2,1,0:T(8,128)(2,1)S(1)} all-to-all(bf16[8,32,384]{2,1,0:T(8,128)(2,1)S(1)} %broadcast_select_fusion), channel_id=1, replica_groups=mesh['seq'=8,'fsdp'=4] {'seq'}, dimensions={0} | all-to-all | bytes 393216 | tf_op jit(solution)/shard_map/all_to_all | solution.py:318
  105.2 0.7 copy.45
  (156 shorter events, 5.6 us)
Async XLA Ops:
  0.0 44.6 %copy-start = (bf16[2048,384]{1,0:T(8,128)(2,1)S(1)}, bf16[2048,384]{1,0:T(8,128)(2,1)}, u32[]{:S(2)}) copy-start(bf16[2048,384]{1,0:T(8,128)(2,1)} %param.18) | copy-start | bytes 4718596
  0.0 11.1 %copy-start.2 = (bf16[256,512]{1,0:T(8,128)(2,1)S(1)}, bf16[256,512]{1,0:T(8,128)(2,1)}, u32[]{:S(2)}) copy-start(bf16[256,512]{1,0:T(8,128)(2,1)} %param.15) | copy-start | bytes 786436
  1.6 2.7 %collective-permute-start = (f32[256,256]{1,0:T(8,128)S(1)}, f32[256,256]{1,0:T(8,128)S(1)}, u32[]{:S(2)}, u32[]{:S(2)}) collective-permute-start(f32[256,256]{1,0:T(8,128)S(1)} %constant_dynamic-slice_fusion.10), channel_id=1, source_target_pairs={{0,1},{1,0},{2,3},{3,2},{4,5},{5,4},{6,7},{7,6},{8,9},{9,8},{10,11... | collective-permute-start | bytes 786440 | tf_op jit(solution)/shard_map/ppermute | solution.py:114
  4.4 14.7 %copy-start.32 = (s32[4]{0:T(128)S(1)}, s32[4]{0:T(128)}, u32[]{:S(2)}) copy-start(s32[4]{0:T(128)} %param.17) | copy-start | bytes 52
  4.4 6.7 %collective-permute-start.1 = (f32[256,128]{1,0:T(8,128)S(1)}, f32[256,128]{1,0:T(8,128)S(1)}, u32[]{:S(2)}, u32[]{:S(2)}) collective-permute-start(f32[256,128]{1,0:T(8,128)S(1)} %constant_dynamic-slice_fusion.9), channel_id=1, source_target_pairs={{0,2},{1,3},{2,0},{3,1},{4,6},{5,7},{6,4},{7,5},{8,10},{9,11},{10,... | collective-permute-start | bytes 393224 | tf_op jit(solution)/shard_map/ppermute | solution.py:114
  12.3 17.7 %all-to-all-start = ((bf16[8,32,768]{2,1,0:T(8,128)(2,1)}), bf16[8,32,768]{2,1,0:T(8,128)(2,1)S(1)}, u32[]{:S(2)}, u32[]{:S(2)}) async-start(bf16[8,32,768]{2,1,0:T(8,128)(2,1)} %fusion.29), calls=%async_computation | async-start | bytes 786432 | tf_op jit(solution)/shard_map/all_to_all | solution.py:216
  30.0 4.0 %copy-start.20 = (s32[4]{0:T(128)S(1)}, s32[4]{0:T(128)}, u32[]{:S(2)}) copy-start(s32[4]{0:T(128)} %constant.162.clone) | copy-start | bytes 52
  30.8 9.5 %copy-start.22 = (f32[4,384]{1,0:T(4,128)S(1)}, f32[4,384]{1,0:T(4,128)}, u32[]{:S(2)}) copy-start(f32[4,384]{1,0:T(4,128)} %param.22) | copy-start | bytes 18436
  31.6 9.4 %copy-start.21 = (f32[4,512]{1,0:T(4,128)S(1)}, f32[4,512]{1,0:T(4,128)}, u32[]{:S(2)}) copy-start(f32[4,512]{1,0:T(4,128)} %param.23) | copy-start | bytes 24580
  31.6 10.1 %copy-start.33 = (f32[6]{0:T(128)S(1)}, f32[6]{0:T(128)}, u32[]{:S(2)}) copy-start(f32[6]{0:T(128)} %param.25) | copy-start | bytes 76
  31.8 8.5 %collective-permute-start.2 = (bf16[256,768]{1,0:T(8,128)(2,1)S(1)}, bf16[256,768]{1,0:T(8,128)(2,1)S(1)}, u32[]{:S(2)}, u32[]{:S(2)}) collective-permute-start(bf16[256,768]{1,0:T(8,128)(2,1)S(1)} %pad_maximum_fusion.6), channel_id=1, source_target_pairs={{0,2},{1,3},{2,0},{3,1},{4,6},{5,7},{6,4},{7,5},{8,10},{9,11},{10,... | collective-permute-start | bytes 1179656 | tf_op jit(solution)/shard_map/ppermute | solution.py:59
  39.1 0.6 copy-start.29
  40.3 2.1 %copy-start.1 = (bf16[256,768]{1,0:T(8,128)(2,1)}, bf16[256,768]{1,0:T(8,128)(2,1)S(1)}, u32[]{:S(2)}) copy-start(bf16[256,768]{1,0:T(8,128)(2,1)S(1)} %collective-permute-done.2) | copy-start | bytes 1179652
  40.4 2.4 %collective-permute-start.3 = (bf16[256,1536]{1,0:T(8,128)(2,1)S(1)}, bf16[256,1536]{1,0:T(8,128)(2,1)S(1)}, u32[]{:S(2)}, u32[]{:S(2)}) collective-permute-start(bf16[256,1536]{1,0:T(8,128)(2,1)S(1)} %pad_maximum_fusion.2), channel_id=1, source_target_pairs={{0,1},{1,0},{2,3},{3,2},{4,5},{5,4},{6,7},{7,6},{8,9},{9,8},{10,11... | collective-permute-start | bytes 2359304 | tf_op jit(solution)/shard_map/ppermute | solution.py:59
  45.1 0.8 copy-start.3
  45.1 0.8 copy-start.5
  45.1 0.9 copy-start.7
  45.1 0.9 copy-start.9
  45.2 0.9 copy-start.31
  45.2 0.9 copy-start.34
  46.1 2.1 %copy-start.28 = (pred[256]{0:T(512)(128)(4,1)S(1)}, pred[256]{0:T(512)(128)(4,1)}, u32[]{:S(2)}) copy-start(pred[256]{0:T(512)(128)(4,1)} %get-tuple-element.37) | copy-start | bytes 772
  46.1 2.1 %copy-start.30 = (pred[256]{0:T(512)(128)(4,1)S(1)}, pred[256]{0:T(512)(128)(4,1)}, u32[]{:S(2)}) copy-start(pred[256]{0:T(512)(128)(4,1)} %copy-done.29) | copy-start | bytes 772
  46.5 2.0 %copy-start.18 = (f32[256,6]{0,1:T(8,128)}, f32[256,6]{0,1:T(8,128)S(1)}, u32[]{:S(2)}) copy-start(f32[256,6]{0,1:T(8,128)S(1)} %compare_select_fusion) | copy-start | bytes 18436
  46.5 2.0 %copy-start.14 = (f32[896]{0:T(1024)S(1)}, f32[896]{0:T(1024)}, u32[]{:S(2)}) copy-start(f32[896]{0:T(1024)} %get-tuple-element.17) | copy-start | bytes 10756
  46.5 2.0 %copy-start.15 = (f32[896]{0:T(1024)S(1)}, f32[896]{0:T(1024)}, u32[]{:S(2)}) copy-start(f32[896]{0:T(1024)} %get-tuple-element.18) | copy-start | bytes 10756
  46.5 2.0 %copy-start.16 = (f32[896]{0:T(1024)S(1)}, f32[896]{0:T(1024)}, u32[]{:S(2)}) copy-start(f32[896]{0:T(1024)} %get-tuple-element.19) | copy-start | bytes 10756
  46.5 2.0 %copy-start.17 = (f32[896]{0:T(1024)S(1)}, f32[896]{0:T(1024)}, u32[]{:S(2)}) copy-start(f32[896]{0:T(1024)} %get-tuple-element.20) | copy-start | bytes 10756
  46.6 2.0 %copy-start.24 = (f32[256]{0:T(256)S(1)}, f32[256]{0:T(256)}, u32[]{:S(2)}) copy-start(f32[256]{0:T(256)} %get-tuple-element.39) | copy-start | bytes 3076
  46.6 2.0 %copy-start.25 = (f32[256]{0:T(256)S(1)}, f32[256]{0:T(256)}, u32[]{:S(2)}) copy-start(f32[256]{0:T(256)} %get-tuple-element.40) | copy-start | bytes 3076
  46.6 2.0 %copy-start.26 = (f32[256]{0:T(256)S(1)}, f32[256]{0:T(256)}, u32[]{:S(2)}) copy-start(f32[256]{0:T(256)} %get-tuple-element.41) | copy-start | bytes 3076
  46.8 1.6 %copy-start.12 = (f32[256,6]{0,1:T(8,128)}, f32[256,6]{0,1:T(8,128)S(1)}, u32[]{:S(2)}) copy-start(f32[256,6]{0,1:T(8,128)S(1)} %fusion.47) | copy-start | bytes 18436
  49.3 10.9 %copy-start.4 = (bf16[256,512]{1,0:T(8,128)(2,1)S(1)}, bf16[256,512]{1,0:T(8,128)(2,1)}, u32[]{:S(2)}) copy-start(bf16[256,512]{1,0:T(8,128)(2,1)} %copy-done.3) | copy-start | bytes 786436
  49.5 10.7 %copy-start.6 = (bf16[256,512]{1,0:T(8,128)(2,1)S(1)}, bf16[256,512]{1,0:T(8,128)(2,1)}, u32[]{:S(2)}) copy-start(bf16[256,512]{1,0:T(8,128)(2,1)} %copy-done.5) | copy-start | bytes 786436
  49.5 10.7 %copy-start.8 = (bf16[256,512]{1,0:T(8,128)(2,1)S(1)}, bf16[256,512]{1,0:T(8,128)(2,1)}, u32[]{:S(2)}) copy-start(bf16[256,512]{1,0:T(8,128)(2,1)} %copy-done.7) | copy-start | bytes 786436
  49.5 10.7 %copy-start.10 = (bf16[256,512]{1,0:T(8,128)(2,1)S(1)}, bf16[256,512]{1,0:T(8,128)(2,1)}, u32[]{:S(2)}) copy-start(bf16[256,512]{1,0:T(8,128)(2,1)} %copy-done.9) | copy-start | bytes 786436
  52.9 11.8 %collective-permute-start.5 = (bf16[6,66,256]{2,1,0:T(8,128)(2,1)}, bf16[6,66,256]{2,1,0:T(8,128)(2,1)}, u32[]{:S(2)}, u32[]{:S(2)}) collective-permute-start(bf16[6,66,256]{2,1,0:T(8,128)(2,1)} %fusion.41), channel_id=1, source_target_pairs={{0,4},{4,8},{8,12},{12,16},{16,20},{20,24},{24,28},{1,5},{5,9},{9,... | collective-permute-start | bytes 608264 | tf_op jit(solution)/shard_map/ppermute | solution.py:12
  58.2 7.5 %collective-permute-start.4 = (bf16[6,66,256]{2,1,0:T(8,128)(2,1)}, bf16[6,66,256]{2,1,0:T(8,128)(2,1)}, u32[]{:S(2)}, u32[]{:S(2)}) collective-permute-start(bf16[6,66,256]{2,1,0:T(8,128)(2,1)} %fusion.41), channel_id=1, source_target_pairs={{0,8},{4,12},{8,16},{12,20},{16,24},{20,28},{1,9},{5,13},{9,17},{1... | collective-permute-start | bytes 608264 | tf_op jit(solution)/shard_map/ppermute | solution.py:12
  64.3 2.6 %copy-start.23 = (pred[66]{0:T(512)(128)(4,1)S(1)}, pred[66]{0:T(512)(128)(4,1)}, u32[]{:S(2)}) copy-start(pred[66]{0:T(512)(128)(4,1)} %iota_compare_fusion.3) | copy-start | bytes 202
  64.7 5.7 %copy-start.11 = (pred[256,256]{1,0:T(8,128)(4,1)S(1)}, pred[256,256]{1,0:T(8,128)(4,1)}, u32[]{:S(2)}) copy-start(pred[256,256]{1,0:T(8,128)(4,1)} %fusion.46) | copy-start | bytes 196612
  64.7 5.7 %copy-start.13 = (f32[256,6]{0,1:T(8,128)S(1)}, f32[256,6]{0,1:T(8,128)}, u32[]{:S(2)}) copy-start(f32[256,6]{0,1:T(8,128)} %copy-done.12) | copy-start | bytes 18436
  64.8 5.7 %copy-start.19 = (f32[256,6]{0,1:T(8,128)S(1)}, f32[256,6]{0,1:T(8,128)}, u32[]{:S(2)}) copy-start(f32[256,6]{0,1:T(8,128)} %copy-done.18) | copy-start | bytes 18436
  64.8 5.7 %copy-start.35 = (f32[6]{0:T(128)S(1)}, f32[6]{0:T(128)}, u32[]{:S(2)}) copy-start(f32[6]{0:T(128)} %param.26) | copy-start | bytes 76
  67.0 7.6 %collective-permute-start.6 = (bf16[6,66,256]{2,1,0:T(8,128)(2,1)S(1)}, bf16[6,66,256]{2,1,0:T(8,128)(2,1)S(1)}, u32[]{:S(2)}, u32[]{:S(2)}) collective-permute-start(bf16[6,66,256]{2,1,0:T(8,128)(2,1)S(1)} %fusion.42), channel_id=1, source_target_pairs={{0,8},{4,12},{8,16},{12,20},{16,24},{20,28},{1,9},{5,13},{9,17},{1... | collective-permute-start | bytes 608264 | tf_op jit(solution)/shard_map/ppermute | solution.py:12
  74.9 8.6 %collective-permute-start.7 = (bf16[6,66,256]{2,1,0:T(8,128)(2,1)S(1)}, bf16[6,66,256]{2,1,0:T(8,128)(2,1)S(1)}, u32[]{:S(2)}, u32[]{:S(2)}) collective-permute-start(bf16[6,66,256]{2,1,0:T(8,128)(2,1)S(1)} %fusion.43), channel_id=1, source_target_pairs={{0,16},{4,20},{8,24},{12,28},{1,17},{5,21},{9,25},{13,29},{2,18},{... | collective-permute-start | bytes 608264 | tf_op jit(solution)/shard_map/ppermute | solution.py:12
  83.5 1.8 %copy-start.27 = (pred[8]{0:T(512)(128)(4,1)S(1)}, pred[8]{0:T(512)(128)(4,1)}, u32[]{:S(2)}) copy-start(pred[8]{0:T(512)(128)(4,1)} %get-tuple-element.21) | copy-start | bytes 28

commit v13 on v10

--- a/solution.py
+++ b/solution.py
@@ -12,39 +12,45 @@
     return lax.ppermute(array, axis, pairs)
 
 
-def combine_packed(earlier, later):
-    rows = later.shape[1] - 2
-    d_e, d_l = earlier[:, rows : rows + 1, :], later[:, rows : rows + 1, :]
-    state = d_l * earlier[:, :rows, :] + later[:, :rows, :]
+def combine_packed(earlier, later, heads):
+    extra = -(-2 * heads // 16) * 16
+    rows = later.shape[0] - extra
+    d_e = earlier[rows : rows + heads]
+    d_l = later[rows : rows + heads]
+    head_dim = rows // heads
+    state = d_l[:, None, :] * earlier[:rows].reshape(heads, head_dim, -1) + later[:rows].reshape(heads, head_dim, -1)
     decay = d_e * d_l
-    return jnp.concatenate([state, decay, decay], axis=1)
-
-
-def received(packed, axis, by):
+    spare = jnp.zeros((extra - 2 * heads, later.shape[1]), later.dtype)
+    return jnp.concatenate([state.reshape(rows, -1), decay, decay, spare], axis=0)
+
+
+def received(packed, axis, by, heads):
     place = lax.axis_index(axis)
-    rows = packed.shape[1] - 2
-    row = lax.broadcasted_iota(jnp.int32, packed.shape, 1)
+    extra = -(-2 * heads // 16) * 16
+    rows = packed.shape[0] - extra
+    row = lax.broadcasted_iota(jnp.int32, packed.shape, 0)
     high = packed.astype(jnp.bfloat16)
     low = (packed - high.astype(jnp.float32)).astype(jnp.bfloat16)
-    wire = jnp.where(row == rows + 1, low, high)
+    wire = jnp.where((row >= rows + heads) & (row < rows + 2 * heads), low, high)
     got = shifted(wire, axis, by).astype(jnp.float32)
     missing = (place < by).astype(jnp.float32)
-    decay = got[:, rows : rows + 1, :] + got[:, rows + 1 :, :] + missing
-    return jnp.concatenate([got[:, :rows, :], decay, decay], axis=1)
-
-
-def exclusive_scan(packed, axis, side):
+    decay = got[rows : rows + heads] + got[rows + heads : rows + 2 * heads] + missing
+    spare = jnp.zeros((extra - 2 * heads, packed.shape[1]), packed.dtype)
+    return jnp.concatenate([got[:rows], decay, decay, spare], axis=0)
+
+
+def exclusive_scan(packed, axis, side, heads):
     count = lax.axis_size(axis)
     if count == 1:
-        return received(packed, axis, 1), side
-    held = received(packed, axis, 1)
+        return received(packed, axis, 1, heads), side
+    held = received(packed, axis, 1, heads)
     if count > 2:
-        held = combine_packed(received(packed, axis, 2), held)
+        held = combine_packed(received(packed, axis, 2, heads), held, heads)
     cover = 2
     while cover < count - 1:
         if cover * 2 >= count - 1:
             held, side = lax.optimization_barrier((held, side))
-        held = combine_packed(received(held, axis, cover), held)
+        held = combine_packed(received(held, axis, cover, heads), held, heads)
         cover *= 2
     return held, side
 
@@ -208,17 +214,27 @@
     intra, state_out, carry_in, block_decay = local_terms(
         x_heads, b_rows, c_rows, step_size, decay_log, segment_ids, seg_before
     )
-    decay_rows = jnp.broadcast_to(block_decay[:, None, None], (heads_dev, 2, state_dim))
-    packed = jnp.concatenate([state_out, decay_rows], axis=1)
-    local_y = intra + skip_gain[None, :, None] * x_heads
+    decay_rows = jnp.broadcast_to(block_decay[:, None], (heads_dev, state_dim))
+    spare = jnp.zeros((-(-2 * heads_dev // 16) * 16 - 2 * heads_dev, state_dim), jnp.float32)
+    packed = jnp.concatenate(
+        [state_out.reshape(heads_dev * head_dim, state_dim), decay_rows, decay_rows, spare], axis=0
+    )
     gate = jax.nn.silu(z_raw.astype(jnp.float32)).reshape(tok_dev, heads_dev, head_dim)
-    scanned, (local_y, gate, carry_in) = exclusive_scan(packed, "seq", (local_y, gate, carry_in))
-    state_in = scanned[:, :head_dim, :]
-    incoming = jnp.einsum("tn,hpn->thp", c_rows, state_in, precision=precise)
-    y_block = local_y + carry_in[:, :, None] * incoming
-    gated = (y_block * gate).reshape(tok_dev, inner_dev).astype(jnp.bfloat16)
-    ordered = gated.reshape(seq_count, piece_rows, inner_dev)
-    outgoing = jnp.take(ordered, dealt_row, axis=0)
+    local_gated = (intra + skip_gain[None, :, None] * x_heads) * gate
+    carry_gated = carry_in[:, :, None] * gate
+
+    def dealt(rows):
+        return jnp.take(rows.reshape((seq_count, piece_rows) + rows.shape[1:]), dealt_row, axis=0).reshape(
+            rows.shape
+        )
+
+    side = (dealt(local_gated), dealt(carry_gated), dealt(c_rows))
+    scanned, (local_gated, carry_gated, c_dealt) = exclusive_scan(packed, "seq", side, heads_dev)
+    state_in = scanned[: heads_dev * head_dim].reshape(heads_dev, head_dim, state_dim)
+    incoming = jnp.einsum("tn,hpn->thp", c_dealt, state_in, precision=precise)
+    outgoing = (local_gated + carry_gated * incoming).astype(jnp.bfloat16).reshape(
+        seq_count, piece_rows, inner_dev
+    )
     returned = lax.all_to_all(outgoing, "seq", split_axis=0, concat_axis=0, tiled=True)
     return returned.reshape(tok_dev, inner_dev)
 

time: 98.8 us -> 115 us (1.16)
  other arithmetic: 7.83 us -> 19.3 us
  local copies, waits for them, and re-layouts: 8.56 us -> 17.9 us
  waiting for transfers between devices: 23.8 us -> 19.2 us
  starting transfers between devices: 30 us -> 27.3 us
    select_n x5 -> x8, other arithmetic: 1.14 us -> 5.46 us  [the longest x5 3.05 us: dealt(): jnp.take(rows.reshape((seq_count, piece_rows) + rows.shape[1:]), dealt_ro...]
    ppermute x5, waiting for transfers between devices: 8.39 us -> 4.38 us  [shifted(): return lax.ppermute(array, axis, pairs)]
    mul x0 -> x2, other arithmetic: none -> 2.34 us  [the longest x1 1.56 us: per_device(): carry_gated = carry_in[:, :, None] * gate]
    gather x1 -> x3, local copies, waits for them, and re-layouts: 0.59 us -> 2.87 us  [dealt(): jnp.take(rows.reshape((seq_count, piece_rows) + rows.shape[1:]), dealt_ro...]
    ppermute x5, starting transfers between devices: 19.5 us -> 17.6 us  [shifted(): return lax.ppermute(array, axis, pairs)]
    convert_element_type x3, other arithmetic: 0.09 us -> 1.95 us  [received(): got = shifted(wire, axis, by).astype(jnp.float32)]
    slice x2, local copies, waits for them, and re-layouts: 1.93 us -> 0.19 us  [per_device(): x_heads = activated[:, :inner_dev].reshape(tok_dev, heads_dev, head_dim)]
    slice x1 -> x5, local copies, waits for them, and re-layouts: 0.01 us -> 1.66 us  [the longest x1 0.94 us: received(): return jnp.concatenate([got[:rows], decay, decay, spare], axis=0)]
  transfers between devices with their start and end apart: 11 -> 11, of which waited for: 8 -> 5; matrix products, arithmetic and copies ran while one was open for 10% -> 22% of each run, Pallas kernels for 0% -> 0%
where the time goes in v13:
time: 115 us; the launch traced here: 114 us
  starting transfers between devices  27.3 us (24%)
  blocking collectives  19.7 us (17%)
  other arithmetic  19.3 us (17%)
  waiting for transfers between devices  19.2 us (17%)
  local copies, waits for them, and re-layouts  17.9 us (16%)
  matrix products  6.55 us (6%)
  between operations  3.78 us (3%)
    all_to_all x1, blocking collectives, per_device(): lax.all_to_all(outgoing, 'seq', split_axis=0, concat_axis=0, tiled=True)  19.7 us
    ppermute x5, starting transfers between devices, shifted(): return lax.ppermute(array, axis, pairs)  17.6 us
    all_to_all x1, starting transfers between devices, per_device(): lax.all_to_all(slot_rows, 'seq', split_axis=0, concat_axis=0, tiled=True)  7.41 us
    ppermute x2, waiting for transfers between devices, exchange(): other = lax.ppermute(held, axis, [(i, i ^ bit) for i in range(count)])  6.95 us
    ppermute x1, waiting for transfers between devices, summed_columns(): kept = kept + lax.ppermute(kept, axis, [(i, i ^ bit) for i in range(count)])  5.08 us
    ppermute x5, waiting for transfers between devices, shifted(): return lax.ppermute(array, axis, pairs)  4.38 us
    select_n x5, other arithmetic, dealt(): jnp.take(rows.reshape((seq_count, piece_rows) + rows.shape[1:]), dealt_ro...  3.05 us
    gather x3, local copies, waits for them, and re-layouts, dealt(): jnp.take(rows.reshape((seq_count, piece_rows) + rows.shape[1:]), dealt_ro...  2.87 us
  transfers between devices with their start and end apart: 11, of which 5 were waited for; matrix products, arithmetic and copies ran while one was open for 22% of the time, Pallas kernels for 0%

profile of v13, /device:TPU:0, one launch (start us, length us, event | category | flops | bytes accessed | tf_op | source)
XLA Modules:
  0.0 113.7 jit_solution(14082216915171785682)
XLA Ops:
  0.0 7.4 %all-to-all-start = ((bf16[8,32,512]{2,1,0:T(8,128)(2,1)}), bf16[8,32,512]{2,1,0:T(8,128)(2,1)S(1)}, u32[]{:S(2)}, u32[]{:S(2)}) async-start(bf16[8,32,512]{2,1,0:T(8,128)(2,1)} %bitcast.67), calls=%async_computation | async-start | bytes 524288 | tf_op jit(solution)/shard_map/all_to_all | solution.py:176
  7.4 0.7 compare_and_fusion
  8.1 1.0 sort.17
  9.1 0.8 reduce-window.8
  10.7 0.7 fusion.52
  12.1 0.7 exponential_negate_fusion
  12.8 0.7 broadcast_compare_fusion.1
  13.5 2.8 %all-to-all-done = bf16[8,32,512]{2,1,0:T(8,128)(2,1)S(1)} async-done(((bf16[8,32,512]{2,1,0:T(8,128)(2,1)}), bf16[8,32,512]{2,1,0:T(8,128)(2,1)S(1)}, u32[]{:S(2)}, u32[]{:S(2)}) %all-to-all-start) | async-done | bytes 262176 | tf_op jit(solution)/shard_map/all_to_all | solution.py:176
  18.1 0.7 fusion.36
  18.9 1.5 %collective-permute-start = (bf16[256,512]{1,0:T(8,128)(2,1)S(1)}, bf16[256,512]{1,0:T(8,128)(2,1)S(1)}, u32[]{:S(2)}, u32[]{:S(2)}) collective-permute-start(bf16[256,512]{1,0:T(8,128)(2,1)S(1)} %bitcast_select_fusion.1), channel_id=1, source_target_pairs={{0,2},{1,3},{2,0},{3,1},{4,6},{5,7},{6,4},{7,5},{8,10},{9,11},{10,... | collective-permute-start | bytes 786440 | tf_op jit(solution)/shard_map/ppermute | solution.py:65
  21.0 6.9 %collective-permute-done = bf16[256,512]{1,0:T(8,128)(2,1)S(1)} collective-permute-done((bf16[256,512]{1,0:T(8,128)(2,1)S(1)}, bf16[256,512]{1,0:T(8,128)(2,1)S(1)}, u32[]{:S(2)}, u32[]{:S(2)}) %collective-permute-start) | collective-permute-done | bytes 262176 | tf_op jit(solution)/shard_map/ppermute | solution.py:65
  28.1 5.1 %collective-permute-done.3 = f32[256,256]{1,0:T(8,128)S(1)} collective-permute-done((f32[256,256]{1,0:T(8,128)S(1)}, f32[256,256]{1,0:T(8,128)S(1)}, u32[]{:S(2)}, u32[]{:S(2)}) %collective-permute-start.3) | collective-permute-done | bytes 262176 | tf_op jit(solution)/shard_map/ppermute | solution.py:103
  33.8 0.7 fusion.59
  38.5 1.1 %pad_maximum_fusion = bf16[256,2048]{1,0:T(8,128)(2,1)S(1)} fusion(bf16[256,1024]{1,0:T(8,128)(2,1)} %collective-permute-done.1, bf16[256,512]{1,0:T(8,128)(2,1)S(1)} %collective-permute-done, bf16[256,512]{1,0:T(8,128)(2,1)S(1)} %bitcast_select_fusion.1), kind=kLoop, calls=%fused_computation.19 | loop fusion | flops 3145728 | bytes 2097152 | tf_op jit(solution)/shard_map/concatenate | solution.py:66
  41.5 0.8 copy.40
  42.4 0.7 convolution_convert_fusion.1
  43.1 0.7 copy-done.18
  43.8 0.7 divide_multiply_fusion.1
  44.5 3.3 %collective-permute-start.5 = (bf16[3,896]{1,0:T(4,128)(2,1)S(1)}, bf16[3,896]{1,0:T(4,128)(2,1)S(1)}, u32[]{:S(2)}, u32[]{:S(2)}) collective-permute-start(bf16[3,896]{1,0:T(4,128)(2,1)S(1)} %pad_maximum_fusion.3), channel_id=1, source_target_pairs={{0,4},{4,8},{8,12},{12,16},{16,20},{20,24},{24,28},{1,5},{5,9},{9,... | collective-permute-start | bytes 16136 | tf_op jit(solution)/shard_map/ppermute | solution.py:12
  47.9 1.2 %reshape.209 = f32[8,32,6,64]{3,2,1,0:T(8,128)} reshape(f32[256,384]{1,0:T(8,128)S(1)} %divide_multiply_fusion.1) | data formatting | bytes 786432 | tf_op jit(solution)/shard_map/reshape | solution.py:222
  49.1 1.6 %broadcast_multiply_fusion = f32[8,32,6,64]{3,2,1,0:T(8,128)S(1)} fusion(f32[8,32,6,64]{3,2,1,0:T(8,128)} %reshape.209, f32[8,32,6]{2,1,0:T(8,128)} %bitcast.65), kind=kLoop, calls=%fused_computation.39 | loop fusion | flops 98304 | bytes 792576 | tf_op jit(solution)/shard_map/mul | solution.py:224
  50.6 1.6 %gather_fusion.3 = f32[8,32,6,64]{3,2,1,0:T(8,128)} fusion(f32[8,32,6,64]{3,2,1,0:T(8,128)S(1)} %broadcast_multiply_fusion, s32[1024]{0:T(1024)S(1)} %get-tuple-element.42), kind=kCustom, calls=%fused_computation.1.clone | custom fusion | bytes 786464 | tf_op jit(solution)/shard_map/jit(_take)/gather | solution.py:227
  52.2 1.4 %broadcast_select_fusion = f32[8,32,6,64]{3,2,1,0:T(8,128)S(1)} fusion(f32[8,32,6,64]{3,2,1,0:T(8,128)} %gather_fusion.3, pred[8]{0:T(512)(128)(4,1)S(1)} %get-tuple-element.20), kind=kLoop, calls=%fused_computation.38 | loop fusion | flops 98304 | bytes 786440 | tf_op jit(solution)/shard_map/jit(_take)/select_n | solution.py:227
  53.6 1.1 %broadcast_select_fusion.2 = f32[6]{0:T(128)} fusion(pred[]{:T(512)} %bitcast.14, f32[6]{0:T(128)S(1)} %slice_reduce_fusion), kind=kLoop, calls=%fused_computation.118 | loop fusion | flops 6 | bytes 49 | tf_op jit(solution)/shard_map/jit(_where)/select_n | solution.py:153
  54.8 1.0 copy.31
  55.7 1.1 copy.36
  56.9 0.7 divide_multiply_fusion
  58.2 0.8 multiply_multiply_fusion
  59.5 0.7 broadcast_in_dim.114
  60.3 1.4 %fusion.32 = bf16[400,256]{1,0:T(8,128)(2,1)} fusion(f32[6,256]{1,0:T(8,128)S(1)} %broadcast_in_dim.114, f32[384,256]{1,0:T(8,128)S(1)} %fusion.40, f32[400]{0:T(512)S(1)} %pad.11.clone, pred[400]{0:T(512)(128)(4,1)} %fusion.51), kind=kLoop, calls=%fused_computation.57 | loop fusion | flops 819200 | bytes 606160 | tf_op jit(solution)/shard_map/jit(_where)/select_n | solution.py:34
  61.7 3.7 %collective-permute-start.7 = (bf16[400,256]{1,0:T(8,128)(2,1)}, bf16[400,256]{1,0:T(8,128)(2,1)}, u32[]{:S(2)}, u32[]{:S(2)}) collective-permute-start(bf16[400,256]{1,0:T(8,128)(2,1)} %fusion.32), channel_id=1, source_target_pairs={{0,4},{4,8},{8,12},{12,16},{16,20},{20,24},{24,28},{1,5},{5,9},{9,... | collective-permute-start | bytes 614408 | tf_op jit(solution)/shard_map/ppermute | solution.py:12
  65.4 2.5 %collective-permute-start.6 = (bf16[400,256]{1,0:T(8,128)(2,1)}, bf16[400,256]{1,0:T(8,128)(2,1)}, u32[]{:S(2)}, u32[]{:S(2)}) collective-permute-start(bf16[400,256]{1,0:T(8,128)(2,1)} %fusion.32), channel_id=1, source_target_pairs={{0,8},{4,12},{8,16},{12,20},{16,24},{20,28},{1,9},{5,13},{9,17},{1... | collective-permute-start | bytes 614408 | tf_op jit(solution)/shard_map/ppermute | solution.py:12
  67.9 1.9 %fusion.11 = f32[256,6,64]{0,2,1:T(8,128)S(1)} fusion(f32[256,6,64]{0,2,1:T(8,128)S(1)} %bitcast.66, f32[6,256]{1,0:T(8,128)S(1)} %bitcast.68, f32[256,256]{1,0:T(8,128)S(1)} %fusion.38, pred[256,256]{1,0:T(8,128)(4,1)S(1)} %copy-done.6, f32[256,6,64]{0,2,1:T(8,128)S(1)} %bitcast.60, f32[6]{0:T(128)S(1)} %copy-done.21, f32[256,6]{0,1:T(8,128)S(1)} %copy-done.10), kind=kOutput, calls=%fused_computation.11 | convolution fusion | flops 303562752 | bytes 1519640 | tf_op jit(solution)/shard_map/hts,shp->thp/dot_general | solution.py:144
  71.0 0.7 slice-done
  71.7 0.7 gather_fusion.1
  72.4 1.0 convert_element_type.93
  73.3 1.0 convert_element_type.91
  74.6 3.0 %collective-permute-start.8 = (bf16[400,256]{1,0:T(8,128)(2,1)S(1)}, bf16[400,256]{1,0:T(8,128)(2,1)S(1)}, u32[]{:S(2)}, u32[]{:S(2)}) collective-permute-start(bf16[400,256]{1,0:T(8,128)(2,1)S(1)} %fusion.33), channel_id=1, source_target_pairs={{0,8},{4,12},{8,16},{12,20},{16,24},{20,28},{1,9},{5,13},{9,17},{1... | collective-permute-start | bytes 614408 | tf_op jit(solution)/shard_map/ppermute | solution.py:12
  77.6 0.8 bitcast_select_fusion
  78.4 2.7 %collective-permute-done.8 = bf16[400,256]{1,0:T(8,128)(2,1)S(1)} collective-permute-done((bf16[400,256]{1,0:T(8,128)(2,1)S(1)}, bf16[400,256]{1,0:T(8,128)(2,1)S(1)}, u32[]{:S(2)}, u32[]{:S(2)}) %collective-permute-start.8) | collective-permute-done | bytes 204832 | tf_op jit(solution)/shard_map/ppermute | solution.py:12
  81.3 0.8 fusion.34
  82.2 5.1 %collective-permute-start.9 = (bf16[400,256]{1,0:T(8,128)(2,1)}, bf16[400,256]{1,0:T(8,128)(2,1)}, u32[]{:S(2)}, u32[]{:S(2)}) collective-permute-start(bf16[400,256]{1,0:T(8,128)(2,1)} %fusion.34), channel_id=1, source_target_pairs={{0,16},{4,20},{8,24},{12,28},{1,17},{5,21},{9,25},{13,29},{2,18},{... | collective-permute-start | bytes 614408 | tf_op jit(solution)/shard_map/ppermute | solution.py:12
  87.3 1.0 copy.38
  88.6 1.6 %collective-permute-done.9 = bf16[400,256]{1,0:T(8,128)(2,1)} collective-permute-done((bf16[400,256]{1,0:T(8,128)(2,1)}, bf16[400,256]{1,0:T(8,128)(2,1)}, u32[]{:S(2)}, u32[]{:S(2)}) %collective-permute-start.9) | collective-permute-done | bytes 204832 | tf_op jit(solution)/shard_map/ppermute | solution.py:12
  90.2 0.9 slice.162
  91.2 1.5 %fusion.15 = bf16[256,6,64]{0,2,1:T(8,128)(2,1)S(1)} fusion(f32[256,6,64]{0,2,1:T(8,128)S(1)} %copy-done.3, f32[256,6,64]{0,2,1:T(8,128)S(1)} %copy.37, f32[6,64,256]{2,1,0:T(8,128)S(1)} %bitcast.61, bf16[6,64,256]{2,1,0:T(8,128)(2,1)S(1)} %bitcast.63, f32[256,256]{1,0:T(8,128)} %bitcast_select_fusion, f32[6,256]{1,0:T(8,128)S(1)} %slice.130), kind=kOutput, calls=%fused_computation.14 | convolution fusion | flops 302579712 | bytes 1841152 | tf_op jit(solution)/shard_map/tn,hpn->thp/dot_general | solution.py:234
  93.3 19.7 %all_to_all.10 = bf16[8,32,384]{2,1,0:T(8,128)(2,1)S(1)} all-to-all(bf16[8,32,384]{2,1,0:T(8,128)(2,1)S(1)} %reshape.215), channel_id=1, replica_groups=mesh['seq'=8,'fsdp'=4] {'seq'}, dimensions={0} | all-to-all | bytes 393216 | tf_op jit(solution)/shard_map/all_to_all | solution.py:238
  113.0 0.7 copy.43
  (111 shorter events, 11.1 us)
Async XLA Ops:
  0.0 42.4 %copy-start = (bf16[2048,384]{1,0:T(8,128)(2,1)S(1)}, bf16[2048,384]{1,0:T(8,128)(2,1)}, u32[]{:S(2)}) copy-start(bf16[2048,384]{1,0:T(8,128)(2,1)} %param.18) | copy-start | bytes 4718596
  0.0 17.0 %copy-start.4 = (bf16[512,512]{1,0:T(8,128)(2,1)S(1)}, bf16[512,512]{1,0:T(8,128)(2,1)}, u32[]{:S(2)}) copy-start(bf16[512,512]{1,0:T(8,128)(2,1)} %param.20) | copy-start | bytes 1572868
  0.0 16.3 %all-to-all-start = ((bf16[8,32,512]{2,1,0:T(8,128)(2,1)}), bf16[8,32,512]{2,1,0:T(8,128)(2,1)S(1)}, u32[]{:S(2)}, u32[]{:S(2)}) async-start(bf16[8,32,512]{2,1,0:T(8,128)(2,1)} %bitcast.67), calls=%async_computation | async-start | bytes 524288 | tf_op jit(solution)/shard_map/all_to_all | solution.py:176
  8.1 44.1 %copy-start.14 = (pred[8]{0:T(512)(128)(4,1)}, pred[8]{0:T(512)(128)(4,1)S(1)}, u32[]{:S(2)}) copy-start(pred[8]{0:T(512)(128)(4,1)S(1)} %get-tuple-element.20) | copy-start | bytes 28
  16.9 4.1 %copy-start.13 = (f32[4,384]{1,0:T(4,128)S(1)}, f32[4,384]{1,0:T(4,128)}, u32[]{:S(2)}) copy-start(f32[4,384]{1,0:T(4,128)} %param.22) | copy-start | bytes 18436
  16.9 4.1 %copy-start.12 = (f32[4,512]{1,0:T(4,128)S(1)}, f32[4,512]{1,0:T(4,128)}, u32[]{:S(2)}) copy-start(f32[4,512]{1,0:T(4,128)} %param.23) | copy-start | bytes 24580
  17.4 16.4 %copy-start.11 = (s32[4]{0:T(128)S(1)}, s32[4]{0:T(128)}, u32[]{:S(2)}) copy-start(s32[4]{0:T(128)} %constant.105.clone) | copy-start | bytes 52
  17.4 3.0 %collective-permute-start.2 = (f32[256,256]{1,0:T(8,128)S(1)}, f32[256,256]{1,0:T(8,128)S(1)}, u32[]{:S(2)}, u32[]{:S(2)}) collective-permute-start(f32[256,256]{1,0:T(8,128)S(1)} %constant_dynamic-slice_fusion), channel_id=1, source_target_pairs={{0,1},{1,0},{2,3},{3,2},{4,5},{5,4},{6,7},{7,6},{8,9},{9,8},{10,11... | collective-permute-start | bytes 786440 | tf_op jit(solution)/shard_map/ppermute | solution.py:100
  18.9 9.1 %collective-permute-start = (bf16[256,512]{1,0:T(8,128)(2,1)S(1)}, bf16[256,512]{1,0:T(8,128)(2,1)S(1)}, u32[]{:S(2)}, u32[]{:S(2)}) collective-permute-start(bf16[256,512]{1,0:T(8,128)(2,1)S(1)} %bitcast_select_fusion.1), channel_id=1, source_target_pairs={{0,2},{1,3},{2,0},{3,1},{4,6},{5,7},{6,4},{7,5},{8,10},{9,11},{10,... | collective-permute-start | bytes 786440 | tf_op jit(solution)/shard_map/ppermute | solution.py:65
  20.4 12.8 %collective-permute-start.3 = (f32[256,256]{1,0:T(8,128)S(1)}, f32[256,256]{1,0:T(8,128)S(1)}, u32[]{:S(2)}, u32[]{:S(2)}) collective-permute-start(f32[256,256]{1,0:T(8,128)S(1)} %dynamic-slice_add_fusion), channel_id=1, source_target_pairs={{0,2},{1,3},{2,0},{3,1},{4,6},{5,7},{6,4},{7,5},{8,10},{9,11},{10,... | collective-permute-start | bytes 786440 | tf_op jit(solution)/shard_map/ppermute | solution.py:103
  28.0 10.5 %collective-permute-start.1 = (bf16[256,1024]{1,0:T(8,128)(2,1)S(1)}, bf16[256,1024]{1,0:T(8,128)(2,1)}, u32[]{:S(2)}, u32[]{:S(2)}) collective-permute-start(bf16[256,1024]{1,0:T(8,128)(2,1)S(1)} %pad_maximum_fusion.2), channel_id=1, source_target_pairs={{0,1},{1,0},{2,3},{3,2},{4,5},{5,4},{6,7},{7,6},{8,9},{9,8},{10,11... | collective-permute-start | bytes 1572872 | tf_op jit(solution)/shard_map/ppermute | solution.py:65
  33.2 5.2 %collective-permute-start.4 = (bf16[256,256]{1,0:T(8,128)(2,1)S(1)}, bf16[256,256]{1,0:T(8,128)(2,1)S(1)}, u32[]{:S(2)}, u32[]{:S(2)}) collective-permute-start(bf16[256,256]{1,0:T(8,128)(2,1)S(1)} %add_convert_fusion), channel_id=1, source_target_pairs={{0,1},{1,0},{2,3},{3,2},{4,5},{5,4},{6,7},{7,6},{8,9},{9,8},{10,11... | collective-permute-start | bytes 393224 | tf_op jit(solution)/shard_map/ppermute | solution.py:106
  39.7 0.8 copy-start.19
  39.7 0.8 copy-start.20
  40.9 0.6 copy-start.9
  41.1 1.3 %copy-start.7 = (f32[256,6]{0,1:T(8,128)}, f32[256,6]{0,1:T(8,128)S(1)}, u32[]{:S(2)}) copy-start(f32[256,6]{0,1:T(8,128)S(1)} %fusion.37) | copy-start | bytes 18436
  42.4 1.4 %copy-start.18 = (bf16[2048,384]{1,0:T(8,128)(2,1)S(1)}, bf16[2048,384]{1,0:T(8,128)(2,1)}, u32[]{:S(2)}) copy-start(bf16[2048,384]{1,0:T(8,128)(2,1)} %param.19) | copy-start | bytes 4718596
  44.5 12.2 %collective-permute-start.5 = (bf16[3,896]{1,0:T(4,128)(2,1)S(1)}, bf16[3,896]{1,0:T(4,128)(2,1)S(1)}, u32[]{:S(2)}, u32[]{:S(2)}) collective-permute-start(bf16[3,896]{1,0:T(4,128)(2,1)S(1)} %pad_maximum_fusion.3), channel_id=1, source_target_pairs={{0,4},{4,8},{8,12},{12,16},{16,20},{20,24},{24,28},{1,5},{5,9},{9,... | collective-permute-start | bytes 16136 | tf_op jit(solution)/shard_map/ppermute | solution.py:12
  57.6 1.5 %copy-start.1 = (f32[256,896]{1,0:T(8,128)}, f32[256,896]{1,0:T(8,128)S(1)}, u32[]{:S(2)}) copy-start(f32[256,896]{1,0:T(8,128)S(1)} %divide_multiply_fusion) | copy-start | bytes 2752516
  58.2 9.7 %copy-start.5 = (f32[256,384]{0,1:T(8,128)S(1)}, f32[256,384]{0,1:T(8,128)}, u32[]{:S(2)}) copy-start(f32[256,384]{0,1:T(8,128)} %copy.31) | copy-start | bytes 1179652
  58.2 9.6 %copy-start.6 = (pred[256,256]{1,0:T(8,128)(4,1)S(1)}, pred[256,256]{1,0:T(8,128)(4,1)}, u32[]{:S(2)}) copy-start(pred[256,256]{1,0:T(8,128)(4,1)} %fusion.36) | copy-start | bytes 196612
  58.2 9.6 %copy-start.8 = (f32[256,6]{0,1:T(8,128)S(1)}, f32[256,6]{0,1:T(8,128)}, u32[]{:S(2)}) copy-start(f32[256,6]{0,1:T(8,128)} %copy-done.7) | copy-start | bytes 18436
  58.2 9.6 %copy-start.10 = (f32[256,6]{0,1:T(8,128)S(1)}, f32[256,6]{0,1:T(8,128)}, u32[]{:S(2)}) copy-start(f32[256,6]{0,1:T(8,128)} %copy-done.9) | copy-start | bytes 18436
  58.2 9.6 %copy-start.21 = (f32[6]{0:T(128)S(1)}, f32[6]{0:T(128)}, u32[]{:S(2)}) copy-start(f32[6]{0:T(128)} %param.26) | copy-start | bytes 76
  61.7 10.7 %collective-permute-start.7 = (bf16[400,256]{1,0:T(8,128)(2,1)}, bf16[400,256]{1,0:T(8,128)(2,1)}, u32[]{:S(2)}, u32[]{:S(2)}) collective-permute-start(bf16[400,256]{1,0:T(8,128)(2,1)} %fusion.32), channel_id=1, source_target_pairs={{0,4},{4,8},{8,12},{12,16},{16,20},{20,24},{24,28},{1,5},{5,9},{9,... | collective-permute-start | bytes 614408 | tf_op jit(solution)/shard_map/ppermute | solution.py:12
  65.4 8.0 %collective-permute-start.6 = (bf16[400,256]{1,0:T(8,128)(2,1)}, bf16[400,256]{1,0:T(8,128)(2,1)}, u32[]{:S(2)}, u32[]{:S(2)}) collective-permute-start(bf16[400,256]{1,0:T(8,128)(2,1)} %fusion.32), channel_id=1, source_target_pairs={{0,8},{4,12},{8,16},{12,20},{16,24},{20,28},{1,9},{5,13},{9,17},{1... | collective-permute-start | bytes 614408 | tf_op jit(solution)/shard_map/ppermute | solution.py:12
  70.0 0.7 copy-start.15
  70.7 1.0 slice-start
  71.0 3.4 %copy-start.16 = (pred[400]{0:T(512)(128)(4,1)S(1)}, pred[400]{0:T(512)(128)(4,1)}, u32[]{:S(2)}) copy-start(pred[400]{0:T(512)(128)(4,1)} %fusion.51) | copy-start | bytes 1204
  72.4 5.2 %copy-start.17 = (pred[256]{0:T(512)(128)(4,1)S(1)}, pred[256]{0:T(512)(128)(4,1)}, u32[]{:S(2)}) copy-start(pred[256]{0:T(512)(128)(4,1)} %broadcast_in_dim.119) | copy-start | bytes 772
  74.6 6.5 %collective-permute-start.8 = (bf16[400,256]{1,0:T(8,128)(2,1)S(1)}, bf16[400,256]{1,0:T(8,128)(2,1)S(1)}, u32[]{:S(2)}, u32[]{:S(2)}) collective-permute-start(bf16[400,256]{1,0:T(8,128)(2,1)S(1)} %fusion.33), channel_id=1, source_target_pairs={{0,8},{4,12},{8,16},{12,20},{16,24},{20,28},{1,9},{5,13},{9,17},{1... | collective-permute-start | bytes 614408 | tf_op jit(solution)/shard_map/ppermute | solution.py:12
  81.2 7.1 %copy-start.2 = (f32[8,32,6,64]{3,1,0,2:T(8,128)S(1)}, f32[8,32,6,64]{3,1,0,2:T(8,128)}, u32[]{:S(2)}) copy-start(f32[8,32,6,64]{3,1,0,2:T(8,128)} %copy.36) | copy-start | bytes 1179652
  82.2 8.1 %collective-permute-start.9 = (bf16[400,256]{1,0:T(8,128)(2,1)}, bf16[400,256]{1,0:T(8,128)(2,1)}, u32[]{:S(2)}, u32[]{:S(2)}) collective-permute-start(bf16[400,256]{1,0:T(8,128)(2,1)} %fusion.34), channel_id=1, source_target_pairs={{0,16},{4,20},{8,24},{12,28},{1,17},{5,21},{9,25},{13,29},{2,18},{... | collective-permute-start | bytes 614408 | tf_op jit(solution)/shard_map/ppermute | solution.py:12
  88.3 2.8 %copy-start.3 = (f32[256,6,64]{0,2,1:T(8,128)S(1)}, f32[256,6,64]{0,2,1:T(8,128)}, u32[]{:S(2)}) copy-start(f32[256,6,64]{0,2,1:T(8,128)} %copy.38) | copy-start | bytes 1179652

commit v14 on v13

--- a/solution.py
+++ b/solution.py
@@ -219,22 +219,15 @@
     packed = jnp.concatenate(
         [state_out.reshape(heads_dev * head_dim, state_dim), decay_rows, decay_rows, spare], axis=0
     )
+    local_y = intra + skip_gain[None, :, None] * x_heads
     gate = jax.nn.silu(z_raw.astype(jnp.float32)).reshape(tok_dev, heads_dev, head_dim)
-    local_gated = (intra + skip_gain[None, :, None] * x_heads) * gate
-    carry_gated = carry_in[:, :, None] * gate
-
-    def dealt(rows):
-        return jnp.take(rows.reshape((seq_count, piece_rows) + rows.shape[1:]), dealt_row, axis=0).reshape(
-            rows.shape
-        )
-
-    side = (dealt(local_gated), dealt(carry_gated), dealt(c_rows))
-    scanned, (local_gated, carry_gated, c_dealt) = exclusive_scan(packed, "seq", side, heads_dev)
+    scanned, (local_y, gate, carry_in) = exclusive_scan(packed, "seq", (local_y, gate, carry_in), heads_dev)
     state_in = scanned[: heads_dev * head_dim].reshape(heads_dev, head_dim, state_dim)
-    incoming = jnp.einsum("tn,hpn->thp", c_dealt, state_in, precision=precise)
-    outgoing = (local_gated + carry_gated * incoming).astype(jnp.bfloat16).reshape(
-        seq_count, piece_rows, inner_dev
-    )
+    incoming = jnp.einsum("tn,hpn->thp", c_rows, state_in, precision=precise)
+    y_block = local_y + carry_in[:, :, None] * incoming
+    gated = (y_block * gate).reshape(tok_dev, inner_dev).astype(jnp.bfloat16)
+    ordered = gated.reshape(seq_count, piece_rows, inner_dev)
+    outgoing = jnp.take(ordered, dealt_row, axis=0)
     returned = lax.all_to_all(outgoing, "seq", split_axis=0, concat_axis=0, tiled=True)
     return returned.reshape(tok_dev, inner_dev)
 

time: 115 us -> 97.5 us (0.85)
  other arithmetic: 19.3 us -> 8.04 us
  local copies, waits for them, and re-layouts: 17.9 us -> 8.67 us
  waiting for transfers between devices: 19.2 us -> 23.1 us
  starting transfers between devices: 27.3 us -> 30 us
  blocking collectives: 19.7 us -> 17.7 us
    ppermute x5, waiting for transfers between devices: 4.38 us -> 7.67 us  [shifted(): return lax.ppermute(array, axis, pairs)]
    gather x3 -> x1, local copies, waits for them, and re-layouts: 2.87 us -> 0.59 us  [per_device(): outgoing = jnp.take(ordered, dealt_row, axis=0)]
    select_n x5 -> x2, other arithmetic: 3.05 us -> 0.79 us  [per_device(): outgoing = jnp.take(ordered, dealt_row, axis=0)]
    all_to_all x1, blocking collectives: 19.7 us -> 17.7 us  [per_device(): lax.all_to_all(outgoing, 'seq', split_axis=0, concat_axis=0, tiled=True)]
    ppermute x5, starting transfers between devices: 17.6 us -> 19.5 us  [shifted(): return lax.ppermute(array, axis, pairs)]
    select_n x3, other arithmetic: 2.41 us -> 0.46 us  [received(): jnp.where((row >= rows + heads) & (row < rows + 2 * heads), low, high)]
    convert_element_type x3, other arithmetic: 1.95 us -> 0.09 us  [received(): got = shifted(wire, axis, by).astype(jnp.float32)]
    slice x2, local copies, waits for them, and re-layouts: 0.19 us -> 1.93 us  [per_device(): x_heads = activated[:, :inner_dev].reshape(tok_dev, heads_dev, head_dim)]
  transfers between devices with their start and end apart: 11 -> 11, of which waited for: 5 -> 8; matrix products, arithmetic and copies ran while one was open for 22% -> 10% of each run, Pallas kernels for 0% -> 0%
where the time goes in v14:
time: 97.5 us; the launch traced here: 96.9 us
  starting transfers between devices  30 us (31%)
  waiting for transfers between devices  23.1 us (24%)
  blocking collectives  17.7 us (18%)
  local copies, waits for them, and re-layouts  8.67 us (9%)
  other arithmetic  8.04 us (8%)
  matrix products  5.61 us (6%)
  between operations  3.71 us (4%)
    ppermute x5, starting transfers between devices, shifted(): return lax.ppermute(array, axis, pairs)  19.5 us
    all_to_all x1, blocking collectives, per_device(): lax.all_to_all(outgoing, 'seq', split_axis=0, concat_axis=0, tiled=True)  17.7 us
    ppermute x5, waiting for transfers between devices, shifted(): return lax.ppermute(array, axis, pairs)  7.67 us
    all_to_all x1, starting transfers between devices, per_device(): lax.all_to_all(slot_rows, 'seq', split_axis=0, concat_axis=0, tiled=True)  7.41 us
    ppermute x2, waiting for transfers between devices, exchange(): other = lax.ppermute(held, axis, [(i, i ^ bit) for i in range(count)])  6.25 us
    ppermute x1, waiting for transfers between devices, summed_columns(): kept = kept + lax.ppermute(kept, axis, [(i, i ^ bit) for i in range(count)])  5.06 us
    all_to_all x1, waiting for transfers between devices, per_device(): lax.all_to_all(slot_rows, 'seq', split_axis=0, concat_axis=0, tiled=True)  4.13 us
    unnamed x22, local copies, waits for them, and re-layouts  2.03 us
  transfers between devices with their start and end apart: 11, of which 8 were waited for; matrix products, arithmetic and copies ran while one was open for 10% of the time, Pallas kernels for 0%

profile of v14, /device:TPU:0, one launch (start us, length us, event | category | flops | bytes accessed | tf_op | source)
XLA Modules:
  0.0 96.9 jit_solution(16946606418836655373)
XLA Ops:
  0.0 7.4 %all-to-all-start = ((bf16[8,32,512]{2,1,0:T(8,128)(2,1)}), bf16[8,32,512]{2,1,0:T(8,128)(2,1)S(1)}, u32[]{:S(2)}, u32[]{:S(2)}) async-start(bf16[8,32,512]{2,1,0:T(8,128)(2,1)} %bitcast.53), calls=%async_computation | async-start | bytes 524288 | tf_op jit(solution)/shard_map/all_to_all | solution.py:176
  7.4 0.8 reduce-window.8
  8.3 0.7 compare_and_fusion.1
  9.0 1.0 sort.17
  10.2 0.6 fusion.57
  11.5 0.7 broadcast_compare_fusion.1
  12.2 4.1 %all-to-all-done = bf16[8,32,512]{2,1,0:T(8,128)(2,1)S(1)} async-done(((bf16[8,32,512]{2,1,0:T(8,128)(2,1)}), bf16[8,32,512]{2,1,0:T(8,128)(2,1)S(1)}, u32[]{:S(2)}, u32[]{:S(2)}) %all-to-all-start) | async-done | bytes 262176 | tf_op jit(solution)/shard_map/all_to_all | solution.py:176
  16.3 0.6 gather_fusion
  17.1 0.3 fusion.59
  17.7 1.6 %collective-permute-start = (bf16[256,512]{1,0:T(8,128)(2,1)S(1)}, bf16[256,512]{1,0:T(8,128)(2,1)S(1)}, u32[]{:S(2)}, u32[]{:S(2)}) collective-permute-start(bf16[256,512]{1,0:T(8,128)(2,1)S(1)} %bitcast_select_fusion), channel_id=1, source_target_pairs={{0,2},{1,3},{2,0},{3,1},{4,6},{5,7},{6,4},{7,5},{8,10},{9,11},{10,... | collective-permute-start | bytes 786440 | tf_op jit(solution)/shard_map/ppermute | solution.py:65
  19.3 1.3 %collective-permute-start.3 = (f32[256,256]{1,0:T(8,128)S(1)}, f32[256,256]{1,0:T(8,128)S(1)}, u32[]{:S(2)}, u32[]{:S(2)}) collective-permute-start(f32[256,256]{1,0:T(8,128)S(1)} %dynamic-slice_add_fusion), channel_id=1, source_target_pairs={{0,2},{1,3},{2,0},{3,1},{4,6},{5,7},{6,4},{7,5},{8,10},{9,11},{10,... | collective-permute-start | bytes 786440 | tf_op jit(solution)/shard_map/ppermute | solution.py:103
  20.6 6.2 %collective-permute-done = bf16[256,512]{1,0:T(8,128)(2,1)S(1)} collective-permute-done((bf16[256,512]{1,0:T(8,128)(2,1)S(1)}, bf16[256,512]{1,0:T(8,128)(2,1)S(1)}, u32[]{:S(2)}, u32[]{:S(2)}) %collective-permute-start) | collective-permute-done | bytes 262176 | tf_op jit(solution)/shard_map/ppermute | solution.py:65
  27.0 5.1 %collective-permute-done.3 = f32[256,256]{1,0:T(8,128)S(1)} collective-permute-done((f32[256,256]{1,0:T(8,128)S(1)}, f32[256,256]{1,0:T(8,128)S(1)}, u32[]{:S(2)}, u32[]{:S(2)}) %collective-permute-start.3) | collective-permute-done | bytes 262176 | tf_op jit(solution)/shard_map/ppermute | solution.py:103
  32.2 0.7 fusion.58
  35.4 0.6 slice.119
  36.3 1.1 %pad_maximum_fusion = bf16[256,2048]{1,0:T(8,128)(2,1)S(1)} fusion(bf16[256,1024]{1,0:T(8,128)(2,1)} %collective-permute-done.1, bf16[256,512]{1,0:T(8,128)(2,1)S(1)} %collective-permute-done, bf16[256,512]{1,0:T(8,128)(2,1)S(1)} %bitcast_select_fusion), kind=kLoop, calls=%fused_computation.17 | loop fusion | flops 3145728 | bytes 2097152 | tf_op jit(solution)/shard_map/concatenate | solution.py:66
  37.6 0.6 copy-done.6
  38.2 0.4 compare_select_fusion
  38.6 0.2 fusion.35
  38.8 0.2 slice_reduce_fusion
  39.1 0.7 convolution_convert_fusion.1
  39.8 0.7 copy-done.5
  40.5 0.7 divide_multiply_fusion.1
  41.2 3.3 %collective-permute-start.5 = (bf16[3,896]{1,0:T(4,128)(2,1)S(1)}, bf16[3,896]{1,0:T(4,128)(2,1)S(1)}, u32[]{:S(2)}, u32[]{:S(2)}) collective-permute-start(bf16[3,896]{1,0:T(4,128)(2,1)S(1)} %pad_maximum_fusion.3), channel_id=1, source_target_pairs={{0,4},{4,8},{8,12},{12,16},{16,20},{20,24},{24,28},{1,5},{5,9},{9,... | collective-permute-start | bytes 16136 | tf_op jit(solution)/shard_map/ppermute | solution.py:12
  44.6 0.6 broadcast_select_fusion.1
  45.4 0.5 collective-permute-done.5
  46.0 0.7 divide_multiply_fusion
  46.7 0.8 slice.145
  47.5 1.2 %copy.21 = f32[256,384]{0,1:T(8,128)S(1)} copy(f32[256,384]{1,0:T(8,128)} %slice.145) | data formatting | bytes 786432 | tf_op jit(solution)/shard_map/slice | solution.py:211
  48.7 0.5 fusion.40
  49.4 4.2 %collective-permute-start.7 = (bf16[400,256]{1,0:T(8,128)(2,1)S(1)}, bf16[400,256]{1,0:T(8,128)(2,1)S(1)}, u32[]{:S(2)}, u32[]{:S(2)}) collective-permute-start(bf16[400,256]{1,0:T(8,128)(2,1)S(1)} %fusion.30), channel_id=1, source_target_pairs={{0,4},{4,8},{8,12},{12,16},{16,20},{20,24},{24,28},{1,5},{5,9},{9,... | collective-permute-start | bytes 614408 | tf_op jit(solution)/shard_map/ppermute | solution.py:12
  53.6 2.5 %collective-permute-start.6 = (bf16[400,256]{1,0:T(8,128)(2,1)S(1)}, bf16[400,256]{1,0:T(8,128)(2,1)S(1)}, u32[]{:S(2)}, u32[]{:S(2)}) collective-permute-start(bf16[400,256]{1,0:T(8,128)(2,1)S(1)} %fusion.30), channel_id=1, source_target_pairs={{0,8},{4,12},{8,16},{12,20},{16,24},{20,28},{1,9},{5,13},{9,17},{1... | collective-permute-start | bytes 614408 | tf_op jit(solution)/shard_map/ppermute | solution.py:12
  56.1 0.4 fusion.37
  56.5 0.9 collective-permute-done.7
  57.4 2.4 %collective-permute-done.6 = bf16[400,256]{1,0:T(8,128)(2,1)S(1)} collective-permute-done((bf16[400,256]{1,0:T(8,128)(2,1)S(1)}, bf16[400,256]{1,0:T(8,128)(2,1)S(1)}, u32[]{:S(2)}, u32[]{:S(2)}) %collective-permute-start.6) | collective-permute-done | bytes 204832 | tf_op jit(solution)/shard_map/ppermute | solution.py:12
  60.0 0.2 fusion.31
  60.2 5.2 %collective-permute-start.8 = (bf16[400,256]{1,0:T(8,128)(2,1)S(1)}, bf16[400,256]{1,0:T(8,128)(2,1)S(1)}, u32[]{:S(2)}, u32[]{:S(2)}) collective-permute-start(bf16[400,256]{1,0:T(8,128)(2,1)S(1)} %fusion.31), channel_id=1, source_target_pairs={{0,8},{4,12},{8,16},{12,20},{16,24},{20,28},{1,9},{5,13},{9,17},{1... | collective-permute-start | bytes 614408 | tf_op jit(solution)/shard_map/ppermute | solution.py:12
  65.3 1.9 %fusion.8 = f32[256,6,64]{0,2,1:T(8,128)S(1)} fusion(f32[6,256]{1,0:T(8,128)S(1)} %bitcast.54, f32[256,256]{1,0:T(8,128)S(1)} %fusion.37, pred[256,256]{1,0:T(8,128)(4,1)S(1)} %fusion.34, f32[256,6,64]{0,2,1:T(8,128)S(1)} %bitcast.48, f32[6]{0:T(128)S(1)} %copy-done.9, f32[256,6]{0,1:T(8,128)S(1)} %compare_select_fusion), kind=kOutput, calls=%fused_computation.8 | convolution fusion | flops 303464448 | bytes 1126424 | tf_op jit(solution)/shard_map/hts,shp->thp/dot_general | solution.py:144
  67.2 1.4 %collective-permute-done.8 = bf16[400,256]{1,0:T(8,128)(2,1)S(1)} collective-permute-done((bf16[400,256]{1,0:T(8,128)(2,1)S(1)}, bf16[400,256]{1,0:T(8,128)(2,1)S(1)}, u32[]{:S(2)}, u32[]{:S(2)}) %collective-permute-start.8) | collective-permute-done | bytes 204832 | tf_op jit(solution)/shard_map/ppermute | solution.py:12
  68.9 4.4 %collective-permute-start.9 = (bf16[400,256]{1,0:T(8,128)(2,1)S(1)}, bf16[400,256]{1,0:T(8,128)(2,1)S(1)}, u32[]{:S(2)}, u32[]{:S(2)}) collective-permute-start(bf16[400,256]{1,0:T(8,128)(2,1)S(1)} %fusion.32), channel_id=1, source_target_pairs={{0,16},{4,20},{8,24},{12,28},{1,17},{5,21},{9,25},{13,29},{2,18},{... | collective-permute-start | bytes 614408 | tf_op jit(solution)/shard_map/ppermute | solution.py:12
  73.3 0.7 fusion.52
  74.1 2.5 %collective-permute-done.9 = bf16[400,256]{1,0:T(8,128)(2,1)S(1)} collective-permute-done((bf16[400,256]{1,0:T(8,128)(2,1)S(1)}, bf16[400,256]{1,0:T(8,128)(2,1)S(1)}, u32[]{:S(2)}, u32[]{:S(2)}) %collective-permute-start.9) | collective-permute-done | bytes 204832 | tf_op jit(solution)/shard_map/ppermute | solution.py:12
  76.6 0.5 fusion.13
  77.2 0.3 copy.23
  77.5 0.3 convert_element_type.109
  77.8 0.6 gather_fusion.1
  78.5 17.7 %all_to_all.10 = bf16[8,32,384]{2,1,0:T(8,128)(2,1)S(1)} all-to-all(bf16[8,32,384]{2,1,0:T(8,128)(2,1)S(1)} %broadcast_select_fusion), channel_id=1, replica_groups=mesh['seq'=8,'fsdp'=4] {'seq'}, dimensions={0} | all-to-all | bytes 393216 | tf_op jit(solution)/shard_map/all_to_all | solution.py:231
  96.2 0.7 copy.26
  (69 shorter events, 2.6 us)
Async XLA Ops:
  0.0 39.1 %copy-start = (bf16[2048,384]{1,0:T(8,128)(2,1)S(1)}, bf16[2048,384]{1,0:T(8,128)(2,1)}, u32[]{:S(2)}) copy-start(bf16[2048,384]{1,0:T(8,128)(2,1)} %param.16) | copy-start | bytes 4718596
  0.0 17.0 %copy-start.1 = (bf16[512,512]{1,0:T(8,128)(2,1)S(1)}, bf16[512,512]{1,0:T(8,128)(2,1)}, u32[]{:S(2)}) copy-start(bf16[512,512]{1,0:T(8,128)(2,1)} %param.18) | copy-start | bytes 1572868
  0.0 16.3 %all-to-all-start = ((bf16[8,32,512]{2,1,0:T(8,128)(2,1)}), bf16[8,32,512]{2,1,0:T(8,128)(2,1)S(1)}, u32[]{:S(2)}, u32[]{:S(2)}) async-start(bf16[8,32,512]{2,1,0:T(8,128)(2,1)} %bitcast.53), calls=%async_computation | async-start | bytes 524288 | tf_op jit(solution)/shard_map/all_to_all | solution.py:176
  7.4 10.1 %copy-start.7 = (f32[6]{0:T(128)S(1)}, f32[6]{0:T(128)}, u32[]{:S(2)}) copy-start(f32[6]{0:T(128)} %param.23) | copy-start | bytes 76
  16.9 3.7 %copy-start.4 = (f32[4,384]{1,0:T(4,128)S(1)}, f32[4,384]{1,0:T(4,128)}, u32[]{:S(2)}) copy-start(f32[4,384]{1,0:T(4,128)} %param.20) | copy-start | bytes 18436
  16.9 3.7 %copy-start.3 = (f32[4,512]{1,0:T(4,128)S(1)}, f32[4,512]{1,0:T(4,128)}, u32[]{:S(2)}) copy-start(f32[4,512]{1,0:T(4,128)} %param.21) | copy-start | bytes 24580
  17.4 14.9 %copy-start.2 = (s32[4]{0:T(128)S(1)}, s32[4]{0:T(128)}, u32[]{:S(2)}) copy-start(s32[4]{0:T(128)} %constant.94.clone) | copy-start | bytes 52
  17.4 1.9 %collective-permute-start.2 = (f32[256,256]{1,0:T(8,128)S(1)}, f32[256,256]{1,0:T(8,128)S(1)}, u32[]{:S(2)}, u32[]{:S(2)}) collective-permute-start(f32[256,256]{1,0:T(8,128)S(1)} %constant_dynamic-slice_fusion), channel_id=1, source_target_pairs={{0,1},{1,0},{2,3},{3,2},{4,5},{5,4},{6,7},{7,6},{8,9},{9,8},{10,11... | collective-permute-start | bytes 786440 | tf_op jit(solution)/shard_map/ppermute | solution.py:100
  17.7 9.2 %collective-permute-start = (bf16[256,512]{1,0:T(8,128)(2,1)S(1)}, bf16[256,512]{1,0:T(8,128)(2,1)S(1)}, u32[]{:S(2)}, u32[]{:S(2)}) collective-permute-start(bf16[256,512]{1,0:T(8,128)(2,1)S(1)} %bitcast_select_fusion), channel_id=1, source_target_pairs={{0,2},{1,3},{2,0},{3,1},{4,6},{5,7},{6,4},{7,5},{8,10},{9,11},{10,... | collective-permute-start | bytes 786440 | tf_op jit(solution)/shard_map/ppermute | solution.py:65
  19.3 12.8 %collective-permute-start.3 = (f32[256,256]{1,0:T(8,128)S(1)}, f32[256,256]{1,0:T(8,128)S(1)}, u32[]{:S(2)}, u32[]{:S(2)}) collective-permute-start(f32[256,256]{1,0:T(8,128)S(1)} %dynamic-slice_add_fusion), channel_id=1, source_target_pairs={{0,2},{1,3},{2,0},{3,1},{4,6},{5,7},{6,4},{7,5},{8,10},{9,11},{10,... | collective-permute-start | bytes 786440 | tf_op jit(solution)/shard_map/ppermute | solution.py:103
  26.9 9.4 %collective-permute-start.1 = (bf16[256,1024]{1,0:T(8,128)(2,1)S(1)}, bf16[256,1024]{1,0:T(8,128)(2,1)}, u32[]{:S(2)}, u32[]{:S(2)}) collective-permute-start(bf16[256,1024]{1,0:T(8,128)(2,1)S(1)} %pad_maximum_fusion.2), channel_id=1, source_target_pairs={{0,1},{1,0},{2,3},{3,2},{4,5},{5,4},{6,7},{7,6},{8,9},{9,8},{10,11... | collective-permute-start | bytes 1572872 | tf_op jit(solution)/shard_map/ppermute | solution.py:65
  32.1 4.1 %collective-permute-start.4 = (bf16[256,256]{1,0:T(8,128)(2,1)S(1)}, bf16[256,256]{1,0:T(8,128)(2,1)S(1)}, u32[]{:S(2)}, u32[]{:S(2)}) collective-permute-start(bf16[256,256]{1,0:T(8,128)(2,1)S(1)} %add_convert_fusion), channel_id=1, source_target_pairs={{0,1},{1,0},{2,3},{3,2},{4,5},{5,4},{6,7},{7,6},{8,9},{9,8},{10,11... | collective-permute-start | bytes 393224 | tf_op jit(solution)/shard_map/ppermute | solution.py:106
  37.4 0.8 copy-start.6
  37.5 0.8 copy-start.8
  39.1 1.4 %copy-start.5 = (bf16[2048,384]{1,0:T(8,128)(2,1)S(1)}, bf16[2048,384]{1,0:T(8,128)(2,1)}, u32[]{:S(2)}) copy-start(bf16[2048,384]{1,0:T(8,128)(2,1)} %param.17) | copy-start | bytes 4718596
  41.2 4.7 %collective-permute-start.5 = (bf16[3,896]{1,0:T(4,128)(2,1)S(1)}, bf16[3,896]{1,0:T(4,128)(2,1)S(1)}, u32[]{:S(2)}, u32[]{:S(2)}) collective-permute-start(bf16[3,896]{1,0:T(4,128)(2,1)S(1)} %pad_maximum_fusion.3), channel_id=1, source_target_pairs={{0,4},{4,8},{8,12},{12,16},{16,20},{20,24},{24,28},{1,5},{5,9},{9,... | collective-permute-start | bytes 16136 | tf_op jit(solution)/shard_map/ppermute | solution.py:12
  49.4 8.0 %collective-permute-start.7 = (bf16[400,256]{1,0:T(8,128)(2,1)S(1)}, bf16[400,256]{1,0:T(8,128)(2,1)S(1)}, u32[]{:S(2)}, u32[]{:S(2)}) collective-permute-start(bf16[400,256]{1,0:T(8,128)(2,1)S(1)} %fusion.30), channel_id=1, source_target_pairs={{0,4},{4,8},{8,12},{12,16},{16,20},{20,24},{24,28},{1,5},{5,9},{9,... | collective-permute-start | bytes 614408 | tf_op jit(solution)/shard_map/ppermute | solution.py:12
  53.6 6.2 %collective-permute-start.6 = (bf16[400,256]{1,0:T(8,128)(2,1)S(1)}, bf16[400,256]{1,0:T(8,128)(2,1)S(1)}, u32[]{:S(2)}, u32[]{:S(2)}) collective-permute-start(bf16[400,256]{1,0:T(8,128)(2,1)S(1)} %fusion.30), channel_id=1, source_target_pairs={{0,8},{4,12},{8,16},{12,20},{16,24},{20,28},{1,9},{5,13},{9,17},{1... | collective-permute-start | bytes 614408 | tf_op jit(solution)/shard_map/ppermute | solution.py:12
  56.5 8.8 %copy-start.9 = (f32[6]{0:T(128)S(1)}, f32[6]{0:T(128)}, u32[]{:S(2)}) copy-start(f32[6]{0:T(128)} %param.24) | copy-start | bytes 76
  60.2 8.4 %collective-permute-start.8 = (bf16[400,256]{1,0:T(8,128)(2,1)S(1)}, bf16[400,256]{1,0:T(8,128)(2,1)S(1)}, u32[]{:S(2)}, u32[]{:S(2)}) collective-permute-start(bf16[400,256]{1,0:T(8,128)(2,1)S(1)} %fusion.31), channel_id=1, source_target_pairs={{0,8},{4,12},{8,16},{12,20},{16,24},{20,28},{1,9},{5,13},{9,17},{1... | collective-permute-start | bytes 614408 | tf_op jit(solution)/shard_map/ppermute | solution.py:12
  68.9 7.7 %collective-permute-start.9 = (bf16[400,256]{1,0:T(8,128)(2,1)S(1)}, bf16[400,256]{1,0:T(8,128)(2,1)S(1)}, u32[]{:S(2)}, u32[]{:S(2)}) collective-permute-start(bf16[400,256]{1,0:T(8,128)(2,1)S(1)} %fusion.32), channel_id=1, source_target_pairs={{0,16},{4,20},{8,24},{12,28},{1,17},{5,21},{9,25},{13,29},{2,18},{... | collective-permute-start | bytes 614408 | tf_op jit(solution)/shard_map/ppermute | solution.py:12

commit v15 on v14

--- a/solution.py
+++ b/solution.py
@@ -100,7 +100,8 @@
     kept = kept + lax.ppermute(sent, axis, [(i, i ^ 1) for i in range(count)])
     bit = 2
     while bit < count:
-        kept = kept + lax.ppermute(kept, axis, [(i, i ^ bit) for i in range(count)])
+        crossed = lax.ppermute(kept.astype(jnp.bfloat16), axis, [(i, i ^ bit) for i in range(count)])
+        kept = kept + crossed.astype(jnp.float32)
         bit *= 2
     kept = kept.astype(jnp.bfloat16)
     other = lax.ppermute(kept, axis, [(i, i ^ 1) for i in range(count)])

time: 97.5 us -> 97.9 us (level)
  waiting for transfers between devices: 23.1 us -> 18.6 us
  other arithmetic: 8.04 us -> 11 us
  local copies, waits for them, and re-layouts: 8.67 us -> 10.4 us
  blocking collectives: 17.7 us -> 18.8 us
  starting transfers between devices: 30 us -> 29 us
    ppermute x1, waiting for transfers between devices: 5.06 us -> 2.24 us  [summed_columns(): lax.ppermute(kept.astype(jnp.bfloat16), axis, [(i, i ^ bit) for i in rang...]
    all_to_all x1, waiting for transfers between devices: 4.13 us -> 1.96 us  [per_device(): lax.all_to_all(slot_rows, 'seq', split_axis=0, concat_axis=0, tiled=True)]
    neg x1, other arithmetic: 0.01 us -> 1.21 us  [local_terms(): log_decay = -jnp.exp(decay_log)[None, :] * step_size]
    all_to_all x1, blocking collectives: 17.7 us -> 18.8 us  [per_device(): lax.all_to_all(outgoing, 'seq', split_axis=0, concat_axis=0, tiled=True)]
    unnamed x22 -> x34, local copies, waits for them, and re-layouts: 2.03 us -> 2.29 us
  transfers between devices with their start and end apart: 11 -> 11, of which waited for: 8 -> 8; matrix products, arithmetic and copies ran while one was open for 10% -> 15% of each run, Pallas kernels for 0% -> 0%
where the time goes in v15:
time: 97.9 us; the launch traced here: 97.1 us
  starting transfers between devices  29 us (30%)
  blocking collectives  18.8 us (19%)
  waiting for transfers between devices  18.6 us (19%)
  other arithmetic  11 us (11%)
  local copies, waits for them, and re-layouts  10.4 us (11%)
  matrix products  5.61 us (6%)
  between operations  3.63 us (4%)
    ppermute x5, starting transfers between devices, shifted(): return lax.ppermute(array, axis, pairs)  19.1 us
    all_to_all x1, blocking collectives, per_device(): lax.all_to_all(outgoing, 'seq', split_axis=0, concat_axis=0, tiled=True)  18.8 us
    ppermute x5, waiting for transfers between devices, shifted(): return lax.ppermute(array, axis, pairs)  7.61 us
    all_to_all x1, starting transfers between devices, per_device(): lax.all_to_all(slot_rows, 'seq', split_axis=0, concat_axis=0, tiled=True)  7.41 us
    ppermute x2, waiting for transfers between devices, exchange(): other = lax.ppermute(held, axis, [(i, i ^ bit) for i in range(count)])  6.81 us
    unnamed x34, local copies, waits for them, and re-layouts  2.29 us
    ppermute x1, waiting for transfers between devices, summed_columns(): lax.ppermute(kept.astype(jnp.bfloat16), axis, [(i, i ^ bit) for i in rang...  2.24 us
    all_to_all x1, waiting for transfers between devices, per_device(): lax.all_to_all(slot_rows, 'seq', split_axis=0, concat_axis=0, tiled=True)  1.96 us
  transfers between devices with their start and end apart: 11, of which 8 were waited for; matrix products, arithmetic and copies ran while one was open for 15% of the time, Pallas kernels for 0%

profile of v15, /device:TPU:0, one launch (start us, length us, event | category | flops | bytes accessed | tf_op | source)
XLA Modules:
  0.0 97.1 jit_solution(6241559903923993854)
XLA Ops:
  0.0 7.4 %all-to-all-start = ((bf16[8,32,512]{2,1,0:T(8,128)(2,1)}), bf16[8,32,512]{2,1,0:T(8,128)(2,1)S(1)}, u32[]{:S(2)}, u32[]{:S(2)}) async-start(bf16[8,32,512]{2,1,0:T(8,128)(2,1)} %bitcast.53), calls=%async_computation | async-start | bytes 524288 | tf_op jit(solution)/shard_map/all_to_all | solution.py:177
  7.4 1.2 %compare_and_fusion.1 = (pred[8]{0:T(512)(128)(4,1)}, s32[8]{0:T(128)S(1)}) fusion(s32[8,8]{1,0:T(8,128)} %param.14, s32[]{:T(128)S(6)} %select_n.119), kind=kLoop, calls=%fused_computation.108 | loop fusion | flops 48 | bytes 76 | tf_op jit(solution)/shard_map/jit(_take)/and | solution.py:231
  8.7 1.0 sort.17
  9.6 0.8 reduce-window.8
  10.5 0.6 fusion.58
  11.9 1.2 %exponential_negate_fusion = f32[6]{0:T(128)} fusion(f32[6]{0:T(128)} %param.23), kind=kLoop, calls=%fused_computation.118 | loop fusion | flops 6 | bytes 48 | tf_op jit(solution)/shard_map/neg | solution.py:134
  13.1 1.3 %broadcast_compare_fusion.1 = (pred[256]{0:T(512)(128)(4,1)}, pred[256]{0:T(512)(128)(4,1)}, f32[256]{0:T(256)}, f32[256]{0:T(256)}, f32[256]{0:T(256)}) fusion(s32[]{:T(128)} %bitcast.10, s32[259]{0:T(512)S(1)} %convert_reduce_fusion, s32[]{:T(128)S(6)} %select_n.138), kind=kLoop, calls=%fused_computation.119 | loop fusion | flops 2048 | bytes 7688 | tf_op jit(solution)/shard_map/eq | solution.py:148
  14.4 2.0 %all-to-all-done = bf16[8,32,512]{2,1,0:T(8,128)(2,1)S(1)} async-done(((bf16[8,32,512]{2,1,0:T(8,128)(2,1)}), bf16[8,32,512]{2,1,0:T(8,128)(2,1)S(1)}, u32[]{:S(2)}, u32[]{:S(2)}) %all-to-all-start) | async-done | bytes 262176 | tf_op jit(solution)/shard_map/all_to_all | solution.py:177
  16.3 0.6 gather_fusion
  17.0 0.3 fusion.60
  17.6 0.7 fusion.34
  18.3 1.5 %collective-permute-start = (bf16[256,512]{1,0:T(8,128)(2,1)S(1)}, bf16[256,512]{1,0:T(8,128)(2,1)S(1)}, u32[]{:S(2)}, u32[]{:S(2)}) collective-permute-start(bf16[256,512]{1,0:T(8,128)(2,1)S(1)} %bitcast_select_fusion), channel_id=1, source_target_pairs={{0,2},{1,3},{2,0},{3,1},{4,6},{5,7},{6,4},{7,5},{8,10},{9,11},{10,... | collective-permute-start | bytes 786440 | tf_op jit(solution)/shard_map/ppermute | solution.py:65
  19.8 0.7 collective-permute-start.3
  20.6 6.8 %collective-permute-done = bf16[256,512]{1,0:T(8,128)(2,1)S(1)} collective-permute-done((bf16[256,512]{1,0:T(8,128)(2,1)S(1)}, bf16[256,512]{1,0:T(8,128)(2,1)S(1)}, u32[]{:S(2)}, u32[]{:S(2)}) %collective-permute-start) | collective-permute-done | bytes 262176 | tf_op jit(solution)/shard_map/ppermute | solution.py:65
  27.5 2.2 %collective-permute-done.3 = bf16[256,256]{1,0:T(8,128)(2,1)S(1)} collective-permute-done((bf16[256,256]{1,0:T(8,128)(2,1)S(1)}, bf16[256,256]{1,0:T(8,128)(2,1)S(1)}, u32[]{:S(2)}, u32[]{:S(2)}) %collective-permute-start.3) | collective-permute-done | bytes 131104 | tf_op jit(solution)/shard_map/ppermute | solution.py:103
  30.0 1.5 %fusion.59 = (s32[1]{0:T(128)}, s32[1]{0:T(128)}, s32[1]{0:T(128)}, s32[1]{0:T(128)}) fusion(s32[4]{0:T(128)} %constant.94.clone, s32[]{:T(128)S(6)} %select_n.123, s32[]{:T(128)S(6)} %select_n.125, s32[]{:T(128)S(6)} %select_n.129, s32[]{:T(128)S(6)} %select_n.127), kind=kLoop, calls=%fused_computation.123 | loop fusion | bytes 48 | tf_op jit(solution)/shard_map/dynamic_slice | solution.py:83
  33.9 1.3 %slice.119 = pred[1]{0:T(512)(128)(4,1)} slice(pred[256]{0:T(512)(128)(4,1)} %get-tuple-element.30), slice={[255:256]} | slice | bytes 2 | tf_op jit(solution)/shard_map/slice | solution.py:154
  35.5 1.1 %pad_maximum_fusion = bf16[256,2048]{1,0:T(8,128)(2,1)S(1)} fusion(bf16[256,1024]{1,0:T(8,128)(2,1)} %collective-permute-done.1, bf16[256,512]{1,0:T(8,128)(2,1)S(1)} %collective-permute-done, bf16[256,512]{1,0:T(8,128)(2,1)S(1)} %bitcast_select_fusion), kind=kLoop, calls=%fused_computation.17 | loop fusion | flops 3145728 | bytes 2097152 | tf_op jit(solution)/shard_map/concatenate | solution.py:66
  36.8 0.6 copy-done.12
  37.4 0.4 compare_select_fusion
  38.2 0.2 slice_reduce_fusion
  38.5 0.7 convolution_convert_fusion.1
  39.2 0.7 copy-done.11
  39.9 0.7 divide_multiply_fusion.1
  40.7 3.3 %collective-permute-start.5 = (bf16[3,896]{1,0:T(4,128)(2,1)S(1)}, bf16[3,896]{1,0:T(4,128)(2,1)S(1)}, u32[]{:S(2)}, u32[]{:S(2)}) collective-permute-start(bf16[3,896]{1,0:T(4,128)(2,1)S(1)} %pad_maximum_fusion.3), channel_id=1, source_target_pairs={{0,4},{4,8},{8,12},{12,16},{16,20},{20,24},{24,28},{1,5},{5,9},{9,... | collective-permute-start | bytes 16136 | tf_op jit(solution)/shard_map/ppermute | solution.py:12
  44.1 0.6 broadcast_select_fusion.1
  45.0 0.4 collective-permute-done.5
  45.5 0.7 divide_multiply_fusion
  46.2 0.8 slice.145
  47.0 1.2 %copy.21 = f32[256,384]{0,1:T(8,128)S(1)} copy(f32[256,384]{1,0:T(8,128)} %slice.145) | data formatting | bytes 786432 | tf_op jit(solution)/shard_map/slice | solution.py:212
  48.2 0.5 fusion.40
  48.9 4.2 %collective-permute-start.7 = (bf16[400,256]{1,0:T(8,128)(2,1)S(1)}, bf16[400,256]{1,0:T(8,128)(2,1)S(1)}, u32[]{:S(2)}, u32[]{:S(2)}) collective-permute-start(bf16[400,256]{1,0:T(8,128)(2,1)S(1)} %fusion.30), channel_id=1, source_target_pairs={{0,4},{4,8},{8,12},{12,16},{16,20},{20,24},{24,28},{1,5},{5,9},{9,... | collective-permute-start | bytes 614408 | tf_op jit(solution)/shard_map/ppermute | solution.py:12
  53.1 2.5 %collective-permute-start.6 = (bf16[400,256]{1,0:T(8,128)(2,1)S(1)}, bf16[400,256]{1,0:T(8,128)(2,1)S(1)}, u32[]{:S(2)}, u32[]{:S(2)}) collective-permute-start(bf16[400,256]{1,0:T(8,128)(2,1)S(1)} %fusion.30), channel_id=1, source_target_pairs={{0,8},{4,12},{8,16},{12,20},{16,24},{20,28},{1,9},{5,13},{9,17},{1... | collective-permute-start | bytes 614408 | tf_op jit(solution)/shard_map/ppermute | solution.py:12
  55.6 0.4 fusion.37
  56.0 0.8 collective-permute-done.7
  56.9 2.4 %collective-permute-done.6 = bf16[400,256]{1,0:T(8,128)(2,1)S(1)} collective-permute-done((bf16[400,256]{1,0:T(8,128)(2,1)S(1)}, bf16[400,256]{1,0:T(8,128)(2,1)S(1)}, u32[]{:S(2)}, u32[]{:S(2)}) %collective-permute-start.6) | collective-permute-done | bytes 204832 | tf_op jit(solution)/shard_map/ppermute | solution.py:12
  59.7 5.2 %collective-permute-start.8 = (bf16[400,256]{1,0:T(8,128)(2,1)S(1)}, bf16[400,256]{1,0:T(8,128)(2,1)S(1)}, u32[]{:S(2)}, u32[]{:S(2)}) collective-permute-start(bf16[400,256]{1,0:T(8,128)(2,1)S(1)} %fusion.31), channel_id=1, source_target_pairs={{0,8},{4,12},{8,16},{12,20},{16,24},{20,28},{1,9},{5,13},{9,17},{1... | collective-permute-start | bytes 614408 | tf_op jit(solution)/shard_map/ppermute | solution.py:12
  64.8 1.9 %fusion.8 = f32[256,6,64]{0,2,1:T(8,128)S(1)} fusion(f32[6,256]{1,0:T(8,128)S(1)} %bitcast.54, f32[256,256]{1,0:T(8,128)S(1)} %fusion.37, pred[256,256]{1,0:T(8,128)(4,1)S(1)} %copy-done.2, f32[256,6,64]{0,2,1:T(8,128)S(1)} %bitcast.48, f32[6]{0:T(128)S(1)} %copy-done.14, f32[256,6]{0,1:T(8,128)S(1)} %compare_select_fusion), kind=kOutput, calls=%fused_computation.8 | convolution fusion | flops 303464448 | bytes 1126424 | tf_op jit(solution)/shard_map/hts,shp->thp/dot_general | solution.py:145
  66.7 1.3 %collective-permute-done.8 = bf16[400,256]{1,0:T(8,128)(2,1)S(1)} collective-permute-done((bf16[400,256]{1,0:T(8,128)(2,1)S(1)}, bf16[400,256]{1,0:T(8,128)(2,1)S(1)}, u32[]{:S(2)}, u32[]{:S(2)}) %collective-permute-start.8) | collective-permute-done | bytes 204832 | tf_op jit(solution)/shard_map/ppermute | solution.py:12
  68.4 4.0 %collective-permute-start.9 = (bf16[400,256]{1,0:T(8,128)(2,1)S(1)}, bf16[400,256]{1,0:T(8,128)(2,1)S(1)}, u32[]{:S(2)}, u32[]{:S(2)}) collective-permute-start(bf16[400,256]{1,0:T(8,128)(2,1)S(1)} %fusion.32), channel_id=1, source_target_pairs={{0,16},{4,20},{8,24},{12,28},{1,17},{5,21},{9,25},{13,29},{2,18},{... | collective-permute-start | bytes 614408 | tf_op jit(solution)/shard_map/ppermute | solution.py:12
  72.4 0.7 fusion.53
  73.2 2.5 %collective-permute-done.9 = bf16[400,256]{1,0:T(8,128)(2,1)S(1)} collective-permute-done((bf16[400,256]{1,0:T(8,128)(2,1)S(1)}, bf16[400,256]{1,0:T(8,128)(2,1)S(1)}, u32[]{:S(2)}, u32[]{:S(2)}) %collective-permute-start.9) | collective-permute-done | bytes 204832 | tf_op jit(solution)/shard_map/ppermute | solution.py:12
  75.7 0.5 fusion.13
  76.3 0.3 copy.23
  76.6 0.3 convert_element_type.117
  76.9 0.6 gather_fusion.1
  77.6 18.8 %all_to_all.10 = bf16[8,32,384]{2,1,0:T(8,128)(2,1)S(1)} all-to-all(bf16[8,32,384]{2,1,0:T(8,128)(2,1)S(1)} %broadcast_select_fusion), channel_id=1, replica_groups=mesh['seq'=8,'fsdp'=4] {'seq'}, dimensions={0} | all-to-all | bytes 393216 | tf_op jit(solution)/shard_map/all_to_all | solution.py:232
  96.5 0.7 copy.26
  (81 shorter events, 3.1 us)
Async XLA Ops:
  0.0 38.5 %copy-start = (bf16[2048,384]{1,0:T(8,128)(2,1)S(1)}, bf16[2048,384]{1,0:T(8,128)(2,1)}, u32[]{:S(2)}) copy-start(bf16[2048,384]{1,0:T(8,128)(2,1)} %param.16) | copy-start | bytes 4718596
  0.0 17.0 %copy-start.1 = (bf16[512,512]{1,0:T(8,128)(2,1)S(1)}, bf16[512,512]{1,0:T(8,128)(2,1)}, u32[]{:S(2)}) copy-start(bf16[512,512]{1,0:T(8,128)(2,1)} %param.18) | copy-start | bytes 1572868
  0.0 16.3 %all-to-all-start = ((bf16[8,32,512]{2,1,0:T(8,128)(2,1)}), bf16[8,32,512]{2,1,0:T(8,128)(2,1)S(1)}, u32[]{:S(2)}, u32[]{:S(2)}) async-start(bf16[8,32,512]{2,1,0:T(8,128)(2,1)} %bitcast.53), calls=%async_computation | async-start | bytes 524288 | tf_op jit(solution)/shard_map/all_to_all | solution.py:177
  7.4 10.0 %copy-start.4 = (f32[4,384]{1,0:T(4,128)S(1)}, f32[4,384]{1,0:T(4,128)}, u32[]{:S(2)}) copy-start(f32[4,384]{1,0:T(4,128)} %param.20) | copy-start | bytes 18436
  17.0 3.6 %copy-start.3 = (f32[4,512]{1,0:T(4,128)S(1)}, f32[4,512]{1,0:T(4,128)}, u32[]{:S(2)}) copy-start(f32[4,512]{1,0:T(4,128)} %param.21) | copy-start | bytes 24580
  17.4 2.4 %collective-permute-start.2 = (f32[256,256]{1,0:T(8,128)S(1)}, f32[256,256]{1,0:T(8,128)S(1)}, u32[]{:S(2)}, u32[]{:S(2)}) collective-permute-start(f32[256,256]{1,0:T(8,128)S(1)} %constant_dynamic-slice_fusion), channel_id=1, source_target_pairs={{0,1},{1,0},{2,3},{3,2},{4,5},{5,4},{6,7},{7,6},{8,9},{9,8},{10,11... | collective-permute-start | bytes 786440 | tf_op jit(solution)/shard_map/ppermute | solution.py:100
  18.3 9.1 %collective-permute-start = (bf16[256,512]{1,0:T(8,128)(2,1)S(1)}, bf16[256,512]{1,0:T(8,128)(2,1)S(1)}, u32[]{:S(2)}, u32[]{:S(2)}) collective-permute-start(bf16[256,512]{1,0:T(8,128)(2,1)S(1)} %bitcast_select_fusion), channel_id=1, source_target_pairs={{0,2},{1,3},{2,0},{3,1},{4,6},{5,7},{6,4},{7,5},{8,10},{9,11},{10,... | collective-permute-start | bytes 786440 | tf_op jit(solution)/shard_map/ppermute | solution.py:65
  19.8 9.9 %collective-permute-start.3 = (bf16[256,256]{1,0:T(8,128)(2,1)S(1)}, bf16[256,256]{1,0:T(8,128)(2,1)S(1)}, u32[]{:S(2)}, u32[]{:S(2)}) collective-permute-start(bf16[256,256]{1,0:T(8,128)(2,1)S(1)} %fusion.44), channel_id=1, source_target_pairs={{0,2},{1,3},{2,0},{3,1},{4,6},{5,7},{6,4},{7,5},{8,10},{9,11},{10,... | collective-permute-start | bytes 393224 | tf_op jit(solution)/shard_map/ppermute | solution.py:103
  27.5 8.0 %collective-permute-start.1 = (bf16[256,1024]{1,0:T(8,128)(2,1)S(1)}, bf16[256,1024]{1,0:T(8,128)(2,1)}, u32[]{:S(2)}, u32[]{:S(2)}) collective-permute-start(bf16[256,1024]{1,0:T(8,128)(2,1)S(1)} %pad_maximum_fusion.2), channel_id=1, source_target_pairs={{0,1},{1,0},{2,3},{3,2},{4,5},{5,4},{6,7},{7,6},{8,9},{9,8},{10,11... | collective-permute-start | bytes 1572872 | tf_op jit(solution)/shard_map/ppermute | solution.py:65
  29.8 5.5 %collective-permute-start.4 = (bf16[256,256]{1,0:T(8,128)(2,1)S(1)}, bf16[256,256]{1,0:T(8,128)(2,1)S(1)}, u32[]{:S(2)}, u32[]{:S(2)}) collective-permute-start(bf16[256,256]{1,0:T(8,128)(2,1)S(1)} %add_convert_fusion), channel_id=1, source_target_pairs={{0,1},{1,0},{2,3},{3,2},{4,5},{5,4},{6,7},{7,6},{8,9},{9,8},{10,11... | collective-permute-start | bytes 393224 | tf_op jit(solution)/shard_map/ppermute | solution.py:107
  36.6 0.8 copy-start.12
  36.7 0.8 copy-start.13
  37.4 0.6 copy-start.15
  38.5 1.4 %copy-start.11 = (bf16[2048,384]{1,0:T(8,128)(2,1)S(1)}, bf16[2048,384]{1,0:T(8,128)(2,1)}, u32[]{:S(2)}) copy-start(bf16[2048,384]{1,0:T(8,128)(2,1)} %param.17) | copy-start | bytes 4718596
  39.9 4.1 %copy-start.9 = (pred[256]{0:T(512)(128)(4,1)S(1)}, pred[256]{0:T(512)(128)(4,1)}, u32[]{:S(2)}) copy-start(pred[256]{0:T(512)(128)(4,1)} %get-tuple-element.29) | copy-start | bytes 772
  39.9 4.1 %copy-start.10 = (pred[256]{0:T(512)(128)(4,1)S(1)}, pred[256]{0:T(512)(128)(4,1)}, u32[]{:S(2)}) copy-start(pred[256]{0:T(512)(128)(4,1)} %get-tuple-element.30) | copy-start | bytes 772
  40.7 4.8 %copy-start.5 = (f32[256]{0:T(256)S(1)}, f32[256]{0:T(256)}, u32[]{:S(2)}) copy-start(f32[256]{0:T(256)} %get-tuple-element.31) | copy-start | bytes 3076
  40.7 4.8 %copy-start.6 = (f32[256]{0:T(256)S(1)}, f32[256]{0:T(256)}, u32[]{:S(2)}) copy-start(f32[256]{0:T(256)} %get-tuple-element.32) | copy-start | bytes 3076
  40.7 4.8 %copy-start.7 = (f32[256]{0:T(256)S(1)}, f32[256]{0:T(256)}, u32[]{:S(2)}) copy-start(f32[256]{0:T(256)} %get-tuple-element.33) | copy-start | bytes 3076
  40.7 4.7 %collective-permute-start.5 = (bf16[3,896]{1,0:T(4,128)(2,1)S(1)}, bf16[3,896]{1,0:T(4,128)(2,1)S(1)}, u32[]{:S(2)}, u32[]{:S(2)}) collective-permute-start(bf16[3,896]{1,0:T(4,128)(2,1)S(1)} %pad_maximum_fusion.3), channel_id=1, source_target_pairs={{0,4},{4,8},{8,12},{12,16},{16,20},{20,24},{24,28},{1,5},{5,9},{9,... | collective-permute-start | bytes 16136 | tf_op jit(solution)/shard_map/ppermute | solution.py:12
  48.9 8.0 %collective-permute-start.7 = (bf16[400,256]{1,0:T(8,128)(2,1)S(1)}, bf16[400,256]{1,0:T(8,128)(2,1)S(1)}, u32[]{:S(2)}, u32[]{:S(2)}) collective-permute-start(bf16[400,256]{1,0:T(8,128)(2,1)S(1)} %fusion.30), channel_id=1, source_target_pairs={{0,4},{4,8},{8,12},{12,16},{16,20},{20,24},{24,28},{1,5},{5,9},{9,... | collective-permute-start | bytes 614408 | tf_op jit(solution)/shard_map/ppermute | solution.py:12
  53.1 6.2 %collective-permute-start.6 = (bf16[400,256]{1,0:T(8,128)(2,1)S(1)}, bf16[400,256]{1,0:T(8,128)(2,1)S(1)}, u32[]{:S(2)}, u32[]{:S(2)}) collective-permute-start(bf16[400,256]{1,0:T(8,128)(2,1)S(1)} %fusion.30), channel_id=1, source_target_pairs={{0,8},{4,12},{8,16},{12,20},{16,24},{20,28},{1,9},{5,13},{9,17},{1... | collective-permute-start | bytes 614408 | tf_op jit(solution)/shard_map/ppermute | solution.py:12
  56.0 8.8 %copy-start.2 = (pred[256,256]{1,0:T(8,128)(4,1)S(1)}, pred[256,256]{1,0:T(8,128)(4,1)}, u32[]{:S(2)}) copy-start(pred[256,256]{1,0:T(8,128)(4,1)} %fusion.34) | copy-start | bytes 196612
  56.0 8.8 %copy-start.14 = (f32[6]{0:T(128)S(1)}, f32[6]{0:T(128)}, u32[]{:S(2)}) copy-start(f32[6]{0:T(128)} %param.24) | copy-start | bytes 76
  59.7 8.4 %collective-permute-start.8 = (bf16[400,256]{1,0:T(8,128)(2,1)S(1)}, bf16[400,256]{1,0:T(8,128)(2,1)S(1)}, u32[]{:S(2)}, u32[]{:S(2)}) collective-permute-start(bf16[400,256]{1,0:T(8,128)(2,1)S(1)} %fusion.31), channel_id=1, source_target_pairs={{0,8},{4,12},{8,16},{12,20},{16,24},{20,28},{1,9},{5,13},{9,17},{1... | collective-permute-start | bytes 614408 | tf_op jit(solution)/shard_map/ppermute | solution.py:12
  68.4 7.3 %collective-permute-start.9 = (bf16[400,256]{1,0:T(8,128)(2,1)S(1)}, bf16[400,256]{1,0:T(8,128)(2,1)S(1)}, u32[]{:S(2)}, u32[]{:S(2)}) collective-permute-start(bf16[400,256]{1,0:T(8,128)(2,1)S(1)} %fusion.32), channel_id=1, source_target_pairs={{0,16},{4,20},{8,24},{12,28},{1,17},{5,21},{9,25},{13,29},{2,18},{... | collective-permute-start | bytes 614408 | tf_op jit(solution)/shard_map/ppermute | solution.py:12
  75.7 1.8 %copy-start.8 = (pred[8]{0:T(512)(128)(4,1)S(1)}, pred[8]{0:T(512)(128)(4,1)}, u32[]{:S(2)}) copy-start(pred[8]{0:T(512)(128)(4,1)} %get-tuple-element.19) | copy-start | bytes 28

commit v16 on v14

--- a/solution.py
+++ b/solution.py
@@ -24,7 +24,7 @@
     return jnp.concatenate([state.reshape(rows, -1), decay, decay, spare], axis=0)
 
 
-def received(packed, axis, by, heads):
+def received(packed, axis, by, heads, skip_first=False):
     place = lax.axis_index(axis)
     extra = -(-2 * heads // 16) * 16
     rows = packed.shape[0] - extra
@@ -32,8 +32,11 @@
     high = packed.astype(jnp.bfloat16)
     low = (packed - high.astype(jnp.float32)).astype(jnp.bfloat16)
     wire = jnp.where((row >= rows + heads) & (row < rows + 2 * heads), low, high)
-    got = shifted(wire, axis, by).astype(jnp.float32)
-    missing = (place < by).astype(jnp.float32)
+    count = lax.axis_size(axis)
+    first = 1 if skip_first else 0
+    pairs = [(i, i + by) for i in range(first, count) if i + by < count]
+    got = lax.ppermute(wire, axis, pairs).astype(jnp.float32)
+    missing = (place < by + first).astype(jnp.float32)
     decay = got[rows : rows + heads] + got[rows + heads : rows + 2 * heads] + missing
     spare = jnp.zeros((extra - 2 * heads, packed.shape[1]), packed.dtype)
     return jnp.concatenate([got[:rows], decay, decay, spare], axis=0)
@@ -50,7 +53,7 @@
     while cover < count - 1:
         if cover * 2 >= count - 1:
             held, side = lax.optimization_barrier((held, side))
-        held = combine_packed(received(held, axis, cover, heads), held, heads)
+        held = combine_packed(received(held, axis, cover, heads, skip_first=True), held, heads)
         cover *= 2
     return held, side
 

time: 97.5 us -> 97.5 us (level)
  blocking collectives: 17.7 us -> 29.8 us
  starting transfers between devices: 30 us -> 21.8 us
  waiting for transfers between devices: 23.1 us -> 19.2 us
    ppermute x5 -> x1, starting transfers between devices: 19.5 us -> 3.32 us  [shifted(): return lax.ppermute(array, axis, pairs)]
    all_to_all x1, blocking collectives: 17.7 us -> 29.8 us  [per_device(): lax.all_to_all(outgoing, 'seq', split_axis=0, concat_axis=0, tiled=True)]
    ppermute x0 -> x4, starting transfers between devices: none -> 8.02 us  [received(): got = lax.ppermute(wire, axis, pairs).astype(jnp.float32)]
    ppermute x5 -> x1, waiting for transfers between devices: 7.67 us -> 0.47 us  [shifted(): return lax.ppermute(array, axis, pairs)]
    ppermute x0 -> x4, waiting for transfers between devices: none -> 3.3 us  [received(): got = lax.ppermute(wire, axis, pairs).astype(jnp.float32)]
  transfers between devices with their start and end apart: 11 -> 11, of which waited for: 8 -> 6; matrix products, arithmetic and copies ran while one was open for 10% -> 10% of each run, Pallas kernels for 0% -> 0%
where the time goes in v16:
time: 97.5 us; the launch traced here: 96.9 us
  blocking collectives  29.8 us (31%)
  starting transfers between devices  21.8 us (22%)
  waiting for transfers between devices  19.2 us (20%)
  local copies, waits for them, and re-layouts  8.67 us (9%)
  other arithmetic  8.04 us (8%)
  matrix products  5.61 us (6%)
  between operations  3.74 us (4%)
    all_to_all x1, blocking collectives, per_device(): lax.all_to_all(outgoing, 'seq', split_axis=0, concat_axis=0, tiled=True)  29.8 us
    ppermute x4, starting transfers between devices, received(): got = lax.ppermute(wire, axis, pairs).astype(jnp.float32)  8.02 us
    all_to_all x1, starting transfers between devices, per_device(): lax.all_to_all(slot_rows, 'seq', split_axis=0, concat_axis=0, tiled=True)  7.41 us
    ppermute x2, waiting for transfers between devices, exchange(): other = lax.ppermute(held, axis, [(i, i ^ bit) for i in range(count)])  6.25 us
    ppermute x1, waiting for transfers between devices, summed_columns(): kept = kept + lax.ppermute(kept, axis, [(i, i ^ bit) for i in range(count)])  5.06 us
    all_to_all x1, waiting for transfers between devices, per_device(): lax.all_to_all(slot_rows, 'seq', split_axis=0, concat_axis=0, tiled=True)  4.13 us
    ppermute x1, starting transfers between devices, shifted(): return lax.ppermute(array, axis, pairs)  3.32 us
    ppermute x4, waiting for transfers between devices, received(): got = lax.ppermute(wire, axis, pairs).astype(jnp.float32)  3.3 us
  transfers between devices with their start and end apart: 11, of which 6 were waited for; matrix products, arithmetic and copies ran while one was open for 10% of the time, Pallas kernels for 0%

profile of v16, /device:TPU:0, one launch (start us, length us, event | category | flops | bytes accessed | tf_op | source)
XLA Modules:
  0.0 96.9 jit_solution(12891951532847531402)
XLA Ops:
  0.0 7.4 %all-to-all-start = ((bf16[8,32,512]{2,1,0:T(8,128)(2,1)}), bf16[8,32,512]{2,1,0:T(8,128)(2,1)S(1)}, u32[]{:S(2)}, u32[]{:S(2)}) async-start(bf16[8,32,512]{2,1,0:T(8,128)(2,1)} %bitcast.53), calls=%async_computation | async-start | bytes 524288 | tf_op jit(solution)/shard_map/all_to_all | solution.py:179
  7.4 0.8 reduce-window.8
  8.3 0.7 compare_and_fusion.1
  9.0 1.0 sort.17
  10.2 0.6 fusion.57
  11.5 0.7 broadcast_compare_fusion.1
  12.2 4.1 %all-to-all-done = bf16[8,32,512]{2,1,0:T(8,128)(2,1)S(1)} async-done(((bf16[8,32,512]{2,1,0:T(8,128)(2,1)}), bf16[8,32,512]{2,1,0:T(8,128)(2,1)S(1)}, u32[]{:S(2)}, u32[]{:S(2)}) %all-to-all-start) | async-done | bytes 262176 | tf_op jit(solution)/shard_map/all_to_all | solution.py:179
  16.3 0.6 gather_fusion
  17.1 0.3 fusion.59
  17.7 1.6 %collective-permute-start = (bf16[256,512]{1,0:T(8,128)(2,1)S(1)}, bf16[256,512]{1,0:T(8,128)(2,1)S(1)}, u32[]{:S(2)}, u32[]{:S(2)}) collective-permute-start(bf16[256,512]{1,0:T(8,128)(2,1)S(1)} %bitcast_select_fusion), channel_id=1, source_target_pairs={{0,2},{1,3},{2,0},{3,1},{4,6},{5,7},{6,4},{7,5},{8,10},{9,11},{10,... | collective-permute-start | bytes 786440 | tf_op jit(solution)/shard_map/ppermute | solution.py:68
  19.3 1.3 %collective-permute-start.3 = (f32[256,256]{1,0:T(8,128)S(1)}, f32[256,256]{1,0:T(8,128)S(1)}, u32[]{:S(2)}, u32[]{:S(2)}) collective-permute-start(f32[256,256]{1,0:T(8,128)S(1)} %dynamic-slice_add_fusion), channel_id=1, source_target_pairs={{0,2},{1,3},{2,0},{3,1},{4,6},{5,7},{6,4},{7,5},{8,10},{9,11},{10,... | collective-permute-start | bytes 786440 | tf_op jit(solution)/shard_map/ppermute | solution.py:106
  20.6 6.2 %collective-permute-done = bf16[256,512]{1,0:T(8,128)(2,1)S(1)} collective-permute-done((bf16[256,512]{1,0:T(8,128)(2,1)S(1)}, bf16[256,512]{1,0:T(8,128)(2,1)S(1)}, u32[]{:S(2)}, u32[]{:S(2)}) %collective-permute-start) | collective-permute-done | bytes 262176 | tf_op jit(solution)/shard_map/ppermute | solution.py:68
  27.0 5.1 %collective-permute-done.3 = f32[256,256]{1,0:T(8,128)S(1)} collective-permute-done((f32[256,256]{1,0:T(8,128)S(1)}, f32[256,256]{1,0:T(8,128)S(1)}, u32[]{:S(2)}, u32[]{:S(2)}) %collective-permute-start.3) | collective-permute-done | bytes 262176 | tf_op jit(solution)/shard_map/ppermute | solution.py:106
  32.2 0.7 fusion.58
  35.4 0.6 slice.119
  36.3 1.1 %pad_maximum_fusion = bf16[256,2048]{1,0:T(8,128)(2,1)S(1)} fusion(bf16[256,1024]{1,0:T(8,128)(2,1)} %collective-permute-done.1, bf16[256,512]{1,0:T(8,128)(2,1)S(1)} %collective-permute-done, bf16[256,512]{1,0:T(8,128)(2,1)S(1)} %bitcast_select_fusion), kind=kLoop, calls=%fused_computation.17 | loop fusion | flops 3145728 | bytes 2097152 | tf_op jit(solution)/shard_map/concatenate | solution.py:69
  37.6 0.6 copy-done.6
  38.2 0.4 compare_select_fusion
  38.6 0.2 fusion.35
  38.8 0.2 slice_reduce_fusion
  39.1 0.7 convolution_convert_fusion.1
  39.8 0.7 copy-done.5
  40.5 0.7 divide_multiply_fusion.1
  41.3 3.3 %collective-permute-start.5 = (bf16[3,896]{1,0:T(4,128)(2,1)S(1)}, bf16[3,896]{1,0:T(4,128)(2,1)S(1)}, u32[]{:S(2)}, u32[]{:S(2)}) collective-permute-start(bf16[3,896]{1,0:T(4,128)(2,1)S(1)} %pad_maximum_fusion.3), channel_id=1, source_target_pairs={{0,4},{4,8},{8,12},{12,16},{16,20},{20,24},{24,28},{1,5},{5,9},{9,... | collective-permute-start | bytes 16136 | tf_op jit(solution)/shard_map/ppermute | solution.py:12
  44.7 0.6 broadcast_select_fusion.1
  45.3 0.2 copy.22
  45.5 0.5 collective-permute-done.5
  46.0 0.7 divide_multiply_fusion
  46.7 0.8 slice.145
  47.5 1.2 %copy.21 = f32[256,384]{0,1:T(8,128)S(1)} copy(f32[256,384]{1,0:T(8,128)} %slice.145) | data formatting | bytes 786432 | tf_op jit(solution)/shard_map/slice | solution.py:214
  48.7 0.5 fusion.40
  49.2 0.2 fusion.30
  49.4 4.2 %collective-permute-start.7 = (bf16[400,256]{1,0:T(8,128)(2,1)S(1)}, bf16[400,256]{1,0:T(8,128)(2,1)S(1)}, u32[]{:S(2)}, u32[]{:S(2)}) collective-permute-start(bf16[400,256]{1,0:T(8,128)(2,1)S(1)} %fusion.30), channel_id=1, source_target_pairs={{0,4},{4,8},{8,12},{12,16},{16,20},{20,24},{24,28},{1,5},{5,9},{9,... | collective-permute-start | bytes 614408 | tf_op jit(solution)/shard_map/ppermute | solution.py:38
  53.6 2.5 %collective-permute-start.6 = (bf16[400,256]{1,0:T(8,128)(2,1)S(1)}, bf16[400,256]{1,0:T(8,128)(2,1)S(1)}, u32[]{:S(2)}, u32[]{:S(2)}) collective-permute-start(bf16[400,256]{1,0:T(8,128)(2,1)S(1)} %fusion.30), channel_id=1, source_target_pairs={{0,8},{4,12},{8,16},{12,20},{16,24},{20,28},{1,9},{5,13},{9,17},{1... | collective-permute-start | bytes 614408 | tf_op jit(solution)/shard_map/ppermute | solution.py:38
  56.1 0.4 fusion.37
  56.5 0.9 collective-permute-done.7
  57.4 2.4 %collective-permute-done.6 = bf16[400,256]{1,0:T(8,128)(2,1)S(1)} collective-permute-done((bf16[400,256]{1,0:T(8,128)(2,1)S(1)}, bf16[400,256]{1,0:T(8,128)(2,1)S(1)}, u32[]{:S(2)}, u32[]{:S(2)}) %collective-permute-start.6) | collective-permute-done | bytes 204832 | tf_op jit(solution)/shard_map/ppermute | solution.py:38
  60.0 0.2 fusion.31
  60.2 0.7 collective-permute-start.8
  60.8 1.9 %fusion.8 = f32[256,6,64]{0,2,1:T(8,128)S(1)} fusion(f32[6,256]{1,0:T(8,128)S(1)} %bitcast.54, f32[256,256]{1,0:T(8,128)S(1)} %fusion.37, pred[256,256]{1,0:T(8,128)(4,1)S(1)} %fusion.34, f32[256,6,64]{0,2,1:T(8,128)S(1)} %bitcast.48, f32[6]{0:T(128)S(1)} %copy-done.9, f32[256,6]{0,1:T(8,128)S(1)} %compare_select_fusion), kind=kOutput, calls=%fused_computation.8 | convolution fusion | flops 303464448 | bytes 1126424 | tf_op jit(solution)/shard_map/hts,shp->thp/dot_general | solution.py:147
  63.1 0.7 collective-permute-start.9
  63.8 0.7 fusion.52
  64.6 0.5 fusion.13
  65.1 0.3 copy.23
  65.4 0.3 convert_element_type.112
  65.7 0.6 gather_fusion.1
  66.4 29.8 %all_to_all.10 = bf16[8,32,384]{2,1,0:T(8,128)(2,1)S(1)} all-to-all(bf16[8,32,384]{2,1,0:T(8,128)(2,1)S(1)} %broadcast_select_fusion), channel_id=1, replica_groups=mesh['seq'=8,'fsdp'=4] {'seq'}, dimensions={0} | all-to-all | bytes 393216 | tf_op jit(solution)/shard_map/all_to_all | solution.py:234
  96.2 0.7 copy.26
  (69 shorter events, 2.2 us)
Async XLA Ops:
  0.0 39.1 %copy-start = (bf16[2048,384]{1,0:T(8,128)(2,1)S(1)}, bf16[2048,384]{1,0:T(8,128)(2,1)}, u32[]{:S(2)}) copy-start(bf16[2048,384]{1,0:T(8,128)(2,1)} %param.16) | copy-start | bytes 4718596
  0.0 17.0 %copy-start.1 = (bf16[512,512]{1,0:T(8,128)(2,1)S(1)}, bf16[512,512]{1,0:T(8,128)(2,1)}, u32[]{:S(2)}) copy-start(bf16[512,512]{1,0:T(8,128)(2,1)} %param.18) | copy-start | bytes 1572868
  0.0 16.3 %all-to-all-start = ((bf16[8,32,512]{2,1,0:T(8,128)(2,1)}), bf16[8,32,512]{2,1,0:T(8,128)(2,1)S(1)}, u32[]{:S(2)}, u32[]{:S(2)}) async-start(bf16[8,32,512]{2,1,0:T(8,128)(2,1)} %bitcast.53), calls=%async_computation | async-start | bytes 524288 | tf_op jit(solution)/shard_map/all_to_all | solution.py:179
  7.4 10.1 %copy-start.7 = (f32[6]{0:T(128)S(1)}, f32[6]{0:T(128)}, u32[]{:S(2)}) copy-start(f32[6]{0:T(128)} %param.23) | copy-start | bytes 76
  16.9 3.7 %copy-start.4 = (f32[4,384]{1,0:T(4,128)S(1)}, f32[4,384]{1,0:T(4,128)}, u32[]{:S(2)}) copy-start(f32[4,384]{1,0:T(4,128)} %param.20) | copy-start | bytes 18436
  16.9 3.7 %copy-start.3 = (f32[4,512]{1,0:T(4,128)S(1)}, f32[4,512]{1,0:T(4,128)}, u32[]{:S(2)}) copy-start(f32[4,512]{1,0:T(4,128)} %param.21) | copy-start | bytes 24580
  17.4 14.9 %copy-start.2 = (s32[4]{0:T(128)S(1)}, s32[4]{0:T(128)}, u32[]{:S(2)}) copy-start(s32[4]{0:T(128)} %constant.94.clone) | copy-start | bytes 52
  17.4 1.9 %collective-permute-start.2 = (f32[256,256]{1,0:T(8,128)S(1)}, f32[256,256]{1,0:T(8,128)S(1)}, u32[]{:S(2)}, u32[]{:S(2)}) collective-permute-start(f32[256,256]{1,0:T(8,128)S(1)} %constant_dynamic-slice_fusion), channel_id=1, source_target_pairs={{0,1},{1,0},{2,3},{3,2},{4,5},{5,4},{6,7},{7,6},{8,9},{9,8},{10,11... | collective-permute-start | bytes 786440 | tf_op jit(solution)/shard_map/ppermute | solution.py:103
  17.7 9.2 %collective-permute-start = (bf16[256,512]{1,0:T(8,128)(2,1)S(1)}, bf16[256,512]{1,0:T(8,128)(2,1)S(1)}, u32[]{:S(2)}, u32[]{:S(2)}) collective-permute-start(bf16[256,512]{1,0:T(8,128)(2,1)S(1)} %bitcast_select_fusion), channel_id=1, source_target_pairs={{0,2},{1,3},{2,0},{3,1},{4,6},{5,7},{6,4},{7,5},{8,10},{9,11},{10,... | collective-permute-start | bytes 786440 | tf_op jit(solution)/shard_map/ppermute | solution.py:68
  19.3 12.8 %collective-permute-start.3 = (f32[256,256]{1,0:T(8,128)S(1)}, f32[256,256]{1,0:T(8,128)S(1)}, u32[]{:S(2)}, u32[]{:S(2)}) collective-permute-start(f32[256,256]{1,0:T(8,128)S(1)} %dynamic-slice_add_fusion), channel_id=1, source_target_pairs={{0,2},{1,3},{2,0},{3,1},{4,6},{5,7},{6,4},{7,5},{8,10},{9,11},{10,... | collective-permute-start | bytes 786440 | tf_op jit(solution)/shard_map/ppermute | solution.py:106
  26.9 9.4 %collective-permute-start.1 = (bf16[256,1024]{1,0:T(8,128)(2,1)S(1)}, bf16[256,1024]{1,0:T(8,128)(2,1)}, u32[]{:S(2)}, u32[]{:S(2)}) collective-permute-start(bf16[256,1024]{1,0:T(8,128)(2,1)S(1)} %pad_maximum_fusion.2), channel_id=1, source_target_pairs={{0,1},{1,0},{2,3},{3,2},{4,5},{5,4},{6,7},{7,6},{8,9},{9,8},{10,11... | collective-permute-start | bytes 1572872 | tf_op jit(solution)/shard_map/ppermute | solution.py:68
  32.1 4.1 %collective-permute-start.4 = (bf16[256,256]{1,0:T(8,128)(2,1)S(1)}, bf16[256,256]{1,0:T(8,128)(2,1)S(1)}, u32[]{:S(2)}, u32[]{:S(2)}) collective-permute-start(bf16[256,256]{1,0:T(8,128)(2,1)S(1)} %add_convert_fusion), channel_id=1, source_target_pairs={{0,1},{1,0},{2,3},{3,2},{4,5},{5,4},{6,7},{7,6},{8,9},{9,8},{10,11... | collective-permute-start | bytes 393224 | tf_op jit(solution)/shard_map/ppermute | solution.py:109
  37.5 0.8 copy-start.6
  37.5 0.8 copy-start.8
  39.1 1.4 %copy-start.5 = (bf16[2048,384]{1,0:T(8,128)(2,1)S(1)}, bf16[2048,384]{1,0:T(8,128)(2,1)}, u32[]{:S(2)}) copy-start(bf16[2048,384]{1,0:T(8,128)(2,1)} %param.17) | copy-start | bytes 4718596
  41.3 4.7 %collective-permute-start.5 = (bf16[3,896]{1,0:T(4,128)(2,1)S(1)}, bf16[3,896]{1,0:T(4,128)(2,1)S(1)}, u32[]{:S(2)}, u32[]{:S(2)}) collective-permute-start(bf16[3,896]{1,0:T(4,128)(2,1)S(1)} %pad_maximum_fusion.3), channel_id=1, source_target_pairs={{0,4},{4,8},{8,12},{12,16},{16,20},{20,24},{24,28},{1,5},{5,9},{9,... | collective-permute-start | bytes 16136 | tf_op jit(solution)/shard_map/ppermute | solution.py:12
  49.4 8.0 %collective-permute-start.7 = (bf16[400,256]{1,0:T(8,128)(2,1)S(1)}, bf16[400,256]{1,0:T(8,128)(2,1)S(1)}, u32[]{:S(2)}, u32[]{:S(2)}) collective-permute-start(bf16[400,256]{1,0:T(8,128)(2,1)S(1)} %fusion.30), channel_id=1, source_target_pairs={{0,4},{4,8},{8,12},{12,16},{16,20},{20,24},{24,28},{1,5},{5,9},{9,... | collective-permute-start | bytes 614408 | tf_op jit(solution)/shard_map/ppermute | solution.py:38
  53.6 6.2 %collective-permute-start.6 = (bf16[400,256]{1,0:T(8,128)(2,1)S(1)}, bf16[400,256]{1,0:T(8,128)(2,1)S(1)}, u32[]{:S(2)}, u32[]{:S(2)}) collective-permute-start(bf16[400,256]{1,0:T(8,128)(2,1)S(1)} %fusion.30), channel_id=1, source_target_pairs={{0,8},{4,12},{8,16},{12,20},{16,24},{20,28},{1,9},{5,13},{9,17},{1... | collective-permute-start | bytes 614408 | tf_op jit(solution)/shard_map/ppermute | solution.py:38
  56.5 4.3 %copy-start.9 = (f32[6]{0:T(128)S(1)}, f32[6]{0:T(128)}, u32[]{:S(2)}) copy-start(f32[6]{0:T(128)} %param.24) | copy-start | bytes 76
  60.2 2.6 %collective-permute-start.8 = (bf16[400,256]{1,0:T(8,128)(2,1)S(1)}, bf16[400,256]{1,0:T(8,128)(2,1)S(1)}, u32[]{:S(2)}, u32[]{:S(2)}) collective-permute-start(bf16[400,256]{1,0:T(8,128)(2,1)S(1)} %fusion.31), channel_id=1, source_target_pairs={{4,12},{8,16},{12,20},{16,24},{20,28},{5,13},{9,17},{13,21},{17,25... | collective-permute-start | bytes 614408 | tf_op jit(solution)/shard_map/ppermute | solution.py:38
  63.1 1.4 %collective-permute-start.9 = (bf16[400,256]{1,0:T(8,128)(2,1)S(1)}, bf16[400,256]{1,0:T(8,128)(2,1)S(1)}, u32[]{:S(2)}, u32[]{:S(2)}) collective-permute-start(bf16[400,256]{1,0:T(8,128)(2,1)S(1)} %fusion.32), channel_id=1, source_target_pairs={{4,20},{8,24},{12,28},{5,21},{9,25},{13,29},{6,22},{10,26},{14,30}... | collective-permute-start | bytes 614408 | tf_op jit(solution)/shard_map/ppermute | solution.py:38

commit v17 on v14

--- a/solution.py
+++ b/solution.py
@@ -185,14 +185,13 @@
     bc_raw = summed_columns(bc_partial, "fsdp")
     feature_held, codes = exchange(stream_block, "fsdp", 1)
     feature_part = to_natural(feature_held, codes, "fsdp", 1)
-    x_acc, z_acc, step_acc = tuple(
+    x_acc, step_acc = tuple(
         (
             jnp.dot(feature_part, weight, preferred_element_type=jnp.float32)
-            for weight in (x_weight, z_weight, step_weight)
+            for weight in (x_weight, step_weight)
         )
     )
     x_raw = x_acc.astype(jnp.bfloat16)
-    z_raw = z_acc.astype(jnp.bfloat16)
     step_size = jax.nn.softplus(step_acc + step_bias[None, :])
     mixed_in = jnp.concatenate([x_raw, bc_raw], axis=1)
     conv_width = conv_heads.shape[0]
@@ -219,6 +218,8 @@
     packed = jnp.concatenate(
         [state_out.reshape(heads_dev * head_dim, state_dim), decay_rows, decay_rows, spare], axis=0
     )
+    packed, z_features = lax.optimization_barrier((packed, feature_part))
+    z_raw = jnp.dot(z_features, z_weight, preferred_element_type=jnp.float32).astype(jnp.bfloat16)
     local_y = intra + skip_gain[None, :, None] * x_heads
     gate = jax.nn.silu(z_raw.astype(jnp.float32)).reshape(tok_dev, heads_dev, head_dim)
     scanned, (local_y, gate, carry_in) = exclusive_scan(packed, "seq", (local_y, gate, carry_in), heads_dev)

time: 97.5 us -> 102 us (1.046)
  other arithmetic: 8.04 us -> 15.5 us
  waiting for transfers between devices: 23.1 us -> 19.4 us
  blocking collectives: 17.7 us -> 16 us
  local copies, waits for them, and re-layouts: 8.67 us -> 9.86 us
    ppermute x5, waiting for transfers between devices: 7.67 us -> 4.4 us  [shifted(): return lax.ppermute(array, axis, pairs)]
    convert_element_type x3, other arithmetic: 0.09 us -> 1.99 us  [received(): got = shifted(wire, axis, by).astype(jnp.float32)]
    all_to_all x1, blocking collectives: 17.7 us -> 16 us  [per_device(): lax.all_to_all(outgoing, 'seq', split_axis=0, concat_axis=0, tiled=True)]
    dot_general x0 -> x1, matrix products: none -> 1.51 us  [per_device(): jnp.dot(z_features, z_weight, preferred_element_type=jnp.float32)]
    unnamed x22 -> x48, local copies, waits for them, and re-layouts: 2.03 us -> 0.79 us
    all_to_all x1, waiting for transfers between devices: 4.13 us -> 2.99 us  [per_device(): lax.all_to_all(slot_rows, 'seq', split_axis=0, concat_axis=0, tiled=True)]
    mul x1, other arithmetic: 0.04 us -> 1.15 us  [local_terms(): x_step * to_end[:, :, None]]
  transfers between devices with their start and end apart: 11 -> 11, of which waited for: 8 -> 5; matrix products, arithmetic and copies ran while one was open for 10% -> 18% of each run, Pallas kernels for 0% -> 0%
where the time goes in v17:
time: 102 us; the launch traced here: 101 us
  starting transfers between devices  30.1 us (30%)
  waiting for transfers between devices  19.4 us (19%)
  blocking collectives  16 us (16%)
  other arithmetic  15.5 us (15%)
  local copies, waits for them, and re-layouts  9.86 us (10%)
  matrix products  6.37 us (6%)
  between operations  3.84 us (4%)
    ppermute x5, starting transfers between devices, shifted(): return lax.ppermute(array, axis, pairs)  20.4 us
    all_to_all x1, blocking collectives, per_device(): lax.all_to_all(outgoing, 'seq', split_axis=0, concat_axis=0, tiled=True)  16 us
    all_to_all x1, starting transfers between devices, per_device(): lax.all_to_all(slot_rows, 'seq', split_axis=0, concat_axis=0, tiled=True)  7.41 us
    ppermute x2, waiting for transfers between devices, exchange(): other = lax.ppermute(held, axis, [(i, i ^ bit) for i in range(count)])  6.95 us
    ppermute x1, waiting for transfers between devices, summed_columns(): kept = kept + lax.ppermute(kept, axis, [(i, i ^ bit) for i in range(count)])  5.07 us
    ppermute x5, waiting for transfers between devices, shifted(): return lax.ppermute(array, axis, pairs)  4.4 us
    all_to_all x1, waiting for transfers between devices, per_device(): lax.all_to_all(slot_rows, 'seq', split_axis=0, concat_axis=0, tiled=True)  2.99 us
    slice x2, local copies, waits for them, and re-layouts, per_device(): x_heads = activated[:, :inner_dev].reshape(tok_dev, heads_dev, head_dim)  2.69 us
  transfers between devices with their start and end apart: 11, of which 5 were waited for; matrix products, arithmetic and copies ran while one was open for 18% of the time, Pallas kernels for 0%

profile of v17, /device:TPU:0, one launch (start us, length us, event | category | flops | bytes accessed | tf_op | source)
XLA Modules:
  0.0 101.1 jit_solution(15397166685194055887)
XLA Ops:
  0.0 7.4 %all-to-all-start = ((bf16[8,32,512]{2,1,0:T(8,128)(2,1)}), bf16[8,32,512]{2,1,0:T(8,128)(2,1)S(1)}, u32[]{:S(2)}, u32[]{:S(2)}) async-start(bf16[8,32,512]{2,1,0:T(8,128)(2,1)} %bitcast.56), calls=%async_computation | async-start | bytes 524288 | tf_op jit(solution)/shard_map/all_to_all | solution.py:176
  7.4 1.2 %compare_and_fusion.1 = (pred[8]{0:T(512)(128)(4,1)}, s32[8]{0:T(128)S(1)}) fusion(s32[8,8]{1,0:T(8,128)} %param.14, s32[]{:T(128)S(6)} %select_n.119), kind=kLoop, calls=%fused_computation.107 | loop fusion | flops 48 | bytes 76 | tf_op jit(solution)/shard_map/jit(_take)/and | solution.py:231
  8.7 1.0 sort.17
  9.8 0.8 reduce-window.8
  10.7 0.6 fusion.57
  12.0 1.3 %broadcast_compare_fusion.1 = (pred[256]{0:T(512)(128)(4,1)}, pred[256]{0:T(512)(128)(4,1)S(1)}, f32[256]{0:T(256)}, f32[256]{0:T(256)}, f32[256]{0:T(256)}) fusion(s32[]{:T(128)} %bitcast.10, s32[259]{0:T(512)S(1)} %convert_reduce_fusion, s32[]{:T(128)S(6)} %select_n.138), kind=kLoop, calls=%fused_computation.118 | loop fusion | flops 2048 | bytes 7688 | tf_op jit(solution)/shard_map/eq | solution.py:147
  13.3 3.0 %all-to-all-done = bf16[8,32,512]{2,1,0:T(8,128)(2,1)S(1)} async-done(((bf16[8,32,512]{2,1,0:T(8,128)(2,1)}), bf16[8,32,512]{2,1,0:T(8,128)(2,1)S(1)}, u32[]{:S(2)}, u32[]{:S(2)}) %all-to-all-start) | async-done | bytes 262176 | tf_op jit(solution)/shard_map/all_to_all | solution.py:176
  16.3 0.6 gather_fusion
  17.5 0.6 exponential_negate_fusion
  18.1 0.7 fusion.34
  18.9 1.5 %collective-permute-start = (bf16[256,512]{1,0:T(8,128)(2,1)S(1)}, bf16[256,512]{1,0:T(8,128)(2,1)S(1)}, u32[]{:S(2)}, u32[]{:S(2)}) collective-permute-start(bf16[256,512]{1,0:T(8,128)(2,1)S(1)} %bitcast_select_fusion), channel_id=1, source_target_pairs={{0,2},{1,3},{2,0},{3,1},{4,6},{5,7},{6,4},{7,5},{8,10},{9,11},{10,... | collective-permute-start | bytes 786440 | tf_op jit(solution)/shard_map/ppermute | solution.py:65
  20.4 0.6 collective-permute-start.3
  21.0 6.9 %collective-permute-done = bf16[256,512]{1,0:T(8,128)(2,1)S(1)} collective-permute-done((bf16[256,512]{1,0:T(8,128)(2,1)S(1)}, bf16[256,512]{1,0:T(8,128)(2,1)S(1)}, u32[]{:S(2)}, u32[]{:S(2)}) %collective-permute-start) | collective-permute-done | bytes 262176 | tf_op jit(solution)/shard_map/ppermute | solution.py:65
  28.1 5.1 %collective-permute-done.3 = f32[256,256]{1,0:T(8,128)S(1)} collective-permute-done((f32[256,256]{1,0:T(8,128)S(1)}, f32[256,256]{1,0:T(8,128)S(1)}, u32[]{:S(2)}, u32[]{:S(2)}) %collective-permute-start.3) | collective-permute-done | bytes 262176 | tf_op jit(solution)/shard_map/ppermute | solution.py:103
  33.4 0.7 fusion.58
  36.5 0.6 slice.119
  37.4 1.1 %pad_maximum_fusion = bf16[256,2048]{1,0:T(8,128)(2,1)S(1)} fusion(bf16[256,1024]{1,0:T(8,128)(2,1)} %collective-permute-done.1, bf16[256,512]{1,0:T(8,128)(2,1)S(1)} %collective-permute-done, bf16[256,512]{1,0:T(8,128)(2,1)S(1)} %bitcast_select_fusion), kind=kLoop, calls=%fused_computation.17 | loop fusion | flops 3145728 | bytes 2097152 | tf_op jit(solution)/shard_map/concatenate | solution.py:66
  38.9 0.7 convolution_convert_fusion.1
  39.6 3.3 %collective-permute-start.5 = (bf16[3,896]{1,0:T(4,128)(2,1)S(1)}, bf16[3,896]{1,0:T(4,128)(2,1)S(1)}, u32[]{:S(2)}, u32[]{:S(2)}) collective-permute-start(bf16[3,896]{1,0:T(4,128)(2,1)S(1)} %pad_maximum_fusion.3), channel_id=1, source_target_pairs={{0,4},{4,8},{8,12},{12,16},{16,20},{20,24},{24,28},{1,5},{5,9},{9,... | collective-permute-start | bytes 16136 | tf_op jit(solution)/shard_map/ppermute | solution.py:12
  43.0 0.4 compare_select_fusion
  43.8 0.7 select_exponential_fusion
  44.5 1.2 %broadcast_select_fusion.1 = f32[6]{0:T(128)} fusion(pred[]{:T(512)} %bitcast.14, f32[6]{0:T(128)S(1)} %slice_reduce_fusion), kind=kLoop, calls=%fused_computation.114 | loop fusion | flops 6 | bytes 49 | tf_op jit(solution)/shard_map/jit(_where)/select_n | solution.py:153
  45.9 0.7 divide_multiply_fusion
  46.6 0.8 slice.145
  47.4 1.9 %copy.21 = f32[256,384]{0,1:T(8,128)} copy(f32[256,384]{1,0:T(8,128)} %slice.145) | data formatting | bytes 786432 | tf_op jit(solution)/shard_map/slice | solution.py:210
  49.3 1.2 %multiply_multiply_fusion = f32[256,6,64]{0,2,1:T(8,128)S(1)} fusion(f32[256,6,64]{0,2,1:T(8,128)} %bitcast.50, f32[256,6]{0,1:T(8,128)} %get-tuple-element.32, f32[256,6]{0,1:T(8,128)S(1)} %compare_select_fusion), kind=kLoop, calls=%fused_computation.51 | loop fusion | flops 196608 | bytes 798720 | tf_op jit(solution)/shard_map/mul | solution.py:150
  50.4 0.5 fusion.40
  50.9 0.7 broadcast_in_dim.102
  51.8 0.8 fusion.30
  52.6 4.0 %collective-permute-start.6 = (bf16[400,256]{1,0:T(8,128)(2,1)}, bf16[400,256]{1,0:T(8,128)(2,1)}, u32[]{:S(2)}, u32[]{:S(2)}) collective-permute-start(bf16[400,256]{1,0:T(8,128)(2,1)} %fusion.30), channel_id=1, source_target_pairs={{0,8},{4,12},{8,16},{12,20},{16,24},{20,28},{1,9},{5,13},{9,17},{1... | collective-permute-start | bytes 614408 | tf_op jit(solution)/shard_map/ppermute | solution.py:12
  56.5 2.9 %collective-permute-start.7 = (bf16[400,256]{1,0:T(8,128)(2,1)}, bf16[400,256]{1,0:T(8,128)(2,1)}, u32[]{:S(2)}, u32[]{:S(2)}) collective-permute-start(bf16[400,256]{1,0:T(8,128)(2,1)} %fusion.30), channel_id=1, source_target_pairs={{0,4},{4,8},{8,12},{12,16},{16,20},{20,24},{24,28},{1,5},{5,9},{9,... | collective-permute-start | bytes 614408 | tf_op jit(solution)/shard_map/ppermute | solution.py:12
  59.4 1.5 %divide_multiply_fusion.1 = f32[256,384]{1,0:T(8,128)} fusion(bf16[256,2048]{1,0:T(8,128)(2,1)S(1)} %pad_maximum_fusion.1, bf16[2048,384]{1,0:T(8,128)(2,1)S(1)} %copy-done.19), kind=kOutput, calls=%fused_computation.49 | convolution fusion | flops 403243008 | bytes 3014656 | tf_op jit(solution)/shard_map/dot_general | solution.py:222
  60.9 1.2 %copy.22 = f32[256,384]{0,1:T(8,128)S(1)} copy(f32[256,384]{1,0:T(8,128)} %divide_multiply_fusion.1) | data formatting | bytes 786432 | tf_op jit(solution)/shard_map/jit(silu)/mul | solution.py:224
  62.1 0.4 fusion.37
  62.6 1.0 convert_element_type.95
  63.6 1.0 convert_element_type.97
  64.8 5.8 %collective-permute-start.8 = (bf16[400,256]{1,0:T(8,128)(2,1)S(1)}, bf16[400,256]{1,0:T(8,128)(2,1)S(1)}, u32[]{:S(2)}, u32[]{:S(2)}) collective-permute-start(bf16[400,256]{1,0:T(8,128)(2,1)S(1)} %fusion.31), channel_id=1, source_target_pairs={{0,8},{4,12},{8,16},{12,20},{16,24},{20,28},{1,9},{5,13},{9,17},{1... | collective-permute-start | bytes 614408 | tf_op jit(solution)/shard_map/ppermute | solution.py:12
  70.6 1.9 %fusion.8 = f32[256,6,64]{0,2,1:T(8,128)S(1)} fusion(f32[6,256]{1,0:T(8,128)S(1)} %bitcast.57, f32[256,256]{1,0:T(8,128)S(1)} %fusion.37, pred[256,256]{1,0:T(8,128)(4,1)S(1)} %copy-done.3, f32[256,6,64]{0,2,1:T(8,128)S(1)} %bitcast.51, f32[6]{0:T(128)S(1)} %copy-done.21, f32[256,6]{0,1:T(8,128)S(1)} %compare_select_fusion), kind=kOutput, calls=%fused_computation.8 | convolution fusion | flops 303464448 | bytes 1126424 | tf_op jit(solution)/shard_map/hts,shp->thp/dot_general | solution.py:144
  72.5 1.9 %collective-permute-done.8 = bf16[400,256]{1,0:T(8,128)(2,1)S(1)} collective-permute-done((bf16[400,256]{1,0:T(8,128)(2,1)S(1)}, bf16[400,256]{1,0:T(8,128)(2,1)S(1)}, u32[]{:S(2)}, u32[]{:S(2)}) %collective-permute-start.8) | collective-permute-done | bytes 204832 | tf_op jit(solution)/shard_map/ppermute | solution.py:12
  74.8 4.5 %collective-permute-start.9 = (bf16[400,256]{1,0:T(8,128)(2,1)S(1)}, bf16[400,256]{1,0:T(8,128)(2,1)S(1)}, u32[]{:S(2)}, u32[]{:S(2)}) collective-permute-start(bf16[400,256]{1,0:T(8,128)(2,1)S(1)} %fusion.32), channel_id=1, source_target_pairs={{0,16},{4,20},{8,24},{12,28},{1,17},{5,21},{9,25},{13,29},{2,18},{... | collective-permute-start | bytes 614408 | tf_op jit(solution)/shard_map/ppermute | solution.py:12
  79.3 0.7 fusion.52
  80.0 2.5 %collective-permute-done.9 = bf16[400,256]{1,0:T(8,128)(2,1)S(1)} collective-permute-done((bf16[400,256]{1,0:T(8,128)(2,1)S(1)}, bf16[400,256]{1,0:T(8,128)(2,1)S(1)}, u32[]{:S(2)}, u32[]{:S(2)}) %collective-permute-start.9) | collective-permute-done | bytes 204832 | tf_op jit(solution)/shard_map/ppermute | solution.py:12
  82.5 0.5 fusion.13
  83.1 0.3 copy.23
  83.4 0.3 convert_element_type.109
  83.7 0.6 gather_fusion.1
  84.4 16.0 %all_to_all.10 = bf16[8,32,384]{2,1,0:T(8,128)(2,1)S(1)} all-to-all(bf16[8,32,384]{2,1,0:T(8,128)(2,1)S(1)} %broadcast_select_fusion), channel_id=1, replica_groups=mesh['seq'=8,'fsdp'=4] {'seq'}, dimensions={0} | all-to-all | bytes 393216 | tf_op jit(solution)/shard_map/all_to_all | solution.py:232
  100.4 0.7 copy.26
  (97 shorter events, 3.1 us)
Async XLA Ops:
  0.0 38.8 %copy-start = (bf16[2048,384]{1,0:T(8,128)(2,1)S(1)}, bf16[2048,384]{1,0:T(8,128)(2,1)}, u32[]{:S(2)}) copy-start(bf16[2048,384]{1,0:T(8,128)(2,1)} %param.16) | copy-start | bytes 4718596
  0.0 17.0 %copy-start.2 = (bf16[512,512]{1,0:T(8,128)(2,1)S(1)}, bf16[512,512]{1,0:T(8,128)(2,1)}, u32[]{:S(2)}) copy-start(bf16[512,512]{1,0:T(8,128)(2,1)} %param.18) | copy-start | bytes 1572868
  0.0 16.3 %all-to-all-start = ((bf16[8,32,512]{2,1,0:T(8,128)(2,1)}), bf16[8,32,512]{2,1,0:T(8,128)(2,1)S(1)}, u32[]{:S(2)}, u32[]{:S(2)}) async-start(bf16[8,32,512]{2,1,0:T(8,128)(2,1)} %bitcast.56), calls=%async_computation | async-start | bytes 524288 | tf_op jit(solution)/shard_map/all_to_all | solution.py:176
  7.4 10.1 %copy-start.20 = (f32[6]{0:T(128)S(1)}, f32[6]{0:T(128)}, u32[]{:S(2)}) copy-start(f32[6]{0:T(128)} %param.23) | copy-start | bytes 76
  13.3 23.2 %copy-start.16 = (pred[256]{0:T(512)(128)(4,1)}, pred[256]{0:T(512)(128)(4,1)S(1)}, u32[]{:S(2)}) copy-start(pred[256]{0:T(512)(128)(4,1)S(1)} %get-tuple-element.34) | copy-start | bytes 772
  16.9 4.1 %copy-start.10 = (f32[4,384]{1,0:T(4,128)S(1)}, f32[4,384]{1,0:T(4,128)}, u32[]{:S(2)}) copy-start(f32[4,384]{1,0:T(4,128)} %param.20) | copy-start | bytes 18436
  16.9 4.1 %copy-start.9 = (f32[4,512]{1,0:T(4,128)S(1)}, f32[4,512]{1,0:T(4,128)}, u32[]{:S(2)}) copy-start(f32[4,512]{1,0:T(4,128)} %param.21) | copy-start | bytes 24580
  17.4 16.0 %copy-start.8 = (s32[4]{0:T(128)S(1)}, s32[4]{0:T(128)}, u32[]{:S(2)}) copy-start(s32[4]{0:T(128)} %constant.94.clone) | copy-start | bytes 52
  17.4 3.0 %collective-permute-start.2 = (f32[256,256]{1,0:T(8,128)S(1)}, f32[256,256]{1,0:T(8,128)S(1)}, u32[]{:S(2)}, u32[]{:S(2)}) collective-permute-start(f32[256,256]{1,0:T(8,128)S(1)} %constant_dynamic-slice_fusion), channel_id=1, source_target_pairs={{0,1},{1,0},{2,3},{3,2},{4,5},{5,4},{6,7},{7,6},{8,9},{9,8},{10,11... | collective-permute-start | bytes 786440 | tf_op jit(solution)/shard_map/ppermute | solution.py:100
  18.9 9.1 %collective-permute-start = (bf16[256,512]{1,0:T(8,128)(2,1)S(1)}, bf16[256,512]{1,0:T(8,128)(2,1)S(1)}, u32[]{:S(2)}, u32[]{:S(2)}) collective-permute-start(bf16[256,512]{1,0:T(8,128)(2,1)S(1)} %bitcast_select_fusion), channel_id=1, source_target_pairs={{0,2},{1,3},{2,0},{3,1},{4,6},{5,7},{6,4},{7,5},{8,10},{9,11},{10,... | collective-permute-start | bytes 786440 | tf_op jit(solution)/shard_map/ppermute | solution.py:65
  20.4 12.8 %collective-permute-start.3 = (f32[256,256]{1,0:T(8,128)S(1)}, f32[256,256]{1,0:T(8,128)S(1)}, u32[]{:S(2)}, u32[]{:S(2)}) collective-permute-start(f32[256,256]{1,0:T(8,128)S(1)} %dynamic-slice_add_fusion), channel_id=1, source_target_pairs={{0,2},{1,3},{2,0},{3,1},{4,6},{5,7},{6,4},{7,5},{8,10},{9,11},{10,... | collective-permute-start | bytes 786440 | tf_op jit(solution)/shard_map/ppermute | solution.py:103
  28.0 9.3 %collective-permute-start.1 = (bf16[256,1024]{1,0:T(8,128)(2,1)S(1)}, bf16[256,1024]{1,0:T(8,128)(2,1)}, u32[]{:S(2)}, u32[]{:S(2)}) collective-permute-start(bf16[256,1024]{1,0:T(8,128)(2,1)S(1)} %pad_maximum_fusion.2), channel_id=1, source_target_pairs={{0,1},{1,0},{2,3},{3,2},{4,5},{5,4},{6,7},{7,6},{8,9},{9,8},{10,11... | collective-permute-start | bytes 1572872 | tf_op jit(solution)/shard_map/ppermute | solution.py:65
  33.2 4.0 %collective-permute-start.4 = (bf16[256,256]{1,0:T(8,128)(2,1)S(1)}, bf16[256,256]{1,0:T(8,128)(2,1)S(1)}, u32[]{:S(2)}, u32[]{:S(2)}) collective-permute-start(bf16[256,256]{1,0:T(8,128)(2,1)S(1)} %add_convert_fusion), channel_id=1, source_target_pairs={{0,1},{1,0},{2,3},{3,2},{4,5},{5,4},{6,7},{7,6},{8,9},{9,8},{10,11... | collective-permute-start | bytes 393224 | tf_op jit(solution)/shard_map/ppermute | solution.py:106
  38.8 4.1 %copy-start.5 = (bf16[2048,6]{0,1:T(8,128)(2,1)S(1)}, bf16[2048,6]{0,1:T(8,128)(2,1)}, u32[]{:S(2)}) copy-start(bf16[2048,6]{0,1:T(8,128)(2,1)} %param.19) | copy-start | bytes 73732
  38.8 4.1 %copy-start.18 = (f32[6]{0:T(128)S(1)}, f32[6]{0:T(128)}, u32[]{:S(2)}) copy-start(f32[6]{0:T(128)} %param.22) | copy-start | bytes 76
  38.8 4.5 %copy-start.22 = (f32[6]{0:T(128)S(1)}, f32[6]{0:T(128)}, u32[]{:S(2)}) copy-start(f32[6]{0:T(128)} %exponential_negate_fusion) | copy-start | bytes 76
  38.9 5.0 %copy-start.15 = (pred[256]{0:T(512)(128)(4,1)S(1)}, pred[256]{0:T(512)(128)(4,1)}, u32[]{:S(2)}) copy-start(pred[256]{0:T(512)(128)(4,1)} %get-tuple-element.33) | copy-start | bytes 772
  38.9 5.0 %copy-start.17 = (pred[256]{0:T(512)(128)(4,1)S(1)}, pred[256]{0:T(512)(128)(4,1)}, u32[]{:S(2)}) copy-start(pred[256]{0:T(512)(128)(4,1)} %copy-done.16) | copy-start | bytes 772
  39.6 6.3 %copy-start.11 = (f32[256]{0:T(256)S(1)}, f32[256]{0:T(256)}, u32[]{:S(2)}) copy-start(f32[256]{0:T(256)} %get-tuple-element.35) | copy-start | bytes 3076
  39.6 6.3 %copy-start.12 = (f32[256]{0:T(256)S(1)}, f32[256]{0:T(256)}, u32[]{:S(2)}) copy-start(f32[256]{0:T(256)} %get-tuple-element.36) | copy-start | bytes 3076
  39.6 6.3 %copy-start.13 = (f32[256]{0:T(256)S(1)}, f32[256]{0:T(256)}, u32[]{:S(2)}) copy-start(f32[256]{0:T(256)} %get-tuple-element.37) | copy-start | bytes 3076
  39.6 6.1 %collective-permute-start.5 = (bf16[3,896]{1,0:T(4,128)(2,1)S(1)}, bf16[3,896]{1,0:T(4,128)(2,1)S(1)}, u32[]{:S(2)}, u32[]{:S(2)}) collective-permute-start(bf16[3,896]{1,0:T(4,128)(2,1)S(1)} %pad_maximum_fusion.3), channel_id=1, source_target_pairs={{0,4},{4,8},{8,12},{12,16},{16,20},{20,24},{24,28},{1,5},{5,9},{9,... | collective-permute-start | bytes 16136 | tf_op jit(solution)/shard_map/ppermute | solution.py:12
  43.6 2.2 %copy-start.6 = (f32[256,6]{0,1:T(8,128)}, f32[256,6]{0,1:T(8,128)S(1)}, u32[]{:S(2)}) copy-start(f32[256,6]{0,1:T(8,128)S(1)} %fusion.35) | copy-start | bytes 18436
  49.3 10.2 %copy-start.19 = (bf16[2048,384]{1,0:T(8,128)(2,1)S(1)}, bf16[2048,384]{1,0:T(8,128)(2,1)}, u32[]{:S(2)}) copy-start(bf16[2048,384]{1,0:T(8,128)(2,1)} %param.17) | copy-start | bytes 4718596
  52.6 10.0 %collective-permute-start.6 = (bf16[400,256]{1,0:T(8,128)(2,1)}, bf16[400,256]{1,0:T(8,128)(2,1)}, u32[]{:S(2)}, u32[]{:S(2)}) collective-permute-start(bf16[400,256]{1,0:T(8,128)(2,1)} %fusion.30), channel_id=1, source_target_pairs={{0,8},{4,12},{8,16},{12,20},{16,24},{20,28},{1,9},{5,13},{9,17},{1... | collective-permute-start | bytes 614408 | tf_op jit(solution)/shard_map/ppermute | solution.py:12
  56.5 7.0 %collective-permute-start.7 = (bf16[400,256]{1,0:T(8,128)(2,1)}, bf16[400,256]{1,0:T(8,128)(2,1)}, u32[]{:S(2)}, u32[]{:S(2)}) collective-permute-start(bf16[400,256]{1,0:T(8,128)(2,1)} %fusion.30), channel_id=1, source_target_pairs={{0,4},{4,8},{8,12},{12,16},{16,20},{20,24},{24,28},{1,5},{5,9},{9,... | collective-permute-start | bytes 614408 | tf_op jit(solution)/shard_map/ppermute | solution.py:12
  62.5 8.1 %copy-start.1 = (f32[256,384]{0,1:T(8,128)S(1)}, f32[256,384]{0,1:T(8,128)}, u32[]{:S(2)}) copy-start(f32[256,384]{0,1:T(8,128)} %copy.21) | copy-start | bytes 1179652
  62.5 8.1 %copy-start.3 = (pred[256,256]{1,0:T(8,128)(4,1)S(1)}, pred[256,256]{1,0:T(8,128)(4,1)}, u32[]{:S(2)}) copy-start(pred[256,256]{1,0:T(8,128)(4,1)} %fusion.34) | copy-start | bytes 196612
  62.5 8.1 %copy-start.7 = (f32[256,6]{0,1:T(8,128)S(1)}, f32[256,6]{0,1:T(8,128)}, u32[]{:S(2)}) copy-start(f32[256,6]{0,1:T(8,128)} %copy-done.6) | copy-start | bytes 18436
  62.5 8.1 %copy-start.21 = (f32[6]{0:T(128)S(1)}, f32[6]{0:T(128)}, u32[]{:S(2)}) copy-start(f32[6]{0:T(128)} %param.24) | copy-start | bytes 76
  64.8 9.6 %collective-permute-start.8 = (bf16[400,256]{1,0:T(8,128)(2,1)S(1)}, bf16[400,256]{1,0:T(8,128)(2,1)S(1)}, u32[]{:S(2)}, u32[]{:S(2)}) collective-permute-start(bf16[400,256]{1,0:T(8,128)(2,1)S(1)} %fusion.31), channel_id=1, source_target_pairs={{0,8},{4,12},{8,16},{12,20},{16,24},{20,28},{1,9},{5,13},{9,17},{1... | collective-permute-start | bytes 614408 | tf_op jit(solution)/shard_map/ppermute | solution.py:12
  74.5 8.0 %copy-start.4 = (f32[256,6]{0,1:T(8,128)S(1)}, f32[256,6]{0,1:T(8,128)}, u32[]{:S(2)}) copy-start(f32[256,6]{0,1:T(8,128)} %get-tuple-element.16) | copy-start | bytes 18436
  74.8 7.7 %collective-permute-start.9 = (bf16[400,256]{1,0:T(8,128)(2,1)S(1)}, bf16[400,256]{1,0:T(8,128)(2,1)S(1)}, u32[]{:S(2)}, u32[]{:S(2)}) collective-permute-start(bf16[400,256]{1,0:T(8,128)(2,1)S(1)} %fusion.32), channel_id=1, source_target_pairs={{0,16},{4,20},{8,24},{12,28},{1,17},{5,21},{9,25},{13,29},{2,18},{... | collective-permute-start | bytes 614408 | tf_op jit(solution)/shard_map/ppermute | solution.py:12
  82.5 1.8 %copy-start.14 = (pred[8]{0:T(512)(128)(4,1)S(1)}, pred[8]{0:T(512)(128)(4,1)}, u32[]{:S(2)}) copy-start(pred[8]{0:T(512)(128)(4,1)} %get-tuple-element.23) | copy-start | bytes 28

commit v18 on v14

--- a/solution.py
+++ b/solution.py
@@ -147,7 +147,7 @@
             (segment_ids == segment_ids[-1])[:, None], cum_decay[-1][None, :] - cum_decay, -jnp.inf
         )
     )
-    state_out = jnp.einsum("shp,sn->hpn", x_step * to_end[:, :, None], b_rows, precision=precise)
+    state_out = jnp.einsum("shp,sn->hpn", x_step * to_end[:, :, None], b_rows)
     carried = segment_ids == seg_before
     carry_in = jnp.exp(jnp.where(carried[:, None], cum_decay, -jnp.inf))
     block_decay = jnp.where(carried[-1], jnp.exp(cum_decay[-1]), 0.0)
@@ -223,7 +223,7 @@
     gate = jax.nn.silu(z_raw.astype(jnp.float32)).reshape(tok_dev, heads_dev, head_dim)
     scanned, (local_y, gate, carry_in) = exclusive_scan(packed, "seq", (local_y, gate, carry_in), heads_dev)
     state_in = scanned[: heads_dev * head_dim].reshape(heads_dev, head_dim, state_dim)
-    incoming = jnp.einsum("tn,hpn->thp", c_rows, state_in, precision=precise)
+    incoming = jnp.einsum("tn,hpn->thp", c_rows, state_in, precision=lax.Precision.HIGH)
     y_block = local_y + carry_in[:, :, None] * incoming
     gated = (y_block * gate).reshape(tok_dev, inner_dev).astype(jnp.bfloat16)
     ordered = gated.reshape(seq_count, piece_rows, inner_dev)

time: 97.5 us -> 97.1 us (level)
  no operation moved by 1% of the time
where the time goes in v18:
time: 97.1 us; the launch traced here: 96.5 us
  starting transfers between devices  30 us (31%)
  waiting for transfers between devices  23.1 us (24%)
  blocking collectives  17.7 us (18%)
  local copies, waits for them, and re-layouts  8.67 us (9%)
  other arithmetic  8.05 us (8%)
  matrix products  5.2 us (5%)
  between operations  3.71 us (4%)
    ppermute x5, starting transfers between devices, shifted(): return lax.ppermute(array, axis, pairs)  19.5 us
    all_to_all x1, blocking collectives, per_device(): lax.all_to_all(outgoing, 'seq', split_axis=0, concat_axis=0, tiled=True)  17.7 us
    ppermute x5, waiting for transfers between devices, shifted(): return lax.ppermute(array, axis, pairs)  7.67 us
    all_to_all x1, starting transfers between devices, per_device(): lax.all_to_all(slot_rows, 'seq', split_axis=0, concat_axis=0, tiled=True)  7.41 us
    ppermute x2, waiting for transfers between devices, exchange(): other = lax.ppermute(held, axis, [(i, i ^ bit) for i in range(count)])  6.25 us
    ppermute x1, waiting for transfers between devices, summed_columns(): kept = kept + lax.ppermute(kept, axis, [(i, i ^ bit) for i in range(count)])  5.06 us
    all_to_all x1, waiting for transfers between devices, per_device(): lax.all_to_all(slot_rows, 'seq', split_axis=0, concat_axis=0, tiled=True)  4.13 us
    unnamed x22, local copies, waits for them, and re-layouts  2.03 us
  transfers between devices with their start and end apart: 11, of which 8 were waited for; matrix products, arithmetic and copies ran while one was open for 10% of the time, Pallas kernels for 0%

profile of v18, /device:TPU:0, one launch (start us, length us, event | category | flops | bytes accessed | tf_op | source)
XLA Modules:
  0.0 96.5 jit_solution(12106838998959068945)
XLA Ops:
  0.0 7.4 %all-to-all-start = ((bf16[8,32,512]{2,1,0:T(8,128)(2,1)}), bf16[8,32,512]{2,1,0:T(8,128)(2,1)S(1)}, u32[]{:S(2)}, u32[]{:S(2)}) async-start(bf16[8,32,512]{2,1,0:T(8,128)(2,1)} %bitcast.53), calls=%async_computation | async-start | bytes 524288 | tf_op jit(solution)/shard_map/all_to_all | solution.py:176
  7.4 0.8 reduce-window.8
  8.3 0.7 compare_and_fusion.1
  9.0 1.0 sort.17
  10.2 0.6 fusion.57
  11.5 0.7 broadcast_compare_fusion.1
  12.2 4.1 %all-to-all-done = bf16[8,32,512]{2,1,0:T(8,128)(2,1)S(1)} async-done(((bf16[8,32,512]{2,1,0:T(8,128)(2,1)}), bf16[8,32,512]{2,1,0:T(8,128)(2,1)S(1)}, u32[]{:S(2)}, u32[]{:S(2)}) %all-to-all-start) | async-done | bytes 262176 | tf_op jit(solution)/shard_map/all_to_all | solution.py:176
  16.3 0.6 gather_fusion
  17.1 0.3 fusion.59
  17.7 1.6 %collective-permute-start = (bf16[256,512]{1,0:T(8,128)(2,1)S(1)}, bf16[256,512]{1,0:T(8,128)(2,1)S(1)}, u32[]{:S(2)}, u32[]{:S(2)}) collective-permute-start(bf16[256,512]{1,0:T(8,128)(2,1)S(1)} %bitcast_select_fusion), channel_id=1, source_target_pairs={{0,2},{1,3},{2,0},{3,1},{4,6},{5,7},{6,4},{7,5},{8,10},{9,11},{10,... | collective-permute-start | bytes 786440 | tf_op jit(solution)/shard_map/ppermute | solution.py:65
  19.3 1.3 %collective-permute-start.3 = (f32[256,256]{1,0:T(8,128)S(1)}, f32[256,256]{1,0:T(8,128)S(1)}, u32[]{:S(2)}, u32[]{:S(2)}) collective-permute-start(f32[256,256]{1,0:T(8,128)S(1)} %dynamic-slice_add_fusion), channel_id=1, source_target_pairs={{0,2},{1,3},{2,0},{3,1},{4,6},{5,7},{6,4},{7,5},{8,10},{9,11},{10,... | collective-permute-start | bytes 786440 | tf_op jit(solution)/shard_map/ppermute | solution.py:103
  20.6 6.2 %collective-permute-done = bf16[256,512]{1,0:T(8,128)(2,1)S(1)} collective-permute-done((bf16[256,512]{1,0:T(8,128)(2,1)S(1)}, bf16[256,512]{1,0:T(8,128)(2,1)S(1)}, u32[]{:S(2)}, u32[]{:S(2)}) %collective-permute-start) | collective-permute-done | bytes 262176 | tf_op jit(solution)/shard_map/ppermute | solution.py:65
  27.0 5.1 %collective-permute-done.3 = f32[256,256]{1,0:T(8,128)S(1)} collective-permute-done((f32[256,256]{1,0:T(8,128)S(1)}, f32[256,256]{1,0:T(8,128)S(1)}, u32[]{:S(2)}, u32[]{:S(2)}) %collective-permute-start.3) | collective-permute-done | bytes 262176 | tf_op jit(solution)/shard_map/ppermute | solution.py:103
  32.2 0.7 fusion.58
  35.4 0.6 slice.119
  36.3 1.1 %pad_maximum_fusion = bf16[256,2048]{1,0:T(8,128)(2,1)S(1)} fusion(bf16[256,1024]{1,0:T(8,128)(2,1)} %collective-permute-done.1, bf16[256,512]{1,0:T(8,128)(2,1)S(1)} %collective-permute-done, bf16[256,512]{1,0:T(8,128)(2,1)S(1)} %bitcast_select_fusion), kind=kLoop, calls=%fused_computation.17 | loop fusion | flops 3145728 | bytes 2097152 | tf_op jit(solution)/shard_map/concatenate | solution.py:66
  37.6 0.6 copy-done.6
  38.2 0.4 compare_select_fusion
  38.6 0.2 fusion.35
  38.8 0.2 slice_reduce_fusion
  39.1 0.7 convolution_convert_fusion.1
  39.8 0.7 copy-done.5
  40.5 0.7 divide_multiply_fusion.1
  41.2 3.3 %collective-permute-start.5 = (bf16[3,896]{1,0:T(4,128)(2,1)S(1)}, bf16[3,896]{1,0:T(4,128)(2,1)S(1)}, u32[]{:S(2)}, u32[]{:S(2)}) collective-permute-start(bf16[3,896]{1,0:T(4,128)(2,1)S(1)} %pad_maximum_fusion.3), channel_id=1, source_target_pairs={{0,4},{4,8},{8,12},{12,16},{16,20},{20,24},{24,28},{1,5},{5,9},{9,... | collective-permute-start | bytes 16136 | tf_op jit(solution)/shard_map/ppermute | solution.py:12
  44.6 0.6 broadcast_select_fusion.1
  45.4 0.5 collective-permute-done.5
  46.0 0.7 divide_multiply_fusion
  46.7 0.8 slice.145
  47.5 1.2 %copy.21 = f32[256,384]{0,1:T(8,128)S(1)} copy(f32[256,384]{1,0:T(8,128)} %slice.145) | data formatting | bytes 786432 | tf_op jit(solution)/shard_map/slice | solution.py:211
  48.7 0.2 fusion.40
  49.0 0.2 fusion.30
  49.1 4.2 %collective-permute-start.7 = (bf16[400,256]{1,0:T(8,128)(2,1)S(1)}, bf16[400,256]{1,0:T(8,128)(2,1)S(1)}, u32[]{:S(2)}, u32[]{:S(2)}) collective-permute-start(bf16[400,256]{1,0:T(8,128)(2,1)S(1)} %fusion.30), channel_id=1, source_target_pairs={{0,4},{4,8},{8,12},{12,16},{16,20},{20,24},{24,28},{1,5},{5,9},{9,... | collective-permute-start | bytes 614408 | tf_op jit(solution)/shard_map/ppermute | solution.py:12
  53.3 2.5 %collective-permute-start.6 = (bf16[400,256]{1,0:T(8,128)(2,1)S(1)}, bf16[400,256]{1,0:T(8,128)(2,1)S(1)}, u32[]{:S(2)}, u32[]{:S(2)}) collective-permute-start(bf16[400,256]{1,0:T(8,128)(2,1)S(1)} %fusion.30), channel_id=1, source_target_pairs={{0,8},{4,12},{8,16},{12,20},{16,24},{20,28},{1,9},{5,13},{9,17},{1... | collective-permute-start | bytes 614408 | tf_op jit(solution)/shard_map/ppermute | solution.py:12
  55.8 0.4 fusion.37
  56.3 0.9 collective-permute-done.7
  57.1 2.4 %collective-permute-done.6 = bf16[400,256]{1,0:T(8,128)(2,1)S(1)} collective-permute-done((bf16[400,256]{1,0:T(8,128)(2,1)S(1)}, bf16[400,256]{1,0:T(8,128)(2,1)S(1)}, u32[]{:S(2)}, u32[]{:S(2)}) %collective-permute-start.6) | collective-permute-done | bytes 204832 | tf_op jit(solution)/shard_map/ppermute | solution.py:12
  59.9 5.2 %collective-permute-start.8 = (bf16[400,256]{1,0:T(8,128)(2,1)S(1)}, bf16[400,256]{1,0:T(8,128)(2,1)S(1)}, u32[]{:S(2)}, u32[]{:S(2)}) collective-permute-start(bf16[400,256]{1,0:T(8,128)(2,1)S(1)} %fusion.31), channel_id=1, source_target_pairs={{0,8},{4,12},{8,16},{12,20},{16,24},{20,28},{1,9},{5,13},{9,17},{1... | collective-permute-start | bytes 614408 | tf_op jit(solution)/shard_map/ppermute | solution.py:12
  65.1 1.9 %fusion.8 = f32[256,6,64]{0,2,1:T(8,128)S(1)} fusion(f32[6,256]{1,0:T(8,128)S(1)} %bitcast.54, f32[256,256]{1,0:T(8,128)S(1)} %fusion.37, pred[256,256]{1,0:T(8,128)(4,1)S(1)} %fusion.34, f32[256,6,64]{0,2,1:T(8,128)S(1)} %bitcast.48, f32[6]{0:T(128)S(1)} %copy-done.9, f32[256,6]{0,1:T(8,128)S(1)} %compare_select_fusion), kind=kOutput, calls=%fused_computation.8 | convolution fusion | flops 303464448 | bytes 1126424 | tf_op jit(solution)/shard_map/hts,shp->thp/dot_general | solution.py:144
  66.9 1.4 %collective-permute-done.8 = bf16[400,256]{1,0:T(8,128)(2,1)S(1)} collective-permute-done((bf16[400,256]{1,0:T(8,128)(2,1)S(1)}, bf16[400,256]{1,0:T(8,128)(2,1)S(1)}, u32[]{:S(2)}, u32[]{:S(2)}) %collective-permute-start.8) | collective-permute-done | bytes 204832 | tf_op jit(solution)/shard_map/ppermute | solution.py:12
  68.7 4.4 %collective-permute-start.9 = (bf16[400,256]{1,0:T(8,128)(2,1)S(1)}, bf16[400,256]{1,0:T(8,128)(2,1)S(1)}, u32[]{:S(2)}, u32[]{:S(2)}) collective-permute-start(bf16[400,256]{1,0:T(8,128)(2,1)S(1)} %fusion.32), channel_id=1, source_target_pairs={{0,16},{4,20},{8,24},{12,28},{1,17},{5,21},{9,25},{13,29},{2,18},{... | collective-permute-start | bytes 614408 | tf_op jit(solution)/shard_map/ppermute | solution.py:12
  73.1 0.7 fusion.52
  73.8 2.5 %collective-permute-done.9 = bf16[400,256]{1,0:T(8,128)(2,1)S(1)} collective-permute-done((bf16[400,256]{1,0:T(8,128)(2,1)S(1)}, bf16[400,256]{1,0:T(8,128)(2,1)S(1)}, u32[]{:S(2)}, u32[]{:S(2)}) %collective-permute-start.9) | collective-permute-done | bytes 204832 | tf_op jit(solution)/shard_map/ppermute | solution.py:12
  76.4 0.4 fusion.13
  76.8 0.3 copy.23
  77.1 0.3 convert_element_type.109
  77.4 0.6 gather_fusion.1
  78.1 17.7 %all_to_all.10 = bf16[8,32,384]{2,1,0:T(8,128)(2,1)S(1)} all-to-all(bf16[8,32,384]{2,1,0:T(8,128)(2,1)S(1)} %broadcast_select_fusion), channel_id=1, replica_groups=mesh['seq'=8,'fsdp'=4] {'seq'}, dimensions={0} | all-to-all | bytes 393216 | tf_op jit(solution)/shard_map/all_to_all | solution.py:231
  95.8 0.7 copy.26
  (69 shorter events, 2.6 us)
Async XLA Ops:
  0.0 39.1 %copy-start = (bf16[2048,384]{1,0:T(8,128)(2,1)S(1)}, bf16[2048,384]{1,0:T(8,128)(2,1)}, u32[]{:S(2)}) copy-start(bf16[2048,384]{1,0:T(8,128)(2,1)} %param.16) | copy-start | bytes 4718596
  0.0 17.0 %copy-start.1 = (bf16[512,512]{1,0:T(8,128)(2,1)S(1)}, bf16[512,512]{1,0:T(8,128)(2,1)}, u32[]{:S(2)}) copy-start(bf16[512,512]{1,0:T(8,128)(2,1)} %param.18) | copy-start | bytes 1572868
  0.0 16.3 %all-to-all-start = ((bf16[8,32,512]{2,1,0:T(8,128)(2,1)}), bf16[8,32,512]{2,1,0:T(8,128)(2,1)S(1)}, u32[]{:S(2)}, u32[]{:S(2)}) async-start(bf16[8,32,512]{2,1,0:T(8,128)(2,1)} %bitcast.53), calls=%async_computation | async-start | bytes 524288 | tf_op jit(solution)/shard_map/all_to_all | solution.py:176
  7.4 10.1 %copy-start.7 = (f32[6]{0:T(128)S(1)}, f32[6]{0:T(128)}, u32[]{:S(2)}) copy-start(f32[6]{0:T(128)} %param.23) | copy-start | bytes 76
  16.9 3.7 %copy-start.4 = (f32[4,384]{1,0:T(4,128)S(1)}, f32[4,384]{1,0:T(4,128)}, u32[]{:S(2)}) copy-start(f32[4,384]{1,0:T(4,128)} %param.20) | copy-start | bytes 18436
  16.9 3.7 %copy-start.3 = (f32[4,512]{1,0:T(4,128)S(1)}, f32[4,512]{1,0:T(4,128)}, u32[]{:S(2)}) copy-start(f32[4,512]{1,0:T(4,128)} %param.21) | copy-start | bytes 24580
  17.4 14.9 %copy-start.2 = (s32[4]{0:T(128)S(1)}, s32[4]{0:T(128)}, u32[]{:S(2)}) copy-start(s32[4]{0:T(128)} %constant.94.clone) | copy-start | bytes 52
  17.4 1.9 %collective-permute-start.2 = (f32[256,256]{1,0:T(8,128)S(1)}, f32[256,256]{1,0:T(8,128)S(1)}, u32[]{:S(2)}, u32[]{:S(2)}) collective-permute-start(f32[256,256]{1,0:T(8,128)S(1)} %constant_dynamic-slice_fusion), channel_id=1, source_target_pairs={{0,1},{1,0},{2,3},{3,2},{4,5},{5,4},{6,7},{7,6},{8,9},{9,8},{10,11... | collective-permute-start | bytes 786440 | tf_op jit(solution)/shard_map/ppermute | solution.py:100
  17.7 9.2 %collective-permute-start = (bf16[256,512]{1,0:T(8,128)(2,1)S(1)}, bf16[256,512]{1,0:T(8,128)(2,1)S(1)}, u32[]{:S(2)}, u32[]{:S(2)}) collective-permute-start(bf16[256,512]{1,0:T(8,128)(2,1)S(1)} %bitcast_select_fusion), channel_id=1, source_target_pairs={{0,2},{1,3},{2,0},{3,1},{4,6},{5,7},{6,4},{7,5},{8,10},{9,11},{10,... | collective-permute-start | bytes 786440 | tf_op jit(solution)/shard_map/ppermute | solution.py:65
  19.3 12.8 %collective-permute-start.3 = (f32[256,256]{1,0:T(8,128)S(1)}, f32[256,256]{1,0:T(8,128)S(1)}, u32[]{:S(2)}, u32[]{:S(2)}) collective-permute-start(f32[256,256]{1,0:T(8,128)S(1)} %dynamic-slice_add_fusion), channel_id=1, source_target_pairs={{0,2},{1,3},{2,0},{3,1},{4,6},{5,7},{6,4},{7,5},{8,10},{9,11},{10,... | collective-permute-start | bytes 786440 | tf_op jit(solution)/shard_map/ppermute | solution.py:103
  26.9 9.4 %collective-permute-start.1 = (bf16[256,1024]{1,0:T(8,128)(2,1)S(1)}, bf16[256,1024]{1,0:T(8,128)(2,1)}, u32[]{:S(2)}, u32[]{:S(2)}) collective-permute-start(bf16[256,1024]{1,0:T(8,128)(2,1)S(1)} %pad_maximum_fusion.2), channel_id=1, source_target_pairs={{0,1},{1,0},{2,3},{3,2},{4,5},{5,4},{6,7},{7,6},{8,9},{9,8},{10,11... | collective-permute-start | bytes 1572872 | tf_op jit(solution)/shard_map/ppermute | solution.py:65
  32.1 4.1 %collective-permute-start.4 = (bf16[256,256]{1,0:T(8,128)(2,1)S(1)}, bf16[256,256]{1,0:T(8,128)(2,1)S(1)}, u32[]{:S(2)}, u32[]{:S(2)}) collective-permute-start(bf16[256,256]{1,0:T(8,128)(2,1)S(1)} %add_convert_fusion), channel_id=1, source_target_pairs={{0,1},{1,0},{2,3},{3,2},{4,5},{5,4},{6,7},{7,6},{8,9},{9,8},{10,11... | collective-permute-start | bytes 393224 | tf_op jit(solution)/shard_map/ppermute | solution.py:106
  37.4 0.8 copy-start.6
  37.5 0.8 copy-start.8
  39.1 1.4 %copy-start.5 = (bf16[2048,384]{1,0:T(8,128)(2,1)S(1)}, bf16[2048,384]{1,0:T(8,128)(2,1)}, u32[]{:S(2)}) copy-start(bf16[2048,384]{1,0:T(8,128)(2,1)} %param.17) | copy-start | bytes 4718596
  41.2 4.7 %collective-permute-start.5 = (bf16[3,896]{1,0:T(4,128)(2,1)S(1)}, bf16[3,896]{1,0:T(4,128)(2,1)S(1)}, u32[]{:S(2)}, u32[]{:S(2)}) collective-permute-start(bf16[3,896]{1,0:T(4,128)(2,1)S(1)} %pad_maximum_fusion.3), channel_id=1, source_target_pairs={{0,4},{4,8},{8,12},{12,16},{16,20},{20,24},{24,28},{1,5},{5,9},{9,... | collective-permute-start | bytes 16136 | tf_op jit(solution)/shard_map/ppermute | solution.py:12
  49.1 8.0 %collective-permute-start.7 = (bf16[400,256]{1,0:T(8,128)(2,1)S(1)}, bf16[400,256]{1,0:T(8,128)(2,1)S(1)}, u32[]{:S(2)}, u32[]{:S(2)}) collective-permute-start(bf16[400,256]{1,0:T(8,128)(2,1)S(1)} %fusion.30), channel_id=1, source_target_pairs={{0,4},{4,8},{8,12},{12,16},{16,20},{20,24},{24,28},{1,5},{5,9},{9,... | collective-permute-start | bytes 614408 | tf_op jit(solution)/shard_map/ppermute | solution.py:12
  53.3 6.2 %collective-permute-start.6 = (bf16[400,256]{1,0:T(8,128)(2,1)S(1)}, bf16[400,256]{1,0:T(8,128)(2,1)S(1)}, u32[]{:S(2)}, u32[]{:S(2)}) collective-permute-start(bf16[400,256]{1,0:T(8,128)(2,1)S(1)} %fusion.30), channel_id=1, source_target_pairs={{0,8},{4,12},{8,16},{12,20},{16,24},{20,28},{1,9},{5,13},{9,17},{1... | collective-permute-start | bytes 614408 | tf_op jit(solution)/shard_map/ppermute | solution.py:12
  56.2 8.8 %copy-start.9 = (f32[6]{0:T(128)S(1)}, f32[6]{0:T(128)}, u32[]{:S(2)}) copy-start(f32[6]{0:T(128)} %param.24) | copy-start | bytes 76
  59.9 8.4 %collective-permute-start.8 = (bf16[400,256]{1,0:T(8,128)(2,1)S(1)}, bf16[400,256]{1,0:T(8,128)(2,1)S(1)}, u32[]{:S(2)}, u32[]{:S(2)}) collective-permute-start(bf16[400,256]{1,0:T(8,128)(2,1)S(1)} %fusion.31), channel_id=1, source_target_pairs={{0,8},{4,12},{8,16},{12,20},{16,24},{20,28},{1,9},{5,13},{9,17},{1... | collective-permute-start | bytes 614408 | tf_op jit(solution)/shard_map/ppermute | solution.py:12
  68.7 7.7 %collective-permute-start.9 = (bf16[400,256]{1,0:T(8,128)(2,1)S(1)}, bf16[400,256]{1,0:T(8,128)(2,1)S(1)}, u32[]{:S(2)}, u32[]{:S(2)}) collective-permute-start(bf16[400,256]{1,0:T(8,128)(2,1)S(1)} %fusion.32), channel_id=1, source_target_pairs={{0,16},{4,20},{8,24},{12,28},{1,17},{5,21},{9,25},{13,29},{2,18},{... | collective-permute-start | bytes 614408 | tf_op jit(solution)/shard_map/ppermute | solution.py:12

commit v19 on v18

--- a/solution.py
+++ b/solution.py
@@ -48,7 +48,7 @@
         held = combine_packed(received(packed, axis, 2, heads), held, heads)
     cover = 2
     while cover < count - 1:
-        if cover * 2 >= count - 1:
+        if cover == 2:
             held, side = lax.optimization_barrier((held, side))
         held = combine_packed(received(held, axis, cover, heads), held, heads)
         cover *= 2

time: 97.1 us -> 99.9 us (1.029)
  other arithmetic: 8.05 us -> 11.2 us
  starting transfers between devices: 30 us -> 27.6 us
  blocking collectives: 17.7 us -> 19.9 us
    all_to_all x1, blocking collectives: 17.7 us -> 19.9 us  [per_device(): lax.all_to_all(outgoing, 'seq', split_axis=0, concat_axis=0, tiled=True)]
    ppermute x5, starting transfers between devices: 19.5 us -> 17.7 us  [shifted(): return lax.ppermute(array, axis, pairs)]
    slice x2, local copies, waits for them, and re-layouts: 1.93 us -> 0.19 us  [per_device(): x_heads = activated[:, :inner_dev].reshape(tok_dev, heads_dev, head_dim)]
    unnamed x22 -> x36, local copies, waits for them, and re-layouts: 2.03 us -> 1.4 us
  transfers between devices with their start and end apart: 11 -> 11, of which waited for: 8 -> 7; matrix products, arithmetic and copies ran while one was open for 10% -> 13% of each run, Pallas kernels for 0% -> 0%
where the time goes in v19:
time: 99.9 us; the launch traced here: 99.3 us
  starting transfers between devices  27.6 us (28%)
  waiting for transfers between devices  24 us (24%)
  blocking collectives  19.9 us (20%)
  other arithmetic  11.2 us (11%)
  local copies, waits for them, and re-layouts  7.73 us (8%)
  matrix products  5.21 us (5%)
  between operations  3.76 us (4%)
    all_to_all x1, blocking collectives, per_device(): lax.all_to_all(outgoing, 'seq', split_axis=0, concat_axis=0, tiled=True)  19.9 us
    ppermute x5, starting transfers between devices, shifted(): return lax.ppermute(array, axis, pairs)  17.7 us
    ppermute x5, waiting for transfers between devices, shifted(): return lax.ppermute(array, axis, pairs)  8.48 us
    all_to_all x1, starting transfers between devices, per_device(): lax.all_to_all(slot_rows, 'seq', split_axis=0, concat_axis=0, tiled=True)  7.41 us
    ppermute x2, waiting for transfers between devices, exchange(): other = lax.ppermute(held, axis, [(i, i ^ bit) for i in range(count)])  6.81 us
    ppermute x1, waiting for transfers between devices, summed_columns(): kept = kept + lax.ppermute(kept, axis, [(i, i ^ bit) for i in range(count)])  5.06 us
    all_to_all x1, waiting for transfers between devices, per_device(): lax.all_to_all(slot_rows, 'seq', split_axis=0, concat_axis=0, tiled=True)  3.63 us
  transfers between devices with their start and end apart: 11, of which 7 were waited for; matrix products, arithmetic and copies ran while one was open for 13% of the time, Pallas kernels for 0%

profile of v19, /device:TPU:0, one launch (start us, length us, event | category | flops | bytes accessed | tf_op | source)
XLA Modules:
  0.0 99.3 jit_solution(15342156415926015168)
XLA Ops:
  0.0 7.4 %all-to-all-start = ((bf16[8,32,512]{2,1,0:T(8,128)(2,1)}), bf16[8,32,512]{2,1,0:T(8,128)(2,1)S(1)}, u32[]{:S(2)}, u32[]{:S(2)}) async-start(bf16[8,32,512]{2,1,0:T(8,128)(2,1)} %bitcast.57), calls=%async_computation | async-start | bytes 524288 | tf_op jit(solution)/shard_map/all_to_all | solution.py:176
  7.4 1.2 %compare_and_fusion.1 = (pred[8]{0:T(512)(128)(4,1)}, s32[8]{0:T(128)S(1)}) fusion(s32[8,8]{1,0:T(8,128)} %param.14, s32[]{:T(128)S(6)} %select_n.119), kind=kLoop, calls=%fused_computation.110 | loop fusion | flops 48 | bytes 76 | tf_op jit(solution)/shard_map/jit(_take)/and | solution.py:230
  8.7 1.0 sort.17
  9.8 0.8 reduce-window.8
  10.7 0.6 fusion.62
  12.0 0.7 broadcast_compare_fusion.1
  12.7 3.6 %all-to-all-done = bf16[8,32,512]{2,1,0:T(8,128)(2,1)S(1)} async-done(((bf16[8,32,512]{2,1,0:T(8,128)(2,1)}), bf16[8,32,512]{2,1,0:T(8,128)(2,1)S(1)}, u32[]{:S(2)}, u32[]{:S(2)}) %all-to-all-start) | async-done | bytes 262176 | tf_op jit(solution)/shard_map/all_to_all | solution.py:176
  16.3 0.6 gather_fusion
  17.1 0.3 fusion.64
  17.6 0.7 fusion.36
  18.3 1.5 %collective-permute-start = (bf16[256,512]{1,0:T(8,128)(2,1)S(1)}, bf16[256,512]{1,0:T(8,128)(2,1)S(1)}, u32[]{:S(2)}, u32[]{:S(2)}) collective-permute-start(bf16[256,512]{1,0:T(8,128)(2,1)S(1)} %bitcast_select_fusion), channel_id=1, source_target_pairs={{0,2},{1,3},{2,0},{3,1},{4,6},{5,7},{6,4},{7,5},{8,10},{9,11},{10,... | collective-permute-start | bytes 786440 | tf_op jit(solution)/shard_map/ppermute | solution.py:65
  19.9 0.7 collective-permute-start.3
  20.6 6.8 %collective-permute-done = bf16[256,512]{1,0:T(8,128)(2,1)S(1)} collective-permute-done((bf16[256,512]{1,0:T(8,128)(2,1)S(1)}, bf16[256,512]{1,0:T(8,128)(2,1)S(1)}, u32[]{:S(2)}, u32[]{:S(2)}) %collective-permute-start) | collective-permute-done | bytes 262176 | tf_op jit(solution)/shard_map/ppermute | solution.py:65
  27.6 5.1 %collective-permute-done.3 = f32[256,256]{1,0:T(8,128)S(1)} collective-permute-done((f32[256,256]{1,0:T(8,128)S(1)}, f32[256,256]{1,0:T(8,128)S(1)}, u32[]{:S(2)}, u32[]{:S(2)}) %collective-permute-start.3) | collective-permute-done | bytes 262176 | tf_op jit(solution)/shard_map/ppermute | solution.py:103
  32.8 0.7 fusion.63
  36.0 0.6 slice.119
  36.8 1.1 %pad_maximum_fusion = bf16[256,2048]{1,0:T(8,128)(2,1)S(1)} fusion(bf16[256,1024]{1,0:T(8,128)(2,1)} %collective-permute-done.1, bf16[256,512]{1,0:T(8,128)(2,1)S(1)} %collective-permute-done, bf16[256,512]{1,0:T(8,128)(2,1)S(1)} %bitcast_select_fusion), kind=kLoop, calls=%fused_computation.17 | loop fusion | flops 3145728 | bytes 2097152 | tf_op jit(solution)/shard_map/concatenate | solution.py:66
  38.2 0.7 divide_multiply_fusion.1
  38.9 0.6 copy-done.12
  39.6 0.7 convolution_convert_fusion.1
  40.3 3.3 %collective-permute-start.5 = (bf16[3,896]{1,0:T(4,128)(2,1)S(1)}, bf16[3,896]{1,0:T(4,128)(2,1)S(1)}, u32[]{:S(2)}, u32[]{:S(2)}) collective-permute-start(bf16[3,896]{1,0:T(4,128)(2,1)S(1)} %pad_maximum_fusion.3), channel_id=1, source_target_pairs={{0,4},{4,8},{8,12},{12,16},{16,20},{20,24},{24,28},{1,5},{5,9},{9,... | collective-permute-start | bytes 16136 | tf_op jit(solution)/shard_map/ppermute | solution.py:12
  43.6 0.4 compare_select_fusion
  44.0 0.2 fusion.37
  44.2 0.3 slice_reduce_fusion
  44.5 0.7 select_exponential_fusion
  45.2 1.2 %broadcast_select_fusion.1 = f32[6]{0:T(128)} fusion(pred[]{:T(512)} %bitcast.14, f32[6]{0:T(128)S(1)} %slice_reduce_fusion), kind=kLoop, calls=%fused_computation.117 | loop fusion | flops 6 | bytes 49 | tf_op jit(solution)/shard_map/jit(_where)/select_n | solution.py:153
  46.4 0.9 copy.22
  47.4 0.7 divide_multiply_fusion
  48.1 0.4 fusion.39
  48.8 0.8 multiply_multiply_fusion
  49.6 0.2 fusion.42
  49.8 0.7 broadcast_in_dim.102
  50.7 3.0 %collective-permute-start.6 = (bf16[400,256]{1,0:T(8,128)(2,1)S(1)}, bf16[400,256]{1,0:T(8,128)(2,1)S(1)}, u32[]{:S(2)}, u32[]{:S(2)}) collective-permute-start(bf16[400,256]{1,0:T(8,128)(2,1)S(1)} %fusion.32), channel_id=1, source_target_pairs={{0,4},{4,8},{8,12},{12,16},{16,20},{20,24},{24,28},{1,5},{5,9},{9,... | collective-permute-start | bytes 614408 | tf_op jit(solution)/shard_map/ppermute | solution.py:12
  53.7 2.5 %collective-permute-start.7 = (bf16[400,256]{1,0:T(8,128)(2,1)S(1)}, bf16[400,256]{1,0:T(8,128)(2,1)S(1)}, u32[]{:S(2)}, u32[]{:S(2)}) collective-permute-start(bf16[400,256]{1,0:T(8,128)(2,1)S(1)} %fusion.32), channel_id=1, source_target_pairs={{0,8},{4,12},{8,16},{12,20},{16,24},{20,28},{1,9},{5,13},{9,17},{1... | collective-permute-start | bytes 614408 | tf_op jit(solution)/shard_map/ppermute | solution.py:12
  56.2 1.9 %fusion.8 = f32[256,6,64]{0,2,1:T(8,128)S(1)} fusion(f32[6,256]{1,0:T(8,128)S(1)} %bitcast.58, f32[256,256]{1,0:T(8,128)S(1)} %fusion.39, pred[256,256]{1,0:T(8,128)(4,1)S(1)} %copy-done.3, f32[256,6,64]{0,2,1:T(8,128)S(1)} %bitcast.50, f32[6]{0:T(128)S(1)} %copy-done.16, f32[256,6]{0,1:T(8,128)S(1)} %copy-done.7), kind=kOutput, calls=%fused_computation.8 | convolution fusion | flops 303464448 | bytes 1126424 | tf_op jit(solution)/shard_map/hts,shp->thp/dot_general | solution.py:144
  58.1 0.3 collective-permute-done.6
  58.4 2.2 %collective-permute-done.7 = bf16[400,256]{1,0:T(8,128)(2,1)S(1)} collective-permute-done((bf16[400,256]{1,0:T(8,128)(2,1)S(1)}, bf16[400,256]{1,0:T(8,128)(2,1)S(1)}, u32[]{:S(2)}, u32[]{:S(2)}) %collective-permute-start.7) | collective-permute-done | bytes 204832 | tf_op jit(solution)/shard_map/ppermute | solution.py:12
  60.9 4.4 %collective-permute-start.8 = (bf16[400,256]{1,0:T(8,128)(2,1)S(1)}, bf16[400,256]{1,0:T(8,128)(2,1)S(1)}, u32[]{:S(2)}, u32[]{:S(2)}) collective-permute-start(bf16[400,256]{1,0:T(8,128)(2,1)S(1)} %fusion.33), channel_id=1, source_target_pairs={{0,8},{4,12},{8,16},{12,20},{16,24},{20,28},{1,9},{5,13},{9,17},{1... | collective-permute-start | bytes 614408 | tf_op jit(solution)/shard_map/ppermute | solution.py:12
  65.3 3.5 %collective-permute-done.8 = bf16[400,256]{1,0:T(8,128)(2,1)S(1)} collective-permute-done((bf16[400,256]{1,0:T(8,128)(2,1)S(1)}, bf16[400,256]{1,0:T(8,128)(2,1)S(1)}, u32[]{:S(2)}, u32[]{:S(2)}) %collective-permute-start.8) | collective-permute-done | bytes 204832 | tf_op jit(solution)/shard_map/ppermute | solution.py:12
  69.2 4.5 %collective-permute-start.9 = (bf16[400,256]{1,0:T(8,128)(2,1)S(1)}, bf16[400,256]{1,0:T(8,128)(2,1)S(1)}, u32[]{:S(2)}, u32[]{:S(2)}) collective-permute-start(bf16[400,256]{1,0:T(8,128)(2,1)S(1)} %fusion.34), channel_id=1, source_target_pairs={{0,16},{4,20},{8,24},{12,28},{1,17},{5,21},{9,25},{13,29},{2,18},{... | collective-permute-start | bytes 614408 | tf_op jit(solution)/shard_map/ppermute | solution.py:12
  73.7 0.7 fusion.55
  74.4 2.5 %collective-permute-done.9 = bf16[400,256]{1,0:T(8,128)(2,1)S(1)} collective-permute-done((bf16[400,256]{1,0:T(8,128)(2,1)S(1)}, bf16[400,256]{1,0:T(8,128)(2,1)S(1)}, u32[]{:S(2)}, u32[]{:S(2)}) %collective-permute-start.9) | collective-permute-done | bytes 204832 | tf_op jit(solution)/shard_map/ppermute | solution.py:12
  77.0 0.4 fusion.13
  77.4 0.3 copy.23
  77.7 0.3 convert_element_type.109
  78.0 0.6 gather_fusion.1
  78.7 19.9 %all_to_all.10 = bf16[8,32,384]{2,1,0:T(8,128)(2,1)S(1)} all-to-all(bf16[8,32,384]{2,1,0:T(8,128)(2,1)S(1)} %broadcast_select_fusion), channel_id=1, replica_groups=mesh['seq'=8,'fsdp'=4] {'seq'}, dimensions={0} | all-to-all | bytes 393216 | tf_op jit(solution)/shard_map/all_to_all | solution.py:231
  98.6 0.7 copy.26
  (82 shorter events, 2.5 us)
Async XLA Ops:
  0.0 38.1 %copy-start = (bf16[2048,384]{1,0:T(8,128)(2,1)S(1)}, bf16[2048,384]{1,0:T(8,128)(2,1)}, u32[]{:S(2)}) copy-start(bf16[2048,384]{1,0:T(8,128)(2,1)} %param.17) | copy-start | bytes 4718596
  0.0 17.0 %copy-start.2 = (bf16[512,512]{1,0:T(8,128)(2,1)S(1)}, bf16[512,512]{1,0:T(8,128)(2,1)}, u32[]{:S(2)}) copy-start(bf16[512,512]{1,0:T(8,128)(2,1)} %param.18) | copy-start | bytes 1572868
  0.0 16.3 %all-to-all-start = ((bf16[8,32,512]{2,1,0:T(8,128)(2,1)}), bf16[8,32,512]{2,1,0:T(8,128)(2,1)S(1)}, u32[]{:S(2)}, u32[]{:S(2)}) async-start(bf16[8,32,512]{2,1,0:T(8,128)(2,1)} %bitcast.57), calls=%async_computation | async-start | bytes 524288 | tf_op jit(solution)/shard_map/all_to_all | solution.py:176
  7.4 10.1 %copy-start.14 = (f32[6]{0:T(128)S(1)}, f32[6]{0:T(128)}, u32[]{:S(2)}) copy-start(f32[6]{0:T(128)} %param.23) | copy-start | bytes 76
  16.9 3.7 %copy-start.10 = (f32[4,384]{1,0:T(4,128)S(1)}, f32[4,384]{1,0:T(4,128)}, u32[]{:S(2)}) copy-start(f32[4,384]{1,0:T(4,128)} %param.20) | copy-start | bytes 18436
  16.9 3.7 %copy-start.9 = (f32[4,512]{1,0:T(4,128)S(1)}, f32[4,512]{1,0:T(4,128)}, u32[]{:S(2)}) copy-start(f32[4,512]{1,0:T(4,128)} %param.21) | copy-start | bytes 24580
  17.4 15.4 %copy-start.8 = (s32[4]{0:T(128)S(1)}, s32[4]{0:T(128)}, u32[]{:S(2)}) copy-start(s32[4]{0:T(128)} %constant.94.clone) | copy-start | bytes 52
  17.4 2.4 %collective-permute-start.2 = (f32[256,256]{1,0:T(8,128)S(1)}, f32[256,256]{1,0:T(8,128)S(1)}, u32[]{:S(2)}, u32[]{:S(2)}) collective-permute-start(f32[256,256]{1,0:T(8,128)S(1)} %constant_dynamic-slice_fusion), channel_id=1, source_target_pairs={{0,1},{1,0},{2,3},{3,2},{4,5},{5,4},{6,7},{7,6},{8,9},{9,8},{10,11... | collective-permute-start | bytes 786440 | tf_op jit(solution)/shard_map/ppermute | solution.py:100
  18.3 9.1 %collective-permute-start = (bf16[256,512]{1,0:T(8,128)(2,1)S(1)}, bf16[256,512]{1,0:T(8,128)(2,1)S(1)}, u32[]{:S(2)}, u32[]{:S(2)}) collective-permute-start(bf16[256,512]{1,0:T(8,128)(2,1)S(1)} %bitcast_select_fusion), channel_id=1, source_target_pairs={{0,2},{1,3},{2,0},{3,1},{4,6},{5,7},{6,4},{7,5},{8,10},{9,11},{10,... | collective-permute-start | bytes 786440 | tf_op jit(solution)/shard_map/ppermute | solution.py:65
  19.9 12.8 %collective-permute-start.3 = (f32[256,256]{1,0:T(8,128)S(1)}, f32[256,256]{1,0:T(8,128)S(1)}, u32[]{:S(2)}, u32[]{:S(2)}) collective-permute-start(f32[256,256]{1,0:T(8,128)S(1)} %dynamic-slice_add_fusion), channel_id=1, source_target_pairs={{0,2},{1,3},{2,0},{3,1},{4,6},{5,7},{6,4},{7,5},{8,10},{9,11},{10,... | collective-permute-start | bytes 786440 | tf_op jit(solution)/shard_map/ppermute | solution.py:103
  27.5 9.4 %collective-permute-start.1 = (bf16[256,1024]{1,0:T(8,128)(2,1)S(1)}, bf16[256,1024]{1,0:T(8,128)(2,1)}, u32[]{:S(2)}, u32[]{:S(2)}) collective-permute-start(bf16[256,1024]{1,0:T(8,128)(2,1)S(1)} %pad_maximum_fusion.2), channel_id=1, source_target_pairs={{0,1},{1,0},{2,3},{3,2},{4,5},{5,4},{6,7},{7,6},{8,9},{9,8},{10,11... | collective-permute-start | bytes 1572872 | tf_op jit(solution)/shard_map/ppermute | solution.py:65
  32.7 4.0 %collective-permute-start.4 = (bf16[256,256]{1,0:T(8,128)(2,1)S(1)}, bf16[256,256]{1,0:T(8,128)(2,1)S(1)}, u32[]{:S(2)}, u32[]{:S(2)}) collective-permute-start(bf16[256,256]{1,0:T(8,128)(2,1)S(1)} %add_convert_fusion), channel_id=1, source_target_pairs={{0,1},{1,0},{2,3},{3,2},{4,5},{5,4},{6,7},{7,6},{8,9},{9,8},{10,11... | collective-permute-start | bytes 393224 | tf_op jit(solution)/shard_map/ppermute | solution.py:106
  38.1 1.4 %copy-start.12 = (bf16[2048,384]{1,0:T(8,128)(2,1)S(1)}, bf16[2048,384]{1,0:T(8,128)(2,1)}, u32[]{:S(2)}) copy-start(bf16[2048,384]{1,0:T(8,128)(2,1)} %param.16) | copy-start | bytes 4718596
  39.6 4.1 %copy-start.13 = (bf16[2048,6]{0,1:T(8,128)(2,1)S(1)}, bf16[2048,6]{0,1:T(8,128)(2,1)}, u32[]{:S(2)}) copy-start(bf16[2048,6]{0,1:T(8,128)(2,1)} %param.19) | copy-start | bytes 73732
  39.6 4.1 %copy-start.15 = (f32[6]{0:T(128)S(1)}, f32[6]{0:T(128)}, u32[]{:S(2)}) copy-start(f32[6]{0:T(128)} %param.22) | copy-start | bytes 76
  40.3 7.0 %collective-permute-start.5 = (bf16[3,896]{1,0:T(4,128)(2,1)S(1)}, bf16[3,896]{1,0:T(4,128)(2,1)S(1)}, u32[]{:S(2)}, u32[]{:S(2)}) collective-permute-start(bf16[3,896]{1,0:T(4,128)(2,1)S(1)} %pad_maximum_fusion.3), channel_id=1, source_target_pairs={{0,4},{4,8},{8,12},{12,16},{16,20},{20,24},{24,28},{1,5},{5,9},{9,... | collective-permute-start | bytes 16136 | tf_op jit(solution)/shard_map/ppermute | solution.py:12
  44.0 4.1 %copy-start.6 = (f32[256,6]{0,1:T(8,128)}, f32[256,6]{0,1:T(8,128)S(1)}, u32[]{:S(2)}) copy-start(f32[256,6]{0,1:T(8,128)S(1)} %compare_select_fusion) | copy-start | bytes 18436
  44.2 3.9 %copy-start.4 = (f32[256,6]{0,1:T(8,128)}, f32[256,6]{0,1:T(8,128)S(1)}, u32[]{:S(2)}) copy-start(f32[256,6]{0,1:T(8,128)S(1)} %fusion.37) | copy-start | bytes 18436
  48.7 7.5 %copy-start.3 = (pred[256,256]{1,0:T(8,128)(4,1)S(1)}, pred[256,256]{1,0:T(8,128)(4,1)}, u32[]{:S(2)}) copy-start(pred[256,256]{1,0:T(8,128)(4,1)} %fusion.36) | copy-start | bytes 196612
  48.7 7.5 %copy-start.5 = (f32[256,6]{0,1:T(8,128)S(1)}, f32[256,6]{0,1:T(8,128)}, u32[]{:S(2)}) copy-start(f32[256,6]{0,1:T(8,128)} %copy-done.4) | copy-start | bytes 18436
  48.7 7.5 %copy-start.7 = (f32[256,6]{0,1:T(8,128)S(1)}, f32[256,6]{0,1:T(8,128)}, u32[]{:S(2)}) copy-start(f32[256,6]{0,1:T(8,128)} %copy-done.6) | copy-start | bytes 18436
  48.8 7.5 %copy-start.16 = (f32[6]{0:T(128)S(1)}, f32[6]{0:T(128)}, u32[]{:S(2)}) copy-start(f32[6]{0:T(128)} %param.24) | copy-start | bytes 76
  50.7 7.7 %collective-permute-start.6 = (bf16[400,256]{1,0:T(8,128)(2,1)S(1)}, bf16[400,256]{1,0:T(8,128)(2,1)S(1)}, u32[]{:S(2)}, u32[]{:S(2)}) collective-permute-start(bf16[400,256]{1,0:T(8,128)(2,1)S(1)} %fusion.32), channel_id=1, source_target_pairs={{0,4},{4,8},{8,12},{12,16},{16,20},{20,24},{24,28},{1,5},{5,9},{9,... | collective-permute-start | bytes 614408 | tf_op jit(solution)/shard_map/ppermute | solution.py:12
  53.7 6.8 %collective-permute-start.7 = (bf16[400,256]{1,0:T(8,128)(2,1)S(1)}, bf16[400,256]{1,0:T(8,128)(2,1)S(1)}, u32[]{:S(2)}, u32[]{:S(2)}) collective-permute-start(bf16[400,256]{1,0:T(8,128)(2,1)S(1)} %fusion.32), channel_id=1, source_target_pairs={{0,8},{4,12},{8,16},{12,20},{16,24},{20,28},{1,9},{5,13},{9,17},{1... | collective-permute-start | bytes 614408 | tf_op jit(solution)/shard_map/ppermute | solution.py:12
  60.9 7.9 %collective-permute-start.8 = (bf16[400,256]{1,0:T(8,128)(2,1)S(1)}, bf16[400,256]{1,0:T(8,128)(2,1)S(1)}, u32[]{:S(2)}, u32[]{:S(2)}) collective-permute-start(bf16[400,256]{1,0:T(8,128)(2,1)S(1)} %fusion.33), channel_id=1, source_target_pairs={{0,8},{4,12},{8,16},{12,20},{16,24},{20,28},{1,9},{5,13},{9,17},{1... | collective-permute-start | bytes 614408 | tf_op jit(solution)/shard_map/ppermute | solution.py:12
  68.9 8.1 %copy-start.1 = (f32[256,384]{0,1:T(8,128)S(1)}, f32[256,384]{0,1:T(8,128)}, u32[]{:S(2)}) copy-start(f32[256,384]{0,1:T(8,128)} %copy.22) | copy-start | bytes 1179652
  69.2 7.8 %collective-permute-start.9 = (bf16[400,256]{1,0:T(8,128)(2,1)S(1)}, bf16[400,256]{1,0:T(8,128)(2,1)S(1)}, u32[]{:S(2)}, u32[]{:S(2)}) collective-permute-start(bf16[400,256]{1,0:T(8,128)(2,1)S(1)} %fusion.34), channel_id=1, source_target_pairs={{0,16},{4,20},{8,24},{12,28},{1,17},{5,21},{9,25},{13,29},{2,18},{... | collective-permute-start | bytes 614408 | tf_op jit(solution)/shard_map/ppermute | solution.py:12
  77.0 1.7 %copy-start.11 = (pred[8]{0:T(512)(128)(4,1)S(1)}, pred[8]{0:T(512)(128)(4,1)}, u32[]{:S(2)}) copy-start(pred[8]{0:T(512)(128)(4,1)} %get-tuple-element.19) | copy-start | bytes 28

commit v20 on v14

--- a/solution.py
+++ b/solution.py
@@ -227,7 +227,10 @@
     y_block = local_y + carry_in[:, :, None] * incoming
     gated = (y_block * gate).reshape(tok_dev, inner_dev).astype(jnp.bfloat16)
     ordered = gated.reshape(seq_count, piece_rows, inner_dev)
-    outgoing = jnp.take(ordered, dealt_row, axis=0)
+    chooser = (dealt_row[:, None] == jnp.arange(seq_count, dtype=dealt_row.dtype)[None, :]).astype(jnp.bfloat16)
+    outgoing = jnp.einsum("mp,pri->mri", chooser, ordered, preferred_element_type=jnp.float32).astype(
+        jnp.bfloat16
+    )
     returned = lax.all_to_all(outgoing, "seq", split_axis=0, concat_axis=0, tiled=True)
     return returned.reshape(tok_dev, inner_dev)
 

time: 97.5 us -> 97.3 us (level)
  other arithmetic: 8.04 us -> 6.57 us
  transfers between devices with their start and end apart: 11 -> 11, of which waited for: 8 -> 8; matrix products, arithmetic and copies ran while one was open for 10% -> 9% of each run, Pallas kernels for 0% -> 0%
where the time goes in v20:
time: 97.3 us; the launch traced here: 96.7 us
  starting transfers between devices  30 us (31%)
  waiting for transfers between devices  23.9 us (25%)
  blocking collectives  17.7 us (18%)
  local copies, waits for them, and re-layouts  9.01 us (9%)
  other arithmetic  6.57 us (7%)
  matrix products  5.87 us (6%)
  between operations  3.61 us (4%)
    ppermute x5, starting transfers between devices, shifted(): return lax.ppermute(array, axis, pairs)  19.5 us
    all_to_all x1, blocking collectives, per_device(): lax.all_to_all(outgoing, 'seq', split_axis=0, concat_axis=0, tiled=True)  17.7 us
    ppermute x5, waiting for transfers between devices, shifted(): return lax.ppermute(array, axis, pairs)  8.35 us
    all_to_all x1, starting transfers between devices, per_device(): lax.all_to_all(slot_rows, 'seq', split_axis=0, concat_axis=0, tiled=True)  7.41 us
    ppermute x2, waiting for transfers between devices, exchange(): other = lax.ppermute(held, axis, [(i, i ^ bit) for i in range(count)])  6.25 us
    ppermute x1, waiting for transfers between devices, summed_columns(): kept = kept + lax.ppermute(kept, axis, [(i, i ^ bit) for i in range(count)])  5.06 us
    all_to_all x1, waiting for transfers between devices, per_device(): lax.all_to_all(slot_rows, 'seq', split_axis=0, concat_axis=0, tiled=True)  4.24 us
    unnamed x22, local copies, waits for them, and re-layouts  2.03 us
  transfers between devices with their start and end apart: 11, of which 8 were waited for; matrix products, arithmetic and copies ran while one was open for 9% of the time, Pallas kernels for 0%

profile of v20, /device:TPU:0, one launch (start us, length us, event | category | flops | bytes accessed | tf_op | source)
XLA Modules:
  0.0 96.7 jit_solution(8398875214708053156)
XLA Ops:
  0.0 7.4 %all-to-all-start = ((bf16[8,32,512]{2,1,0:T(8,128)(2,1)}), bf16[8,32,512]{2,1,0:T(8,128)(2,1)S(1)}, u32[]{:S(2)}, u32[]{:S(2)}) async-start(bf16[8,32,512]{2,1,0:T(8,128)(2,1)} %bitcast.54), calls=%async_computation | async-start | bytes 524288 | tf_op jit(solution)/shard_map/all_to_all | solution.py:176
  7.4 0.8 reduce-window.8
  8.3 0.7 fusion.55
  9.0 1.0 sort.17
  10.2 0.6 fusion.58
  11.4 0.7 broadcast_compare_fusion.1
  12.1 4.2 %all-to-all-done = bf16[8,32,512]{2,1,0:T(8,128)(2,1)S(1)} async-done(((bf16[8,32,512]{2,1,0:T(8,128)(2,1)}), bf16[8,32,512]{2,1,0:T(8,128)(2,1)S(1)}, u32[]{:S(2)}, u32[]{:S(2)}) %all-to-all-start) | async-done | bytes 262176 | tf_op jit(solution)/shard_map/all_to_all | solution.py:176
  16.3 0.6 gather_fusion
  17.1 0.3 fusion.60
  17.7 1.6 %collective-permute-start = (bf16[256,512]{1,0:T(8,128)(2,1)S(1)}, bf16[256,512]{1,0:T(8,128)(2,1)S(1)}, u32[]{:S(2)}, u32[]{:S(2)}) collective-permute-start(bf16[256,512]{1,0:T(8,128)(2,1)S(1)} %bitcast_select_fusion), channel_id=1, source_target_pairs={{0,2},{1,3},{2,0},{3,1},{4,6},{5,7},{6,4},{7,5},{8,10},{9,11},{10,... | collective-permute-start | bytes 786440 | tf_op jit(solution)/shard_map/ppermute | solution.py:65
  19.3 1.3 %collective-permute-start.3 = (f32[256,256]{1,0:T(8,128)S(1)}, f32[256,256]{1,0:T(8,128)S(1)}, u32[]{:S(2)}, u32[]{:S(2)}) collective-permute-start(f32[256,256]{1,0:T(8,128)S(1)} %dynamic-slice_add_fusion), channel_id=1, source_target_pairs={{0,2},{1,3},{2,0},{3,1},{4,6},{5,7},{6,4},{7,5},{8,10},{9,11},{10,... | collective-permute-start | bytes 786440 | tf_op jit(solution)/shard_map/ppermute | solution.py:103
  20.6 6.2 %collective-permute-done = bf16[256,512]{1,0:T(8,128)(2,1)S(1)} collective-permute-done((bf16[256,512]{1,0:T(8,128)(2,1)S(1)}, bf16[256,512]{1,0:T(8,128)(2,1)S(1)}, u32[]{:S(2)}, u32[]{:S(2)}) %collective-permute-start) | collective-permute-done | bytes 262176 | tf_op jit(solution)/shard_map/ppermute | solution.py:65
  27.0 5.1 %collective-permute-done.3 = f32[256,256]{1,0:T(8,128)S(1)} collective-permute-done((f32[256,256]{1,0:T(8,128)S(1)}, f32[256,256]{1,0:T(8,128)S(1)}, u32[]{:S(2)}, u32[]{:S(2)}) %collective-permute-start.3) | collective-permute-done | bytes 262176 | tf_op jit(solution)/shard_map/ppermute | solution.py:103
  32.2 0.7 fusion.59
  35.4 0.7 slice.119
  36.3 1.1 %pad_maximum_fusion = bf16[256,2048]{1,0:T(8,128)(2,1)S(1)} fusion(bf16[256,1024]{1,0:T(8,128)(2,1)} %collective-permute-done.1, bf16[256,512]{1,0:T(8,128)(2,1)S(1)} %collective-permute-done, bf16[256,512]{1,0:T(8,128)(2,1)S(1)} %bitcast_select_fusion), kind=kLoop, calls=%fused_computation.17 | loop fusion | flops 3145728 | bytes 2097152 | tf_op jit(solution)/shard_map/concatenate | solution.py:66
  37.6 0.6 copy-done.6
  38.2 0.4 compare_select_fusion
  38.6 0.2 fusion.35
  38.8 0.2 slice_reduce_fusion
  39.1 0.7 convolution_convert_fusion.2
  39.8 0.7 copy-done.5
  40.5 0.7 divide_multiply_fusion.1
  41.3 3.3 %collective-permute-start.5 = (bf16[3,896]{1,0:T(4,128)(2,1)S(1)}, bf16[3,896]{1,0:T(4,128)(2,1)S(1)}, u32[]{:S(2)}, u32[]{:S(2)}) collective-permute-start(bf16[3,896]{1,0:T(4,128)(2,1)S(1)} %pad_maximum_fusion.3), channel_id=1, source_target_pairs={{0,4},{4,8},{8,12},{12,16},{16,20},{20,24},{24,28},{1,5},{5,9},{9,... | collective-permute-start | bytes 16136 | tf_op jit(solution)/shard_map/ppermute | solution.py:12
  44.6 0.6 broadcast_select_fusion
  45.5 0.4 collective-permute-done.5
  46.0 0.7 divide_multiply_fusion
  46.7 0.8 slice.143
  47.5 1.2 %copy.28 = f32[256,384]{0,1:T(8,128)S(1)} copy(f32[256,384]{1,0:T(8,128)} %slice.143) | data formatting | bytes 786432 | tf_op jit(solution)/shard_map/slice | solution.py:211
  48.7 0.5 fusion.40
  49.2 0.2 fusion.30
  49.4 4.2 %collective-permute-start.7 = (bf16[400,256]{1,0:T(8,128)(2,1)S(1)}, bf16[400,256]{1,0:T(8,128)(2,1)S(1)}, u32[]{:S(2)}, u32[]{:S(2)}) collective-permute-start(bf16[400,256]{1,0:T(8,128)(2,1)S(1)} %fusion.30), channel_id=1, source_target_pairs={{0,4},{4,8},{8,12},{12,16},{16,20},{20,24},{24,28},{1,5},{5,9},{9,... | collective-permute-start | bytes 614408 | tf_op jit(solution)/shard_map/ppermute | solution.py:12
  53.6 2.5 %collective-permute-start.6 = (bf16[400,256]{1,0:T(8,128)(2,1)S(1)}, bf16[400,256]{1,0:T(8,128)(2,1)S(1)}, u32[]{:S(2)}, u32[]{:S(2)}) collective-permute-start(bf16[400,256]{1,0:T(8,128)(2,1)S(1)} %fusion.30), channel_id=1, source_target_pairs={{0,8},{4,12},{8,16},{12,20},{16,24},{20,28},{1,9},{5,13},{9,17},{1... | collective-permute-start | bytes 614408 | tf_op jit(solution)/shard_map/ppermute | solution.py:12
  56.1 0.4 fusion.37
  56.5 0.9 collective-permute-done.7
  57.4 2.4 %collective-permute-done.6 = bf16[400,256]{1,0:T(8,128)(2,1)S(1)} collective-permute-done((bf16[400,256]{1,0:T(8,128)(2,1)S(1)}, bf16[400,256]{1,0:T(8,128)(2,1)S(1)}, u32[]{:S(2)}, u32[]{:S(2)}) %collective-permute-start.6) | collective-permute-done | bytes 204832 | tf_op jit(solution)/shard_map/ppermute | solution.py:12
  60.0 0.2 fusion.31
  60.1 5.2 %collective-permute-start.8 = (bf16[400,256]{1,0:T(8,128)(2,1)S(1)}, bf16[400,256]{1,0:T(8,128)(2,1)S(1)}, u32[]{:S(2)}, u32[]{:S(2)}) collective-permute-start(bf16[400,256]{1,0:T(8,128)(2,1)S(1)} %fusion.31), channel_id=1, source_target_pairs={{0,8},{4,12},{8,16},{12,20},{16,24},{20,28},{1,9},{5,13},{9,17},{1... | collective-permute-start | bytes 614408 | tf_op jit(solution)/shard_map/ppermute | solution.py:12
  65.3 1.9 %fusion.8 = f32[256,6,64]{0,2,1:T(8,128)S(1)} fusion(f32[6,256]{1,0:T(8,128)S(1)} %bitcast.55, f32[256,256]{1,0:T(8,128)S(1)} %fusion.37, pred[256,256]{1,0:T(8,128)(4,1)S(1)} %fusion.34, f32[256,6,64]{0,2,1:T(8,128)S(1)} %bitcast.49, f32[6]{0:T(128)S(1)} %copy-done.9, f32[256,6]{0,1:T(8,128)S(1)} %compare_select_fusion), kind=kOutput, calls=%fused_computation.7 | convolution fusion | flops 303464448 | bytes 1126424 | tf_op jit(solution)/shard_map/hts,shp->thp/dot_general | solution.py:144
  67.2 1.4 %collective-permute-done.8 = bf16[400,256]{1,0:T(8,128)(2,1)S(1)} collective-permute-done((bf16[400,256]{1,0:T(8,128)(2,1)S(1)}, bf16[400,256]{1,0:T(8,128)(2,1)S(1)}, u32[]{:S(2)}, u32[]{:S(2)}) %collective-permute-start.8) | collective-permute-done | bytes 204832 | tf_op jit(solution)/shard_map/ppermute | solution.py:12
  68.9 4.4 %collective-permute-start.9 = (bf16[400,256]{1,0:T(8,128)(2,1)S(1)}, bf16[400,256]{1,0:T(8,128)(2,1)S(1)}, u32[]{:S(2)}, u32[]{:S(2)}) collective-permute-start(bf16[400,256]{1,0:T(8,128)(2,1)S(1)} %fusion.32), channel_id=1, source_target_pairs={{0,16},{4,20},{8,24},{12,28},{1,17},{5,21},{9,25},{13,29},{2,18},{... | collective-permute-start | bytes 614408 | tf_op jit(solution)/shard_map/ppermute | solution.py:12
  73.4 3.2 %collective-permute-done.9 = bf16[400,256]{1,0:T(8,128)(2,1)S(1)} collective-permute-done((bf16[400,256]{1,0:T(8,128)(2,1)S(1)}, bf16[400,256]{1,0:T(8,128)(2,1)S(1)}, u32[]{:S(2)}, u32[]{:S(2)}) %collective-permute-start.9) | collective-permute-done | bytes 204832 | tf_op jit(solution)/shard_map/ppermute | solution.py:12
  76.6 0.5 fusion.13
  77.2 0.3 reshape.166
  77.5 0.5 copy.31
  78.0 0.3 convolution_convert_fusion
  78.3 17.7 %all_to_all.10 = bf16[8,32,384]{2,1,0:T(8,128)(2,1)S(1)} all-to-all(bf16[8,32,384]{2,1,0:T(8,128)(2,1)S(1)} %copy.32), channel_id=1, replica_groups=mesh['seq'=8,'fsdp'=4] {'seq'}, dimensions={0} | all-to-all | bytes 393216 | tf_op jit(solution)/shard_map/all_to_all | solution.py:234
  96.0 0.7 copy.37
  (67 shorter events, 2.3 us)
Async XLA Ops:
  0.0 39.1 %copy-start = (bf16[2048,384]{1,0:T(8,128)(2,1)S(1)}, bf16[2048,384]{1,0:T(8,128)(2,1)}, u32[]{:S(2)}) copy-start(bf16[2048,384]{1,0:T(8,128)(2,1)} %param.16) | copy-start | bytes 4718596
  0.0 17.0 %copy-start.1 = (bf16[512,512]{1,0:T(8,128)(2,1)S(1)}, bf16[512,512]{1,0:T(8,128)(2,1)}, u32[]{:S(2)}) copy-start(bf16[512,512]{1,0:T(8,128)(2,1)} %param.18) | copy-start | bytes 1572868
  0.0 16.3 %all-to-all-start = ((bf16[8,32,512]{2,1,0:T(8,128)(2,1)}), bf16[8,32,512]{2,1,0:T(8,128)(2,1)S(1)}, u32[]{:S(2)}, u32[]{:S(2)}) async-start(bf16[8,32,512]{2,1,0:T(8,128)(2,1)} %bitcast.54), calls=%async_computation | async-start | bytes 524288 | tf_op jit(solution)/shard_map/all_to_all | solution.py:176
  7.4 10.1 %copy-start.7 = (f32[6]{0:T(128)S(1)}, f32[6]{0:T(128)}, u32[]{:S(2)}) copy-start(f32[6]{0:T(128)} %param.23) | copy-start | bytes 76
  16.9 3.7 %copy-start.4 = (f32[4,384]{1,0:T(4,128)S(1)}, f32[4,384]{1,0:T(4,128)}, u32[]{:S(2)}) copy-start(f32[4,384]{1,0:T(4,128)} %param.20) | copy-start | bytes 18436
  16.9 3.7 %copy-start.3 = (f32[4,512]{1,0:T(4,128)S(1)}, f32[4,512]{1,0:T(4,128)}, u32[]{:S(2)}) copy-start(f32[4,512]{1,0:T(4,128)} %param.21) | copy-start | bytes 24580
  17.4 14.9 %copy-start.2 = (s32[4]{0:T(128)S(1)}, s32[4]{0:T(128)}, u32[]{:S(2)}) copy-start(s32[4]{0:T(128)} %constant.82.clone) | copy-start | bytes 52
  17.4 1.9 %collective-permute-start.2 = (f32[256,256]{1,0:T(8,128)S(1)}, f32[256,256]{1,0:T(8,128)S(1)}, u32[]{:S(2)}, u32[]{:S(2)}) collective-permute-start(f32[256,256]{1,0:T(8,128)S(1)} %constant_dynamic-slice_fusion), channel_id=1, source_target_pairs={{0,1},{1,0},{2,3},{3,2},{4,5},{5,4},{6,7},{7,6},{8,9},{9,8},{10,11... | collective-permute-start | bytes 786440 | tf_op jit(solution)/shard_map/ppermute | solution.py:100
  17.7 9.2 %collective-permute-start = (bf16[256,512]{1,0:T(8,128)(2,1)S(1)}, bf16[256,512]{1,0:T(8,128)(2,1)S(1)}, u32[]{:S(2)}, u32[]{:S(2)}) collective-permute-start(bf16[256,512]{1,0:T(8,128)(2,1)S(1)} %bitcast_select_fusion), channel_id=1, source_target_pairs={{0,2},{1,3},{2,0},{3,1},{4,6},{5,7},{6,4},{7,5},{8,10},{9,11},{10,... | collective-permute-start | bytes 786440 | tf_op jit(solution)/shard_map/ppermute | solution.py:65
  19.3 12.8 %collective-permute-start.3 = (f32[256,256]{1,0:T(8,128)S(1)}, f32[256,256]{1,0:T(8,128)S(1)}, u32[]{:S(2)}, u32[]{:S(2)}) collective-permute-start(f32[256,256]{1,0:T(8,128)S(1)} %dynamic-slice_add_fusion), channel_id=1, source_target_pairs={{0,2},{1,3},{2,0},{3,1},{4,6},{5,7},{6,4},{7,5},{8,10},{9,11},{10,... | collective-permute-start | bytes 786440 | tf_op jit(solution)/shard_map/ppermute | solution.py:103
  26.9 9.4 %collective-permute-start.1 = (bf16[256,1024]{1,0:T(8,128)(2,1)S(1)}, bf16[256,1024]{1,0:T(8,128)(2,1)}, u32[]{:S(2)}, u32[]{:S(2)}) collective-permute-start(bf16[256,1024]{1,0:T(8,128)(2,1)S(1)} %pad_maximum_fusion.2), channel_id=1, source_target_pairs={{0,1},{1,0},{2,3},{3,2},{4,5},{5,4},{6,7},{7,6},{8,9},{9,8},{10,11... | collective-permute-start | bytes 1572872 | tf_op jit(solution)/shard_map/ppermute | solution.py:65
  32.1 4.1 %collective-permute-start.4 = (bf16[256,256]{1,0:T(8,128)(2,1)S(1)}, bf16[256,256]{1,0:T(8,128)(2,1)S(1)}, u32[]{:S(2)}, u32[]{:S(2)}) collective-permute-start(bf16[256,256]{1,0:T(8,128)(2,1)S(1)} %add_convert_fusion), channel_id=1, source_target_pairs={{0,1},{1,0},{2,3},{3,2},{4,5},{5,4},{6,7},{7,6},{8,9},{9,8},{10,11... | collective-permute-start | bytes 393224 | tf_op jit(solution)/shard_map/ppermute | solution.py:106
  37.5 0.8 copy-start.6
  37.5 0.8 copy-start.8
  39.1 1.4 %copy-start.5 = (bf16[2048,384]{1,0:T(8,128)(2,1)S(1)}, bf16[2048,384]{1,0:T(8,128)(2,1)}, u32[]{:S(2)}) copy-start(bf16[2048,384]{1,0:T(8,128)(2,1)} %param.17) | copy-start | bytes 4718596
  41.3 4.7 %collective-permute-start.5 = (bf16[3,896]{1,0:T(4,128)(2,1)S(1)}, bf16[3,896]{1,0:T(4,128)(2,1)S(1)}, u32[]{:S(2)}, u32[]{:S(2)}) collective-permute-start(bf16[3,896]{1,0:T(4,128)(2,1)S(1)} %pad_maximum_fusion.3), channel_id=1, source_target_pairs={{0,4},{4,8},{8,12},{12,16},{16,20},{20,24},{24,28},{1,5},{5,9},{9,... | collective-permute-start | bytes 16136 | tf_op jit(solution)/shard_map/ppermute | solution.py:12
  49.4 8.0 %collective-permute-start.7 = (bf16[400,256]{1,0:T(8,128)(2,1)S(1)}, bf16[400,256]{1,0:T(8,128)(2,1)S(1)}, u32[]{:S(2)}, u32[]{:S(2)}) collective-permute-start(bf16[400,256]{1,0:T(8,128)(2,1)S(1)} %fusion.30), channel_id=1, source_target_pairs={{0,4},{4,8},{8,12},{12,16},{16,20},{20,24},{24,28},{1,5},{5,9},{9,... | collective-permute-start | bytes 614408 | tf_op jit(solution)/shard_map/ppermute | solution.py:12
  53.6 6.2 %collective-permute-start.6 = (bf16[400,256]{1,0:T(8,128)(2,1)S(1)}, bf16[400,256]{1,0:T(8,128)(2,1)S(1)}, u32[]{:S(2)}, u32[]{:S(2)}) collective-permute-start(bf16[400,256]{1,0:T(8,128)(2,1)S(1)} %fusion.30), channel_id=1, source_target_pairs={{0,8},{4,12},{8,16},{12,20},{16,24},{20,28},{1,9},{5,13},{9,17},{1... | collective-permute-start | bytes 614408 | tf_op jit(solution)/shard_map/ppermute | solution.py:12
  56.5 8.8 %copy-start.9 = (f32[6]{0:T(128)S(1)}, f32[6]{0:T(128)}, u32[]{:S(2)}) copy-start(f32[6]{0:T(128)} %param.24) | copy-start | bytes 76
  60.1 8.4 %collective-permute-start.8 = (bf16[400,256]{1,0:T(8,128)(2,1)S(1)}, bf16[400,256]{1,0:T(8,128)(2,1)S(1)}, u32[]{:S(2)}, u32[]{:S(2)}) collective-permute-start(bf16[400,256]{1,0:T(8,128)(2,1)S(1)} %fusion.31), channel_id=1, source_target_pairs={{0,8},{4,12},{8,16},{12,20},{16,24},{20,28},{1,9},{5,13},{9,17},{1... | collective-permute-start | bytes 614408 | tf_op jit(solution)/shard_map/ppermute | solution.py:12
  68.9 7.7 %collective-permute-start.9 = (bf16[400,256]{1,0:T(8,128)(2,1)S(1)}, bf16[400,256]{1,0:T(8,128)(2,1)S(1)}, u32[]{:S(2)}, u32[]{:S(2)}) collective-permute-start(bf16[400,256]{1,0:T(8,128)(2,1)S(1)} %fusion.32), channel_id=1, source_target_pairs={{0,16},{4,20},{8,24},{12,28},{1,17},{5,21},{9,25},{13,29},{2,18},{... | collective-permute-start | bytes 614408 | tf_op jit(solution)/shard_map/ppermute | solution.py:12

commit v21 on v14

--- a/solution.py
+++ b/solution.py
@@ -104,8 +104,8 @@
         bit *= 2
     kept = kept.astype(jnp.bfloat16)
     other = lax.ppermute(kept, axis, [(i, i ^ 1) for i in range(count)])
-    both = jnp.concatenate([kept, other], axis=1)
-    return jnp.where(side == 0, both, jnp.concatenate([other, kept], axis=1))
+    triple = jnp.concatenate([other, kept, other], axis=1)
+    return lax.dynamic_slice_in_dim(triple, (1 - side) * half, 2 * half, axis=1)
 
 
 def segment_of(positions, lengths):

time: 97.5 us -> 97.6 us (level)
  no operation moved by 1% of the time
where the time goes in v21:
time: 97.6 us; the launch traced here: 96.9 us
  starting transfers between devices  30 us (31%)
  waiting for transfers between devices  23.1 us (24%)
  blocking collectives  17.7 us (18%)
  local copies, waits for them, and re-layouts  8.67 us (9%)
  other arithmetic  8.07 us (8%)
  matrix products  5.61 us (6%)
  between operations  3.72 us (4%)
    ppermute x5, starting transfers between devices, shifted(): return lax.ppermute(array, axis, pairs)  19.5 us
    all_to_all x1, blocking collectives, per_device(): lax.all_to_all(outgoing, 'seq', split_axis=0, concat_axis=0, tiled=True)  17.7 us
    ppermute x5, waiting for transfers between devices, shifted(): return lax.ppermute(array, axis, pairs)  7.68 us
    all_to_all x1, starting transfers between devices, per_device(): lax.all_to_all(slot_rows, 'seq', split_axis=0, concat_axis=0, tiled=True)  7.41 us
    ppermute x2, waiting for transfers between devices, exchange(): other = lax.ppermute(held, axis, [(i, i ^ bit) for i in range(count)])  6.25 us
    ppermute x1, waiting for transfers between devices, summed_columns(): kept = kept + lax.ppermute(kept, axis, [(i, i ^ bit) for i in range(count)])  5.06 us
    all_to_all x1, waiting for transfers between devices, per_device(): lax.all_to_all(slot_rows, 'seq', split_axis=0, concat_axis=0, tiled=True)  4.13 us
    unnamed x22, local copies, waits for them, and re-layouts  2.03 us
  transfers between devices with their start and end apart: 11, of which 8 were waited for; matrix products, arithmetic and copies ran while one was open for 10% of the time, Pallas kernels for 0%

profile of v21, /device:TPU:0, one launch (start us, length us, event | category | flops | bytes accessed | tf_op | source)
XLA Modules:
  0.0 96.9 jit_solution(13021904852701705391)
XLA Ops:
  0.0 7.4 %all-to-all-start = ((bf16[8,32,512]{2,1,0:T(8,128)(2,1)}), bf16[8,32,512]{2,1,0:T(8,128)(2,1)S(1)}, u32[]{:S(2)}, u32[]{:S(2)}) async-start(bf16[8,32,512]{2,1,0:T(8,128)(2,1)} %bitcast.53), calls=%async_computation | async-start | bytes 524288 | tf_op jit(solution)/shard_map/all_to_all | solution.py:176
  7.4 0.8 reduce-window.8
  8.3 0.7 compare_and_fusion.1
  9.0 1.0 sort.17
  10.2 0.6 fusion.59
  11.5 0.7 broadcast_compare_fusion.1
  12.2 4.1 %all-to-all-done = bf16[8,32,512]{2,1,0:T(8,128)(2,1)S(1)} async-done(((bf16[8,32,512]{2,1,0:T(8,128)(2,1)}), bf16[8,32,512]{2,1,0:T(8,128)(2,1)S(1)}, u32[]{:S(2)}, u32[]{:S(2)}) %all-to-all-start) | async-done | bytes 262176 | tf_op jit(solution)/shard_map/all_to_all | solution.py:176
  16.3 0.6 gather_fusion
  17.1 0.3 fusion.61
  17.7 1.6 %collective-permute-start = (bf16[256,512]{1,0:T(8,128)(2,1)S(1)}, bf16[256,512]{1,0:T(8,128)(2,1)S(1)}, u32[]{:S(2)}, u32[]{:S(2)}) collective-permute-start(bf16[256,512]{1,0:T(8,128)(2,1)S(1)} %bitcast_select_fusion), channel_id=1, source_target_pairs={{0,2},{1,3},{2,0},{3,1},{4,6},{5,7},{6,4},{7,5},{8,10},{9,11},{10,... | collective-permute-start | bytes 786440 | tf_op jit(solution)/shard_map/ppermute | solution.py:65
  19.3 1.3 %collective-permute-start.3 = (f32[256,256]{1,0:T(8,128)S(1)}, f32[256,256]{1,0:T(8,128)S(1)}, u32[]{:S(2)}, u32[]{:S(2)}) collective-permute-start(f32[256,256]{1,0:T(8,128)S(1)} %dynamic-slice_add_fusion), channel_id=1, source_target_pairs={{0,2},{1,3},{2,0},{3,1},{4,6},{5,7},{6,4},{7,5},{8,10},{9,11},{10,... | collective-permute-start | bytes 786440 | tf_op jit(solution)/shard_map/ppermute | solution.py:103
  20.6 6.2 %collective-permute-done = bf16[256,512]{1,0:T(8,128)(2,1)S(1)} collective-permute-done((bf16[256,512]{1,0:T(8,128)(2,1)S(1)}, bf16[256,512]{1,0:T(8,128)(2,1)S(1)}, u32[]{:S(2)}, u32[]{:S(2)}) %collective-permute-start) | collective-permute-done | bytes 262176 | tf_op jit(solution)/shard_map/ppermute | solution.py:65
  27.0 5.1 %collective-permute-done.3 = f32[256,256]{1,0:T(8,128)S(1)} collective-permute-done((f32[256,256]{1,0:T(8,128)S(1)}, f32[256,256]{1,0:T(8,128)S(1)}, u32[]{:S(2)}, u32[]{:S(2)}) %collective-permute-start.3) | collective-permute-done | bytes 262176 | tf_op jit(solution)/shard_map/ppermute | solution.py:103
  32.2 0.7 fusion.60
  35.4 0.6 slice.119
  36.3 1.1 %pad_maximum_fusion = bf16[256,2048]{1,0:T(8,128)(2,1)S(1)} fusion(bf16[256,1024]{1,0:T(8,128)(2,1)} %collective-permute-done.1, bf16[256,512]{1,0:T(8,128)(2,1)S(1)} %collective-permute-done, bf16[256,512]{1,0:T(8,128)(2,1)S(1)} %bitcast_select_fusion), kind=kLoop, calls=%fused_computation.17 | loop fusion | flops 3145728 | bytes 2097152 | tf_op jit(solution)/shard_map/concatenate | solution.py:66
  37.6 0.6 copy-done.6
  38.2 0.4 compare_select_fusion
  38.6 0.2 fusion.37
  38.8 0.2 slice_reduce_fusion
  39.1 0.7 convolution_convert_fusion.1
  39.8 0.7 copy-done.5
  40.5 0.7 divide_multiply_fusion.1
  41.3 3.3 %collective-permute-start.5 = (bf16[3,896]{1,0:T(4,128)(2,1)S(1)}, bf16[3,896]{1,0:T(4,128)(2,1)S(1)}, u32[]{:S(2)}, u32[]{:S(2)}) collective-permute-start(bf16[3,896]{1,0:T(4,128)(2,1)S(1)} %pad_maximum_fusion.3), channel_id=1, source_target_pairs={{0,4},{4,8},{8,12},{12,16},{16,20},{20,24},{24,28},{1,5},{5,9},{9,... | collective-permute-start | bytes 16136 | tf_op jit(solution)/shard_map/ppermute | solution.py:12
  44.7 0.6 broadcast_select_fusion.1
  45.5 0.5 collective-permute-done.5
  46.0 0.7 divide_multiply_fusion
  46.7 0.8 slice.145
  47.5 1.2 %copy.21 = f32[256,384]{0,1:T(8,128)S(1)} copy(f32[256,384]{1,0:T(8,128)} %slice.145) | data formatting | bytes 786432 | tf_op jit(solution)/shard_map/slice | solution.py:211
  48.7 0.5 fusion.42
  49.4 4.2 %collective-permute-start.7 = (bf16[400,256]{1,0:T(8,128)(2,1)S(1)}, bf16[400,256]{1,0:T(8,128)(2,1)S(1)}, u32[]{:S(2)}, u32[]{:S(2)}) collective-permute-start(bf16[400,256]{1,0:T(8,128)(2,1)S(1)} %fusion.30), channel_id=1, source_target_pairs={{0,4},{4,8},{8,12},{12,16},{16,20},{20,24},{24,28},{1,5},{5,9},{9,... | collective-permute-start | bytes 614408 | tf_op jit(solution)/shard_map/ppermute | solution.py:12
  53.7 2.5 %collective-permute-start.6 = (bf16[400,256]{1,0:T(8,128)(2,1)S(1)}, bf16[400,256]{1,0:T(8,128)(2,1)S(1)}, u32[]{:S(2)}, u32[]{:S(2)}) collective-permute-start(bf16[400,256]{1,0:T(8,128)(2,1)S(1)} %fusion.30), channel_id=1, source_target_pairs={{0,8},{4,12},{8,16},{12,20},{16,24},{20,28},{1,9},{5,13},{9,17},{1... | collective-permute-start | bytes 614408 | tf_op jit(solution)/shard_map/ppermute | solution.py:12
  56.1 0.4 fusion.39
  56.6 0.9 collective-permute-done.7
  57.5 2.4 %collective-permute-done.6 = bf16[400,256]{1,0:T(8,128)(2,1)S(1)} collective-permute-done((bf16[400,256]{1,0:T(8,128)(2,1)S(1)}, bf16[400,256]{1,0:T(8,128)(2,1)S(1)}, u32[]{:S(2)}, u32[]{:S(2)}) %collective-permute-start.6) | collective-permute-done | bytes 204832 | tf_op jit(solution)/shard_map/ppermute | solution.py:12
  60.0 0.2 fusion.31
  60.2 5.2 %collective-permute-start.8 = (bf16[400,256]{1,0:T(8,128)(2,1)S(1)}, bf16[400,256]{1,0:T(8,128)(2,1)S(1)}, u32[]{:S(2)}, u32[]{:S(2)}) collective-permute-start(bf16[400,256]{1,0:T(8,128)(2,1)S(1)} %fusion.31), channel_id=1, source_target_pairs={{0,8},{4,12},{8,16},{12,20},{16,24},{20,28},{1,9},{5,13},{9,17},{1... | collective-permute-start | bytes 614408 | tf_op jit(solution)/shard_map/ppermute | solution.py:12
  65.4 1.9 %fusion.8 = f32[256,6,64]{0,2,1:T(8,128)S(1)} fusion(f32[6,256]{1,0:T(8,128)S(1)} %bitcast.54, f32[256,256]{1,0:T(8,128)S(1)} %fusion.39, pred[256,256]{1,0:T(8,128)(4,1)S(1)} %fusion.36, f32[256,6,64]{0,2,1:T(8,128)S(1)} %bitcast.48, f32[6]{0:T(128)S(1)} %copy-done.9, f32[256,6]{0,1:T(8,128)S(1)} %compare_select_fusion), kind=kOutput, calls=%fused_computation.8 | convolution fusion | flops 303464448 | bytes 1126424 | tf_op jit(solution)/shard_map/hts,shp->thp/dot_general | solution.py:144
  67.2 1.4 %collective-permute-done.8 = bf16[400,256]{1,0:T(8,128)(2,1)S(1)} collective-permute-done((bf16[400,256]{1,0:T(8,128)(2,1)S(1)}, bf16[400,256]{1,0:T(8,128)(2,1)S(1)}, u32[]{:S(2)}, u32[]{:S(2)}) %collective-permute-start.8) | collective-permute-done | bytes 204832 | tf_op jit(solution)/shard_map/ppermute | solution.py:12
  69.0 4.4 %collective-permute-start.9 = (bf16[400,256]{1,0:T(8,128)(2,1)S(1)}, bf16[400,256]{1,0:T(8,128)(2,1)S(1)}, u32[]{:S(2)}, u32[]{:S(2)}) collective-permute-start(bf16[400,256]{1,0:T(8,128)(2,1)S(1)} %fusion.32), channel_id=1, source_target_pairs={{0,16},{4,20},{8,24},{12,28},{1,17},{5,21},{9,25},{13,29},{2,18},{... | collective-permute-start | bytes 614408 | tf_op jit(solution)/shard_map/ppermute | solution.py:12
  73.4 0.7 fusion.54
  74.1 2.5 %collective-permute-done.9 = bf16[400,256]{1,0:T(8,128)(2,1)S(1)} collective-permute-done((bf16[400,256]{1,0:T(8,128)(2,1)S(1)}, bf16[400,256]{1,0:T(8,128)(2,1)S(1)}, u32[]{:S(2)}, u32[]{:S(2)}) %collective-permute-start.9) | collective-permute-done | bytes 204832 | tf_op jit(solution)/shard_map/ppermute | solution.py:12
  76.7 0.5 fusion.13
  77.2 0.3 copy.23
  77.5 0.3 convert_element_type.109
  77.8 0.6 gather_fusion.1
  78.5 17.7 %all_to_all.10 = bf16[8,32,384]{2,1,0:T(8,128)(2,1)S(1)} all-to-all(bf16[8,32,384]{2,1,0:T(8,128)(2,1)S(1)} %broadcast_select_fusion), channel_id=1, replica_groups=mesh['seq'=8,'fsdp'=4] {'seq'}, dimensions={0} | all-to-all | bytes 393216 | tf_op jit(solution)/shard_map/all_to_all | solution.py:231
  96.2 0.7 copy.26
  (69 shorter events, 2.6 us)
Async XLA Ops:
  0.0 39.1 %copy-start = (bf16[2048,384]{1,0:T(8,128)(2,1)S(1)}, bf16[2048,384]{1,0:T(8,128)(2,1)}, u32[]{:S(2)}) copy-start(bf16[2048,384]{1,0:T(8,128)(2,1)} %param.16) | copy-start | bytes 4718596
  0.0 17.0 %copy-start.1 = (bf16[512,512]{1,0:T(8,128)(2,1)S(1)}, bf16[512,512]{1,0:T(8,128)(2,1)}, u32[]{:S(2)}) copy-start(bf16[512,512]{1,0:T(8,128)(2,1)} %param.18) | copy-start | bytes 1572868
  0.0 16.3 %all-to-all-start = ((bf16[8,32,512]{2,1,0:T(8,128)(2,1)}), bf16[8,32,512]{2,1,0:T(8,128)(2,1)S(1)}, u32[]{:S(2)}, u32[]{:S(2)}) async-start(bf16[8,32,512]{2,1,0:T(8,128)(2,1)} %bitcast.53), calls=%async_computation | async-start | bytes 524288 | tf_op jit(solution)/shard_map/all_to_all | solution.py:176
  7.4 10.1 %copy-start.7 = (f32[6]{0:T(128)S(1)}, f32[6]{0:T(128)}, u32[]{:S(2)}) copy-start(f32[6]{0:T(128)} %param.23) | copy-start | bytes 76
  16.9 3.7 %copy-start.4 = (f32[4,384]{1,0:T(4,128)S(1)}, f32[4,384]{1,0:T(4,128)}, u32[]{:S(2)}) copy-start(f32[4,384]{1,0:T(4,128)} %param.20) | copy-start | bytes 18436
  16.9 3.7 %copy-start.3 = (f32[4,512]{1,0:T(4,128)S(1)}, f32[4,512]{1,0:T(4,128)}, u32[]{:S(2)}) copy-start(f32[4,512]{1,0:T(4,128)} %param.21) | copy-start | bytes 24580
  17.4 14.9 %copy-start.2 = (s32[4]{0:T(128)S(1)}, s32[4]{0:T(128)}, u32[]{:S(2)}) copy-start(s32[4]{0:T(128)} %constant.96.clone) | copy-start | bytes 52
  17.4 1.9 %collective-permute-start.2 = (f32[256,256]{1,0:T(8,128)S(1)}, f32[256,256]{1,0:T(8,128)S(1)}, u32[]{:S(2)}, u32[]{:S(2)}) collective-permute-start(f32[256,256]{1,0:T(8,128)S(1)} %constant_dynamic-slice_fusion), channel_id=1, source_target_pairs={{0,1},{1,0},{2,3},{3,2},{4,5},{5,4},{6,7},{7,6},{8,9},{9,8},{10,11... | collective-permute-start | bytes 786440 | tf_op jit(solution)/shard_map/ppermute | solution.py:100
  17.7 9.2 %collective-permute-start = (bf16[256,512]{1,0:T(8,128)(2,1)S(1)}, bf16[256,512]{1,0:T(8,128)(2,1)S(1)}, u32[]{:S(2)}, u32[]{:S(2)}) collective-permute-start(bf16[256,512]{1,0:T(8,128)(2,1)S(1)} %bitcast_select_fusion), channel_id=1, source_target_pairs={{0,2},{1,3},{2,0},{3,1},{4,6},{5,7},{6,4},{7,5},{8,10},{9,11},{10,... | collective-permute-start | bytes 786440 | tf_op jit(solution)/shard_map/ppermute | solution.py:65
  19.3 12.8 %collective-permute-start.3 = (f32[256,256]{1,0:T(8,128)S(1)}, f32[256,256]{1,0:T(8,128)S(1)}, u32[]{:S(2)}, u32[]{:S(2)}) collective-permute-start(f32[256,256]{1,0:T(8,128)S(1)} %dynamic-slice_add_fusion), channel_id=1, source_target_pairs={{0,2},{1,3},{2,0},{3,1},{4,6},{5,7},{6,4},{7,5},{8,10},{9,11},{10,... | collective-permute-start | bytes 786440 | tf_op jit(solution)/shard_map/ppermute | solution.py:103
  26.9 9.4 %collective-permute-start.1 = (bf16[256,1024]{1,0:T(8,128)(2,1)S(1)}, bf16[256,1024]{1,0:T(8,128)(2,1)}, u32[]{:S(2)}, u32[]{:S(2)}) collective-permute-start(bf16[256,1024]{1,0:T(8,128)(2,1)S(1)} %pad_maximum_fusion.2), channel_id=1, source_target_pairs={{0,1},{1,0},{2,3},{3,2},{4,5},{5,4},{6,7},{7,6},{8,9},{9,8},{10,11... | collective-permute-start | bytes 1572872 | tf_op jit(solution)/shard_map/ppermute | solution.py:65
  32.1 4.1 %collective-permute-start.4 = (bf16[256,256]{1,0:T(8,128)(2,1)S(1)}, bf16[256,256]{1,0:T(8,128)(2,1)S(1)}, u32[]{:S(2)}, u32[]{:S(2)}) collective-permute-start(bf16[256,256]{1,0:T(8,128)(2,1)S(1)} %add_convert_fusion), channel_id=1, source_target_pairs={{0,1},{1,0},{2,3},{3,2},{4,5},{5,4},{6,7},{7,6},{8,9},{9,8},{10,11... | collective-permute-start | bytes 393224 | tf_op jit(solution)/shard_map/ppermute | solution.py:106
  37.5 0.8 copy-start.6
  37.5 0.8 copy-start.8
  39.1 1.4 %copy-start.5 = (bf16[2048,384]{1,0:T(8,128)(2,1)S(1)}, bf16[2048,384]{1,0:T(8,128)(2,1)}, u32[]{:S(2)}) copy-start(bf16[2048,384]{1,0:T(8,128)(2,1)} %param.17) | copy-start | bytes 4718596
  41.3 4.7 %collective-permute-start.5 = (bf16[3,896]{1,0:T(4,128)(2,1)S(1)}, bf16[3,896]{1,0:T(4,128)(2,1)S(1)}, u32[]{:S(2)}, u32[]{:S(2)}) collective-permute-start(bf16[3,896]{1,0:T(4,128)(2,1)S(1)} %pad_maximum_fusion.3), channel_id=1, source_target_pairs={{0,4},{4,8},{8,12},{12,16},{16,20},{20,24},{24,28},{1,5},{5,9},{9,... | collective-permute-start | bytes 16136 | tf_op jit(solution)/shard_map/ppermute | solution.py:12
  49.4 8.0 %collective-permute-start.7 = (bf16[400,256]{1,0:T(8,128)(2,1)S(1)}, bf16[400,256]{1,0:T(8,128)(2,1)S(1)}, u32[]{:S(2)}, u32[]{:S(2)}) collective-permute-start(bf16[400,256]{1,0:T(8,128)(2,1)S(1)} %fusion.30), channel_id=1, source_target_pairs={{0,4},{4,8},{8,12},{12,16},{16,20},{20,24},{24,28},{1,5},{5,9},{9,... | collective-permute-start | bytes 614408 | tf_op jit(solution)/shard_map/ppermute | solution.py:12
  53.7 6.2 %collective-permute-start.6 = (bf16[400,256]{1,0:T(8,128)(2,1)S(1)}, bf16[400,256]{1,0:T(8,128)(2,1)S(1)}, u32[]{:S(2)}, u32[]{:S(2)}) collective-permute-start(bf16[400,256]{1,0:T(8,128)(2,1)S(1)} %fusion.30), channel_id=1, source_target_pairs={{0,8},{4,12},{8,16},{12,20},{16,24},{20,28},{1,9},{5,13},{9,17},{1... | collective-permute-start | bytes 614408 | tf_op jit(solution)/shard_map/ppermute | solution.py:12
  56.5 8.8 %copy-start.9 = (f32[6]{0:T(128)S(1)}, f32[6]{0:T(128)}, u32[]{:S(2)}) copy-start(f32[6]{0:T(128)} %param.24) | copy-start | bytes 76
  60.2 8.4 %collective-permute-start.8 = (bf16[400,256]{1,0:T(8,128)(2,1)S(1)}, bf16[400,256]{1,0:T(8,128)(2,1)S(1)}, u32[]{:S(2)}, u32[]{:S(2)}) collective-permute-start(bf16[400,256]{1,0:T(8,128)(2,1)S(1)} %fusion.31), channel_id=1, source_target_pairs={{0,8},{4,12},{8,16},{12,20},{16,24},{20,28},{1,9},{5,13},{9,17},{1... | collective-permute-start | bytes 614408 | tf_op jit(solution)/shard_map/ppermute | solution.py:12
  69.0 7.7 %collective-permute-start.9 = (bf16[400,256]{1,0:T(8,128)(2,1)S(1)}, bf16[400,256]{1,0:T(8,128)(2,1)S(1)}, u32[]{:S(2)}, u32[]{:S(2)}) collective-permute-start(bf16[400,256]{1,0:T(8,128)(2,1)S(1)} %fusion.32), channel_id=1, source_target_pairs={{0,16},{4,20},{8,24},{12,28},{1,17},{5,21},{9,25},{13,29},{2,18},{... | collective-permute-start | bytes 614408 | tf_op jit(solution)/shard_map/ppermute | solution.py:12

commit v22 on v14

--- a/solution.py
+++ b/solution.py
@@ -176,7 +176,10 @@
     arrived = lax.all_to_all(slot_rows, "seq", split_axis=0, concat_axis=0, tiled=True)
     dealt_row = lax.dynamic_slice_in_dim(deal_order, own_index, 1, 0)[0]
     inverse = jnp.argsort(dealt_row)
-    stream_block = jnp.take(arrived, inverse, axis=0).reshape(tok_dev, tokens.shape[1])
+    chooser = (dealt_row[None, :] == jnp.arange(seq_count, dtype=dealt_row.dtype)[:, None]).astype(arrived.dtype)
+    stream_block = jnp.einsum(
+        "pm,mri->pri", chooser, arrived, preferred_element_type=jnp.float32
+    ).astype(arrived.dtype).reshape(tok_dev, tokens.shape[1])
     inner_dev = x_weight.shape[1]
     heads_dev = step_weight.shape[1]
     head_dim = inner_dev // heads_dev

time: 97.5 us -> 97.1 us (level)
  waiting for transfers between devices: 23.1 us -> 24.3 us
  other arithmetic: 8.04 us -> 6.93 us
    all_to_all x1, waiting for transfers between devices: 4.13 us -> 5.27 us  [per_device(): lax.all_to_all(slot_rows, 'seq', split_axis=0, concat_axis=0, tiled=True)]
  transfers between devices with their start and end apart: 11 -> 11, of which waited for: 8 -> 8; matrix products, arithmetic and copies ran while one was open for 10% -> 9% of each run, Pallas kernels for 0% -> 0%
where the time goes in v22:
time: 97.1 us; the launch traced here: 96.5 us
  starting transfers between devices  30 us (31%)
  waiting for transfers between devices  24.3 us (25%)
  blocking collectives  17.7 us (18%)
  local copies, waits for them, and re-layouts  7.98 us (8%)
  other arithmetic  6.93 us (7%)
  matrix products  5.87 us (6%)
  between operations  3.69 us (4%)
    ppermute x5, starting transfers between devices, shifted(): return lax.ppermute(array, axis, pairs)  19.5 us
    all_to_all x1, blocking collectives, per_device(): lax.all_to_all(outgoing, 'seq', split_axis=0, concat_axis=0, tiled=True)  17.7 us
    ppermute x5, waiting for transfers between devices, shifted(): return lax.ppermute(array, axis, pairs)  7.7 us
    all_to_all x1, starting transfers between devices, per_device(): lax.all_to_all(slot_rows, 'seq', split_axis=0, concat_axis=0, tiled=True)  7.41 us
    ppermute x2, waiting for transfers between devices, exchange(): other = lax.ppermute(held, axis, [(i, i ^ bit) for i in range(count)])  6.25 us
    all_to_all x1, waiting for transfers between devices, per_device(): lax.all_to_all(slot_rows, 'seq', split_axis=0, concat_axis=0, tiled=True)  5.27 us
    ppermute x1, waiting for transfers between devices, summed_columns(): kept = kept + lax.ppermute(kept, axis, [(i, i ^ bit) for i in range(count)])  5.06 us
    unnamed x22, local copies, waits for them, and re-layouts  2.03 us
  transfers between devices with their start and end apart: 11, of which 8 were waited for; matrix products, arithmetic and copies ran while one was open for 9% of the time, Pallas kernels for 0%

profile of v22, /device:TPU:0, one launch (start us, length us, event | category | flops | bytes accessed | tf_op | source)
XLA Modules:
  0.0 96.5 jit_solution(12773932105217796143)
XLA Ops:
  0.0 7.4 %all-to-all-start = ((bf16[8,32,512]{2,1,0:T(8,128)(2,1)}), bf16[8,32,512]{2,1,0:T(8,128)(2,1)S(1)}, u32[]{:S(2)}, u32[]{:S(2)}) async-start(bf16[8,32,512]{2,1,0:T(8,128)(2,1)} %bitcast.59), calls=%async_computation | async-start | bytes 524288 | tf_op jit(solution)/shard_map/all_to_all | solution.py:176
  7.4 0.8 reduce-window.8
  8.4 0.6 fusion.61
  9.6 0.7 compare_and_fusion
  10.4 0.7 broadcast_compare_fusion.1
  11.1 5.3 %all-to-all-done = bf16[8,32,512]{2,1,0:T(8,128)(2,1)S(1)} async-done(((bf16[8,32,512]{2,1,0:T(8,128)(2,1)}), bf16[8,32,512]{2,1,0:T(8,128)(2,1)S(1)}, u32[]{:S(2)}, u32[]{:S(2)}) %all-to-all-start) | async-done | bytes 262176 | tf_op jit(solution)/shard_map/all_to_all | solution.py:176
  16.3 0.3 convolution_convert_fusion
  16.7 0.3 fusion.63
  17.4 1.6 %collective-permute-start = (bf16[256,512]{1,0:T(8,128)(2,1)S(1)}, bf16[256,512]{1,0:T(8,128)(2,1)S(1)}, u32[]{:S(2)}, u32[]{:S(2)}) collective-permute-start(bf16[256,512]{1,0:T(8,128)(2,1)S(1)} %bitcast.49), channel_id=1, source_target_pairs={{0,2},{1,3},{2,0},{3,1},{4,6},{5,7},{6,4},{7,5},{8,10},{9,11},{10,... | collective-permute-start | bytes 786440 | tf_op jit(solution)/shard_map/ppermute | solution.py:65
  19.0 1.3 %collective-permute-start.3 = (f32[256,256]{1,0:T(8,128)S(1)}, f32[256,256]{1,0:T(8,128)S(1)}, u32[]{:S(2)}, u32[]{:S(2)}) collective-permute-start(f32[256,256]{1,0:T(8,128)S(1)} %dynamic-slice_add_fusion), channel_id=1, source_target_pairs={{0,2},{1,3},{2,0},{3,1},{4,6},{5,7},{6,4},{7,5},{8,10},{9,11},{10,... | collective-permute-start | bytes 786440 | tf_op jit(solution)/shard_map/ppermute | solution.py:103
  20.3 6.2 %collective-permute-done = bf16[256,512]{1,0:T(8,128)(2,1)S(1)} collective-permute-done((bf16[256,512]{1,0:T(8,128)(2,1)S(1)}, bf16[256,512]{1,0:T(8,128)(2,1)S(1)}, u32[]{:S(2)}, u32[]{:S(2)}) %collective-permute-start) | collective-permute-done | bytes 262176 | tf_op jit(solution)/shard_map/ppermute | solution.py:65
  26.7 5.1 %collective-permute-done.3 = f32[256,256]{1,0:T(8,128)S(1)} collective-permute-done((f32[256,256]{1,0:T(8,128)S(1)}, f32[256,256]{1,0:T(8,128)S(1)}, u32[]{:S(2)}, u32[]{:S(2)}) %collective-permute-start.3) | collective-permute-done | bytes 262176 | tf_op jit(solution)/shard_map/ppermute | solution.py:103
  31.9 0.6 fusion.62
  35.0 0.6 slice.119
  35.9 1.1 %pad_maximum_fusion = bf16[256,2048]{1,0:T(8,128)(2,1)S(1)} fusion(bf16[256,1024]{1,0:T(8,128)(2,1)} %collective-permute-done.1, bf16[256,512]{1,0:T(8,128)(2,1)S(1)} %collective-permute-done, bf16[256,512]{1,0:T(8,128)(2,1)S(1)} %bitcast.51), kind=kLoop, calls=%fused_computation.17 | loop fusion | flops 3145728 | bytes 2097152 | tf_op jit(solution)/shard_map/concatenate | solution.py:66
  37.2 0.6 copy-done.6
  37.8 0.4 compare_select_fusion
  38.2 0.2 fusion.36
  38.4 0.2 slice_reduce_fusion
  38.7 0.7 convolution_convert_fusion.2
  39.4 0.7 copy-done.5
  40.1 0.7 divide_multiply_fusion.1
  40.9 3.3 %collective-permute-start.5 = (bf16[3,896]{1,0:T(4,128)(2,1)S(1)}, bf16[3,896]{1,0:T(4,128)(2,1)S(1)}, u32[]{:S(2)}, u32[]{:S(2)}) collective-permute-start(bf16[3,896]{1,0:T(4,128)(2,1)S(1)} %pad_maximum_fusion.3), channel_id=1, source_target_pairs={{0,4},{4,8},{8,12},{12,16},{16,20},{20,24},{24,28},{1,5},{5,9},{9,... | collective-permute-start | bytes 16136 | tf_op jit(solution)/shard_map/ppermute | solution.py:12
  44.3 0.6 broadcast_select_fusion.1
  45.0 0.5 collective-permute-done.5
  45.6 0.7 divide_multiply_fusion
  46.3 0.8 slice.143
  47.1 1.2 %copy.30 = f32[256,384]{0,1:T(8,128)S(1)} copy(f32[256,384]{1,0:T(8,128)} %slice.143) | data formatting | bytes 786432 | tf_op jit(solution)/shard_map/slice | solution.py:214
  48.3 0.5 fusion.41
  48.8 0.2 fusion.30
  49.0 4.2 %collective-permute-start.7 = (bf16[400,256]{1,0:T(8,128)(2,1)S(1)}, bf16[400,256]{1,0:T(8,128)(2,1)S(1)}, u32[]{:S(2)}, u32[]{:S(2)}) collective-permute-start(bf16[400,256]{1,0:T(8,128)(2,1)S(1)} %fusion.30), channel_id=1, source_target_pairs={{0,4},{4,8},{8,12},{12,16},{16,20},{20,24},{24,28},{1,5},{5,9},{9,... | collective-permute-start | bytes 614408 | tf_op jit(solution)/shard_map/ppermute | solution.py:12
  53.2 2.5 %collective-permute-start.6 = (bf16[400,256]{1,0:T(8,128)(2,1)S(1)}, bf16[400,256]{1,0:T(8,128)(2,1)S(1)}, u32[]{:S(2)}, u32[]{:S(2)}) collective-permute-start(bf16[400,256]{1,0:T(8,128)(2,1)S(1)} %fusion.30), channel_id=1, source_target_pairs={{0,8},{4,12},{8,16},{12,20},{16,24},{20,28},{1,9},{5,13},{9,17},{1... | collective-permute-start | bytes 614408 | tf_op jit(solution)/shard_map/ppermute | solution.py:12
  55.7 0.4 fusion.38
  56.1 0.9 collective-permute-done.7
  57.0 2.4 %collective-permute-done.6 = bf16[400,256]{1,0:T(8,128)(2,1)S(1)} collective-permute-done((bf16[400,256]{1,0:T(8,128)(2,1)S(1)}, bf16[400,256]{1,0:T(8,128)(2,1)S(1)}, u32[]{:S(2)}, u32[]{:S(2)}) %collective-permute-start.6) | collective-permute-done | bytes 204832 | tf_op jit(solution)/shard_map/ppermute | solution.py:12
  59.6 0.2 fusion.31
  59.7 5.2 %collective-permute-start.8 = (bf16[400,256]{1,0:T(8,128)(2,1)S(1)}, bf16[400,256]{1,0:T(8,128)(2,1)S(1)}, u32[]{:S(2)}, u32[]{:S(2)}) collective-permute-start(bf16[400,256]{1,0:T(8,128)(2,1)S(1)} %fusion.31), channel_id=1, source_target_pairs={{0,8},{4,12},{8,16},{12,20},{16,24},{20,28},{1,9},{5,13},{9,17},{1... | collective-permute-start | bytes 614408 | tf_op jit(solution)/shard_map/ppermute | solution.py:12
  64.9 1.9 %fusion.8 = f32[256,6,64]{0,2,1:T(8,128)S(1)} fusion(f32[6,256]{1,0:T(8,128)S(1)} %bitcast.60, f32[256,256]{1,0:T(8,128)S(1)} %fusion.38, pred[256,256]{1,0:T(8,128)(4,1)S(1)} %fusion.35, f32[256,6,64]{0,2,1:T(8,128)S(1)} %bitcast.54, f32[6]{0:T(128)S(1)} %copy-done.9, f32[256,6]{0,1:T(8,128)S(1)} %compare_select_fusion), kind=kOutput, calls=%fused_computation.7 | convolution fusion | flops 303464448 | bytes 1126424 | tf_op jit(solution)/shard_map/hts,shp->thp/dot_general | solution.py:144
  66.8 1.4 %collective-permute-done.8 = bf16[400,256]{1,0:T(8,128)(2,1)S(1)} collective-permute-done((bf16[400,256]{1,0:T(8,128)(2,1)S(1)}, bf16[400,256]{1,0:T(8,128)(2,1)S(1)}, u32[]{:S(2)}, u32[]{:S(2)}) %collective-permute-start.8) | collective-permute-done | bytes 204832 | tf_op jit(solution)/shard_map/ppermute | solution.py:12
  68.5 4.4 %collective-permute-start.9 = (bf16[400,256]{1,0:T(8,128)(2,1)S(1)}, bf16[400,256]{1,0:T(8,128)(2,1)S(1)}, u32[]{:S(2)}, u32[]{:S(2)}) collective-permute-start(bf16[400,256]{1,0:T(8,128)(2,1)S(1)} %fusion.32), channel_id=1, source_target_pairs={{0,16},{4,20},{8,24},{12,28},{1,17},{5,21},{9,25},{13,29},{2,18},{... | collective-permute-start | bytes 614408 | tf_op jit(solution)/shard_map/ppermute | solution.py:12
  72.9 0.7 fusion.56
  73.7 2.5 %collective-permute-done.9 = bf16[400,256]{1,0:T(8,128)(2,1)S(1)} collective-permute-done((bf16[400,256]{1,0:T(8,128)(2,1)S(1)}, bf16[400,256]{1,0:T(8,128)(2,1)S(1)}, u32[]{:S(2)}, u32[]{:S(2)}) %collective-permute-start.9) | collective-permute-done | bytes 204832 | tf_op jit(solution)/shard_map/ppermute | solution.py:12
  76.2 0.5 fusion.13
  76.8 0.3 copy.32
  77.1 0.3 convert_element_type.114
  77.4 0.6 gather_fusion
  78.1 17.7 %all_to_all.10 = bf16[8,32,384]{2,1,0:T(8,128)(2,1)S(1)} all-to-all(bf16[8,32,384]{2,1,0:T(8,128)(2,1)S(1)} %broadcast_select_fusion), channel_id=1, replica_groups=mesh['seq'=8,'fsdp'=4] {'seq'}, dimensions={0} | all-to-all | bytes 393216 | tf_op jit(solution)/shard_map/all_to_all | solution.py:234
  95.8 0.7 copy.37
  (62 shorter events, 2.2 us)
Async XLA Ops:
  0.0 38.7 %copy-start = (bf16[2048,384]{1,0:T(8,128)(2,1)S(1)}, bf16[2048,384]{1,0:T(8,128)(2,1)}, u32[]{:S(2)}) copy-start(bf16[2048,384]{1,0:T(8,128)(2,1)} %param.16) | copy-start | bytes 4718596
  0.0 16.7 %copy-start.1 = (bf16[512,512]{1,0:T(8,128)(2,1)S(1)}, bf16[512,512]{1,0:T(8,128)(2,1)}, u32[]{:S(2)}) copy-start(bf16[512,512]{1,0:T(8,128)(2,1)} %param.18) | copy-start | bytes 1572868
  0.0 16.3 %all-to-all-start = ((bf16[8,32,512]{2,1,0:T(8,128)(2,1)}), bf16[8,32,512]{2,1,0:T(8,128)(2,1)S(1)}, u32[]{:S(2)}, u32[]{:S(2)}) async-start(bf16[8,32,512]{2,1,0:T(8,128)(2,1)} %bitcast.59), calls=%async_computation | async-start | bytes 524288 | tf_op jit(solution)/shard_map/all_to_all | solution.py:176
  7.4 9.7 %copy-start.7 = (f32[6]{0:T(128)S(1)}, f32[6]{0:T(128)}, u32[]{:S(2)}) copy-start(f32[6]{0:T(128)} %param.23) | copy-start | bytes 76
  16.6 3.7 %copy-start.4 = (f32[4,384]{1,0:T(4,128)S(1)}, f32[4,384]{1,0:T(4,128)}, u32[]{:S(2)}) copy-start(f32[4,384]{1,0:T(4,128)} %param.20) | copy-start | bytes 18436
  16.6 3.7 %copy-start.3 = (f32[4,512]{1,0:T(4,128)S(1)}, f32[4,512]{1,0:T(4,128)}, u32[]{:S(2)}) copy-start(f32[4,512]{1,0:T(4,128)} %param.21) | copy-start | bytes 24580
  17.0 14.9 %copy-start.2 = (s32[4]{0:T(128)S(1)}, s32[4]{0:T(128)}, u32[]{:S(2)}) copy-start(s32[4]{0:T(128)} %constant.82.clone) | copy-start | bytes 52
  17.1 1.9 %collective-permute-start.2 = (f32[256,256]{1,0:T(8,128)S(1)}, f32[256,256]{1,0:T(8,128)S(1)}, u32[]{:S(2)}, u32[]{:S(2)}) collective-permute-start(f32[256,256]{1,0:T(8,128)S(1)} %constant_dynamic-slice_fusion), channel_id=1, source_target_pairs={{0,1},{1,0},{2,3},{3,2},{4,5},{5,4},{6,7},{7,6},{8,9},{9,8},{10,11... | collective-permute-start | bytes 786440 | tf_op jit(solution)/shard_map/ppermute | solution.py:100
  17.4 9.2 %collective-permute-start = (bf16[256,512]{1,0:T(8,128)(2,1)S(1)}, bf16[256,512]{1,0:T(8,128)(2,1)S(1)}, u32[]{:S(2)}, u32[]{:S(2)}) collective-permute-start(bf16[256,512]{1,0:T(8,128)(2,1)S(1)} %bitcast.49), channel_id=1, source_target_pairs={{0,2},{1,3},{2,0},{3,1},{4,6},{5,7},{6,4},{7,5},{8,10},{9,11},{10,... | collective-permute-start | bytes 786440 | tf_op jit(solution)/shard_map/ppermute | solution.py:65
  19.0 12.8 %collective-permute-start.3 = (f32[256,256]{1,0:T(8,128)S(1)}, f32[256,256]{1,0:T(8,128)S(1)}, u32[]{:S(2)}, u32[]{:S(2)}) collective-permute-start(f32[256,256]{1,0:T(8,128)S(1)} %dynamic-slice_add_fusion), channel_id=1, source_target_pairs={{0,2},{1,3},{2,0},{3,1},{4,6},{5,7},{6,4},{7,5},{8,10},{9,11},{10,... | collective-permute-start | bytes 786440 | tf_op jit(solution)/shard_map/ppermute | solution.py:103
  26.6 9.3 %collective-permute-start.1 = (bf16[256,1024]{1,0:T(8,128)(2,1)S(1)}, bf16[256,1024]{1,0:T(8,128)(2,1)}, u32[]{:S(2)}, u32[]{:S(2)}) collective-permute-start(bf16[256,1024]{1,0:T(8,128)(2,1)S(1)} %pad_maximum_fusion.2), channel_id=1, source_target_pairs={{0,1},{1,0},{2,3},{3,2},{4,5},{5,4},{6,7},{7,6},{8,9},{9,8},{10,11... | collective-permute-start | bytes 1572872 | tf_op jit(solution)/shard_map/ppermute | solution.py:65
  31.8 4.0 %collective-permute-start.4 = (bf16[256,256]{1,0:T(8,128)(2,1)S(1)}, bf16[256,256]{1,0:T(8,128)(2,1)S(1)}, u32[]{:S(2)}, u32[]{:S(2)}) collective-permute-start(bf16[256,256]{1,0:T(8,128)(2,1)S(1)} %add_convert_fusion), channel_id=1, source_target_pairs={{0,1},{1,0},{2,3},{3,2},{4,5},{5,4},{6,7},{7,6},{8,9},{9,8},{10,11... | collective-permute-start | bytes 393224 | tf_op jit(solution)/shard_map/ppermute | solution.py:106
  37.1 0.8 copy-start.6
  37.1 0.8 copy-start.8
  38.7 1.4 %copy-start.5 = (bf16[2048,384]{1,0:T(8,128)(2,1)S(1)}, bf16[2048,384]{1,0:T(8,128)(2,1)}, u32[]{:S(2)}) copy-start(bf16[2048,384]{1,0:T(8,128)(2,1)} %param.17) | copy-start | bytes 4718596
  40.9 4.7 %collective-permute-start.5 = (bf16[3,896]{1,0:T(4,128)(2,1)S(1)}, bf16[3,896]{1,0:T(4,128)(2,1)S(1)}, u32[]{:S(2)}, u32[]{:S(2)}) collective-permute-start(bf16[3,896]{1,0:T(4,128)(2,1)S(1)} %pad_maximum_fusion.3), channel_id=1, source_target_pairs={{0,4},{4,8},{8,12},{12,16},{16,20},{20,24},{24,28},{1,5},{5,9},{9,... | collective-permute-start | bytes 16136 | tf_op jit(solution)/shard_map/ppermute | solution.py:12
  49.0 8.0 %collective-permute-start.7 = (bf16[400,256]{1,0:T(8,128)(2,1)S(1)}, bf16[400,256]{1,0:T(8,128)(2,1)S(1)}, u32[]{:S(2)}, u32[]{:S(2)}) collective-permute-start(bf16[400,256]{1,0:T(8,128)(2,1)S(1)} %fusion.30), channel_id=1, source_target_pairs={{0,4},{4,8},{8,12},{12,16},{16,20},{20,24},{24,28},{1,5},{5,9},{9,... | collective-permute-start | bytes 614408 | tf_op jit(solution)/shard_map/ppermute | solution.py:12
  53.2 6.2 %collective-permute-start.6 = (bf16[400,256]{1,0:T(8,128)(2,1)S(1)}, bf16[400,256]{1,0:T(8,128)(2,1)S(1)}, u32[]{:S(2)}, u32[]{:S(2)}) collective-permute-start(bf16[400,256]{1,0:T(8,128)(2,1)S(1)} %fusion.30), channel_id=1, source_target_pairs={{0,8},{4,12},{8,16},{12,20},{16,24},{20,28},{1,9},{5,13},{9,17},{1... | collective-permute-start | bytes 614408 | tf_op jit(solution)/shard_map/ppermute | solution.py:12
  56.1 8.8 %copy-start.9 = (f32[6]{0:T(128)S(1)}, f32[6]{0:T(128)}, u32[]{:S(2)}) copy-start(f32[6]{0:T(128)} %param.24) | copy-start | bytes 76
  59.7 8.4 %collective-permute-start.8 = (bf16[400,256]{1,0:T(8,128)(2,1)S(1)}, bf16[400,256]{1,0:T(8,128)(2,1)S(1)}, u32[]{:S(2)}, u32[]{:S(2)}) collective-permute-start(bf16[400,256]{1,0:T(8,128)(2,1)S(1)} %fusion.31), channel_id=1, source_target_pairs={{0,8},{4,12},{8,16},{12,20},{16,24},{20,28},{1,9},{5,13},{9,17},{1... | collective-permute-start | bytes 614408 | tf_op jit(solution)/shard_map/ppermute | solution.py:12
  68.5 7.7 %collective-permute-start.9 = (bf16[400,256]{1,0:T(8,128)(2,1)S(1)}, bf16[400,256]{1,0:T(8,128)(2,1)S(1)}, u32[]{:S(2)}, u32[]{:S(2)}) collective-permute-start(bf16[400,256]{1,0:T(8,128)(2,1)S(1)} %fusion.32), channel_id=1, source_target_pairs={{0,16},{4,20},{8,24},{12,28},{1,17},{5,21},{9,25},{13,29},{2,18},{... | collective-permute-start | bytes 614408 | tf_op jit(solution)/shard_map/ppermute | solution.py:12

commit v23 on v22

--- a/solution.py
+++ b/solution.py
@@ -230,7 +230,10 @@
     y_block = local_y + carry_in[:, :, None] * incoming
     gated = (y_block * gate).reshape(tok_dev, inner_dev).astype(jnp.bfloat16)
     ordered = gated.reshape(seq_count, piece_rows, inner_dev)
-    outgoing = jnp.take(ordered, dealt_row, axis=0)
+    picker = (dealt_row[:, None] == jnp.arange(seq_count, dtype=dealt_row.dtype)[None, :]).astype(jnp.bfloat16)
+    outgoing = jnp.einsum("mp,pri->mri", picker, ordered, preferred_element_type=jnp.float32).astype(
+        jnp.bfloat16
+    )
     returned = lax.all_to_all(outgoing, "seq", split_axis=0, concat_axis=0, tiled=True)
     return returned.reshape(tok_dev, inner_dev)
 

time: 97.1 us -> 97 us (level)
  other arithmetic: 6.93 us -> 5.49 us
  transfers between devices with their start and end apart: 11 -> 11, of which waited for: 8 -> 8; matrix products, arithmetic and copies ran while one was open for 9% -> 8% of each run, Pallas kernels for 0% -> 0%
where the time goes in v23:
time: 97 us; the launch traced here: 96.3 us
  starting transfers between devices  30 us (31%)
  waiting for transfers between devices  24.9 us (26%)
  blocking collectives  17.7 us (18%)
  local copies, waits for them, and re-layouts  8.38 us (9%)
  matrix products  6.12 us (6%)
  other arithmetic  5.49 us (6%)
  between operations  3.77 us (4%)
    ppermute x5, starting transfers between devices, shifted(): return lax.ppermute(array, axis, pairs)  19.5 us
    all_to_all x1, blocking collectives, per_device(): lax.all_to_all(outgoing, 'seq', split_axis=0, concat_axis=0, tiled=True)  17.7 us
    ppermute x5, waiting for transfers between devices, shifted(): return lax.ppermute(array, axis, pairs)  8.35 us
    all_to_all x1, starting transfers between devices, per_device(): lax.all_to_all(slot_rows, 'seq', split_axis=0, concat_axis=0, tiled=True)  7.41 us
    ppermute x2, waiting for transfers between devices, exchange(): other = lax.ppermute(held, axis, [(i, i ^ bit) for i in range(count)])  6.25 us
    all_to_all x1, waiting for transfers between devices, per_device(): lax.all_to_all(slot_rows, 'seq', split_axis=0, concat_axis=0, tiled=True)  5.2 us
    ppermute x1, waiting for transfers between devices, summed_columns(): kept = kept + lax.ppermute(kept, axis, [(i, i ^ bit) for i in range(count)])  5.06 us
    unnamed x22, local copies, waits for them, and re-layouts  2.03 us
  transfers between devices with their start and end apart: 11, of which 8 were waited for; matrix products, arithmetic and copies ran while one was open for 8% of the time, Pallas kernels for 0%

profile of v23, /device:TPU:0, one launch (start us, length us, event | category | flops | bytes accessed | tf_op | source)
XLA Modules:
  0.0 96.3 jit_solution(5441527397755993914)
XLA Ops:
  0.0 7.4 %all-to-all-start = ((bf16[8,32,512]{2,1,0:T(8,128)(2,1)}), bf16[8,32,512]{2,1,0:T(8,128)(2,1)S(1)}, u32[]{:S(2)}, u32[]{:S(2)}) async-start(bf16[8,32,512]{2,1,0:T(8,128)(2,1)} %bitcast.60), calls=%async_computation | async-start | bytes 524288 | tf_op jit(solution)/shard_map/all_to_all | solution.py:176
  7.4 0.8 reduce-window.8
  8.4 0.7 fusion.62
  9.7 0.7 fusion.59
  10.4 0.7 broadcast_compare_fusion.1
  11.1 5.2 %all-to-all-done = bf16[8,32,512]{2,1,0:T(8,128)(2,1)S(1)} async-done(((bf16[8,32,512]{2,1,0:T(8,128)(2,1)}), bf16[8,32,512]{2,1,0:T(8,128)(2,1)S(1)}, u32[]{:S(2)}, u32[]{:S(2)}) %all-to-all-start) | async-done | bytes 262176 | tf_op jit(solution)/shard_map/all_to_all | solution.py:176
  16.3 0.3 convolution_convert_fusion
  16.7 0.3 fusion.64
  17.4 1.6 %collective-permute-start = (bf16[256,512]{1,0:T(8,128)(2,1)S(1)}, bf16[256,512]{1,0:T(8,128)(2,1)S(1)}, u32[]{:S(2)}, u32[]{:S(2)}) collective-permute-start(bf16[256,512]{1,0:T(8,128)(2,1)S(1)} %bitcast.50), channel_id=1, source_target_pairs={{0,2},{1,3},{2,0},{3,1},{4,6},{5,7},{6,4},{7,5},{8,10},{9,11},{10,... | collective-permute-start | bytes 786440 | tf_op jit(solution)/shard_map/ppermute | solution.py:65
  19.0 1.3 %collective-permute-start.3 = (f32[256,256]{1,0:T(8,128)S(1)}, f32[256,256]{1,0:T(8,128)S(1)}, u32[]{:S(2)}, u32[]{:S(2)}) collective-permute-start(f32[256,256]{1,0:T(8,128)S(1)} %dynamic-slice_add_fusion), channel_id=1, source_target_pairs={{0,2},{1,3},{2,0},{3,1},{4,6},{5,7},{6,4},{7,5},{8,10},{9,11},{10,... | collective-permute-start | bytes 786440 | tf_op jit(solution)/shard_map/ppermute | solution.py:103
  20.3 6.2 %collective-permute-done = bf16[256,512]{1,0:T(8,128)(2,1)S(1)} collective-permute-done((bf16[256,512]{1,0:T(8,128)(2,1)S(1)}, bf16[256,512]{1,0:T(8,128)(2,1)S(1)}, u32[]{:S(2)}, u32[]{:S(2)}) %collective-permute-start) | collective-permute-done | bytes 262176 | tf_op jit(solution)/shard_map/ppermute | solution.py:65
  26.7 5.1 %collective-permute-done.3 = f32[256,256]{1,0:T(8,128)S(1)} collective-permute-done((f32[256,256]{1,0:T(8,128)S(1)}, f32[256,256]{1,0:T(8,128)S(1)}, u32[]{:S(2)}, u32[]{:S(2)}) %collective-permute-start.3) | collective-permute-done | bytes 262176 | tf_op jit(solution)/shard_map/ppermute | solution.py:103
  31.9 0.6 fusion.63
  35.1 0.6 slice.119
  35.9 1.1 %pad_maximum_fusion = bf16[256,2048]{1,0:T(8,128)(2,1)S(1)} fusion(bf16[256,1024]{1,0:T(8,128)(2,1)} %collective-permute-done.1, bf16[256,512]{1,0:T(8,128)(2,1)S(1)} %collective-permute-done, bf16[256,512]{1,0:T(8,128)(2,1)S(1)} %bitcast.52), kind=kLoop, calls=%fused_computation.17 | loop fusion | flops 3145728 | bytes 2097152 | tf_op jit(solution)/shard_map/concatenate | solution.py:66
  37.2 0.6 copy-done.6
  37.9 0.4 compare_select_fusion
  38.3 0.2 fusion.36
  38.4 0.2 slice_reduce_fusion
  38.7 0.7 convolution_convert_fusion.3
  39.4 0.7 copy-done.5
  40.1 0.7 divide_multiply_fusion.1
  40.9 3.3 %collective-permute-start.5 = (bf16[3,896]{1,0:T(4,128)(2,1)S(1)}, bf16[3,896]{1,0:T(4,128)(2,1)S(1)}, u32[]{:S(2)}, u32[]{:S(2)}) collective-permute-start(bf16[3,896]{1,0:T(4,128)(2,1)S(1)} %pad_maximum_fusion.3), channel_id=1, source_target_pairs={{0,4},{4,8},{8,12},{12,16},{16,20},{20,24},{24,28},{1,5},{5,9},{9,... | collective-permute-start | bytes 16136 | tf_op jit(solution)/shard_map/ppermute | solution.py:12
  44.3 0.6 broadcast_select_fusion
  44.9 0.2 copy.35
  45.1 0.4 collective-permute-done.5
  45.7 0.7 divide_multiply_fusion
  46.3 0.8 slice.141
  47.1 1.2 %copy.34 = f32[256,384]{0,1:T(8,128)S(1)} copy(f32[256,384]{1,0:T(8,128)} %slice.141) | data formatting | bytes 786432 | tf_op jit(solution)/shard_map/slice | solution.py:214
  48.3 0.5 fusion.41
  48.9 0.2 fusion.30
  49.0 4.2 %collective-permute-start.7 = (bf16[400,256]{1,0:T(8,128)(2,1)S(1)}, bf16[400,256]{1,0:T(8,128)(2,1)S(1)}, u32[]{:S(2)}, u32[]{:S(2)}) collective-permute-start(bf16[400,256]{1,0:T(8,128)(2,1)S(1)} %fusion.30), channel_id=1, source_target_pairs={{0,4},{4,8},{8,12},{12,16},{16,20},{20,24},{24,28},{1,5},{5,9},{9,... | collective-permute-start | bytes 614408 | tf_op jit(solution)/shard_map/ppermute | solution.py:12
  53.3 2.5 %collective-permute-start.6 = (bf16[400,256]{1,0:T(8,128)(2,1)S(1)}, bf16[400,256]{1,0:T(8,128)(2,1)S(1)}, u32[]{:S(2)}, u32[]{:S(2)}) collective-permute-start(bf16[400,256]{1,0:T(8,128)(2,1)S(1)} %fusion.30), channel_id=1, source_target_pairs={{0,8},{4,12},{8,16},{12,20},{16,24},{20,28},{1,9},{5,13},{9,17},{1... | collective-permute-start | bytes 614408 | tf_op jit(solution)/shard_map/ppermute | solution.py:12
  55.7 0.4 fusion.38
  56.2 0.9 collective-permute-done.7
  57.1 2.4 %collective-permute-done.6 = bf16[400,256]{1,0:T(8,128)(2,1)S(1)} collective-permute-done((bf16[400,256]{1,0:T(8,128)(2,1)S(1)}, bf16[400,256]{1,0:T(8,128)(2,1)S(1)}, u32[]{:S(2)}, u32[]{:S(2)}) %collective-permute-start.6) | collective-permute-done | bytes 204832 | tf_op jit(solution)/shard_map/ppermute | solution.py:12
  59.6 0.2 fusion.31
  59.8 5.2 %collective-permute-start.8 = (bf16[400,256]{1,0:T(8,128)(2,1)S(1)}, bf16[400,256]{1,0:T(8,128)(2,1)S(1)}, u32[]{:S(2)}, u32[]{:S(2)}) collective-permute-start(bf16[400,256]{1,0:T(8,128)(2,1)S(1)} %fusion.31), channel_id=1, source_target_pairs={{0,8},{4,12},{8,16},{12,20},{16,24},{20,28},{1,9},{5,13},{9,17},{1... | collective-permute-start | bytes 614408 | tf_op jit(solution)/shard_map/ppermute | solution.py:12
  65.0 1.9 %fusion.8 = f32[256,6,64]{0,2,1:T(8,128)S(1)} fusion(f32[6,256]{1,0:T(8,128)S(1)} %bitcast.61, f32[256,256]{1,0:T(8,128)S(1)} %fusion.38, pred[256,256]{1,0:T(8,128)(4,1)S(1)} %fusion.35, f32[256,6,64]{0,2,1:T(8,128)S(1)} %bitcast.55, f32[6]{0:T(128)S(1)} %copy-done.9, f32[256,6]{0,1:T(8,128)S(1)} %compare_select_fusion), kind=kOutput, calls=%fused_computation.6 | convolution fusion | flops 303464448 | bytes 1126424 | tf_op jit(solution)/shard_map/hts,shp->thp/dot_general | solution.py:144
  66.8 1.4 %collective-permute-done.8 = bf16[400,256]{1,0:T(8,128)(2,1)S(1)} collective-permute-done((bf16[400,256]{1,0:T(8,128)(2,1)S(1)}, bf16[400,256]{1,0:T(8,128)(2,1)S(1)}, u32[]{:S(2)}, u32[]{:S(2)}) %collective-permute-start.8) | collective-permute-done | bytes 204832 | tf_op jit(solution)/shard_map/ppermute | solution.py:12
  68.6 4.4 %collective-permute-start.9 = (bf16[400,256]{1,0:T(8,128)(2,1)S(1)}, bf16[400,256]{1,0:T(8,128)(2,1)S(1)}, u32[]{:S(2)}, u32[]{:S(2)}) collective-permute-start(bf16[400,256]{1,0:T(8,128)(2,1)S(1)} %fusion.32), channel_id=1, source_target_pairs={{0,16},{4,20},{8,24},{12,28},{1,17},{5,21},{9,25},{13,29},{2,18},{... | collective-permute-start | bytes 614408 | tf_op jit(solution)/shard_map/ppermute | solution.py:12
  73.0 3.2 %collective-permute-done.9 = bf16[400,256]{1,0:T(8,128)(2,1)S(1)} collective-permute-done((bf16[400,256]{1,0:T(8,128)(2,1)S(1)}, bf16[400,256]{1,0:T(8,128)(2,1)S(1)}, u32[]{:S(2)}, u32[]{:S(2)}) %collective-permute-start.9) | collective-permute-done | bytes 204832 | tf_op jit(solution)/shard_map/ppermute | solution.py:12
  76.3 0.5 fusion.13
  76.8 0.3 reshape.154
  77.1 0.5 copy.37
  77.7 0.3 convolution_convert_fusion.1
  78.0 17.7 %all_to_all.10 = bf16[8,32,384]{2,1,0:T(8,128)(2,1)S(1)} all-to-all(bf16[8,32,384]{2,1,0:T(8,128)(2,1)S(1)} %copy.38), channel_id=1, replica_groups=mesh['seq'=8,'fsdp'=4] {'seq'}, dimensions={0} | all-to-all | bytes 393216 | tf_op jit(solution)/shard_map/all_to_all | solution.py:237
  95.7 0.7 copy.45
  (60 shorter events, 2.0 us)
Async XLA Ops:
  0.0 38.7 %copy-start = (bf16[2048,384]{1,0:T(8,128)(2,1)S(1)}, bf16[2048,384]{1,0:T(8,128)(2,1)}, u32[]{:S(2)}) copy-start(bf16[2048,384]{1,0:T(8,128)(2,1)} %param.16) | copy-start | bytes 4718596
  0.0 16.7 %copy-start.1 = (bf16[512,512]{1,0:T(8,128)(2,1)S(1)}, bf16[512,512]{1,0:T(8,128)(2,1)}, u32[]{:S(2)}) copy-start(bf16[512,512]{1,0:T(8,128)(2,1)} %param.18) | copy-start | bytes 1572868
  0.0 16.3 %all-to-all-start = ((bf16[8,32,512]{2,1,0:T(8,128)(2,1)}), bf16[8,32,512]{2,1,0:T(8,128)(2,1)S(1)}, u32[]{:S(2)}, u32[]{:S(2)}) async-start(bf16[8,32,512]{2,1,0:T(8,128)(2,1)} %bitcast.60), calls=%async_computation | async-start | bytes 524288 | tf_op jit(solution)/shard_map/all_to_all | solution.py:176
  7.4 9.7 %copy-start.7 = (f32[6]{0:T(128)S(1)}, f32[6]{0:T(128)}, u32[]{:S(2)}) copy-start(f32[6]{0:T(128)} %param.23) | copy-start | bytes 76
  16.6 3.7 %copy-start.4 = (f32[4,384]{1,0:T(4,128)S(1)}, f32[4,384]{1,0:T(4,128)}, u32[]{:S(2)}) copy-start(f32[4,384]{1,0:T(4,128)} %param.20) | copy-start | bytes 18436
  16.6 3.7 %copy-start.3 = (f32[4,512]{1,0:T(4,128)S(1)}, f32[4,512]{1,0:T(4,128)}, u32[]{:S(2)}) copy-start(f32[4,512]{1,0:T(4,128)} %param.21) | copy-start | bytes 24580
  17.0 14.9 %copy-start.2 = (s32[4]{0:T(128)S(1)}, s32[4]{0:T(128)}, u32[]{:S(2)}) copy-start(s32[4]{0:T(128)} %constant.68.clone) | copy-start | bytes 52
  17.1 1.9 %collective-permute-start.2 = (f32[256,256]{1,0:T(8,128)S(1)}, f32[256,256]{1,0:T(8,128)S(1)}, u32[]{:S(2)}, u32[]{:S(2)}) collective-permute-start(f32[256,256]{1,0:T(8,128)S(1)} %constant_dynamic-slice_fusion), channel_id=1, source_target_pairs={{0,1},{1,0},{2,3},{3,2},{4,5},{5,4},{6,7},{7,6},{8,9},{9,8},{10,11... | collective-permute-start | bytes 786440 | tf_op jit(solution)/shard_map/ppermute | solution.py:100
  17.4 9.2 %collective-permute-start = (bf16[256,512]{1,0:T(8,128)(2,1)S(1)}, bf16[256,512]{1,0:T(8,128)(2,1)S(1)}, u32[]{:S(2)}, u32[]{:S(2)}) collective-permute-start(bf16[256,512]{1,0:T(8,128)(2,1)S(1)} %bitcast.50), channel_id=1, source_target_pairs={{0,2},{1,3},{2,0},{3,1},{4,6},{5,7},{6,4},{7,5},{8,10},{9,11},{10,... | collective-permute-start | bytes 786440 | tf_op jit(solution)/shard_map/ppermute | solution.py:65
  19.0 12.8 %collective-permute-start.3 = (f32[256,256]{1,0:T(8,128)S(1)}, f32[256,256]{1,0:T(8,128)S(1)}, u32[]{:S(2)}, u32[]{:S(2)}) collective-permute-start(f32[256,256]{1,0:T(8,128)S(1)} %dynamic-slice_add_fusion), channel_id=1, source_target_pairs={{0,2},{1,3},{2,0},{3,1},{4,6},{5,7},{6,4},{7,5},{8,10},{9,11},{10,... | collective-permute-start | bytes 786440 | tf_op jit(solution)/shard_map/ppermute | solution.py:103
  26.6 9.3 %collective-permute-start.1 = (bf16[256,1024]{1,0:T(8,128)(2,1)S(1)}, bf16[256,1024]{1,0:T(8,128)(2,1)}, u32[]{:S(2)}, u32[]{:S(2)}) collective-permute-start(bf16[256,1024]{1,0:T(8,128)(2,1)S(1)} %pad_maximum_fusion.2), channel_id=1, source_target_pairs={{0,1},{1,0},{2,3},{3,2},{4,5},{5,4},{6,7},{7,6},{8,9},{9,8},{10,11... | collective-permute-start | bytes 1572872 | tf_op jit(solution)/shard_map/ppermute | solution.py:65
  31.8 4.0 %collective-permute-start.4 = (bf16[256,256]{1,0:T(8,128)(2,1)S(1)}, bf16[256,256]{1,0:T(8,128)(2,1)S(1)}, u32[]{:S(2)}, u32[]{:S(2)}) collective-permute-start(bf16[256,256]{1,0:T(8,128)(2,1)S(1)} %add_convert_fusion), channel_id=1, source_target_pairs={{0,1},{1,0},{2,3},{3,2},{4,5},{5,4},{6,7},{7,6},{8,9},{9,8},{10,11... | collective-permute-start | bytes 393224 | tf_op jit(solution)/shard_map/ppermute | solution.py:106
  37.1 0.8 copy-start.6
  37.1 0.8 copy-start.8
  38.7 1.4 %copy-start.5 = (bf16[2048,384]{1,0:T(8,128)(2,1)S(1)}, bf16[2048,384]{1,0:T(8,128)(2,1)}, u32[]{:S(2)}) copy-start(bf16[2048,384]{1,0:T(8,128)(2,1)} %param.17) | copy-start | bytes 4718596
  40.9 4.7 %collective-permute-start.5 = (bf16[3,896]{1,0:T(4,128)(2,1)S(1)}, bf16[3,896]{1,0:T(4,128)(2,1)S(1)}, u32[]{:S(2)}, u32[]{:S(2)}) collective-permute-start(bf16[3,896]{1,0:T(4,128)(2,1)S(1)} %pad_maximum_fusion.3), channel_id=1, source_target_pairs={{0,4},{4,8},{8,12},{12,16},{16,20},{20,24},{24,28},{1,5},{5,9},{9,... | collective-permute-start | bytes 16136 | tf_op jit(solution)/shard_map/ppermute | solution.py:12
  49.0 8.0 %collective-permute-start.7 = (bf16[400,256]{1,0:T(8,128)(2,1)S(1)}, bf16[400,256]{1,0:T(8,128)(2,1)S(1)}, u32[]{:S(2)}, u32[]{:S(2)}) collective-permute-start(bf16[400,256]{1,0:T(8,128)(2,1)S(1)} %fusion.30), channel_id=1, source_target_pairs={{0,4},{4,8},{8,12},{12,16},{16,20},{20,24},{24,28},{1,5},{5,9},{9,... | collective-permute-start | bytes 614408 | tf_op jit(solution)/shard_map/ppermute | solution.py:12
  53.3 6.2 %collective-permute-start.6 = (bf16[400,256]{1,0:T(8,128)(2,1)S(1)}, bf16[400,256]{1,0:T(8,128)(2,1)S(1)}, u32[]{:S(2)}, u32[]{:S(2)}) collective-permute-start(bf16[400,256]{1,0:T(8,128)(2,1)S(1)} %fusion.30), channel_id=1, source_target_pairs={{0,8},{4,12},{8,16},{12,20},{16,24},{20,28},{1,9},{5,13},{9,17},{1... | collective-permute-start | bytes 614408 | tf_op jit(solution)/shard_map/ppermute | solution.py:12
  56.2 8.8 %copy-start.9 = (f32[6]{0:T(128)S(1)}, f32[6]{0:T(128)}, u32[]{:S(2)}) copy-start(f32[6]{0:T(128)} %param.24) | copy-start | bytes 76
  59.8 8.4 %collective-permute-start.8 = (bf16[400,256]{1,0:T(8,128)(2,1)S(1)}, bf16[400,256]{1,0:T(8,128)(2,1)S(1)}, u32[]{:S(2)}, u32[]{:S(2)}) collective-permute-start(bf16[400,256]{1,0:T(8,128)(2,1)S(1)} %fusion.31), channel_id=1, source_target_pairs={{0,8},{4,12},{8,16},{12,20},{16,24},{20,28},{1,9},{5,13},{9,17},{1... | collective-permute-start | bytes 614408 | tf_op jit(solution)/shard_map/ppermute | solution.py:12
  68.6 7.7 %collective-permute-start.9 = (bf16[400,256]{1,0:T(8,128)(2,1)S(1)}, bf16[400,256]{1,0:T(8,128)(2,1)S(1)}, u32[]{:S(2)}, u32[]{:S(2)}) collective-permute-start(bf16[400,256]{1,0:T(8,128)(2,1)S(1)} %fusion.32), channel_id=1, source_target_pairs={{0,16},{4,20},{8,24},{12,28},{1,17},{5,21},{9,25},{13,29},{2,18},{... | collective-permute-start | bytes 614408 | tf_op jit(solution)/shard_map/ppermute | solution.py:12
